TPU v7x, 32 devices: a whole 2x2x4 slice. The times are simulated.
32 devices in a mesh: rep: 4 (over z), sy: 2 (over y), sx: 4 (over x, core).
Axes of the slice: x: 2, y: 2, z: 4, core: 2. Of those that a mesh axis runs over, the one named last changes fastest.
Arguments:
- features: bfloat16 [4, 32, 64, 256], P('rep', 'sy', 'sx'), may hold values from -1.5 to 1.5
- cotangent: bfloat16 [4, 32, 64, 256], P('rep', 'sy', 'sx'), may hold values from -15 to 15
- gain_conv: float32 [256], replicated, may hold values from 0.25 to 1.75
- expand_weight: bfloat16 [256, 1024], replicated, may hold values from -0.375 to 0.375
- dw_kernel: float32 [1024, 9], replicated, may hold values from -2 to 2
- project_weight: bfloat16 [1024, 256], replicated, may hold values from -0.1875 to 0.1875
- gain_block: float32 [256], replicated, may hold values from 0.25 to 1.75
- block_inward: bfloat16 [256, 768], replicated, may hold values from -0.375 to 0.375
- block_outward: bfloat16 [256, 256], replicated, may hold values from -0.375 to 0.375
- gain_grid: float32 [256], replicated, may hold values from 0.25 to 1.75
- grid_inward: bfloat16 [256, 768], replicated, may hold values from -0.375 to 0.375
- grid_outward: bfloat16 [256, 256], replicated, may hold values from -0.375 to 0.375
Outputs:
- output_tokens: bfloat16 [4, 32, 64, 256], P('rep', 'sy', 'sx')
- token_grads: bfloat16 [4, 32, 64, 256], P('rep', 'sy', 'sx')
- grad_conv_gain: float32 [256], P('rep')
- grad_expand: float32 [256, 1024], P('rep')
- grad_kernel: float32 [1024, 9], P('rep')
- grad_project: float32 [1024, 256], P('rep')
- grad_block_gain: float32 [256], P('rep')
- grad_block_inward: float32 [256, 768], P('rep')
- grad_block_outward: float32 [256, 256], P('rep')
- grad_grid_gain: float32 [256], P('rep')
- grad_grid_inward: float32 [256, 768], P('rep')
- grad_grid_outward: float32 [256, 256], P('rep')
All inputs are finite; a program needn't handle non-finite values.
Results may differ from a plain program's by a relative error of at most 0.018.
Values may be sent and summed in bfloat16 or wider, within the bound.
No kernel may reach another device: no remote copies, remote signals or barrier semaphores. Data moves between devices by JAX's collectives and lax.ppermute only.
A program may use at most 64 MiB of HBM per device.

v0:
```python
import jax
import jax.numpy as jnp
from jax import lax
from jax.sharding import PartitionSpec as P

HEADS = 8
WIN = 8


EPSILON = 1e-05


def as_sent(value):

    def short(part):
        return part.astype(jnp.bfloat16) if part.dtype == jnp.float32 else part

    return jax.tree.map(short, value)


def extended_2(cells, sides, width):
    for axis, dim in sides:
        count = lax.axis_size(axis)
        ends = count - 1
        head = lax.slice_in_dim(cells, 0, width, axis=dim)
        tail = lax.slice_in_dim(cells, cells.shape[dim] - width, cells.shape[dim], axis=dim)
        cells = jnp.concatenate(
            [
                lax.ppermute(tail, axis, [(i, (i + 1) % count) for i in range(ends)]),
                cells,
                lax.ppermute(head, axis, [((i + 1) % count, i) for i in range(ends)]),
            ],
            axis=dim,
        )
    return cells


def widen(values):
    return lax.optimization_barrier(values).astype(jnp.float32)


def layer_norm(values, gain):
    row_mean = jnp.mean(values, axis=-1, keepdims=True)
    centred = values - row_mean
    variance = jnp.mean(centred * centred, axis=-1, keepdims=True)
    return centred * lax.rsqrt(variance + EPSILON) * gain


def project_rows(values, weight):
    leading = values.shape[:-1]
    flattened = values.reshape(-1, values.shape[-1])
    product = jnp.dot(flattened, weight, preferred_element_type=jnp.float32)
    return product.reshape(leading + (weight.shape[1],))


def outer_sum(left_side, right_side):
    left_flat = left_side.reshape(-1, left_side.shape[-1])
    right_flat = right_side.reshape(-1, right_side.shape[-1]).astype(jnp.bfloat16)
    return lax.dot_general(
        left_flat, right_flat, (((0,), (0,)), ((), ())), preferred_element_type=jnp.float32
    )


def to_windows(image, side):
    height, breadth, channels = image.shape
    blocks = image.reshape(height // side, side, breadth // side, side, channels)
    return blocks.transpose(0, 2, 1, 3, 4).reshape(-1, side * side, channels)


def from_windows(windows, height, breadth, side):
    channels = windows.shape[-1]
    blocks = windows.reshape(height // side, breadth // side, side, side, channels)
    return blocks.transpose(0, 2, 1, 3, 4).reshape(height, breadth, channels)


def to_grid(image, side):
    height, breadth, channels = image.shape
    blocks = image.reshape(side, height // side, side, breadth // side, channels)
    return blocks.transpose(1, 3, 0, 2, 4).reshape(-1, side * side, channels)


def from_grid(windows, height, breadth, side):
    channels = windows.shape[-1]
    blocks = windows.reshape(height // side, breadth // side, side, side, channels)
    return blocks.transpose(2, 0, 3, 1, 4).reshape(height, breadth, channels)


def window_attention(windows, weight, tap_in, heads):
    count, members, channels = windows.shape
    head_width = channels // heads
    qkv_rows = (project_rows(windows, weight) + tap_in).astype(jnp.bfloat16)
    queries = qkv_rows[..., :channels].reshape(count, members, heads, head_width)
    key_rows = qkv_rows[..., channels : 2 * channels].reshape(count, members, heads, head_width)
    value_rows = qkv_rows[..., 2 * channels :].reshape(count, members, heads, head_width)
    scores = jnp.einsum(
        "wqhd,wkhd->whqk", queries, key_rows, preferred_element_type=jnp.float32
    ) * head_width ** (-0.5)
    softmax_out = jax.nn.softmax(scores, axis=-1).astype(jnp.bfloat16)
    attended = jnp.einsum(
        "whqk,wkhd->wqhd", softmax_out, value_rows, preferred_element_type=jnp.float32
    )
    return attended.astype(jnp.bfloat16).reshape(count, members, channels)


def depthwise(extended, kernel):
    height = extended.shape[0] - 2
    breadth = extended.shape[1] - 2
    widened = widen(extended)
    summed = jnp.zeros((height, breadth, extended.shape[2]), jnp.float32)
    for tap_index in range(9):
        row_step, col_step = divmod(tap_index, 3)
        summed = (
            summed
            + widened[row_step : row_step + height, col_step : col_step + breadth]
            * kernel[:, tap_index]
        )
    return summed


def depthwise_back(grad_ext, kernel):
    height = grad_ext.shape[0] - 2
    breadth = grad_ext.shape[1] - 2
    summed = jnp.zeros((height, breadth, grad_ext.shape[2]), jnp.float32)
    for tap_index in range(9):
        row_step, col_step = divmod(tap_index, 3)
        summed = (
            summed
            + grad_ext[2 - row_step : 2 - row_step + height, 2 - col_step : 2 - col_step + breadth]
            * kernel[:, tap_index]
        )
    return summed


def swap_blocks(blocks):
    sy_count, sx_count, row_part, col_part, channels = blocks.shape
    flattened = blocks.reshape(sy_count * sx_count, row_part, col_part, channels)
    moved = lax.all_to_all(
        as_sent(flattened), ("sy", "sx"), split_axis=0, concat_axis=0, tiled=True
    ).astype(flattened.dtype)
    return moved.reshape(blocks.shape)


def to_exchanged(image):
    height, breadth, channels = image.shape
    sy_count = lax.axis_size("sy")
    sx_count = lax.axis_size("sx")
    blocks = image.reshape(height // sy_count, sy_count, breadth // sx_count, sx_count, channels)
    moved = swap_blocks(blocks.transpose(1, 3, 0, 2, 4))
    return moved.transpose(0, 2, 1, 3, 4).reshape(height, breadth, channels)


def to_home(image):
    height, breadth, channels = image.shape
    sy_count = lax.axis_size("sy")
    sx_count = lax.axis_size("sx")
    blocks = image.reshape(sy_count, height // sy_count, sx_count, breadth // sx_count, channels)
    moved = swap_blocks(blocks.transpose(0, 2, 1, 3, 4))
    return moved.transpose(2, 0, 3, 1, 4).reshape(height, breadth, channels)


def body(
    features,
    cotangent,
    gain_conv,
    expand_weight,
    dw_kernel,
    project_weight,
    gain_block,
    block_inward,
    block_outward,
    gain_grid,
    grid_inward,
    grid_outward,
):
    image = features[0]
    height, breadth, channels = image.shape
    expand_units = expand_weight.shape[1]
    window_count = height * breadth // (WIN * WIN)
    zero_width = jnp.zeros((height, breadth, channels), jnp.float32)
    zero_expand = jnp.zeros((height, breadth, expand_units), jnp.float32)
    zero_qkv = jnp.zeros((window_count, WIN * WIN, 3 * channels), jnp.float32)
    widened = image.astype(jnp.float32)

    def conv_front(wide_in, gain_in):
        return layer_norm(wide_in, gain_in).astype(jnp.bfloat16)

    normed, front_back = jax.vjp(conv_front, widened, gain_conv)

    def expand_fn(normed_in, tap_in):
        return jax.nn.gelu(project_rows(normed_in, expand_weight) + tap_in).astype(jnp.bfloat16)

    inner, expand_back = jax.vjp(expand_fn, normed, zero_expand)
    inner_ext = extended_2(inner, (("sy", 0), ("sx", 1)), 1)

    def conv_only(kernel_in):
        return depthwise(inner_ext, kernel_in)

    conv_out, kernel_back = jax.vjp(conv_only, dw_kernel)

    def conv_tail(conv_in, wide_in, tap_in):
        activated_in = jax.nn.gelu(conv_in).astype(jnp.bfloat16)
        return (wide_in + project_rows(activated_in, project_weight) + tap_in, activated_in)

    stream_one, tail_back, activated = jax.vjp(
        conv_tail, conv_out, widened, zero_width, has_aux=True
    )

    def block_layer(stream_in, gain_in, tap_in, tap_out):
        normed_two = layer_norm(stream_in, gain_in).astype(jnp.bfloat16)
        windows = to_windows(normed_two, WIN)
        attended = window_attention(windows, block_inward, tap_in, HEADS)
        attended_home = from_windows(attended, height, breadth, WIN)
        return (
            stream_in + project_rows(attended_home, block_outward) + tap_out,
            (windows, attended_home),
        )

    stream_two, block_back, block_saved = jax.vjp(
        block_layer, stream_one, gain_block, zero_qkv, zero_width, has_aux=True
    )

    def grid_front(stream_in, gain_in):
        return layer_norm(stream_in, gain_in).astype(jnp.bfloat16)

    normed_three, grid_front_back = jax.vjp(grid_front, stream_two, gain_grid)
    grid_windows = to_grid(to_exchanged(normed_three), WIN)

    def grid_core(windows_in, tap_in):
        return window_attention(windows_in, grid_inward, tap_in, HEADS)

    grid_attended, grid_core_back = jax.vjp(grid_core, grid_windows, zero_qkv)
    grid_home = to_home(from_grid(grid_attended, height, breadth, WIN))

    def grid_tail(stream_in, attended_in, tap_in):
        return (stream_in + project_rows(attended_in, grid_outward) + tap_in).astype(jnp.bfloat16)

    output_tile, grid_tail_back = jax.vjp(grid_tail, stream_two, grid_home, zero_width)
    d_stream_two, d_grid_home, tap_grid_out = grid_tail_back(cotangent[0])
    d_grid_attended = to_grid(to_exchanged(d_grid_home), WIN)
    d_grid_windows, tap_grid_in = grid_core_back(d_grid_attended)
    d_normed_three = to_home(from_grid(d_grid_windows, height, breadth, WIN))
    d_stream_extra, d_gain_grid = grid_front_back(d_normed_three)
    d_stream_two = d_stream_two + d_stream_extra
    d_stream_one, d_gain_block, tap_block_in, tap_block_out = block_back(d_stream_two)
    d_conv, d_wide_tail, tap_project = tail_back(d_stream_one)
    d_conv_ext = extended_2(d_conv, (("sy", 0), ("sx", 1)), 1)
    d_kernel = kernel_back(d_conv)[0]
    d_inner = depthwise_back(d_conv_ext, dw_kernel).astype(jnp.bfloat16)
    d_normed, tap_expand = expand_back(d_inner)
    d_wide_front, d_gain_conv = front_back(d_normed)
    token_grad = (d_wide_tail + d_wide_front).astype(jnp.bfloat16)
    local_grads = (
        d_gain_conv,
        outer_sum(normed, tap_expand),
        d_kernel,
        outer_sum(activated, tap_project),
        d_gain_block,
        outer_sum(block_saved[0], tap_block_in),
        outer_sum(block_saved[1], tap_block_out),
        d_gain_grid,
        outer_sum(grid_windows, tap_grid_in),
        outer_sum(grid_home, tap_grid_out),
    )
    whole_sums = lax.psum(
        (
            local_grads[0],
            local_grads[1],
            local_grads[2],
            local_grads[3],
            local_grads[4],
            local_grads[5],
            local_grads[6],
            local_grads[7],
            local_grads[8],
            local_grads[9],
        ),
        ("sy", "sx"),
    )
    summed = (
        lax.psum_scatter(whole_sums[0], "rep", scatter_dimension=0, tiled=True),
        lax.psum_scatter(whole_sums[1], "rep", scatter_dimension=0, tiled=True),
        lax.psum_scatter(whole_sums[2], "rep", scatter_dimension=0, tiled=True),
        lax.psum_scatter(whole_sums[3], "rep", scatter_dimension=0, tiled=True),
        lax.psum_scatter(whole_sums[4], "rep", scatter_dimension=0, tiled=True),
        lax.psum_scatter(whole_sums[5], "rep", scatter_dimension=0, tiled=True),
        lax.psum_scatter(whole_sums[6], "rep", scatter_dimension=0, tiled=True),
        lax.psum_scatter(whole_sums[7], "rep", scatter_dimension=0, tiled=True),
        lax.psum_scatter(whole_sums[8], "rep", scatter_dimension=0, tiled=True),
        lax.psum_scatter(whole_sums[9], "rep", scatter_dimension=0, tiled=True),
    )
    return (
        output_tile[None],
        token_grad[None],
        summed[0],
        summed[1],
        summed[2],
        summed[3],
        summed[4],
        summed[5],
        summed[6],
        summed[7],
        summed[8],
        summed[9],
    )


def solution(mesh):
    return jax.shard_map(
        body,
        mesh=mesh,
        in_specs=(
            P("rep", "sy", "sx", None),
            P("rep", "sy", "sx", None),
            P(),
            P(),
            P(),
            P(),
            P(),
            P(),
            P(),
            P(),
            P(),
            P(),
        ),
        out_specs=(
            P("rep", "sy", "sx", None),
            P("rep", "sy", "sx", None),
            P("rep"),
            P("rep", None),
            P("rep", None),
            P("rep", None),
            P("rep"),
            P("rep", None),
            P("rep", None),
            P("rep"),
            P("rep", None),
            P("rep", None),
        ),
        check_vma=False,
    )
```

profile of v0, /device:TPU:0, one launch (start us, length us, event | category | flops | bytes accessed | tf_op | source)
XLA Modules:
  0.0 337.4 jit_solution(8117348626632107201)
XLA Ops:
  9.5 2.4 multiply_convert_fusion.1
  13.3 4.9 %collective-permute-start = (bf16[1,16,1024]{2,1,0:T(8,128)(2,1)S(1)}, bf16[1,16,1024]{2,1,0:T(8,128)(2,1)S(1)}, u32[]{:S(2)}, u32[]{:S(2)}) collective-permute-start(bf16[1,16,1024]{2,1,0:T(8,128)(2,1)S(1)} %get-tuple-element.51), channel_id=1, source_target_pairs={{0,4},{1,5},{2,6},{3,7},{8,12},{9,13},{10,14},{11,15},{16,20},{17,... | collective-permute-start | bytes 98312 | tf_op jit(solution)/shard_map/ppermute | solution.py:29
  19.2 4.0 %all-to-all-start.2 = ((bf16[8,8,4,256]{3,1,2,0:T(8,128)(2,1)}), bf16[8,8,4,256]{3,1,2,0:T(8,128)(2,1)}, u32[]{:S(2)}, u32[]{:S(2)}) async-start(bf16[8,8,4,256]{3,1,2,0:T(8,128)(2,1)} %bitcast.44), calls=%async_computation.2 | async-start | bytes 262144 | tf_op jit(solution)/shard_map/all_to_all | solution.py:137
  24.6 3.0 collective-permute-start.2
  33.3 3.2 fusion.105
  42.3 6.7 %all-to-all-start = ((bf16[8,8,4,256]{3,1,2,0:T(8,128)(2,1)}), bf16[8,8,4,256]{3,1,2,0:T(8,128)(2,1)}, u32[]{:S(2)}, u32[]{:S(2)}) async-start(bf16[8,8,4,256]{3,1,2,0:T(8,128)(2,1)} %bitcast.24), calls=%async_computation | async-start | bytes 262144 | tf_op jit(solution)/shard_map/all_to_all | solution.py:137
  62.1 2.6 fusion.107
  77.4 7.9 %all_to_all.20 = bf16[8,8,4,256]{3,1,2,0:T(8,128)(2,1)S(1)} all-to-all(bf16[8,8,4,256]{3,1,2,0:T(8,128)(2,1)S(1)} %bitcast.291), channel_id=1, replica_groups=mesh['rep'=4,'sy'=2,'sx'=4] {'sy','sx'}, dimensions={0} | all-to-all | bytes 262144 | tf_op jit(solution)/shard_map/all_to_all | solution.py:137
  92.5 2.2 fusion.7
  96.8 2.1 reshape.413
  103.1 7.9 %all_to_all.21 = bf16[8,8,4,256]{3,1,2,0:T(8,128)(2,1)S(1)} all-to-all(bf16[8,8,4,256]{3,1,2,0:T(8,128)(2,1)S(1)} %bitcast.293), channel_id=1, replica_groups=mesh['rep'=4,'sy'=2,'sx'=4] {'sy','sx'}, dimensions={0} | all-to-all | bytes 262144 | tf_op jit(solution)/shard_map/all_to_all | solution.py:137
  127.0 2.5 convolution_convert_fusion.6
  131.2 2.4 convolution_convert_fusion.7
  136.8 2.1 fusion.109
  144.1 3.7 %multiply_reduce_fusion.8 = (f32[1024]{0:T(1024)S(1)}, f32[1024]{0:T(1024)S(1)}, f32[1024]{0:T(1024)S(1)}, f32[1024]{0:T(1024)S(1)}, f32[1024]{0:T(1024)S(1)}, /...) fusion(f32[18,18,1024]{2,1,0:T(8,128)S(1)} %convert_element_typ, ...), kind=kLoop, calls=%fused_computation.104 | loop fusion | flops 14408704 | bytes 11083776 | tf_op jit(solution)/shard_map/transpose(jvp())/reduce_sum | solution.py:114
  149.1 4.5 %collective-permute-start.4 = (f32[1,16,1024]{2,1,0:T(8,128)S(1)}, f32[1,16,1024]{2,1,0:T(8,128)S(1)}, u32[]{:S(2)}, u32[]{:S(2)}) collective-permute-start(f32[1,16,1024]{2,1,0:T(8,128)S(1)} %get-tuple-element.47), channel_id=1, source_target_pairs={{0,4},{1,5},{2,6},{3,7},{8,12},{9,13},{10,14},{11,15},{16,20},{17,... | collective-permute-start | bytes 196616 | tf_op jit(solution)/shard_map/ppermute | solution.py:29
  156.9 3.0 collective-permute-start.7
  168.5 15.5 %reduce-scatter.14.cloned.1.call-done = f32[64,768]{1,0:T(8,128)} async-done(((f32[256,768]{1,0:T(8,128)}), f32[64,768]{1,0:T(8,128)}) %reduce-scatter.14.cloned.1.call-update) | async-done | bytes 196624 | tf_op jit(solution)/shard_map/reduce_scatter | solution.py:285
  184.1 28.8 %reduce-scatter.12.cloned.1.call-done = f32[256,256]{1,0:T(8,128)} async-done(((f32[1024,256]{1,0:T(8,128)}), f32[256,256]{1,0:T(8,128)}) %reduce-scatter.12.cloned.1.call-update) | async-done | bytes 262160 | tf_op jit(solution)/shard_map/reduce_scatter | solution.py:283
  212.8 28.1 %reduce-scatter.8.cloned.1.call-done = f32[64,1024]{1,0:T(8,128)} async-done(((f32[256,1024]{1,0:T(8,128)}), f32[64,1024]{1,0:T(8,128)}) %reduce-scatter.8.cloned.1.call-update) | async-done | bytes 262160 | tf_op jit(solution)/shard_map/reduce_scatter | solution.py:281
  241.3 9.4 %all-reduce.20 = (f32[256]{0:T(256)S(1)}, f32[256]{0:T(256)S(1)}, f32[256]{0:T(256)S(1)}) all-reduce(f32[256]{0:T(256)S(1)} %get-tuple-element.25, f32[256]{0:T(256)S(1)} %copy-done.52, f32[256]{0:T(256)S(1)} %copy-done.51), channel_id=2, replica_groups=mesh['rep'=4,'sy'=2,'sx'=4] {'rep'}, use_global_device_ids=true, to_apply=%region_20.0.clone | all-reduce | flops 768 | bytes 6144
  250.9 10.5 %reduce-scatter.10.cloned.1.call-done = f32[256,9]{0,1:T(8,128)} async-done(((f32[1024,9]{0,1:T(8,128)}), f32[256,9]{0,1:T(8,128)}) %reduce-scatter.10.cloned.1.call-update) | async-done | bytes 9232 | tf_op jit(solution)/shard_map/reduce_scatter | solution.py:282
  261.5 23.7 %all-reduce.18 = (f32[64]{0:T(128)}, f32[256,9]{0,1:T(8,128)}, f32[64]{0:T(128)}, f32[64]{0:T(128)}) all-reduce(f32[64]{0:T(128)S(1)} %dynamic-slice.1, f32[256,9]{0,1:T(8,128)} %reduce-scatter.10.cloned.1.call-done, f32[64]{0:T(128)S(1)} %dynamic-slice.3, f32[64]{0:T(128)S(1)} %dynamic-slice.5), channel_id=1, replica_groups=mesh['rep'=4,'sy'=2,'sx'=4] {'sy','sx'}, use_global_device_ids=true, to_apply=%region_19.0 | all-reduce | flops 2496 | bytes 19968 | tf_op jit(solution)/shard_map/psum | solution.py:264
  286.0 35.9 %all-reduce.23.cloned.1.call-done = (f32[64,1024]{1,0:T(8,128)}, f32[256,256]{1,0:T(8,128)}, f32[64,768]{1,0:T(8,128)}, f32[64,256]{1,0:T(8,128)}, f32[64,768]{1,0:T(8,128)}, /*index=5*/f32[64,256]{1,0:T(8,128)}) async-done(((f32[64,1024]{1,0:T(8,128)}, f32[256,256]{1,0:T(8,128)}, f32[64,768]{1,0:T(8,128)}, f32[64,256]{1,0:T(8,128)}, f32[64,768]{1,0:T(8,128)}, /*index=5*/f32[64,256]{1,0:T(8,128)}), ...) | async-done | bytes 1048592 | tf_op jit(solution)/shard_map/psum | solution.py:264
  (271 shorter events, 104.4 us)
Async XLA Ops:
  11.8 15.8 %copy-start.45 = (f32[1024,9]{0,1:T(8,128)S(1)}, f32[1024,9]{0,1:T(8,128)}, u32[]{:S(2)}) copy-start(f32[1024,9]{0,1:T(8,128)} %param.16) | copy-start | bytes 110596
  11.8 11.3 %collective-permute-start.1 = (bf16[1,16,1024]{2,1,0:T(8,128)(2,1)S(1)}, bf16[1,16,1024]{2,1,0:T(8,128)(2,1)S(1)}, u32[]{:S(2)}, u32[]{:S(2)}) collective-permute-start(bf16[1,16,1024]{2,1,0:T(8,128)(2,1)S(1)} %get-tuple-element.52), channel_id=1, source_target_pairs={{4,0},{5,1},{6,2},{7,3},{12,8},{13,9},{14,10},{15,11},{20,16},{21,... | collective-permute-start | bytes 98312 | tf_op jit(solution)/shard_map/ppermute | solution.py:31
  13.3 9.9 %collective-permute-start = (bf16[1,16,1024]{2,1,0:T(8,128)(2,1)S(1)}, bf16[1,16,1024]{2,1,0:T(8,128)(2,1)S(1)}, u32[]{:S(2)}, u32[]{:S(2)}) collective-permute-start(bf16[1,16,1024]{2,1,0:T(8,128)(2,1)S(1)} %get-tuple-element.51), channel_id=1, source_target_pairs={{0,4},{1,5},{2,6},{3,7},{8,12},{9,13},{10,14},{11,15},{16,20},{17,... | collective-permute-start | bytes 98312 | tf_op jit(solution)/shard_map/ppermute | solution.py:29
  19.2 23.1 %all-to-all-start.2 = ((bf16[8,8,4,256]{3,1,2,0:T(8,128)(2,1)}), bf16[8,8,4,256]{3,1,2,0:T(8,128)(2,1)}, u32[]{:S(2)}, u32[]{:S(2)}) async-start(bf16[8,8,4,256]{3,1,2,0:T(8,128)(2,1)} %bitcast.44), calls=%async_computation.2 | async-start | bytes 262144 | tf_op jit(solution)/shard_map/all_to_all | solution.py:137
  23.3 4.5 %collective-permute-start.3 = (bf16[18,1,1024]{2,1,0:T(2,128)(2,1)S(1)}, bf16[18,1,1024]{2,1,0:T(2,128)(2,1)S(1)}, u32[]{:S(2)}, u32[]{:S(2)}) collective-permute-start(bf16[18,1,1024]{2,1,0:T(2,128)(2,1)S(1)} %get-tuple-element.50), channel_id=1, source_target_pairs={{1,0},{2,1},{3,2},{5,4},{6,5},{7,6},{9,8},{10,9},{11,10},{13,12},{... | collective-permute-start | bytes 110600 | tf_op jit(solution)/shard_map/ppermute | solution.py:31
  24.6 3.9 %collective-permute-start.2 = (bf16[18,1,1024]{2,1,0:T(2,128)(2,1)S(1)}, bf16[18,1,1024]{2,1,0:T(2,128)(2,1)S(1)}, u32[]{:S(2)}, u32[]{:S(2)}) collective-permute-start(bf16[18,1,1024]{2,1,0:T(2,128)(2,1)S(1)} %get-tuple-element.49), channel_id=1, source_target_pairs={{0,1},{1,2},{2,3},{4,5},{5,6},{6,7},{8,9},{9,10},{10,11},{12,13},{... | collective-permute-start | bytes 110600 | tf_op jit(solution)/shard_map/ppermute | solution.py:29
  42.3 12.4 %all-to-all-start = ((bf16[8,8,4,256]{3,1,2,0:T(8,128)(2,1)}), bf16[8,8,4,256]{3,1,2,0:T(8,128)(2,1)}, u32[]{:S(2)}, u32[]{:S(2)}) async-start(bf16[8,8,4,256]{3,1,2,0:T(8,128)(2,1)} %bitcast.24), calls=%async_computation | async-start | bytes 262144 | tf_op jit(solution)/shard_map/all_to_all | solution.py:137
  49.1 119.4 %reduce-scatter.16.cloned.1.call-start = ((), (), s32[]{:S(2)}) async-start(), calls=%async_computation.15 | async-start | bytes 327680 | tf_op jit(solution)/shard_map/reduce_scatter | solution.py:286
  77.1 12.6 %copy-start.9 = (bf16[1,16,16,256]{3,2,1,0:T(8,128)(2,1)S(1)}, bf16[1,16,16,256]{3,2,1,0:T(8,128)(2,1)}, u32[]{:S(2)}) copy-start(bf16[1,16,16,256]{3,2,1,0:T(8,128)(2,1)} %param.13) | copy-start | bytes 393220
  92.2 76.3 %reduce-scatter.20.cloned.1.call-start = ((), (), s32[]{:S(2)}) async-start(), calls=%async_computation.17 | async-start | bytes 327680 | tf_op jit(solution)/shard_map/reduce_scatter | solution.py:289
  94.7 22.0 %copy-start.3 = (bf16[4,64,768]{2,1,0:T(8,128)(2,1)S(1)}, bf16[4,64,768]{2,1,0:T(8,128)(2,1)}, u32[]{:S(2)}) copy-start(bf16[4,64,768]{2,1,0:T(8,128)(2,1)} %copy-done.2) | copy-start | bytes 1179652
  115.3 53.2 %reduce-scatter.18.cloned.1.call-start = ((), (), s32[]{:S(2)}) async-start(), calls=%async_computation.16 | async-start | bytes 983040 | tf_op jit(solution)/shard_map/reduce_scatter | solution.py:288
  117.9 66.2 %reduce-scatter.14.cloned.1.call-start = ((), (), s32[]{:S(2)}) async-start(), calls=%async_computation.14 | async-start | bytes 983040 | tf_op jit(solution)/shard_map/reduce_scatter | solution.py:285
  138.9 73.9 %reduce-scatter.12.cloned.1.call-start = ((), (), s32[]{:S(2)}) async-start(), calls=%async_computation.13 | async-start | bytes 1310720 | tf_op jit(solution)/shard_map/reduce_scatter | solution.py:283
  143.9 16.0 %copy-start.48 = (f32[256]{0:T(256)S(1)}, f32[256]{0:T(256)}, u32[]{:S(2)}) copy-start(f32[256]{0:T(256)} %param.14) | copy-start | bytes 3076
  144.0 97.0 %reduce-scatter.8.cloned.1.call-start = ((), (), s32[]{:S(2)}) async-start(), calls=%async_computation.11 | async-start | bytes 1310720 | tf_op jit(solution)/shard_map/reduce_scatter | solution.py:281
  147.8 6.2 %collective-permute-start.5 = (f32[1,16,1024]{2,1,0:T(8,128)S(1)}, f32[1,16,1024]{2,1,0:T(8,128)S(1)}, u32[]{:S(2)}, u32[]{:S(2)}) collective-permute-start(f32[1,16,1024]{2,1,0:T(8,128)S(1)} %get-tuple-element.48), channel_id=1, source_target_pairs={{4,0},{5,1},{6,2},{7,3},{12,8},{13,9},{14,10},{15,11},{20,16},{21,... | collective-permute-start | bytes 196616 | tf_op jit(solution)/shard_map/ppermute | solution.py:31
  149.1 6.4 %collective-permute-start.4 = (f32[1,16,1024]{2,1,0:T(8,128)S(1)}, f32[1,16,1024]{2,1,0:T(8,128)S(1)}, u32[]{:S(2)}, u32[]{:S(2)}) collective-permute-start(f32[1,16,1024]{2,1,0:T(8,128)S(1)} %get-tuple-element.47), channel_id=1, source_target_pairs={{0,4},{1,5},{2,6},{3,7},{8,12},{9,13},{10,14},{11,15},{16,20},{17,... | collective-permute-start | bytes 196616 | tf_op jit(solution)/shard_map/ppermute | solution.py:29
  155.6 4.5 %collective-permute-start.6 = (f32[18,1,1024]{2,1,0:T(1,128)S(1)}, f32[18,1,1024]{2,1,0:T(1,128)S(1)}, u32[]{:S(2)}, u32[]{:S(2)}) collective-permute-start(f32[18,1,1024]{2,1,0:T(1,128)S(1)} %get-tuple-element.45), channel_id=1, source_target_pairs={{1,0},{2,1},{3,2},{5,4},{6,5},{7,6},{9,8},{10,9},{11,10},{13,12},{... | collective-permute-start | bytes 221192 | tf_op jit(solution)/shard_map/ppermute | solution.py:31
  156.9 3.9 %collective-permute-start.7 = (f32[18,1,1024]{2,1,0:T(1,128)S(1)}, f32[18,1,1024]{2,1,0:T(1,128)S(1)}, u32[]{:S(2)}, u32[]{:S(2)}) collective-permute-start(f32[18,1,1024]{2,1,0:T(1,128)S(1)} %get-tuple-element.46), channel_id=1, source_target_pairs={{0,1},{1,2},{2,3},{4,5},{5,6},{6,7},{8,9},{9,10},{10,11},{12,13},{... | collective-permute-start | bytes 221192 | tf_op jit(solution)/shard_map/ppermute | solution.py:29
  164.6 96.8 %reduce-scatter.10.cloned.1.call-start = ((), (), s32[]{:S(2)}) async-start(), calls=%async_computation.12 | async-start | bytes 81920 | tf_op jit(solution)/shard_map/reduce_scatter | solution.py:282
  167.6 73.6 %copy-start.51 = (f32[256]{0:T(256)S(1)}, f32[256]{0:T(256)}, u32[]{:S(2)}) copy-start(f32[256]{0:T(256)} %get-tuple-element.21) | copy-start | bytes 3076
  167.6 73.6 %copy-start.52 = (f32[256]{0:T(256)S(1)}, f32[256]{0:T(256)}, u32[]{:S(2)}) copy-start(f32[256]{0:T(256)} %get-tuple-element.23) | copy-start | bytes 3076
  167.6 154.2 %all-reduce.23.cloned.1.call-start = ((), (), s32[]{:S(2)}) async-start(), calls=%async_computation.18 | async-start | bytes 2097152 | tf_op jit(solution)/shard_map/psum | solution.py:264
  (48 other events, 132.7 us)
Sparse Core Ops, SparseCore 0:
  92.4 20.0 reduce-scatter.15
  115.4 20.1 reduce-scatter.19
  137.9 21.5 reduce-scatter.17
  161.6 22.3 reduce-scatter.13
  186.2 26.5 reduce-scatter.11
  215.1 25.7 reduce-scatter.7
  243.7 17.6 reduce-scatter.9
  265.7 56.1 all-reduce.22
where the time goes:
time: 339 us; the launch traced here: 337 us
  waiting for transfers between devices  124 us (37%)
  local copies, waits for them, and re-layouts  51.3 us (15%)
  blocking collectives  48.9 us (14%)
  matrix products  42.2 us (12%)
  starting transfers between devices  32 us (9%)
  other arithmetic  23 us (7%)
  between operations  16 us (5%)
    psum x1, waiting for transfers between devices, body(): lax.psum((local_grads[0], local_grads[1], local_grads[2], local_grads[3],...  35.9 us
    reduce_scatter x1, waiting for transfers between devices, body(): lax.psum_scatter(whole_sums[3], 'rep', scatter_dimension=0, tiled=True)  28.8 us
    reduce_scatter x1, waiting for transfers between devices, body(): lax.psum_scatter(whole_sums[1], 'rep', scatter_dimension=0, tiled=True)  28.1 us
    psum x1, blocking collectives, body(): lax.psum((local_grads[0], local_grads[1], local_grads[2], local_grads[3],...  23.7 us
    all_to_all x2, blocking collectives, swap_blocks(): lax.all_to_all(as_sent(flattened), ('sy', 'sx'), split_axis=0, concat_axi...  15.8 us
    reduce_scatter x1, waiting for transfers between devices, body(): lax.psum_scatter(whole_sums[5], 'rep', scatter_dimension=0, tiled=True)  15.5 us
    ppermute x4, starting transfers between devices, extended_2(): lax.ppermute(tail, axis, [(i, (i + 1) % count) for i in range(ends)])  15.5 us
    unnamed x118, local copies, waits for them, and re-layouts  11.9 us
  transfers between devices with their start and end apart: 18, of which 10 were waited for; matrix products, arithmetic and copies ran while one was open for 21% of the time, Pallas kernels for 0%

commit v1 on v0

--- a/solution.py
+++ b/solution.py
@@ -156,6 +156,25 @@
     blocks = image.reshape(sy_count, height // sy_count, sx_count, breadth // sx_count, channels)
     moved = swap_blocks(blocks.transpose(0, 2, 1, 3, 4))
     return moved.transpose(2, 0, 3, 1, 4).reshape(height, breadth, channels)
+
+
+def reduce_grads(grads, groups):
+    parts = lax.axis_size("rep")
+    results = [None] * len(grads)
+    for group in groups:
+        pieces = [grads[i].reshape(parts, -1) for i in group]
+        sizes = [piece.shape[1] for piece in pieces]
+        width = sum(sizes)
+        padded = -(-width // 1024) * 1024
+        packed = jnp.concatenate(pieces + [jnp.zeros((parts, padded - width), jnp.float32)], axis=1)
+        whole = lax.psum(packed, ("rep", "sy", "sx"))
+        total = lax.dynamic_index_in_dim(whole, lax.axis_index("rep"), 0, keepdims=False)
+        offset = 0
+        for index, size in zip(group, sizes):
+            shape = (grads[index].shape[0] // parts,) + grads[index].shape[1:]
+            results[index] = total[offset : offset + size].reshape(shape)
+            offset += size
+    return tuple(results)
 
 
 def body(
@@ -261,33 +280,7 @@
         outer_sum(grid_windows, tap_grid_in),
         outer_sum(grid_home, tap_grid_out),
     )
-    whole_sums = lax.psum(
-        (
-            local_grads[0],
-            local_grads[1],
-            local_grads[2],
-            local_grads[3],
-            local_grads[4],
-            local_grads[5],
-            local_grads[6],
-            local_grads[7],
-            local_grads[8],
-            local_grads[9],
-        ),
-        ("sy", "sx"),
-    )
-    summed = (
-        lax.psum_scatter(whole_sums[0], "rep", scatter_dimension=0, tiled=True),
-        lax.psum_scatter(whole_sums[1], "rep", scatter_dimension=0, tiled=True),
-        lax.psum_scatter(whole_sums[2], "rep", scatter_dimension=0, tiled=True),
-        lax.psum_scatter(whole_sums[3], "rep", scatter_dimension=0, tiled=True),
-        lax.psum_scatter(whole_sums[4], "rep", scatter_dimension=0, tiled=True),
-        lax.psum_scatter(whole_sums[5], "rep", scatter_dimension=0, tiled=True),
-        lax.psum_scatter(whole_sums[6], "rep", scatter_dimension=0, tiled=True),
-        lax.psum_scatter(whole_sums[7], "rep", scatter_dimension=0, tiled=True),
-        lax.psum_scatter(whole_sums[8], "rep", scatter_dimension=0, tiled=True),
-        lax.psum_scatter(whole_sums[9], "rep", scatter_dimension=0, tiled=True),
-    )
+    summed = reduce_grads(local_grads, ((0, 1, 2, 3, 4, 5, 6, 7, 8, 9),))
     return (
         output_tile[None],
         token_grad[None],

time: 339 us -> 360 us (1.062)
  local copies, waits for them, and re-layouts: 51.3 us -> 101 us
  blocking collectives: 48.9 us -> 0 us
  waiting for transfers between devices: 124 us -> 144 us
  matrix products: 42.2 us -> 33.1 us
  starting transfers between devices: 32 us -> 40.4 us
    psum x1, waiting for transfers between devices: 35.9 us -> 143 us  [reduce_grads(): whole = lax.psum(packed, ('rep', 'sy', 'sx'))]
    reduce_scatter x7 -> x0, waiting for transfers between devices: 83 us -> none  [the longest x1 28.8 us: body(): lax.psum_scatter(whole_sums[3], 'rep', scatter_dimension=0, tiled=True)]
    unnamed x118 -> x159, local copies, waits for them, and re-layouts: 11.9 us -> 36.1 us
    psum x1 -> x0, blocking collectives: 23.7 us -> none  [body(): lax.psum((local_grads[0], local_grads[1], local_grads[2], local_grads[3],...]
    reshape x0 -> x17, local copies, waits for them, and re-layouts: none -> 17.7 us  [the longest x10 13.3 us: reduce_grads(): pieces = [grads[i].reshape(parts, -1) for i in group]]
    all_to_all x2 -> x0, blocking collectives: 15.8 us -> none  [swap_blocks(): lax.all_to_all(as_sent(flattened), ('sy', 'sx'), split_axis=0, concat_axi...]
    unnamed x1 -> x0, blocking collectives: 9.4 us -> none
    slice x0 -> x5, local copies, waits for them, and re-layouts: none -> 9.22 us  [reduce_grads(): results[index] = total[offset:offset + size].reshape(shape)]
  transfers between devices with their start and end apart: 18 -> 13, of which waited for: 10 -> 3; matrix products, arithmetic and copies ran while one was open for 21% -> 15% of each run, Pallas kernels for 0% -> 0%
where the time goes in v1:
time: 360 us; the launch traced here: 358 us
  waiting for transfers between devices  144 us (40%)
  local copies, waits for them, and re-layouts  101 us (28%)
  starting transfers between devices  40.4 us (11%)
  matrix products  33.1 us (9%)
  other arithmetic  24.4 us (7%)
  between operations  15.3 us (4%)
    psum x1, waiting for transfers between devices, reduce_grads(): whole = lax.psum(packed, ('rep', 'sy', 'sx'))  143 us
    unnamed x159, local copies, waits for them, and re-layouts  36.1 us
    all_to_all x4, starting transfers between devices, swap_blocks(): lax.all_to_all(as_sent(flattened), ('sy', 'sx'), split_axis=0, concat_axi...  18.9 us
    ppermute x4, starting transfers between devices, extended_2(): lax.ppermute(tail, axis, [(i, (i + 1) % count) for i in range(ends)])  16.1 us
    reshape x10, local copies, waits for them, and re-layouts, reduce_grads(): pieces = [grads[i].reshape(parts, -1) for i in group]  13.3 us
    slice x5, local copies, waits for them, and re-layouts, reduce_grads(): results[index] = total[offset:offset + size].reshape(shape)  9.22 us
    dot_general x6, matrix products, window_attention(): jnp.einsum('whqk,wkhd->wqhd', softmax_out, value_rows, preferred_element_...  9.06 us
    dot_general x12, matrix products, project_rows(): product = jnp.dot(flattened, weight, preferred_element_type=jnp.float32)  8.28 us
  transfers between devices with their start and end apart: 13, of which 3 were waited for; matrix products, arithmetic and copies ran while one was open for 15% of the time, Pallas kernels for 0%

profile of v1, /device:TPU:0, one launch (start us, length us, event | category | flops | bytes accessed | tf_op | source)
XLA Modules:
  0.0 357.8 jit_solution(1399952603415358524)
XLA Ops:
  10.1 2.4 multiply_convert_fusion.1
  13.9 4.9 %collective-permute-start = (bf16[1,16,1024]{2,1,0:T(8,128)(2,1)S(1)}, bf16[1,16,1024]{2,1,0:T(8,128)(2,1)S(1)}, u32[]{:S(2)}, u32[]{:S(2)}) collective-permute-start(bf16[1,16,1024]{2,1,0:T(8,128)(2,1)S(1)} %get-tuple-element.71), channel_id=1, source_target_pairs={{0,4},{1,5},{2,6},{3,7},{8,12},{9,13},{10,14},{11,15},{16,20},{17,... | collective-permute-start | bytes 98312 | tf_op jit(solution)/shard_map/ppermute | solution.py:29
  19.8 4.0 %all-to-all-start.2 = ((bf16[8,8,4,256]{3,1,2,0:T(8,128)(2,1)}), bf16[8,8,4,256]{3,1,2,0:T(8,128)(2,1)}, u32[]{:S(2)}, u32[]{:S(2)}) async-start(bf16[8,8,4,256]{3,1,2,0:T(8,128)(2,1)} %bitcast.44), calls=%async_computation.2 | async-start | bytes 262144 | tf_op jit(solution)/shard_map/all_to_all | solution.py:137
  26.0 3.0 collective-permute-start.2
  34.8 2.5 fusion.105
  37.9 2.2 fusion.6
  43.9 6.7 %all-to-all-start = ((bf16[8,8,4,256]{3,1,2,0:T(8,128)(2,1)}), bf16[8,8,4,256]{3,1,2,0:T(8,128)(2,1)}, u32[]{:S(2)}, u32[]{:S(2)}) async-start(bf16[8,8,4,256]{3,1,2,0:T(8,128)(2,1)} %bitcast.24), calls=%async_computation | async-start | bytes 262144 | tf_op jit(solution)/shard_map/all_to_all | solution.py:137
  60.6 2.6 fusion.107
  63.8 2.3 fusion.7
  81.8 4.2 %all-to-all-start.3 = ((bf16[8,8,4,256]{3,1,2,0:T(8,128)(2,1)}), bf16[8,8,4,256]{3,1,2,0:T(8,128)(2,1)}, u32[]{:S(2)}, u32[]{:S(2)}) async-start(bf16[8,8,4,256]{3,1,2,0:T(8,128)(2,1)} %bitcast.289), calls=%async_computation.3 | async-start | bytes 262144 | tf_op jit(solution)/shard_map/all_to_all | solution.py:137
  91.3 2.4 reshape.516
  93.8 4.0 %all-to-all-start.1 = ((bf16[8,8,4,256]{3,1,2,0:T(8,128)(2,1)}), bf16[8,8,4,256]{3,1,2,0:T(8,128)(2,1)}, u32[]{:S(2)}, u32[]{:S(2)}) async-start(bf16[8,8,4,256]{3,1,2,0:T(8,128)(2,1)} %bitcast.36), calls=%async_computation.1 | async-start | bytes 262144 | tf_op jit(solution)/shard_map/all_to_all | solution.py:137
  122.6 3.3 multiply_reduce_fusion.8
  127.9 4.6 %collective-permute-start.4 = (f32[1,16,1024]{2,1,0:T(8,128)S(1)}, f32[1,16,1024]{2,1,0:T(8,128)S(1)}, u32[]{:S(2)}, u32[]{:S(2)}) collective-permute-start(f32[1,16,1024]{2,1,0:T(8,128)S(1)} %get-tuple-element.67), channel_id=1, source_target_pairs={{0,4},{1,5},{2,6},{3,7},{8,12},{9,13},{10,14},{11,15},{16,20},{17,... | collective-permute-start | bytes 196616 | tf_op jit(solution)/shard_map/ppermute | solution.py:29
  137.0 3.7 %collective-permute-start.7 = (f32[18,1,1024]{2,1,0:T(1,128)}, f32[18,1,1024]{2,1,0:T(1,128)}, u32[]{:S(2)}, u32[]{:S(2)}) collective-permute-start(f32[18,1,1024]{2,1,0:T(1,128)} %get-tuple-element.66), channel_id=1, source_target_pairs={{0,1},{1,2},{2,3},{4,5},{5,6},{6,7},{8,9},{9,10},{10,11},{12,13},{... | collective-permute-start | bytes 221192 | tf_op jit(solution)/shard_map/ppermute | solution.py:29
  142.6 2.8 reshape.509
  156.4 2.0 reshape.507
  159.8 6.8 %dynamic-update-slice.1 = f32[4,265216]{1,0:T(4,128)} dynamic-update-slice(f32[4,265216]{1,0:T(4,128)} %dynamic-update-slice, f32[4,65536]{1,0:T(4,128)S(1)} %reshape.507, s32[]{} %constant.98, s32[]{} %constant.99) | dynamic-update-slice | bytes 2097156
  168.4 6.9 %dynamic-update-slice.3 = f32[4,265216]{1,0:T(4,128)} dynamic-update-slice(f32[4,265216]{1,0:T(4,128)} %dynamic-update-slice.2, f32[4,65536]{1,0:T(4,128)S(1)} %copy-done.4, s32[]{} %constant.98, s32[]{} %constant.101) | dynamic-update-slice | bytes 2097156
  180.7 5.6 %dynamic-update-slice.8 = f32[4,265216]{1,0:T(4,128)} dynamic-update-slice(f32[4,265216]{1,0:T(4,128)} %dynamic-update-slice.7, f32[4,49152]{1,0:T(4,128)S(1)} %copy-done.5, s32[]{} %constant.98, s32[]{} %constant.106) | dynamic-update-slice | bytes 1572868
  186.2 2.8 dynamic-update-slice.9
  193.7 142.8 %all-reduce.17.cloned.1.call-done = f32[4,265216]{1,0:T(4,128)} async-done(((f32[4,265216]{1,0:T(4,128)}), f32[4,265216]{1,0:T(4,128)}) %all-reduce.17.cloned.1.call-update) | async-done | bytes 4243472 | tf_op jit(solution)/shard_map/psum | solution.py:170
  336.5 3.1 dynamic-slice_reduce_fusion
  342.9 2.5 dynamic-slice_reduce_fusion.2
  (317 shorter events, 114.3 us)
Async XLA Ops:
  8.3 10.5 %copy-start.13 = (bf16[1,16,16,256]{3,2,1,0:T(8,128)(2,1)S(1)}, bf16[1,16,16,256]{3,2,1,0:T(8,128)(2,1)}, u32[]{:S(2)}) copy-start(bf16[1,16,16,256]{3,2,1,0:T(8,128)(2,1)} %param.13) | copy-start | bytes 393220
  8.3 10.5 %copy-start.29 = (bf16[256,256]{1,0:T(8,128)(2,1)S(1)}, bf16[256,256]{1,0:T(8,128)(2,1)}, u32[]{:S(2)}) copy-start(bf16[256,256]{1,0:T(8,128)(2,1)} %param.23) | copy-start | bytes 393220
  10.0 13.8 %copy-start.3 = (bf16[1,16,16,256]{3,2,1,0:T(8,128)(2,1)S(1)}, bf16[1,16,16,256]{3,2,1,0:T(8,128)(2,1)}, u32[]{:S(2)}) copy-start(bf16[1,16,16,256]{3,2,1,0:T(8,128)(2,1)} %param.12) | copy-start | bytes 393220
  10.1 13.8 %copy-start.65 = (f32[256]{0:T(256)S(1)}, f32[256]{0:T(256)}, u32[]{:S(2)}) copy-start(f32[256]{0:T(256)} %param.14) | copy-start | bytes 3076
  12.5 16.6 %copy-start.60 = (f32[1024,9]{0,1:T(8,128)S(1)}, f32[1024,9]{0,1:T(8,128)}, u32[]{:S(2)}) copy-start(f32[1024,9]{0,1:T(8,128)} %param.16) | copy-start | bytes 110596
  12.5 12.1 %collective-permute-start.1 = (bf16[1,16,1024]{2,1,0:T(8,128)(2,1)S(1)}, bf16[1,16,1024]{2,1,0:T(8,128)(2,1)S(1)}, u32[]{:S(2)}, u32[]{:S(2)}) collective-permute-start(bf16[1,16,1024]{2,1,0:T(8,128)(2,1)S(1)} %get-tuple-element.72), channel_id=1, source_target_pairs={{4,0},{5,1},{6,2},{7,3},{12,8},{13,9},{14,10},{15,11},{20,16},{21,... | collective-permute-start | bytes 98312 | tf_op jit(solution)/shard_map/ppermute | solution.py:31
  13.9 10.7 %collective-permute-start = (bf16[1,16,1024]{2,1,0:T(8,128)(2,1)S(1)}, bf16[1,16,1024]{2,1,0:T(8,128)(2,1)S(1)}, u32[]{:S(2)}, u32[]{:S(2)}) collective-permute-start(bf16[1,16,1024]{2,1,0:T(8,128)(2,1)S(1)} %get-tuple-element.71), channel_id=1, source_target_pairs={{0,4},{1,5},{2,6},{3,7},{8,12},{9,13},{10,14},{11,15},{16,20},{17,... | collective-permute-start | bytes 98312 | tf_op jit(solution)/shard_map/ppermute | solution.py:29
  19.8 24.1 %all-to-all-start.2 = ((bf16[8,8,4,256]{3,1,2,0:T(8,128)(2,1)}), bf16[8,8,4,256]{3,1,2,0:T(8,128)(2,1)}, u32[]{:S(2)}, u32[]{:S(2)}) async-start(bf16[8,8,4,256]{3,1,2,0:T(8,128)(2,1)} %bitcast.44), calls=%async_computation.2 | async-start | bytes 262144 | tf_op jit(solution)/shard_map/all_to_all | solution.py:137
  24.7 4.5 %collective-permute-start.3 = (bf16[18,1,1024]{2,1,0:T(2,128)(2,1)S(1)}, bf16[18,1,1024]{2,1,0:T(2,128)(2,1)S(1)}, u32[]{:S(2)}, u32[]{:S(2)}) collective-permute-start(bf16[18,1,1024]{2,1,0:T(2,128)(2,1)S(1)} %get-tuple-element.70), channel_id=1, source_target_pairs={{1,0},{2,1},{3,2},{5,4},{6,5},{7,6},{9,8},{10,9},{11,10},{13,12},{... | collective-permute-start | bytes 110600 | tf_op jit(solution)/shard_map/ppermute | solution.py:31
  26.0 3.9 %collective-permute-start.2 = (bf16[18,1,1024]{2,1,0:T(2,128)(2,1)S(1)}, bf16[18,1,1024]{2,1,0:T(2,128)(2,1)S(1)}, u32[]{:S(2)}, u32[]{:S(2)}) collective-permute-start(bf16[18,1,1024]{2,1,0:T(2,128)(2,1)S(1)} %get-tuple-element.69), channel_id=1, source_target_pairs={{0,1},{1,2},{2,3},{4,5},{5,6},{6,7},{8,9},{9,10},{10,11},{12,13},{... | collective-permute-start | bytes 110600 | tf_op jit(solution)/shard_map/ppermute | solution.py:29
  42.7 58.0 %copy-start.1 = (f32[16,16,256]{2,1,0:T(8,128)}, f32[16,16,256]{2,1,0:T(8,128)S(1)}, u32[]{:S(2)}) copy-start(f32[16,16,256]{2,1,0:T(8,128)S(1)} %get-tuple-element.99) | copy-start | bytes 786436
  43.9 12.4 %all-to-all-start = ((bf16[8,8,4,256]{3,1,2,0:T(8,128)(2,1)}), bf16[8,8,4,256]{3,1,2,0:T(8,128)(2,1)}, u32[]{:S(2)}, u32[]{:S(2)}) async-start(bf16[8,8,4,256]{3,1,2,0:T(8,128)(2,1)} %bitcast.24), calls=%async_computation | async-start | bytes 262144 | tf_op jit(solution)/shard_map/all_to_all | solution.py:137
  81.8 11.9 %all-to-all-start.3 = ((bf16[8,8,4,256]{3,1,2,0:T(8,128)(2,1)}), bf16[8,8,4,256]{3,1,2,0:T(8,128)(2,1)}, u32[]{:S(2)}, u32[]{:S(2)}) async-start(bf16[8,8,4,256]{3,1,2,0:T(8,128)(2,1)} %bitcast.289), calls=%async_computation.3 | async-start | bytes 262144 | tf_op jit(solution)/shard_map/all_to_all | solution.py:137
  93.8 18.0 %all-to-all-start.1 = ((bf16[8,8,4,256]{3,1,2,0:T(8,128)(2,1)}), bf16[8,8,4,256]{3,1,2,0:T(8,128)(2,1)}, u32[]{:S(2)}, u32[]{:S(2)}) async-start(bf16[8,8,4,256]{3,1,2,0:T(8,128)(2,1)} %bitcast.36), calls=%async_computation.1 | async-start | bytes 262144 | tf_op jit(solution)/shard_map/all_to_all | solution.py:137
  97.8 238.8 %all-reduce.17.cloned.1.call-start = ((), (), s32[]{:S(2)}) async-start(), calls=%async_computation.4 | async-start | bytes 8486912 | tf_op jit(solution)/shard_map/psum | solution.py:170
  122.6 9.9 %copy-start.12 = (bf16[2,8,2,8,256]{4,3,1,2,0:T(8,128)(2,1)S(1)}, bf16[2,8,2,8,256]{4,3,1,2,0:T(8,128)(2,1)}, u32[]{:S(2)}) copy-start(bf16[2,8,2,8,256]{4,3,1,2,0:T(8,128)(2,1)} %copy-done.11) | copy-start | bytes 393220
  126.6 8.4 %collective-permute-start.5 = (f32[1,16,1024]{2,1,0:T(8,128)}, f32[1,16,1024]{2,1,0:T(8,128)S(1)}, u32[]{:S(2)}, u32[]{:S(2)}) collective-permute-start(f32[1,16,1024]{2,1,0:T(8,128)} %get-tuple-element.68), channel_id=1, source_target_pairs={{4,0},{5,1},{6,2},{7,3},{12,8},{13,9},{14,10},{15,11},{20,16},{21,... | collective-permute-start | bytes 196616 | tf_op jit(solution)/shard_map/ppermute | solution.py:31
  127.9 7.1 %collective-permute-start.4 = (f32[1,16,1024]{2,1,0:T(8,128)S(1)}, f32[1,16,1024]{2,1,0:T(8,128)S(1)}, u32[]{:S(2)}, u32[]{:S(2)}) collective-permute-start(f32[1,16,1024]{2,1,0:T(8,128)S(1)} %get-tuple-element.67), channel_id=1, source_target_pairs={{0,4},{1,5},{2,6},{3,7},{8,12},{9,13},{10,14},{11,15},{16,20},{17,... | collective-permute-start | bytes 196616 | tf_op jit(solution)/shard_map/ppermute | solution.py:29
  135.8 14.7 %collective-permute-start.6 = (f32[18,1,1024]{2,1,0:T(1,128)}, f32[18,1,1024]{2,1,0:T(1,128)}, u32[]{:S(2)}, u32[]{:S(2)}) collective-permute-start(f32[18,1,1024]{2,1,0:T(1,128)} %get-tuple-element.65), channel_id=1, source_target_pairs={{1,0},{2,1},{3,2},{5,4},{6,5},{7,6},{9,8},{10,9},{11,10},{13,12},{... | collective-permute-start | bytes 221192 | tf_op jit(solution)/shard_map/ppermute | solution.py:31
  137.0 13.5 %collective-permute-start.7 = (f32[18,1,1024]{2,1,0:T(1,128)}, f32[18,1,1024]{2,1,0:T(1,128)}, u32[]{:S(2)}, u32[]{:S(2)}) collective-permute-start(f32[18,1,1024]{2,1,0:T(1,128)} %get-tuple-element.66), channel_id=1, source_target_pairs={{0,1},{1,2},{2,3},{4,5},{5,6},{6,7},{8,9},{9,10},{10,11},{12,13},{... | collective-permute-start | bytes 221192 | tf_op jit(solution)/shard_map/ppermute | solution.py:29
  156.4 11.9 %copy-start.4 = (f32[4,65536]{1,0:T(4,128)S(1)}, f32[4,65536]{1,0:T(4,128)}, u32[]{:S(2)}) copy-start(f32[4,65536]{1,0:T(4,128)} %reshape.509) | copy-start | bytes 3145732
  166.6 10.2 %copy-start.6 = (f32[4,49152]{1,0:T(4,128)S(1)}, f32[4,49152]{1,0:T(4,128)}, u32[]{:S(2)}) copy-start(f32[4,49152]{1,0:T(4,128)} %reshape.512) | copy-start | bytes 2359300
  168.4 12.3 %copy-start.5 = (f32[4,49152]{1,0:T(4,128)S(1)}, f32[4,49152]{1,0:T(4,128)}, u32[]{:S(2)}) copy-start(f32[4,49152]{1,0:T(4,128)} %reshape.516) | copy-start | bytes 2359300
  176.8 9.5 %copy-start.22 = (f32[4,16384]{1,0:T(4,128)S(1)}, f32[4,16384]{1,0:T(4,128)}, u32[]{:S(2)}) copy-start(f32[4,16384]{1,0:T(4,128)} %reshape.517) | copy-start | bytes 786436
  (63 other events, 150.0 us)
Sparse Core Ops, SparseCore 0:
  190.6 145.8 all-reduce.16

commit v2 on v1

--- a/solution.py
+++ b/solution.py
@@ -165,10 +165,14 @@
         pieces = [grads[i].reshape(parts, -1) for i in group]
         sizes = [piece.shape[1] for piece in pieces]
         width = sum(sizes)
-        padded = -(-width // 1024) * 1024
+        padded = -(-width // 8192) * 8192
         packed = jnp.concatenate(pieces + [jnp.zeros((parts, padded - width), jnp.float32)], axis=1)
-        whole = lax.psum(packed, ("rep", "sy", "sx"))
-        total = lax.dynamic_index_in_dim(whole, lax.axis_index("rep"), 0, keepdims=False)
+        tiles = lax.axis_size(("sy", "sx"))
+        local = packed.reshape(parts, tiles, padded // tiles).transpose(1, 0, 2)
+        local = local.reshape(tiles * parts * 8, padded // tiles // 8)
+        local = lax.psum_scatter(local, ("sy", "sx"), scatter_dimension=0, tiled=True)
+        local = lax.psum_scatter(local, "rep", scatter_dimension=0, tiled=True)
+        total = lax.all_gather(local, ("sy", "sx"), axis=0, tiled=True).reshape(-1)
         offset = 0
         for index, size in zip(group, sizes):
             shape = (grads[index].shape[0] // parts,) + grads[index].shape[1:]

time: 360 us -> 336 us (0.933)
  waiting for transfers between devices: 144 us -> 119 us
    psum x1 -> x0, waiting for transfers between devices: 143 us -> none  [reduce_grads(): whole = lax.psum(packed, ('rep', 'sy', 'sx'))]
    reduce_scatter x0 -> x1, waiting for transfers between devices: none -> 55.4 us  [reduce_grads(): lax.psum_scatter(local, ('sy', 'sx'), scatter_dimension=0, tiled=True)]
    unnamed x1 -> x4, waiting for transfers between devices: 0.02 us -> 39.6 us
    all_gather x0 -> x1, waiting for transfers between devices: none -> 22.5 us  [reduce_grads(): total = lax.all_gather(local, ('sy', 'sx'), axis=0, tiled=True).reshape(-1)]
    slice x5, local copies, waits for them, and re-layouts: 9.22 us -> 1.08 us  [reduce_grads(): results[index] = total[offset:offset + size].reshape(shape)]
    reshape x0 -> x2, local copies, waits for them, and re-layouts: none -> 7.16 us  [the longest x1 5.81 us: reduce_grads(): local = local.reshape(tiles * parts * 8, padded // tiles // 8)]
    unnamed x159 -> x163, local copies, waits for them, and re-layouts: 36.1 us -> 37.7 us
  transfers between devices with their start and end apart: 13 -> 15, of which waited for: 3 -> 5; matrix products, arithmetic and copies ran while one was open for 15% -> 17% of each run, Pallas kernels for 0% -> 0%
where the time goes in v2:
time: 336 us; the launch traced here: 334 us
  waiting for transfers between devices  119 us (35%)
  local copies, waits for them, and re-layouts  102 us (30%)
  starting transfers between devices  40.4 us (12%)
  matrix products  33.3 us (10%)
  other arithmetic  24.4 us (7%)
  between operations  15.7 us (5%)
    reduce_scatter x1, waiting for transfers between devices, reduce_grads(): lax.psum_scatter(local, ('sy', 'sx'), scatter_dimension=0, tiled=True)  55.4 us
    unnamed x4, waiting for transfers between devices  39.6 us
    unnamed x163, local copies, waits for them, and re-layouts  37.7 us
    all_gather x1, waiting for transfers between devices, reduce_grads(): total = lax.all_gather(local, ('sy', 'sx'), axis=0, tiled=True).reshape(-1)  22.5 us
    all_to_all x4, starting transfers between devices, swap_blocks(): lax.all_to_all(as_sent(flattened), ('sy', 'sx'), split_axis=0, concat_axi...  18.9 us
    ppermute x4, starting transfers between devices, extended_2(): lax.ppermute(tail, axis, [(i, (i + 1) % count) for i in range(ends)])  16.1 us
    reshape x10, local copies, waits for them, and re-layouts, reduce_grads(): pieces = [grads[i].reshape(parts, -1) for i in group]  13.2 us
    dot_general x6, matrix products, window_attention(): jnp.einsum('whqk,wkhd->wqhd', softmax_out, value_rows, preferred_element_...  9.12 us
  transfers between devices with their start and end apart: 15, of which 5 were waited for; matrix products, arithmetic and copies ran while one was open for 17% of the time, Pallas kernels for 0%

profile of v2, /device:TPU:0, one launch (start us, length us, event | category | flops | bytes accessed | tf_op | source)
XLA Modules:
  0.0 333.9 jit_solution(7796404641213181982)
XLA Ops:
  10.1 2.4 multiply_convert_fusion.1
  14.0 4.9 %collective-permute-start = (bf16[1,16,1024]{2,1,0:T(8,128)(2,1)S(1)}, bf16[1,16,1024]{2,1,0:T(8,128)(2,1)S(1)}, u32[]{:S(2)}, u32[]{:S(2)}) collective-permute-start(bf16[1,16,1024]{2,1,0:T(8,128)(2,1)S(1)} %get-tuple-element.83), channel_id=1, source_target_pairs={{0,4},{1,5},{2,6},{3,7},{8,12},{9,13},{10,14},{11,15},{16,20},{17,... | collective-permute-start | bytes 98312 | tf_op jit(solution)/shard_map/ppermute | solution.py:29
  19.9 4.0 %all-to-all-start.2 = ((bf16[8,8,4,256]{3,1,2,0:T(8,128)(2,1)}), bf16[8,8,4,256]{3,1,2,0:T(8,128)(2,1)}, u32[]{:S(2)}, u32[]{:S(2)}) async-start(bf16[8,8,4,256]{3,1,2,0:T(8,128)(2,1)} %bitcast.44), calls=%async_computation.2 | async-start | bytes 262144 | tf_op jit(solution)/shard_map/all_to_all | solution.py:137
  26.1 3.0 collective-permute-start.2
  34.9 2.5 fusion.109
  37.9 2.2 fusion.6
  43.9 6.7 %all-to-all-start = ((bf16[8,8,4,256]{3,1,2,0:T(8,128)(2,1)}), bf16[8,8,4,256]{3,1,2,0:T(8,128)(2,1)}, u32[]{:S(2)}, u32[]{:S(2)}) async-start(bf16[8,8,4,256]{3,1,2,0:T(8,128)(2,1)} %bitcast.24), calls=%async_computation | async-start | bytes 262144 | tf_op jit(solution)/shard_map/all_to_all | solution.py:137
  60.6 2.7 fusion.111
  63.8 2.3 fusion.7
  82.0 4.2 %all-to-all-start.3 = ((bf16[8,8,4,256]{3,1,2,0:T(8,128)(2,1)}), bf16[8,8,4,256]{3,1,2,0:T(8,128)(2,1)}, u32[]{:S(2)}, u32[]{:S(2)}) async-start(bf16[8,8,4,256]{3,1,2,0:T(8,128)(2,1)} %bitcast.288), calls=%async_computation.3 | async-start | bytes 262144 | tf_op jit(solution)/shard_map/all_to_all | solution.py:137
  91.5 2.5 reshape.508
  94.0 4.0 %all-to-all-start.1 = ((bf16[8,8,4,256]{3,1,2,0:T(8,128)(2,1)}), bf16[8,8,4,256]{3,1,2,0:T(8,128)(2,1)}, u32[]{:S(2)}, u32[]{:S(2)}) async-start(bf16[8,8,4,256]{3,1,2,0:T(8,128)(2,1)} %bitcast.36), calls=%async_computation.1 | async-start | bytes 262144 | tf_op jit(solution)/shard_map/all_to_all | solution.py:137
  122.8 3.3 multiply_reduce_fusion.8
  128.1 4.6 %collective-permute-start.4 = (f32[1,16,1024]{2,1,0:T(8,128)S(1)}, f32[1,16,1024]{2,1,0:T(8,128)S(1)}, u32[]{:S(2)}, u32[]{:S(2)}) collective-permute-start(f32[1,16,1024]{2,1,0:T(8,128)S(1)} %get-tuple-element.79), channel_id=1, source_target_pairs={{0,4},{1,5},{2,6},{3,7},{8,12},{9,13},{10,14},{11,15},{16,20},{17,... | collective-permute-start | bytes 196616 | tf_op jit(solution)/shard_map/ppermute | solution.py:29
  137.2 3.7 %collective-permute-start.7 = (f32[18,1,1024]{2,1,0:T(1,128)}, f32[18,1,1024]{2,1,0:T(1,128)}, u32[]{:S(2)}, u32[]{:S(2)}) collective-permute-start(f32[18,1,1024]{2,1,0:T(1,128)} %get-tuple-element.69), channel_id=1, source_target_pairs={{0,1},{1,2},{2,3},{4,5},{5,6},{6,7},{8,9},{9,10},{10,11},{12,13},{... | collective-permute-start | bytes 221192 | tf_op jit(solution)/shard_map/ppermute | solution.py:29
  142.8 2.8 reshape.501
  159.9 6.8 %dynamic-update-slice.1 = f32[4,270336]{1,0:T(4,128)} dynamic-update-slice(f32[4,270336]{1,0:T(4,128)} %dynamic-update-slice, f32[4,65536]{1,0:T(4,128)S(1)} %reshape.499, s32[]{} %constant.78, s32[]{} %constant.79) | dynamic-update-slice | bytes 2097156
  168.5 6.9 %dynamic-update-slice.3 = f32[4,270336]{1,0:T(4,128)} dynamic-update-slice(f32[4,270336]{1,0:T(4,128)} %dynamic-update-slice.2, f32[4,65536]{1,0:T(4,128)S(1)} %copy-done.4, s32[]{} %constant.78, s32[]{} %constant.81) | dynamic-update-slice | bytes 2097156
  180.7 5.6 %dynamic-update-slice.8 = f32[4,270336]{1,0:T(4,128)} dynamic-update-slice(f32[4,270336]{1,0:T(4,128)} %dynamic-update-slice.7, f32[4,49152]{1,0:T(4,128)S(1)} %copy-done.5, s32[]{} %constant.78, s32[]{} %constant.86) | dynamic-update-slice | bytes 1572868
  186.3 3.0 dynamic-update-slice.9
  191.1 5.8 %reshape.511 = f32[256,4224]{1,0:T(8,128)} reshape(f32[8,4,33792]{2,1,0:T(4,128)} %bitcast.258) | data formatting | bytes 8650752 | tf_op jit(solution)/shard_map/reshape | solution.py:172
  197.1 55.4 %reduce-scatter.2.cloned.1.call-done = f32[32,4224]{1,0:T(8,128)} async-done(((f32[256,4224]{1,0:T(8,128)}), f32[32,4224]{1,0:T(8,128)}) %reduce-scatter.2.cloned.1.call-update) | async-done | bytes 540688 | tf_op jit(solution)/shard_map/reduce_scatter | solution.py:173
  253.8 39.5 %all-reduce.18.cloned.1.call-done = f32[32,4224]{1,0:T(8,128)} async-done(((f32[32,4224]{1,0:T(8,128)}), f32[32,4224]{1,0:T(8,128)}) %all-reduce.18.cloned.1.call-update) | async-done | bytes 540688
  297.3 22.5 %all-gather.2.cloned.1.call-done = f32[64,4224]{1,0:T(8,128)} async-done(((f32[8,4224]{1,0:T(8,128)}), f32[64,4224]{1,0:T(8,128)}) %all-gather.2.cloned.1.call-update) | async-done | bytes 1081360 | tf_op jit(solution)/shard_map/all_gather | solution.py:175
  (329 shorter events, 116.9 us)
Async XLA Ops:
  12.5 12.2 %collective-permute-start.1 = (bf16[1,16,1024]{2,1,0:T(8,128)(2,1)S(1)}, bf16[1,16,1024]{2,1,0:T(8,128)(2,1)S(1)}, u32[]{:S(2)}, u32[]{:S(2)}) collective-permute-start(bf16[1,16,1024]{2,1,0:T(8,128)(2,1)S(1)} %get-tuple-element.84), channel_id=1, source_target_pairs={{4,0},{5,1},{6,2},{7,3},{12,8},{13,9},{14,10},{15,11},{20,16},{21,... | collective-permute-start | bytes 98312 | tf_op jit(solution)/shard_map/ppermute | solution.py:31
  14.0 10.7 %collective-permute-start = (bf16[1,16,1024]{2,1,0:T(8,128)(2,1)S(1)}, bf16[1,16,1024]{2,1,0:T(8,128)(2,1)S(1)}, u32[]{:S(2)}, u32[]{:S(2)}) collective-permute-start(bf16[1,16,1024]{2,1,0:T(8,128)(2,1)S(1)} %get-tuple-element.83), channel_id=1, source_target_pairs={{0,4},{1,5},{2,6},{3,7},{8,12},{9,13},{10,14},{11,15},{16,20},{17,... | collective-permute-start | bytes 98312 | tf_op jit(solution)/shard_map/ppermute | solution.py:29
  19.9 24.1 %all-to-all-start.2 = ((bf16[8,8,4,256]{3,1,2,0:T(8,128)(2,1)}), bf16[8,8,4,256]{3,1,2,0:T(8,128)(2,1)}, u32[]{:S(2)}, u32[]{:S(2)}) async-start(bf16[8,8,4,256]{3,1,2,0:T(8,128)(2,1)} %bitcast.44), calls=%async_computation.2 | async-start | bytes 262144 | tf_op jit(solution)/shard_map/all_to_all | solution.py:137
  24.8 4.5 %collective-permute-start.3 = (bf16[18,1,1024]{2,1,0:T(2,128)(2,1)S(1)}, bf16[18,1,1024]{2,1,0:T(2,128)(2,1)S(1)}, u32[]{:S(2)}, u32[]{:S(2)}) collective-permute-start(bf16[18,1,1024]{2,1,0:T(2,128)(2,1)S(1)} %get-tuple-element.82), channel_id=1, source_target_pairs={{1,0},{2,1},{3,2},{5,4},{6,5},{7,6},{9,8},{10,9},{11,10},{13,12},{... | collective-permute-start | bytes 110600 | tf_op jit(solution)/shard_map/ppermute | solution.py:31
  26.1 3.9 %collective-permute-start.2 = (bf16[18,1,1024]{2,1,0:T(2,128)(2,1)S(1)}, bf16[18,1,1024]{2,1,0:T(2,128)(2,1)S(1)}, u32[]{:S(2)}, u32[]{:S(2)}) collective-permute-start(bf16[18,1,1024]{2,1,0:T(2,128)(2,1)S(1)} %get-tuple-element.81), channel_id=1, source_target_pairs={{0,1},{1,2},{2,3},{4,5},{5,6},{6,7},{8,9},{9,10},{10,11},{12,13},{... | collective-permute-start | bytes 110600 | tf_op jit(solution)/shard_map/ppermute | solution.py:29
  42.8 58.2 %copy-start.1 = (f32[16,16,256]{2,1,0:T(8,128)}, f32[16,16,256]{2,1,0:T(8,128)S(1)}, u32[]{:S(2)}) copy-start(f32[16,16,256]{2,1,0:T(8,128)S(1)} %get-tuple-element.111) | copy-start | bytes 786436
  43.9 12.4 %all-to-all-start = ((bf16[8,8,4,256]{3,1,2,0:T(8,128)(2,1)}), bf16[8,8,4,256]{3,1,2,0:T(8,128)(2,1)}, u32[]{:S(2)}, u32[]{:S(2)}) async-start(bf16[8,8,4,256]{3,1,2,0:T(8,128)(2,1)} %bitcast.24), calls=%async_computation | async-start | bytes 262144 | tf_op jit(solution)/shard_map/all_to_all | solution.py:137
  82.0 12.0 %all-to-all-start.3 = ((bf16[8,8,4,256]{3,1,2,0:T(8,128)(2,1)}), bf16[8,8,4,256]{3,1,2,0:T(8,128)(2,1)}, u32[]{:S(2)}, u32[]{:S(2)}) async-start(bf16[8,8,4,256]{3,1,2,0:T(8,128)(2,1)} %bitcast.288), calls=%async_computation.3 | async-start | bytes 262144 | tf_op jit(solution)/shard_map/all_to_all | solution.py:137
  94.0 17.9 %all-to-all-start.1 = ((bf16[8,8,4,256]{3,1,2,0:T(8,128)(2,1)}), bf16[8,8,4,256]{3,1,2,0:T(8,128)(2,1)}, u32[]{:S(2)}, u32[]{:S(2)}) async-start(bf16[8,8,4,256]{3,1,2,0:T(8,128)(2,1)} %bitcast.36), calls=%async_computation.1 | async-start | bytes 262144 | tf_op jit(solution)/shard_map/all_to_all | solution.py:137
  98.0 154.5 %reduce-scatter.2.cloned.1.call-start = ((), (), s32[]{:S(2)}) async-start(), calls=%async_computation.5 | async-start | bytes 4866048 | tf_op jit(solution)/shard_map/reduce_scatter | solution.py:173
  126.8 8.3 %collective-permute-start.5 = (f32[1,16,1024]{2,1,0:T(8,128)}, f32[1,16,1024]{2,1,0:T(8,128)S(1)}, u32[]{:S(2)}, u32[]{:S(2)}) collective-permute-start(f32[1,16,1024]{2,1,0:T(8,128)} %get-tuple-element.80), channel_id=1, source_target_pairs={{4,0},{5,1},{6,2},{7,3},{12,8},{13,9},{14,10},{15,11},{20,16},{21,... | collective-permute-start | bytes 196616 | tf_op jit(solution)/shard_map/ppermute | solution.py:31
  128.1 7.0 %collective-permute-start.4 = (f32[1,16,1024]{2,1,0:T(8,128)S(1)}, f32[1,16,1024]{2,1,0:T(8,128)S(1)}, u32[]{:S(2)}, u32[]{:S(2)}) collective-permute-start(f32[1,16,1024]{2,1,0:T(8,128)S(1)} %get-tuple-element.79), channel_id=1, source_target_pairs={{0,4},{1,5},{2,6},{3,7},{8,12},{9,13},{10,14},{11,15},{16,20},{17,... | collective-permute-start | bytes 196616 | tf_op jit(solution)/shard_map/ppermute | solution.py:29
  135.9 14.6 %collective-permute-start.6 = (f32[18,1,1024]{2,1,0:T(1,128)}, f32[18,1,1024]{2,1,0:T(1,128)}, u32[]{:S(2)}, u32[]{:S(2)}) collective-permute-start(f32[18,1,1024]{2,1,0:T(1,128)} %get-tuple-element.68), channel_id=1, source_target_pairs={{1,0},{2,1},{3,2},{5,4},{6,5},{7,6},{9,8},{10,9},{11,10},{13,12},{... | collective-permute-start | bytes 221192 | tf_op jit(solution)/shard_map/ppermute | solution.py:31
  137.2 13.3 %collective-permute-start.7 = (f32[18,1,1024]{2,1,0:T(1,128)}, f32[18,1,1024]{2,1,0:T(1,128)}, u32[]{:S(2)}, u32[]{:S(2)}) collective-permute-start(f32[18,1,1024]{2,1,0:T(1,128)} %get-tuple-element.69), channel_id=1, source_target_pairs={{0,1},{1,2},{2,3},{4,5},{5,6},{6,7},{8,9},{9,10},{10,11},{12,13},{... | collective-permute-start | bytes 221192 | tf_op jit(solution)/shard_map/ppermute | solution.py:29
  197.0 55.6 %copy-start.74 = (u32[32]{0:T(128)S(1)}, u32[32]{0:T(128)}, u32[]{:S(2)}) copy-start(u32[32]{0:T(128)} %constant.76) | copy-start | bytes 388
  197.0 98.1 %copy-start.15 = (bf16[8,2,4,4,256]{4,3,2,1,0:T(4,128)(2,1)S(1)}, bf16[8,2,4,4,256]{4,3,2,1,0:T(4,128)(2,1)}, u32[]{:S(2)}) copy-start(bf16[8,2,4,4,256]{4,3,2,1,0:T(4,128)(2,1)} %copy.154) | copy-start | bytes 393220
  197.0 98.1 %copy-start.2 = (f32[16,16,256]{2,1,0:T(8,128)S(1)}, f32[16,16,256]{2,1,0:T(8,128)}, u32[]{:S(2)}) copy-start(f32[16,16,256]{2,1,0:T(8,128)} %copy-done.1) | copy-start | bytes 786436
  197.0 98.1 %copy-start.30 = (bf16[256,256]{1,0:T(8,128)(2,1)S(1)}, bf16[256,256]{1,0:T(8,128)(2,1)}, u32[]{:S(2)}) copy-start(bf16[256,256]{1,0:T(8,128)(2,1)} %param.23) | copy-start | bytes 393220
  197.0 98.9 %copy-start.43 = (f32[16,16]{1,0:T(8,128)S(1)}, f32[16,16]{1,0:T(8,128)}, u32[]{:S(2)}) copy-start(f32[16,16]{1,0:T(8,128)} %get-tuple-element.62) | copy-start | bytes 3076
  197.0 99.0 %copy-start.45 = (f32[16,16]{1,0:T(8,128)S(1)}, f32[16,16]{1,0:T(8,128)}, u32[]{:S(2)}) copy-start(f32[16,16]{1,0:T(8,128)} %copy-done.44) | copy-start | bytes 3076
  197.0 99.1 %copy-start.67 = (f32[256]{0:T(256)S(1)}, f32[256]{0:T(256)}, u32[]{:S(2)}) copy-start(f32[256]{0:T(256)} %param.14) | copy-start | bytes 3076
  197.0 99.4 %copy-start.8 = (f32[16,16,256]{2,1,0:T(8,128)S(1)}, f32[16,16,256]{2,1,0:T(8,128)}, u32[]{:S(2)}) copy-start(f32[16,16,256]{2,1,0:T(8,128)} %copy-done.7) | copy-start | bytes 786436
  197.0 96.3 %all-reduce.18.cloned.1.call-start = ((), (), s32[]{:S(2)}) async-start(), calls=%async_computation.7 | async-start | bytes 1081344
  252.5 67.3 %all-gather.2.cloned.1.call-start = ((), (), s32[]{:S(2)}) async-start(), calls=%async_computation.6 | async-start | bytes 1216512 | tf_op jit(solution)/shard_map/all_gather | solution.py:175
  (66 other events, 257.4 us)
Sparse Core Ops, SparseCore 0:
  197.1 55.3 reduce-scatter.1
  254.8 38.4 all-reduce.17
  296.0 23.8 all-gather.1

commit v3 on v1

--- a/solution.py
+++ b/solution.py
@@ -158,24 +158,50 @@
     return moved.transpose(2, 0, 3, 1, 4).reshape(height, breadth, channels)
 
 
-def reduce_grads(grads, groups):
+def exchange_sum(values, axes, axis):
+    moved = lax.all_to_all(values.astype(jnp.bfloat16), axes, split_axis=axis, concat_axis=axis, tiled=True)
+    return moved.astype(jnp.float32).sum(axis)
+
+
+def reduce_grads(grads):
     parts = lax.axis_size("rep")
-    results = [None] * len(grads)
-    for group in groups:
-        pieces = [grads[i].reshape(parts, -1) for i in group]
-        sizes = [piece.shape[1] for piece in pieces]
-        width = sum(sizes)
-        padded = -(-width // 1024) * 1024
-        packed = jnp.concatenate(pieces + [jnp.zeros((parts, padded - width), jnp.float32)], axis=1)
-        whole = lax.psum(packed, ("rep", "sy", "sx"))
-        total = lax.dynamic_index_in_dim(whole, lax.axis_index("rep"), 0, keepdims=False)
-        offset = 0
-        for index, size in zip(group, sizes):
-            shape = (grads[index].shape[0] // parts,) + grads[index].shape[1:]
-            results[index] = total[offset : offset + size].reshape(shape)
-            offset += size
-    return tuple(results)
-
+    tiles = lax.axis_size(("sy", "sx"))
+    channels = grads[0].shape[0]
+    small = jnp.concatenate(
+        [grads[2].reshape(channels, -1), grads[0][:, None], grads[4][:, None], grads[7][:, None]], axis=1
+    )
+    small_width = small.shape[1]
+    small = jnp.pad(small, ((0, 0), (0, -small_width % 128)))
+    wide = [grads[1], grads[5], grads[6], grads[8], grads[9], grads[3].reshape(channels, -1), small]
+    widths = [piece.shape[1] for piece in wide]
+    packed = jnp.concatenate(wide, axis=1)
+    width = packed.shape[1]
+    rows = channels // parts
+    piece = rows // tiles
+    local = exchange_sum(packed.reshape(parts, tiles, piece, width), ("sy", "sx"), 1)
+    local = exchange_sum(local, "rep", 0)
+    spread = jnp.broadcast_to(local[None], (tiles, piece, width))
+    total = lax.all_to_all(spread, ("sy", "sx"), split_axis=0, concat_axis=0, tiled=True)
+    total = total.reshape(rows, width)
+    cuts = []
+    offset = 0
+    for size in widths:
+        cuts.append(total[:, offset : offset + size])
+        offset += size
+    small = cuts[6]
+    kernel_cols = grads[2].shape[1] * grads[2].shape[0] // channels
+    return (
+        small[:, kernel_cols],
+        cuts[0],
+        small[:, :kernel_cols].reshape(-1, grads[2].shape[1]),
+        cuts[5].reshape(-1, grads[3].shape[1]),
+        small[:, kernel_cols + 1],
+        cuts[1],
+        cuts[2],
+        small[:, kernel_cols + 2],
+        cuts[3],
+        cuts[4],
+    )
 
 def body(
     features,
@@ -280,7 +306,7 @@
         outer_sum(grid_windows, tap_grid_in),
         outer_sum(grid_home, tap_grid_out),
     )
-    summed = reduce_grads(local_grads, ((0, 1, 2, 3, 4, 5, 6, 7, 8, 9),))
+    summed = reduce_grads(local_grads)
     return (
         output_tile[None],
         token_grad[None],

time: 360 us -> 211 us (0.59)
  waiting for transfers between devices: 144 us -> 22.5 us
  local copies, waits for them, and re-layouts: 101 us -> 48.6 us
  blocking collectives: 0 us -> 31.1 us
  between operations: 15.3 us -> 2.54 us
  starting transfers between devices: 40.4 us -> 49.3 us
    psum x1 -> x0, waiting for transfers between devices: 143 us -> none  [reduce_grads(): whole = lax.psum(packed, ('rep', 'sy', 'sx'))]
    unnamed x159 -> x203, local copies, waits for them, and re-layouts: 36.1 us -> 4.36 us
    all_to_all x0 -> x1, blocking collectives: none -> 31.1 us  [exchange_sum(): lax.all_to_all(values.astype(jnp.bfloat16), axes, split_axis=axis, concat...]
    reshape x23 -> x4, local copies, waits for them, and re-layouts: 27.4 us -> 1.74 us  [the longest x2 0.89 us: reduce_grads(): grads[2].reshape(channels, -1)]
    all_to_all x0 -> x2, waiting for transfers between devices: none -> 21.4 us  [the longest x1 14.3 us: reduce_grads(): lax.all_to_all(spread, ('sy', 'sx'), split_axis=0, concat_axis=0, tiled=T...]
    all_to_all x0 -> x2, starting transfers between devices: none -> 9.54 us  [the longest x1 5.98 us: exchange_sum(): lax.all_to_all(values.astype(jnp.bfloat16), axes, split_axis=axis, concat...]
    slice x5, local copies, waits for them, and re-layouts: 9.22 us -> 2.91 us  [the longest x3 2.18 us: reduce_grads(): cuts.append(total[:, offset:offset + size])]
    dot_general x0 -> x5, local copies, waits for them, and re-layouts: none -> 4.72 us  [outer_sum(): lax.dot_general(left_flat, right_flat, (((0,), (0,)), ((), ())), preferre...]
  transfers between devices with their start and end apart: 13 -> 14, of which waited for: 3 -> 3; matrix products, arithmetic and copies ran while one was open for 15% -> 28% of each run, Pallas kernels for 0% -> 0%
where the time goes in v3:
time: 211 us; the launch traced here: 209 us
  starting transfers between devices  49.3 us (23%)
  local copies, waits for them, and re-layouts  48.6 us (23%)
  matrix products  31.9 us (15%)
  blocking collectives  31.1 us (15%)
  other arithmetic  23.4 us (11%)
  waiting for transfers between devices  22.5 us (11%)
  between operations  2.54 us (1%)
    all_to_all x1, blocking collectives, exchange_sum(): lax.all_to_all(values.astype(jnp.bfloat16), axes, split_axis=axis, concat...  31.1 us
    all_to_all x4, starting transfers between devices, swap_blocks(): lax.all_to_all(as_sent(flattened), ('sy', 'sx'), split_axis=0, concat_axi...  18.4 us
    ppermute x4, starting transfers between devices, extended_2(): lax.ppermute(tail, axis, [(i, (i + 1) % count) for i in range(ends)])  16.1 us
    all_to_all x1, waiting for transfers between devices, reduce_grads(): lax.all_to_all(spread, ('sy', 'sx'), split_axis=0, concat_axis=0, tiled=T...  14.3 us
    dot_general x12, matrix products, project_rows(): product = jnp.dot(flattened, weight, preferred_element_type=jnp.float32)  12.5 us
    dot_general x6, matrix products, window_attention(): jnp.einsum('whqk,wkhd->wqhd', softmax_out, value_rows, preferred_element_...  8.88 us
    all_to_all x1, waiting for transfers between devices, exchange_sum(): lax.all_to_all(values.astype(jnp.bfloat16), axes, split_axis=axis, concat...  7.05 us
    all_to_all x1, starting transfers between devices, exchange_sum(): lax.all_to_all(values.astype(jnp.bfloat16), axes, split_axis=axis, concat...  5.98 us
  transfers between devices with their start and end apart: 14, of which 3 were waited for; matrix products, arithmetic and copies ran while one was open for 28% of the time, Pallas kernels for 0%

profile of v3, /device:TPU:0, one launch (start us, length us, event | category | flops | bytes accessed | tf_op | source)
XLA Modules:
  0.0 209.3 jit_solution(17201435075718039487)
XLA Ops:
  3.5 2.4 %multiply_convert_fusion.1 = (bf16[16,16,1024]{2,1,0:T(8,128)(2,1)S(1)}, f32[16,16,1024]{2,1,0:T(8,128)}) fusion(bf16[256,1024]{1,0:T(8,128)(2,1)S(1)} %copy-done, bf16[1,16,16,256]{3,2,1,0:T(8,128)(2,1)} %param.12, f32[256]{0:T(256)} %param.14, f32[16,16]{1,0:T(8,128)S(1)} %fusion.97, f32[16,16]{1,0:T(8,128)S(1)} %broadcast_multiply_fusion.2), kind=kOutput, calls=%fused_computation.120 | convolution fusion | flops 136904704 | bytes 2231296 | tf_op jit(solution)/shard_map/jvp()/dot_general | solution.py:52
  7.4 4.9 %collective-permute-start = (bf16[1,16,1024]{2,1,0:T(8,128)(2,1)S(1)}, bf16[1,16,1024]{2,1,0:T(8,128)(2,1)S(1)}, u32[]{:S(2)}, u32[]{:S(2)}) collective-permute-start(bf16[1,16,1024]{2,1,0:T(8,128)(2,1)S(1)} %get-tuple-element.95), channel_id=1, source_target_pairs={{0,4},{1,5},{2,6},{3,7},{8,12},{9,13},{10,14},{11,15},{16,20},{17,... | collective-permute-start | bytes 98312 | tf_op jit(solution)/shard_map/ppermute | solution.py:29
  13.3 4.0 %all-to-all-start.2 = ((bf16[8,8,4,256]{3,1,2,0:T(8,128)(2,1)}), bf16[8,8,4,256]{3,1,2,0:T(8,128)(2,1)}, u32[]{:S(2)}, u32[]{:S(2)}) async-start(bf16[8,8,4,256]{3,1,2,0:T(8,128)(2,1)} %bitcast.44), calls=%async_computation.2 | async-start | bytes 262144 | tf_op jit(solution)/shard_map/all_to_all | solution.py:137
  18.9 3.0 %collective-permute-start.2 = (bf16[18,1,1024]{2,1,0:T(2,128)(2,1)S(1)}, bf16[18,1,1024]{2,1,0:T(2,128)(2,1)S(1)}, u32[]{:S(2)}, u32[]{:S(2)}) collective-permute-start(bf16[18,1,1024]{2,1,0:T(2,128)(2,1)S(1)} %get-tuple-element.93), channel_id=1, source_target_pairs={{0,1},{1,2},{2,3},{4,5},{5,6},{6,7},{8,9},{9,10},{10,11},{12,13},{... | collective-permute-start | bytes 110600 | tf_op jit(solution)/shard_map/ppermute | solution.py:29
  28.1 2.6 %fusion.114 = (f32[4,8,64]{2,1,0:T(8,128)S(1)}, f32[4,8,64,64]{2,3,1,0:T(8,128)}) fusion(bf16[4,64,8,32]{1,3,2,0:T(8,128)(2,1)} %bitcast.340, bf16[4,64,8,32]{1,3,2,0:T(8,128)(2,1)S(1)} %bitcast.342), kind=kOutput, calls=%fused_computation.228 | convolution fusion | flops 8781887 | bytes 794624 | tf_op jit(solution)/shard_map/jvp()/sub | solution.py:98
  31.3 2.2 %fusion.10 = bf16[4,64,8,32]{1,3,2,0:T(8,128)(2,1)} fusion(bf16[4,64,8,32]{1,3,2,0:T(8,128)(2,1)S(1)} %bitcast.313, f32[4,8,64,64]{2,3,1,0:T(8,128)} %get-tuple-element.121, f32[4,8,64]{2,1,0:T(8,128)S(1)} %get-tuple-element.120), kind=kOutput, calls=%fused_computation.43 | convolution fusion | flops 8716288 | bytes 794624 | tf_op jit(solution)/shard_map/jvp(whqk,wkhd->wqhd)/dot_general | solution.py:99
  39.9 6.2 %all-to-all-start = ((bf16[8,8,4,256]{3,1,2,0:T(8,128)(2,1)}), bf16[8,8,4,256]{3,1,2,0:T(8,128)(2,1)}, u32[]{:S(2)}, u32[]{:S(2)}) async-start(bf16[8,8,4,256]{3,1,2,0:T(8,128)(2,1)} %bitcast.24), calls=%async_computation | async-start | bytes 262144 | tf_op jit(solution)/shard_map/all_to_all | solution.py:137
  60.1 2.6 %fusion.116 = (f32[4,8,64]{2,1,0:T(8,128)S(1)}, f32[4,8,64,64]{2,3,1,0:T(8,128)}) fusion(bf16[4,64,8,32]{1,3,2,0:T(8,128)(2,1)} %bitcast.344, bf16[4,64,8,32]{1,3,2,0:T(8,128)(2,1)} %bitcast.346), kind=kOutput, calls=%fused_computation.230 | convolution fusion | flops 8781887 | bytes 794624 | tf_op jit(solution)/shard_map/jvp()/sub | solution.py:98
  62.7 1.8 fusion.21
  74.2 4.2 %all-to-all-start.3 = ((bf16[8,8,4,256]{3,1,2,0:T(8,128)(2,1)}), bf16[8,8,4,256]{3,1,2,0:T(8,128)(2,1)}, u32[]{:S(2)}, u32[]{:S(2)}) async-start(bf16[8,8,4,256]{3,1,2,0:T(8,128)(2,1)} %bitcast.330), calls=%async_computation.3 | async-start | bytes 262144 | tf_op jit(solution)/shard_map/all_to_all | solution.py:137
  78.4 2.2 %fusion.11 = bf16[4,64,8,32]{1,3,2,0:T(8,128)(2,1)} fusion(bf16[4,64,8,32]{1,3,2,0:T(8,128)(2,1)} %bitcast.316, f32[4,8,64,64]{2,3,1,0:T(8,128)} %get-tuple-element.125, f32[4,8,64]{2,1,0:T(8,128)} %copy-done.95), kind=kOutput, calls=%fused_computation.44 | convolution fusion | flops 8716288 | bytes 794624 | tf_op jit(solution)/shard_map/jvp(whqk,wkhd->wqhd)/dot_general | solution.py:99
  80.7 2.0 copy.212
  85.8 4.0 %all-to-all-start.1 = ((bf16[8,8,4,256]{3,1,2,0:T(8,128)(2,1)}), bf16[8,8,4,256]{3,1,2,0:T(8,128)(2,1)}, u32[]{:S(2)}, u32[]{:S(2)}) async-start(bf16[8,8,4,256]{3,1,2,0:T(8,128)(2,1)} %bitcast.36), calls=%async_computation.1 | async-start | bytes 262144 | tf_op jit(solution)/shard_map/all_to_all | solution.py:137
  92.7 1.8 fusion.103
  97.1 1.8 fusion.26
  106.8 3.3 %multiply_reduce_fusion.8 = (f32[1024]{0:T(1024)}, f32[1024]{0:T(1024)}, f32[1024]{0:T(1024)}, f32[1024]{0:T(1024)}, f32[1024]{0:T(1024)}, /*index=5*/f32[1024]{...) fusion(f32[18,18,1024]{2,1,0:T(8,128)S(1)} %convert_element_type.227, ...), kind=kLoop, calls=%fused_computation.115 | loop fusion | flops 14408704 | bytes 11083776 | tf_op jit(solution)/shard_map/transpose(jvp())/reduce_sum | solution.py:114
  111.5 4.5 %collective-permute-start.4 = (f32[1,16,1024]{2,1,0:T(8,128)S(1)}, f32[1,16,1024]{2,1,0:T(8,128)S(1)}, u32[]{:S(2)}, u32[]{:S(2)}) collective-permute-start(f32[1,16,1024]{2,1,0:T(8,128)S(1)} %get-tuple-element.91), channel_id=1, source_target_pairs={{0,4},{1,5},{2,6},{3,7},{8,12},{9,13},{10,14},{11,15},{16,20},{17,... | collective-permute-start | bytes 196616 | tf_op jit(solution)/shard_map/ppermute | solution.py:29
  122.3 3.7 %collective-permute-start.7 = (f32[18,1,1024]{2,1,0:T(1,128)S(1)}, f32[18,1,1024]{2,1,0:T(1,128)}, u32[]{:S(2)}, u32[]{:S(2)}) collective-permute-start(f32[18,1,1024]{2,1,0:T(1,128)S(1)} %get-tuple-element.84), channel_id=1, source_target_pairs={{0,1},{1,2},{2,3},{4,5},{5,6},{6,7},{8,9},{9,10},{10,11},{12,13},{... | collective-permute-start | bytes 221192 | tf_op jit(solution)/shard_map/ppermute | solution.py:29
  129.4 2.6 %fusion.28 = bf16[16,16,1024]{2,1,0:T(8,128)(2,1)} fusion(f32[16,16,1024]{2,1,0:T(8,128)S(1)} %copy-done.25, f32[18,17,1024]{2,1,0:T(8,128)S(1)} %get-tuple-element.82, f32[16,16,1024]{2,1,0:T(8,128)S(1)} %get-tuple-element.78, f32[1,16,1024]{2,1,0:T(8,128)S(1)} %copy-done.27, f32[18,17,1024]{2,1,0:T(8,128)S(1)} %get-tuple-element.81, ...), kind=kLoop, calls=%fused_computation.71 | loop fusion | flops 10747904 | bytes 9080832 | tf_op jit(solution)/shard_map/transpose(jvp())/add_any | solution.py:235
  137.3 31.1 %all_to_all.35 = bf16[4,8,8,4224]{3,2,0,1:T(8,128)(2,1)S(1)} all-to-all(bf16[4,8,8,4224]{3,2,0,1:T(8,128)(2,1)S(1)} %copy.246), channel_id=1, replica_groups=mesh['rep'=4,'sy'=2,'sx'=4] {'sy','sx'}, dimensions={1} | all-to-all | bytes 4325376 | tf_op jit(solution)/shard_map/all_to_all | solution.py:162
  169.4 6.0 %all-to-all-start.5 = ((bf16[4,8,4224]{2,1,0:T(8,128)(2,1)}), bf16[4,8,4224]{2,1,0:T(8,128)(2,1)S(1)}, u32[]{:S(2)}, u32[]{:S(2)}) async-start(bf16[4,8,4224]{2,1,0:T(8,128)(2,1)} %reduce_sum.322), calls=%async_computation.5 | async-start | bytes 540672 | tf_op jit(solution)/shard_map/all_to_all | solution.py:162
  177.4 7.1 %all-to-all-done.5 = bf16[4,8,4224]{2,1,0:T(8,128)(2,1)S(1)} async-done(((bf16[4,8,4224]{2,1,0:T(8,128)(2,1)}), bf16[4,8,4224]{2,1,0:T(8,128)(2,1)S(1)}, u32[]{:S(2)}, u32[]{:S(2)}) %all-to-all-start.5) | async-done | bytes 270368 | tf_op jit(solution)/shard_map/all_to_all | solution.py:162
  185.6 3.6 %all-to-all-start.6 = ((f32[8,8,4224]{2,1,0:T(8,128)}), f32[8,8,4224]{2,1,0:T(8,128)S(1)}, u32[]{:S(2)}, u32[]{:S(2)}) async-start(f32[8,8,4224]{2,1,0:T(8,128)} %broadcast_in_dim.113), calls=%async_computation.6 | async-start | bytes 2162688 | tf_op jit(solution)/shard_map/all_to_all | solution.py:184
  190.5 14.3 %all-to-all-done.6 = f32[8,8,4224]{2,1,0:T(8,128)S(1)} async-done(((f32[8,8,4224]{2,1,0:T(8,128)}), f32[8,8,4224]{2,1,0:T(8,128)S(1)}, u32[]{:S(2)}, u32[]{:S(2)}) %all-to-all-start.6) | async-done | bytes 1081376 | tf_op jit(solution)/shard_map/all_to_all | solution.py:184
  (359 shorter events, 84.9 us)
Async XLA Ops:
  1.7 10.5 %copy-start.14 = (bf16[1,16,16,256]{3,2,1,0:T(8,128)(2,1)S(1)}, bf16[1,16,16,256]{3,2,1,0:T(8,128)(2,1)}, u32[]{:S(2)}) copy-start(bf16[1,16,16,256]{3,2,1,0:T(8,128)(2,1)} %param.13) | copy-start | bytes 393220
  1.8 10.5 %copy-start.28 = (bf16[256,256]{1,0:T(8,128)(2,1)S(1)}, bf16[256,256]{1,0:T(8,128)(2,1)}, u32[]{:S(2)}) copy-start(bf16[256,256]{1,0:T(8,128)(2,1)} %param.23) | copy-start | bytes 393220
  3.5 13.8 %copy-start.3 = (bf16[1,16,16,256]{3,2,1,0:T(8,128)(2,1)S(1)}, bf16[1,16,16,256]{3,2,1,0:T(8,128)(2,1)}, u32[]{:S(2)}) copy-start(bf16[1,16,16,256]{3,2,1,0:T(8,128)(2,1)} %param.12) | copy-start | bytes 393220
  3.5 13.8 %copy-start.80 = (f32[256]{0:T(256)S(1)}, f32[256]{0:T(256)}, u32[]{:S(2)}) copy-start(f32[256]{0:T(256)} %param.14) | copy-start | bytes 3076
  5.9 16.0 %copy-start.75 = (f32[1024,9]{0,1:T(8,128)S(1)}, f32[1024,9]{0,1:T(8,128)}, u32[]{:S(2)}) copy-start(f32[1024,9]{0,1:T(8,128)} %param.16) | copy-start | bytes 110596
  6.0 11.5 %collective-permute-start.1 = (bf16[1,16,1024]{2,1,0:T(8,128)(2,1)S(1)}, bf16[1,16,1024]{2,1,0:T(8,128)(2,1)S(1)}, u32[]{:S(2)}, u32[]{:S(2)}) collective-permute-start(bf16[1,16,1024]{2,1,0:T(8,128)(2,1)S(1)} %get-tuple-element.96), channel_id=1, source_target_pairs={{4,0},{5,1},{6,2},{7,3},{12,8},{13,9},{14,10},{15,11},{20,16},{21,... | collective-permute-start | bytes 98312 | tf_op jit(solution)/shard_map/ppermute | solution.py:31
  7.4 10.1 %collective-permute-start = (bf16[1,16,1024]{2,1,0:T(8,128)(2,1)S(1)}, bf16[1,16,1024]{2,1,0:T(8,128)(2,1)S(1)}, u32[]{:S(2)}, u32[]{:S(2)}) collective-permute-start(bf16[1,16,1024]{2,1,0:T(8,128)(2,1)S(1)} %get-tuple-element.95), channel_id=1, source_target_pairs={{0,4},{1,5},{2,6},{3,7},{8,12},{9,13},{10,14},{11,15},{16,20},{17,... | collective-permute-start | bytes 98312 | tf_op jit(solution)/shard_map/ppermute | solution.py:29
  13.3 26.6 %all-to-all-start.2 = ((bf16[8,8,4,256]{3,1,2,0:T(8,128)(2,1)}), bf16[8,8,4,256]{3,1,2,0:T(8,128)(2,1)}, u32[]{:S(2)}, u32[]{:S(2)}) async-start(bf16[8,8,4,256]{3,1,2,0:T(8,128)(2,1)} %bitcast.44), calls=%async_computation.2 | async-start | bytes 262144 | tf_op jit(solution)/shard_map/all_to_all | solution.py:137
  17.6 5.8 %collective-permute-start.3 = (bf16[18,1,1024]{2,1,0:T(2,128)(2,1)S(1)}, bf16[18,1,1024]{2,1,0:T(2,128)(2,1)S(1)}, u32[]{:S(2)}, u32[]{:S(2)}) collective-permute-start(bf16[18,1,1024]{2,1,0:T(2,128)(2,1)S(1)} %get-tuple-element.94), channel_id=1, source_target_pairs={{1,0},{2,1},{3,2},{5,4},{6,5},{7,6},{9,8},{10,9},{11,10},{13,12},{... | collective-permute-start | bytes 110600 | tf_op jit(solution)/shard_map/ppermute | solution.py:31
  18.9 4.5 %collective-permute-start.2 = (bf16[18,1,1024]{2,1,0:T(2,128)(2,1)S(1)}, bf16[18,1,1024]{2,1,0:T(2,128)(2,1)S(1)}, u32[]{:S(2)}, u32[]{:S(2)}) collective-permute-start(bf16[18,1,1024]{2,1,0:T(2,128)(2,1)S(1)} %get-tuple-element.93), channel_id=1, source_target_pairs={{0,1},{1,2},{2,3},{4,5},{5,6},{6,7},{8,9},{9,10},{10,11},{12,13},{... | collective-permute-start | bytes 110600 | tf_op jit(solution)/shard_map/ppermute | solution.py:29
  35.1 11.0 %copy-start.93 = (f32[4,8,64]{2,1,0:T(8,128)S(1)}, f32[4,8,64]{2,1,0:T(8,128)}, u32[]{:S(2)}) copy-start(f32[4,8,64]{2,1,0:T(8,128)} %copy-done.92) | copy-start | bytes 24580
  36.3 56.3 %copy-start.1 = (f32[16,16,256]{2,1,0:T(8,128)}, f32[16,16,256]{2,1,0:T(8,128)S(1)}, u32[]{:S(2)}) copy-start(f32[16,16,256]{2,1,0:T(8,128)S(1)} %get-tuple-element.123) | copy-start | bytes 786436
  39.9 11.8 %all-to-all-start = ((bf16[8,8,4,256]{3,1,2,0:T(8,128)(2,1)}), bf16[8,8,4,256]{3,1,2,0:T(8,128)(2,1)}, u32[]{:S(2)}, u32[]{:S(2)}) async-start(bf16[8,8,4,256]{3,1,2,0:T(8,128)(2,1)} %bitcast.24), calls=%async_computation | async-start | bytes 262144 | tf_op jit(solution)/shard_map/all_to_all | solution.py:137
  68.8 11.9 %copy-start.4 = (bf16[4,64,768]{2,1,0:T(8,128)(2,1)}, bf16[4,64,768]{2,1,0:T(8,128)(2,1)S(1)}, u32[]{:S(2)}) copy-start(bf16[4,64,768]{2,1,0:T(8,128)(2,1)S(1)} %copy.223) | copy-start | bytes 1179652
  74.2 11.6 %all-to-all-start.3 = ((bf16[8,8,4,256]{3,1,2,0:T(8,128)(2,1)}), bf16[8,8,4,256]{3,1,2,0:T(8,128)(2,1)}, u32[]{:S(2)}, u32[]{:S(2)}) async-start(bf16[8,8,4,256]{3,1,2,0:T(8,128)(2,1)} %bitcast.330), calls=%async_computation.3 | async-start | bytes 262144 | tf_op jit(solution)/shard_map/all_to_all | solution.py:137
  85.8 31.0 %all-to-all-start.1 = ((bf16[8,8,4,256]{3,1,2,0:T(8,128)(2,1)}), bf16[8,8,4,256]{3,1,2,0:T(8,128)(2,1)}, u32[]{:S(2)}, u32[]{:S(2)}) async-start(bf16[8,8,4,256]{3,1,2,0:T(8,128)(2,1)} %bitcast.36), calls=%async_computation.1 | async-start | bytes 262144 | tf_op jit(solution)/shard_map/all_to_all | solution.py:137
  106.4 9.7 %copy-start.8 = (f32[16,16,256]{2,1,0:T(8,128)}, f32[16,16,256]{2,1,0:T(8,128)S(1)}, u32[]{:S(2)}) copy-start(f32[16,16,256]{2,1,0:T(8,128)S(1)} %add_add_fusion.4) | copy-start | bytes 786436
  110.2 10.7 %collective-permute-start.5 = (f32[1,16,1024]{2,1,0:T(8,128)S(1)}, f32[1,16,1024]{2,1,0:T(8,128)S(1)}, u32[]{:S(2)}, u32[]{:S(2)}) collective-permute-start(f32[1,16,1024]{2,1,0:T(8,128)S(1)} %get-tuple-element.92), channel_id=1, source_target_pairs={{4,0},{5,1},{6,2},{7,3},{12,8},{13,9},{14,10},{15,11},{20,16},{21,... | collective-permute-start | bytes 196616 | tf_op jit(solution)/shard_map/ppermute | solution.py:31
  111.5 9.4 %collective-permute-start.4 = (f32[1,16,1024]{2,1,0:T(8,128)S(1)}, f32[1,16,1024]{2,1,0:T(8,128)S(1)}, u32[]{:S(2)}, u32[]{:S(2)}) collective-permute-start(f32[1,16,1024]{2,1,0:T(8,128)S(1)} %get-tuple-element.91), channel_id=1, source_target_pairs={{0,4},{1,5},{2,6},{3,7},{8,12},{9,13},{10,14},{11,15},{16,20},{17,... | collective-permute-start | bytes 196616 | tf_op jit(solution)/shard_map/ppermute | solution.py:29
  116.7 9.3 %copy-start.83 = (f32[1024]{0:T(1024)S(1)}, f32[1024]{0:T(1024)}, u32[]{:S(2)}) copy-start(f32[1024]{0:T(1024)} %get-tuple-element.60) | copy-start | bytes 12292
  121.0 6.3 %collective-permute-start.6 = (f32[18,1,1024]{2,1,0:T(1,128)S(1)}, f32[18,1,1024]{2,1,0:T(1,128)S(1)}, u32[]{:S(2)}, u32[]{:S(2)}) collective-permute-start(f32[18,1,1024]{2,1,0:T(1,128)S(1)} %get-tuple-element.83), channel_id=1, source_target_pairs={{1,0},{2,1},{3,2},{5,4},{6,5},{7,6},{9,8},{10,9},{11,10},{13,12},{... | collective-permute-start | bytes 221192 | tf_op jit(solution)/shard_map/ppermute | solution.py:31
  122.3 5.6 %collective-permute-start.7 = (f32[18,1,1024]{2,1,0:T(1,128)S(1)}, f32[18,1,1024]{2,1,0:T(1,128)}, u32[]{:S(2)}, u32[]{:S(2)}) collective-permute-start(f32[18,1,1024]{2,1,0:T(1,128)S(1)} %get-tuple-element.84), channel_id=1, source_target_pairs={{0,1},{1,2},{2,3},{4,5},{5,6},{6,7},{8,9},{9,10},{10,11},{12,13},{... | collective-permute-start | bytes 221192 | tf_op jit(solution)/shard_map/ppermute | solution.py:29
  169.4 15.0 %all-to-all-start.5 = ((bf16[4,8,4224]{2,1,0:T(8,128)(2,1)}), bf16[4,8,4224]{2,1,0:T(8,128)(2,1)S(1)}, u32[]{:S(2)}, u32[]{:S(2)}) async-start(bf16[4,8,4224]{2,1,0:T(8,128)(2,1)} %reduce_sum.322), calls=%async_computation.5 | async-start | bytes 540672 | tf_op jit(solution)/shard_map/all_to_all | solution.py:162
  185.6 19.3 %all-to-all-start.6 = ((f32[8,8,4224]{2,1,0:T(8,128)}), f32[8,8,4224]{2,1,0:T(8,128)S(1)}, u32[]{:S(2)}, u32[]{:S(2)}) async-start(f32[8,8,4224]{2,1,0:T(8,128)} %broadcast_in_dim.113), calls=%async_computation.6 | async-start | bytes 2162688 | tf_op jit(solution)/shard_map/all_to_all | solution.py:184
  (90 other events, 302.0 us)

commit v4 on v3

--- a/solution.py
+++ b/solution.py
@@ -163,44 +163,53 @@
     return moved.astype(jnp.float32).sum(axis)
 
 
-def reduce_grads(grads):
+def reduce_packed(wide):
     parts = lax.axis_size("rep")
     tiles = lax.axis_size(("sy", "sx"))
-    channels = grads[0].shape[0]
-    small = jnp.concatenate(
-        [grads[2].reshape(channels, -1), grads[0][:, None], grads[4][:, None], grads[7][:, None]], axis=1
-    )
-    small_width = small.shape[1]
-    small = jnp.pad(small, ((0, 0), (0, -small_width % 128)))
-    wide = [grads[1], grads[5], grads[6], grads[8], grads[9], grads[3].reshape(channels, -1), small]
     widths = [piece.shape[1] for piece in wide]
     packed = jnp.concatenate(wide, axis=1)
-    width = packed.shape[1]
+    channels, width = packed.shape
     rows = channels // parts
     piece = rows // tiles
     local = exchange_sum(packed.reshape(parts, tiles, piece, width), ("sy", "sx"), 1)
     local = exchange_sum(local, "rep", 0)
-    spread = jnp.broadcast_to(local[None], (tiles, piece, width))
+    spread = jnp.broadcast_to(local[None].astype(jnp.bfloat16), (tiles, piece, width))
     total = lax.all_to_all(spread, ("sy", "sx"), split_axis=0, concat_axis=0, tiled=True)
-    total = total.reshape(rows, width)
+    total = total.astype(jnp.float32).reshape(rows, width)
     cuts = []
     offset = 0
     for size in widths:
         cuts.append(total[:, offset : offset + size])
         offset += size
-    small = cuts[6]
-    kernel_cols = grads[2].shape[1] * grads[2].shape[0] // channels
+    return cuts
+
+
+def pad_lanes(columns):
+    joined = jnp.concatenate(columns, axis=1)
+    return jnp.pad(joined, ((0, 0), (0, -joined.shape[1] % 128)))
+
+
+def reduce_grads(grads):
+    channels = grads[0].shape[0]
+    taps = grads[2].shape[1]
+    kernel_cols = taps * grads[2].shape[0] // channels
+    attention = reduce_packed(
+        [grads[5], grads[6], grads[8], grads[9], pad_lanes([grads[4][:, None], grads[7][:, None]])]
+    )
+    conv = reduce_packed(
+        [grads[1], grads[3].reshape(channels, -1), pad_lanes([grads[2].reshape(channels, -1), grads[0][:, None]])]
+    )
     return (
-        small[:, kernel_cols],
-        cuts[0],
-        small[:, :kernel_cols].reshape(-1, grads[2].shape[1]),
-        cuts[5].reshape(-1, grads[3].shape[1]),
-        small[:, kernel_cols + 1],
-        cuts[1],
-        cuts[2],
-        small[:, kernel_cols + 2],
-        cuts[3],
-        cuts[4],
+        conv[2][:, kernel_cols],
+        conv[0],
+        conv[2][:, :kernel_cols].reshape(-1, taps),
+        conv[1].reshape(-1, grads[3].shape[1]),
+        attention[4][:, 0],
+        attention[0],
+        attention[1],
+        attention[4][:, 1],
+        attention[2],
+        attention[3],
     )
 
 def body(

time: 211 us -> 229 us (1.085)
  blocking collectives: 31.1 us -> 0 us
  waiting for transfers between devices: 22.5 us -> 42.6 us
  starting transfers between devices: 49.3 us -> 64.4 us
  local copies, waits for them, and re-layouts: 48.6 us -> 56.7 us
  matrix products: 31.9 us -> 36 us
    all_to_all x1 -> x0, blocking collectives: 31.1 us -> none  [exchange_sum(): lax.all_to_all(values.astype(jnp.bfloat16), axes, split_axis=axis, concat...]
    all_to_all x1 -> x4, waiting for transfers between devices: 7.05 us -> 31.2 us  [exchange_sum(): lax.all_to_all(values.astype(jnp.bfloat16), axes, split_axis=axis, concat...]
    all_to_all x1 -> x4, starting transfers between devices: 5.98 us -> 17.1 us  [exchange_sum(): lax.all_to_all(values.astype(jnp.bfloat16), axes, split_axis=axis, concat...]
    reshape x2 -> x8, local copies, waits for them, and re-layouts: 0.85 us -> 9.95 us  [the longest x2 3.46 us: window_attention(): qkv_rows[..., channels:2 * channels]]
    dot_general x12, matrix products: 12.5 us -> 7.34 us  [project_rows(): product = jnp.dot(flattened, weight, preferred_element_type=jnp.float32)]
    dot_general x6, matrix products: 2.88 us -> 7.64 us  [outer_sum(): lax.dot_general(left_flat, right_flat, (((0,), (0,)), ((), ())), preferre...]
    dot_general x5 -> x1, local copies, waits for them, and re-layouts: 4.72 us -> 0.76 us  [outer_sum(): lax.dot_general(left_flat, right_flat, (((0,), (0,)), ((), ())), preferre...]
    all_to_all x1 -> x2, waiting for transfers between devices: 14.3 us -> 11 us  [reduce_packed(): lax.all_to_all(spread, ('sy', 'sx'), split_axis=0, concat_axis=0, tiled=T...]
  transfers between devices with their start and end apart: 14 -> 18, of which waited for: 3 -> 7; matrix products, arithmetic and copies ran while one was open for 28% -> 29% of each run, Pallas kernels for 0% -> 0%
where the time goes in v4:
time: 229 us; the launch traced here: 227 us
  starting transfers between devices  64.4 us (28%)
  local copies, waits for them, and re-layouts  56.7 us (25%)
  waiting for transfers between devices  42.6 us (19%)
  matrix products  36 us (16%)
  other arithmetic  24.8 us (11%)
  between operations  2.35 us (1%)
    all_to_all x4, waiting for transfers between devices, exchange_sum(): lax.all_to_all(values.astype(jnp.bfloat16), axes, split_axis=axis, concat...  31.2 us
    all_to_all x4, starting transfers between devices, swap_blocks(): lax.all_to_all(as_sent(flattened), ('sy', 'sx'), split_axis=0, concat_axi...  18.9 us
    all_to_all x4, starting transfers between devices, exchange_sum(): lax.all_to_all(values.astype(jnp.bfloat16), axes, split_axis=axis, concat...  17.1 us
    ppermute x4, starting transfers between devices, extended_2(): lax.ppermute(tail, axis, [(i, (i + 1) % count) for i in range(ends)])  16.1 us
    all_to_all x2, waiting for transfers between devices, reduce_packed(): lax.all_to_all(spread, ('sy', 'sx'), split_axis=0, concat_axis=0, tiled=T...  11 us
    dot_general x6, matrix products, window_attention(): jnp.einsum('whqk,wkhd->wqhd', softmax_out, value_rows, preferred_element_...  10.3 us
    dot_general x6, matrix products, outer_sum(): lax.dot_general(left_flat, right_flat, (((0,), (0,)), ((), ())), preferre...  7.64 us
    dot_general x12, matrix products, project_rows(): product = jnp.dot(flattened, weight, preferred_element_type=jnp.float32)  7.34 us
  transfers between devices with their start and end apart: 18, of which 7 were waited for; matrix products, arithmetic and copies ran while one was open for 29% of the time, Pallas kernels for 0%

profile of v4, /device:TPU:0, one launch (start us, length us, event | category | flops | bytes accessed | tf_op | source)
XLA Modules:
  0.0 226.9 jit_solution(2728445972301960073)
XLA Ops:
  3.5 2.4 %multiply_convert_fusion.1 = (bf16[16,16,1024]{2,1,0:T(8,128)(2,1)S(1)}, f32[16,16,1024]{2,1,0:T(8,128)}) fusion(bf16[256,1024]{1,0:T(8,128)(2,1)S(1)} %copy-done, bf16[1,16,16,256]{3,2,1,0:T(8,128)(2,1)} %param.12, f32[256]{0:T(256)} %param.14, f32[16,16]{1,0:T(8,128)S(1)} %fusion.96, f32[16,16]{1,0:T(8,128)S(1)} %broadcast_multiply_fusion.2), kind=kOutput, calls=%fused_computation.120 | convolution fusion | flops 136904704 | bytes 2231296 | tf_op jit(solution)/shard_map/jvp()/dot_general | solution.py:52
  7.4 4.9 %collective-permute-start = (bf16[1,16,1024]{2,1,0:T(8,128)(2,1)S(1)}, bf16[1,16,1024]{2,1,0:T(8,128)(2,1)S(1)}, u32[]{:S(2)}, u32[]{:S(2)}) collective-permute-start(bf16[1,16,1024]{2,1,0:T(8,128)(2,1)S(1)} %get-tuple-element.94), channel_id=1, source_target_pairs={{0,4},{1,5},{2,6},{3,7},{8,12},{9,13},{10,14},{11,15},{16,20},{17,... | collective-permute-start | bytes 98312 | tf_op jit(solution)/shard_map/ppermute | solution.py:29
  13.3 4.0 %all-to-all-start.2 = ((bf16[8,8,4,256]{3,1,2,0:T(8,128)(2,1)}), bf16[8,8,4,256]{3,1,2,0:T(8,128)(2,1)}, u32[]{:S(2)}, u32[]{:S(2)}) async-start(bf16[8,8,4,256]{3,1,2,0:T(8,128)(2,1)} %bitcast.44), calls=%async_computation.2 | async-start | bytes 262144 | tf_op jit(solution)/shard_map/all_to_all | solution.py:137
  18.9 3.0 %collective-permute-start.2 = (bf16[18,1,1024]{2,1,0:T(2,128)(2,1)S(1)}, bf16[18,1,1024]{2,1,0:T(2,128)(2,1)S(1)}, u32[]{:S(2)}, u32[]{:S(2)}) collective-permute-start(bf16[18,1,1024]{2,1,0:T(2,128)(2,1)S(1)} %get-tuple-element.86), channel_id=1, source_target_pairs={{0,1},{1,2},{2,3},{4,5},{5,6},{6,7},{8,9},{9,10},{10,11},{12,13},{... | collective-permute-start | bytes 110600 | tf_op jit(solution)/shard_map/ppermute | solution.py:29
  27.6 2.5 %fusion.113 = (f32[4,8,64]{2,1,0:T(8,128)S(1)}, f32[4,8,64,64]{2,3,1,0:T(8,128)}) fusion(bf16[4,64,8,32]{1,3,2,0:T(8,128)(2,1)S(1)} %bitcast.312, bf16[4,64,8,32]{1,3,2,0:T(8,128)(2,1)} %bitcast.314), kind=kOutput, calls=%fused_computation.229 | convolution fusion | flops 8781887 | bytes 794624 | tf_op jit(solution)/shard_map/jvp()/sub | solution.py:98
  36.7 6.7 %all-to-all-start = ((bf16[8,8,4,256]{3,1,2,0:T(8,128)(2,1)}), bf16[8,8,4,256]{3,1,2,0:T(8,128)(2,1)}, u32[]{:S(2)}, u32[]{:S(2)}) async-start(bf16[8,8,4,256]{3,1,2,0:T(8,128)(2,1)} %bitcast.24), calls=%async_computation | async-start | bytes 262144 | tf_op jit(solution)/shard_map/all_to_all | solution.py:137
  56.9 3.2 %fusion.115 = (f32[4,8,64]{2,1,0:T(8,128)}, f32[4,8,64,64]{2,3,1,0:T(8,128)}) fusion(bf16[4,64,8,32]{1,3,2,0:T(8,128)(2,1)} %bitcast.316, bf16[4,64,8,32]{1,3,2,0:T(8,128)(2,1)} %bitcast.321), kind=kOutput, calls=%fused_computation.231 | convolution fusion | flops 8781887 | bytes 794624 | tf_op jit(solution)/shard_map/jvp()/sub | solution.py:98
  73.5 4.0 %all-to-all-start.3 = ((bf16[8,8,4,256]{3,1,2,0:T(8,128)(2,1)}), bf16[8,8,4,256]{3,1,2,0:T(8,128)(2,1)}, u32[]{:S(2)}, u32[]{:S(2)}) async-start(bf16[8,8,4,256]{3,1,2,0:T(8,128)(2,1)} %bitcast.59), calls=%async_computation.3 | async-start | bytes 262144 | tf_op jit(solution)/shard_map/all_to_all | solution.py:137
  83.9 4.2 %all-to-all-start.1 = ((bf16[8,8,4,256]{3,1,2,0:T(8,128)(2,1)}), bf16[8,8,4,256]{3,1,2,0:T(8,128)(2,1)}, u32[]{:S(2)}, u32[]{:S(2)}) async-start(bf16[8,8,4,256]{3,1,2,0:T(8,128)(2,1)} %bitcast.36), calls=%async_computation.1 | async-start | bytes 262144 | tf_op jit(solution)/shard_map/all_to_all | solution.py:137
  113.0 2.7 %multiply_reduce_fusion.8 = (f32[1024]{0:T(1024)S(1)}, f32[1024]{0:T(1024)S(1)}, f32[1024]{0:T(1024)S(1)}, f32[1024]{0:T(1024)S(1)}, f32[1024]{0:T(1024)S(1)}, /...) fusion(f32[18,18,1024]{2,1,0:T(8,128)S(1)} %convert_element_typ, ...), kind=kLoop, calls=%fused_computation.115 | loop fusion | flops 14408704 | bytes 11083776 | tf_op jit(solution)/shard_map/transpose(jvp())/reduce_sum | solution.py:114
  117.9 4.5 %collective-permute-start.4 = (f32[1,16,1024]{2,1,0:T(8,128)}, f32[1,16,1024]{2,1,0:T(8,128)S(1)}, u32[]{:S(2)}, u32[]{:S(2)}) collective-permute-start(f32[1,16,1024]{2,1,0:T(8,128)} %get-tuple-element.84), channel_id=1, source_target_pairs={{0,4},{1,5},{2,6},{3,7},{8,12},{9,13},{10,14},{11,15},{16,20},{17,... | collective-permute-start | bytes 196616 | tf_op jit(solution)/shard_map/ppermute | solution.py:29
  133.7 3.7 %collective-permute-start.7 = (f32[18,1,1024]{2,1,0:T(1,128)S(1)}, f32[18,1,1024]{2,1,0:T(1,128)}, u32[]{:S(2)}, u32[]{:S(2)}) collective-permute-start(f32[18,1,1024]{2,1,0:T(1,128)S(1)} %get-tuple-element.83), channel_id=1, source_target_pairs={{0,1},{1,2},{2,3},{4,5},{5,6},{6,7},{8,9},{9,10},{10,11},{12,13},{... | collective-permute-start | bytes 221192 | tf_op jit(solution)/shard_map/ppermute | solution.py:29
  140.3 4.2 %all-to-all-start.7 = ((bf16[4,8,8,2176]{3,2,0,1:T(8,128)(2,1)}), bf16[4,8,8,2176]{3,2,0,1:T(8,128)(2,1)}, u32[]{:S(2)}, u32[]{:S(2)}) async-start(bf16[4,8,8,2176]{3,2,0,1:T(8,128)(2,1)} %copy.258), calls=%async_computation.7 | async-start | bytes 2228224 | tf_op jit(solution)/shard_map/all_to_all | solution.py:162
  152.8 7.9 %all-to-all-done.7 = bf16[4,8,8,2176]{3,2,0,1:T(8,128)(2,1)} async-done(((bf16[4,8,8,2176]{3,2,0,1:T(8,128)(2,1)}), bf16[4,8,8,2176]{3,2,0,1:T(8,128)(2,1)}, u32[]{:S(2)}, u32[]{:S(2)}) %all-to-all-start.7) | async-done | bytes 1114144 | tf_op jit(solution)/shard_map/all_to_all | solution.py:162
  160.7 3.6 %all-to-all-start.4 = ((bf16[4,8,8,2176]{3,2,0,1:T(8,128)(2,1)}), bf16[4,8,8,2176]{3,2,0,1:T(8,128)(2,1)S(1)}, u32[]{:S(2)}, u32[]{:S(2)}) async-start(bf16[4,8,8,2176]{3,2,0,1:T(8,128)(2,1)} %copy.251), calls=%async_computation.4 | async-start | bytes 2228224 | tf_op jit(solution)/shard_map/all_to_all | solution.py:162
  167.5 12.8 %all-to-all-done.4 = bf16[4,8,8,2176]{3,2,0,1:T(8,128)(2,1)S(1)} async-done(((bf16[4,8,8,2176]{3,2,0,1:T(8,128)(2,1)}), bf16[4,8,8,2176]{3,2,0,1:T(8,128)(2,1)S(1)}, u32[]{:S(2)}, u32[]{:S(2)}) %all-to-all-start.4) | async-done | bytes 1114144 | tf_op jit(solution)/shard_map/all_to_all | solution.py:162
  180.3 6.0 %all-to-all-start.8 = ((bf16[4,8,2176]{2,1,0:T(8,128)(2,1)}), bf16[4,8,2176]{2,1,0:T(8,128)(2,1)S(1)}, u32[]{:S(2)}, u32[]{:S(2)}) async-start(bf16[4,8,2176]{2,1,0:T(8,128)(2,1)} %reduce_sum.358), calls=%async_computation.8 | async-start | bytes 278528 | tf_op jit(solution)/shard_map/all_to_all | solution.py:162
  187.4 4.8 %all-to-all-done.8 = bf16[4,8,2176]{2,1,0:T(8,128)(2,1)S(1)} async-done(((bf16[4,8,2176]{2,1,0:T(8,128)(2,1)}), bf16[4,8,2176]{2,1,0:T(8,128)(2,1)S(1)}, u32[]{:S(2)}, u32[]{:S(2)}) %all-to-all-start.8) | async-done | bytes 139296 | tf_op jit(solution)/shard_map/all_to_all | solution.py:162
  192.2 3.3 %all-to-all-start.5 = ((bf16[4,8,2176]{2,1,0:T(8,128)(2,1)}), bf16[4,8,2176]{2,1,0:T(8,128)(2,1)S(1)}, u32[]{:S(2)}, u32[]{:S(2)}) async-start(bf16[4,8,2176]{2,1,0:T(8,128)(2,1)} %reduce_sum.351), calls=%async_computation.5 | async-start | bytes 278528 | tf_op jit(solution)/shard_map/all_to_all | solution.py:162
  195.7 5.8 %all-to-all-done.5 = bf16[4,8,2176]{2,1,0:T(8,128)(2,1)S(1)} async-done(((bf16[4,8,2176]{2,1,0:T(8,128)(2,1)}), bf16[4,8,2176]{2,1,0:T(8,128)(2,1)S(1)}, u32[]{:S(2)}, u32[]{:S(2)}) %all-to-all-start.5) | async-done | bytes 139296 | tf_op jit(solution)/shard_map/all_to_all | solution.py:162
  202.2 3.4 %all-to-all-start.9 = ((bf16[8,8,2176]{2,1,0:T(8,128)(2,1)}), bf16[8,8,2176]{2,1,0:T(8,128)(2,1)S(1)}, u32[]{:S(2)}, u32[]{:S(2)}) async-start(bf16[8,8,2176]{2,1,0:T(8,128)(2,1)} %broadcast_in_dim.120), calls=%async_computation.9 | async-start | bytes 557056 | tf_op jit(solution)/shard_map/all_to_all | solution.py:177
  206.5 6.1 %all-to-all-done.9 = bf16[8,8,2176]{2,1,0:T(8,128)(2,1)S(1)} async-done(((bf16[8,8,2176]{2,1,0:T(8,128)(2,1)}), bf16[8,8,2176]{2,1,0:T(8,128)(2,1)S(1)}, u32[]{:S(2)}, u32[]{:S(2)}) %all-to-all-start.9) | async-done | bytes 278560 | tf_op jit(solution)/shard_map/all_to_all | solution.py:177
  213.3 3.4 %all-to-all-start.6 = ((bf16[8,8,2176]{2,1,0:T(8,128)(2,1)}), bf16[8,8,2176]{2,1,0:T(8,128)(2,1)S(1)}, u32[]{:S(2)}, u32[]{:S(2)}) async-start(bf16[8,8,2176]{2,1,0:T(8,128)(2,1)} %broadcast_in_dim.117), calls=%async_computation.6 | async-start | bytes 557056 | tf_op jit(solution)/shard_map/all_to_all | solution.py:177
  218.9 4.9 %all-to-all-done.6 = bf16[8,8,2176]{2,1,0:T(8,128)(2,1)S(1)} async-done(((bf16[8,8,2176]{2,1,0:T(8,128)(2,1)}), bf16[8,8,2176]{2,1,0:T(8,128)(2,1)S(1)}, u32[]{:S(2)}, u32[]{:S(2)}) %all-to-all-start.6) | async-done | bytes 278560 | tf_op jit(solution)/shard_map/all_to_all | solution.py:177
  (353 shorter events, 112.5 us)
Async XLA Ops:
  5.9 16.0 %copy-start.77 = (f32[1024,9]{0,1:T(8,128)S(1)}, f32[1024,9]{0,1:T(8,128)}, u32[]{:S(2)}) copy-start(f32[1024,9]{0,1:T(8,128)} %param.16) | copy-start | bytes 110596
  5.9 11.5 %collective-permute-start.1 = (bf16[1,16,1024]{2,1,0:T(8,128)(2,1)S(1)}, bf16[1,16,1024]{2,1,0:T(8,128)(2,1)S(1)}, u32[]{:S(2)}, u32[]{:S(2)}) collective-permute-start(bf16[1,16,1024]{2,1,0:T(8,128)(2,1)S(1)} %get-tuple-element.95), channel_id=1, source_target_pairs={{4,0},{5,1},{6,2},{7,3},{12,8},{13,9},{14,10},{15,11},{20,16},{21,... | collective-permute-start | bytes 98312 | tf_op jit(solution)/shard_map/ppermute | solution.py:31
  7.4 10.1 %collective-permute-start = (bf16[1,16,1024]{2,1,0:T(8,128)(2,1)S(1)}, bf16[1,16,1024]{2,1,0:T(8,128)(2,1)S(1)}, u32[]{:S(2)}, u32[]{:S(2)}) collective-permute-start(bf16[1,16,1024]{2,1,0:T(8,128)(2,1)S(1)} %get-tuple-element.94), channel_id=1, source_target_pairs={{0,4},{1,5},{2,6},{3,7},{8,12},{9,13},{10,14},{11,15},{16,20},{17,... | collective-permute-start | bytes 98312 | tf_op jit(solution)/shard_map/ppermute | solution.py:29
  13.3 23.4 %all-to-all-start.2 = ((bf16[8,8,4,256]{3,1,2,0:T(8,128)(2,1)}), bf16[8,8,4,256]{3,1,2,0:T(8,128)(2,1)}, u32[]{:S(2)}, u32[]{:S(2)}) async-start(bf16[8,8,4,256]{3,1,2,0:T(8,128)(2,1)} %bitcast.44), calls=%async_computation.2 | async-start | bytes 262144 | tf_op jit(solution)/shard_map/all_to_all | solution.py:137
  17.6 5.2 %collective-permute-start.3 = (bf16[18,1,1024]{2,1,0:T(2,128)(2,1)S(1)}, bf16[18,1,1024]{2,1,0:T(2,128)(2,1)S(1)}, u32[]{:S(2)}, u32[]{:S(2)}) collective-permute-start(bf16[18,1,1024]{2,1,0:T(2,128)(2,1)S(1)} %get-tuple-element.87), channel_id=1, source_target_pairs={{1,0},{2,1},{3,2},{5,4},{6,5},{7,6},{9,8},{10,9},{11,10},{13,12},{... | collective-permute-start | bytes 110600 | tf_op jit(solution)/shard_map/ppermute | solution.py:31
  18.9 3.9 %collective-permute-start.2 = (bf16[18,1,1024]{2,1,0:T(2,128)(2,1)S(1)}, bf16[18,1,1024]{2,1,0:T(2,128)(2,1)S(1)}, u32[]{:S(2)}, u32[]{:S(2)}) collective-permute-start(bf16[18,1,1024]{2,1,0:T(2,128)(2,1)S(1)} %get-tuple-element.86), channel_id=1, source_target_pairs={{0,1},{1,2},{2,3},{4,5},{5,6},{6,7},{8,9},{9,10},{10,11},{12,13},{... | collective-permute-start | bytes 110600 | tf_op jit(solution)/shard_map/ppermute | solution.py:29
  22.1 90.9 %copy-start.52 = (f32[1024,1]{0,1:T(1,128)}, f32[1024,1]{0,1:T(1,128)S(1)}, u32[]{:S(2)}) copy-start(f32[1024,1]{0,1:T(1,128)S(1)} %get-tuple-element.102) | copy-start | bytes 12292
  22.1 90.9 %copy-start.54 = (f32[1024,1]{0,1:T(1,128)}, f32[1024,1]{0,1:T(1,128)S(1)}, u32[]{:S(2)}) copy-start(f32[1024,1]{0,1:T(1,128)S(1)} %get-tuple-element.103) | copy-start | bytes 12292
  35.5 55.4 %copy-start.1 = (f32[16,16,256]{2,1,0:T(8,128)}, f32[16,16,256]{2,1,0:T(8,128)S(1)}, u32[]{:S(2)}) copy-start(f32[16,16,256]{2,1,0:T(8,128)S(1)} %get-tuple-element.122) | copy-start | bytes 786436
  36.7 12.4 %all-to-all-start = ((bf16[8,8,4,256]{3,1,2,0:T(8,128)(2,1)}), bf16[8,8,4,256]{3,1,2,0:T(8,128)(2,1)}, u32[]{:S(2)}, u32[]{:S(2)}) async-start(bf16[8,8,4,256]{3,1,2,0:T(8,128)(2,1)} %bitcast.24), calls=%async_computation | async-start | bytes 262144 | tf_op jit(solution)/shard_map/all_to_all | solution.py:137
  73.5 10.4 %all-to-all-start.3 = ((bf16[8,8,4,256]{3,1,2,0:T(8,128)(2,1)}), bf16[8,8,4,256]{3,1,2,0:T(8,128)(2,1)}, u32[]{:S(2)}, u32[]{:S(2)}) async-start(bf16[8,8,4,256]{3,1,2,0:T(8,128)(2,1)} %bitcast.59), calls=%async_computation.3 | async-start | bytes 262144 | tf_op jit(solution)/shard_map/all_to_all | solution.py:137
  83.9 18.0 %all-to-all-start.1 = ((bf16[8,8,4,256]{3,1,2,0:T(8,128)(2,1)}), bf16[8,8,4,256]{3,1,2,0:T(8,128)(2,1)}, u32[]{:S(2)}, u32[]{:S(2)}) async-start(bf16[8,8,4,256]{3,1,2,0:T(8,128)(2,1)} %bitcast.36), calls=%async_computation.1 | async-start | bytes 262144 | tf_op jit(solution)/shard_map/all_to_all | solution.py:137
  116.5 15.8 %collective-permute-start.5 = (f32[1,16,1024]{2,1,0:T(8,128)}, f32[1,16,1024]{2,1,0:T(8,128)S(1)}, u32[]{:S(2)}, u32[]{:S(2)}) collective-permute-start(f32[1,16,1024]{2,1,0:T(8,128)} %get-tuple-element.85), channel_id=1, source_target_pairs={{4,0},{5,1},{6,2},{7,3},{12,8},{13,9},{14,10},{15,11},{20,16},{21,... | collective-permute-start | bytes 196616 | tf_op jit(solution)/shard_map/ppermute | solution.py:31
  117.9 14.3 %collective-permute-start.4 = (f32[1,16,1024]{2,1,0:T(8,128)}, f32[1,16,1024]{2,1,0:T(8,128)S(1)}, u32[]{:S(2)}, u32[]{:S(2)}) collective-permute-start(f32[1,16,1024]{2,1,0:T(8,128)} %get-tuple-element.84), channel_id=1, source_target_pairs={{0,4},{1,5},{2,6},{3,7},{8,12},{9,13},{10,14},{11,15},{16,20},{17,... | collective-permute-start | bytes 196616 | tf_op jit(solution)/shard_map/ppermute | solution.py:29
  132.4 12.3 %collective-permute-start.6 = (f32[18,1,1024]{2,1,0:T(1,128)S(1)}, f32[18,1,1024]{2,1,0:T(1,128)S(1)}, u32[]{:S(2)}, u32[]{:S(2)}) collective-permute-start(f32[18,1,1024]{2,1,0:T(1,128)S(1)} %get-tuple-element.82), channel_id=1, source_target_pairs={{1,0},{2,1},{3,2},{5,4},{6,5},{7,6},{9,8},{10,9},{11,10},{13,12},{... | collective-permute-start | bytes 221192 | tf_op jit(solution)/shard_map/ppermute | solution.py:31
  133.7 11.6 %collective-permute-start.7 = (f32[18,1,1024]{2,1,0:T(1,128)S(1)}, f32[18,1,1024]{2,1,0:T(1,128)}, u32[]{:S(2)}, u32[]{:S(2)}) collective-permute-start(f32[18,1,1024]{2,1,0:T(1,128)S(1)} %get-tuple-element.83), channel_id=1, source_target_pairs={{0,1},{1,2},{2,3},{4,5},{5,6},{6,7},{8,9},{9,10},{10,11},{12,13},{... | collective-permute-start | bytes 221192 | tf_op jit(solution)/shard_map/ppermute | solution.py:29
  140.3 20.4 %all-to-all-start.7 = ((bf16[4,8,8,2176]{3,2,0,1:T(8,128)(2,1)}), bf16[4,8,8,2176]{3,2,0,1:T(8,128)(2,1)}, u32[]{:S(2)}, u32[]{:S(2)}) async-start(bf16[4,8,8,2176]{3,2,0,1:T(8,128)(2,1)} %copy.258), calls=%async_computation.7 | async-start | bytes 2228224 | tf_op jit(solution)/shard_map/all_to_all | solution.py:162
  160.7 19.6 %all-to-all-start.4 = ((bf16[4,8,8,2176]{3,2,0,1:T(8,128)(2,1)}), bf16[4,8,8,2176]{3,2,0,1:T(8,128)(2,1)S(1)}, u32[]{:S(2)}, u32[]{:S(2)}) async-start(bf16[4,8,8,2176]{3,2,0,1:T(8,128)(2,1)} %copy.251), calls=%async_computation.4 | async-start | bytes 2228224 | tf_op jit(solution)/shard_map/all_to_all | solution.py:162
  164.2 22.0 %copy-start.84 = (f32[256]{0:T(256)S(1)}, f32[256]{0:T(256)}, u32[]{:S(2)}) copy-start(f32[256]{0:T(256)} %param.14) | copy-start | bytes 3076
  167.5 38.1 %copy-start.8 = (f32[16,16,256]{2,1,0:T(8,128)S(1)}, f32[16,16,256]{2,1,0:T(8,128)}, u32[]{:S(2)}) copy-start(f32[16,16,256]{2,1,0:T(8,128)} %copy-done.7) | copy-start | bytes 786436
  180.3 11.9 %all-to-all-start.8 = ((bf16[4,8,2176]{2,1,0:T(8,128)(2,1)}), bf16[4,8,2176]{2,1,0:T(8,128)(2,1)S(1)}, u32[]{:S(2)}, u32[]{:S(2)}) async-start(bf16[4,8,2176]{2,1,0:T(8,128)(2,1)} %reduce_sum.358), calls=%async_computation.8 | async-start | bytes 278528 | tf_op jit(solution)/shard_map/all_to_all | solution.py:162
  192.2 9.2 %all-to-all-start.5 = ((bf16[4,8,2176]{2,1,0:T(8,128)(2,1)}), bf16[4,8,2176]{2,1,0:T(8,128)(2,1)S(1)}, u32[]{:S(2)}, u32[]{:S(2)}) async-start(bf16[4,8,2176]{2,1,0:T(8,128)(2,1)} %reduce_sum.351), calls=%async_computation.5 | async-start | bytes 278528 | tf_op jit(solution)/shard_map/all_to_all | solution.py:162
  202.2 10.5 %all-to-all-start.9 = ((bf16[8,8,2176]{2,1,0:T(8,128)(2,1)}), bf16[8,8,2176]{2,1,0:T(8,128)(2,1)S(1)}, u32[]{:S(2)}, u32[]{:S(2)}) async-start(bf16[8,8,2176]{2,1,0:T(8,128)(2,1)} %broadcast_in_dim.120), calls=%async_computation.9 | async-start | bytes 557056 | tf_op jit(solution)/shard_map/all_to_all | solution.py:177
  213.3 10.5 %all-to-all-start.6 = ((bf16[8,8,2176]{2,1,0:T(8,128)(2,1)}), bf16[8,8,2176]{2,1,0:T(8,128)(2,1)S(1)}, u32[]{:S(2)}, u32[]{:S(2)}) async-start(bf16[8,8,2176]{2,1,0:T(8,128)(2,1)} %broadcast_in_dim.117), calls=%async_computation.6 | async-start | bytes 557056 | tf_op jit(solution)/shard_map/all_to_all | solution.py:177
  (83 other events, 345.3 us)

commit v5 on v3

--- a/solution.py
+++ b/solution.py
@@ -163,37 +163,43 @@
     return moved.astype(jnp.float32).sum(axis)
 
 
-def reduce_grads(grads):
+def reduce_packed(wide):
     parts = lax.axis_size("rep")
     tiles = lax.axis_size(("sy", "sx"))
-    channels = grads[0].shape[0]
-    small = jnp.concatenate(
-        [grads[2].reshape(channels, -1), grads[0][:, None], grads[4][:, None], grads[7][:, None]], axis=1
-    )
-    small_width = small.shape[1]
-    small = jnp.pad(small, ((0, 0), (0, -small_width % 128)))
-    wide = [grads[1], grads[5], grads[6], grads[8], grads[9], grads[3].reshape(channels, -1), small]
     widths = [piece.shape[1] for piece in wide]
     packed = jnp.concatenate(wide, axis=1)
-    width = packed.shape[1]
+    channels, width = packed.shape
     rows = channels // parts
     piece = rows // tiles
     local = exchange_sum(packed.reshape(parts, tiles, piece, width), ("sy", "sx"), 1)
     local = exchange_sum(local, "rep", 0)
-    spread = jnp.broadcast_to(local[None], (tiles, piece, width))
+    spread = jnp.broadcast_to(local[None].astype(jnp.bfloat16), (tiles, piece, width))
     total = lax.all_to_all(spread, ("sy", "sx"), split_axis=0, concat_axis=0, tiled=True)
-    total = total.reshape(rows, width)
+    total = total.astype(jnp.float32).reshape(rows, width)
     cuts = []
     offset = 0
     for size in widths:
         cuts.append(total[:, offset : offset + size])
         offset += size
+    return cuts
+
+
+def pad_lanes(columns):
+    joined = jnp.concatenate(columns, axis=1)
+    return jnp.pad(joined, ((0, 0), (0, -joined.shape[1] % 128)))
+
+
+def reduce_grads(grads):
+    channels = grads[0].shape[0]
+    taps = grads[2].shape[1]
+    kernel_cols = taps * grads[2].shape[0] // channels
+    small = pad_lanes([grads[2].reshape(channels, -1), grads[0][:, None], grads[4][:, None], grads[7][:, None]])
+    cuts = reduce_packed([grads[1], grads[5], grads[6], grads[8], grads[9], grads[3].reshape(channels, -1), small])
     small = cuts[6]
-    kernel_cols = grads[2].shape[1] * grads[2].shape[0] // channels
     return (
         small[:, kernel_cols],
         cuts[0],
-        small[:, :kernel_cols].reshape(-1, grads[2].shape[1]),
+        small[:, :kernel_cols].reshape(-1, taps),
         cuts[5].reshape(-1, grads[3].shape[1]),
         small[:, kernel_cols + 1],
         cuts[1],

time: 211 us -> 201 us (0.953)
  blocking collectives: 31.1 us -> 0 us
  waiting for transfers between devices: 22.5 us -> 40.8 us
  starting transfers between devices: 49.3 us -> 55.4 us
  matrix products: 31.9 us -> 29.5 us
    all_to_all x1 -> x0, blocking collectives: 31.1 us -> none  [exchange_sum(): lax.all_to_all(values.astype(jnp.bfloat16), axes, split_axis=axis, concat...]
    all_to_all x1 -> x2, waiting for transfers between devices: 7.05 us -> 31.4 us  [exchange_sum(): lax.all_to_all(values.astype(jnp.bfloat16), axes, split_axis=axis, concat...]
    all_to_all x1, waiting for transfers between devices: 14.3 us -> 8.7 us  [reduce_packed(): lax.all_to_all(spread, ('sy', 'sx'), split_axis=0, concat_axis=0, tiled=T...]
    all_to_all x1 -> x2, starting transfers between devices: 5.98 us -> 11.4 us  [exchange_sum(): lax.all_to_all(values.astype(jnp.bfloat16), axes, split_axis=axis, concat...]
    unnamed x203 -> x147, local copies, waits for them, and re-layouts: 4.36 us -> 3.53 us
  transfers between devices with their start and end apart: 14 -> 15, of which waited for: 3 -> 5; matrix products, arithmetic and copies ran while one was open for 28% -> 30% of each run, Pallas kernels for 0% -> 0%
where the time goes in v5:
time: 201 us; the launch traced here: 199 us
  starting transfers between devices  55.4 us (28%)
  local copies, waits for them, and re-layouts  47.7 us (24%)
  waiting for transfers between devices  40.8 us (20%)
  matrix products  29.5 us (15%)
  other arithmetic  23.3 us (12%)
  between operations  2.26 us (1%)
    all_to_all x2, waiting for transfers between devices, exchange_sum(): lax.all_to_all(values.astype(jnp.bfloat16), axes, split_axis=axis, concat...  31.4 us
    all_to_all x4, starting transfers between devices, swap_blocks(): lax.all_to_all(as_sent(flattened), ('sy', 'sx'), split_axis=0, concat_axi...  18.9 us
    ppermute x4, starting transfers between devices, extended_2(): lax.ppermute(tail, axis, [(i, (i + 1) % count) for i in range(ends)])  15.5 us
    dot_general x12, matrix products, project_rows(): product = jnp.dot(flattened, weight, preferred_element_type=jnp.float32)  11.4 us
    all_to_all x2, starting transfers between devices, exchange_sum(): lax.all_to_all(values.astype(jnp.bfloat16), axes, split_axis=axis, concat...  11.4 us
    dot_general x6, matrix products, window_attention(): jnp.einsum('whqk,wkhd->wqhd', softmax_out, value_rows, preferred_element_...  8.97 us
    all_to_all x1, waiting for transfers between devices, reduce_packed(): lax.all_to_all(spread, ('sy', 'sx'), split_axis=0, concat_axis=0, tiled=T...  8.7 us
    ppermute x4, starting transfers between devices, extended_2(): lax.ppermute(head, axis, [((i + 1) % count, i) for i in range(ends)])  5.3 us
  transfers between devices with their start and end apart: 15, of which 5 were waited for; matrix products, arithmetic and copies ran while one was open for 30% of the time, Pallas kernels for 0%

profile of v5, /device:TPU:0, one launch (start us, length us, event | category | flops | bytes accessed | tf_op | source)
XLA Modules:
  0.0 198.9 jit_solution(2519167773592595270)
XLA Ops:
  3.0 2.4 %multiply_convert_fusion.1 = (bf16[16,16,1024]{2,1,0:T(8,128)(2,1)S(1)}, f32[16,16,1024]{2,1,0:T(8,128)}) fusion(bf16[256,1024]{1,0:T(8,128)(2,1)S(1)} %copy-done, bf16[1,16,16,256]{3,2,1,0:T(8,128)(2,1)} %param.12, f32[256]{0:T(256)} %param.14, f32[16,16]{1,0:T(8,128)S(1)} %fusion.97, f32[16,16]{1,0:T(8,128)S(1)} %broadcast_multiply_fusion.2), kind=kOutput, calls=%fused_computation.120 | convolution fusion | flops 136904704 | bytes 2231296 | tf_op jit(solution)/shard_map/jvp()/dot_general | solution.py:52
  6.8 4.9 %collective-permute-start = (bf16[1,16,1024]{2,1,0:T(8,128)(2,1)S(1)}, bf16[1,16,1024]{2,1,0:T(8,128)(2,1)S(1)}, u32[]{:S(2)}, u32[]{:S(2)}) collective-permute-start(bf16[1,16,1024]{2,1,0:T(8,128)(2,1)S(1)} %get-tuple-element.95), channel_id=1, source_target_pairs={{0,4},{1,5},{2,6},{3,7},{8,12},{9,13},{10,14},{11,15},{16,20},{17,... | collective-permute-start | bytes 98312 | tf_op jit(solution)/shard_map/ppermute | solution.py:29
  12.7 4.0 %all-to-all-start.2 = ((bf16[8,8,4,256]{3,1,2,0:T(8,128)(2,1)}), bf16[8,8,4,256]{3,1,2,0:T(8,128)(2,1)}, u32[]{:S(2)}, u32[]{:S(2)}) async-start(bf16[8,8,4,256]{3,1,2,0:T(8,128)(2,1)} %bitcast.44), calls=%async_computation.2 | async-start | bytes 262144 | tf_op jit(solution)/shard_map/all_to_all | solution.py:137
  18.3 3.0 %collective-permute-start.2 = (bf16[18,1,1024]{2,1,0:T(2,128)(2,1)S(1)}, bf16[18,1,1024]{2,1,0:T(2,128)(2,1)S(1)}, u32[]{:S(2)}, u32[]{:S(2)}) collective-permute-start(bf16[18,1,1024]{2,1,0:T(2,128)(2,1)S(1)} %get-tuple-element.93), channel_id=1, source_target_pairs={{0,1},{1,2},{2,3},{4,5},{5,6},{6,7},{8,9},{9,10},{10,11},{12,13},{... | collective-permute-start | bytes 110600 | tf_op jit(solution)/shard_map/ppermute | solution.py:29
  27.6 2.5 %fusion.114 = (f32[4,8,64]{2,1,0:T(8,128)S(1)}, f32[4,8,64,64]{2,3,1,0:T(8,128)}) fusion(bf16[4,64,8,32]{1,3,2,0:T(8,128)(2,1)} %bitcast.339, bf16[4,64,8,32]{1,3,2,0:T(8,128)(2,1)} %bitcast.341), kind=kOutput, calls=%fused_computation.228 | convolution fusion | flops 8781887 | bytes 794624 | tf_op jit(solution)/shard_map/jvp()/sub | solution.py:98
  30.1 2.2 %fusion.10 = bf16[4,64,8,32]{1,3,2,0:T(8,128)(2,1)} fusion(bf16[4,64,8,32]{1,3,2,0:T(8,128)(2,1)S(1)} %bitcast.312, f32[4,8,64,64]{2,3,1,0:T(8,128)} %get-tuple-element.121, f32[4,8,64]{2,1,0:T(8,128)S(1)} %get-tuple-element.120), kind=kOutput, calls=%fused_computation.43 | convolution fusion | flops 8716288 | bytes 794624 | tf_op jit(solution)/shard_map/jvp(whqk,wkhd->wqhd)/dot_general | solution.py:99
  38.5 6.8 %all-to-all-start = ((bf16[8,8,4,256]{3,1,2,0:T(8,128)(2,1)}), bf16[8,8,4,256]{3,1,2,0:T(8,128)(2,1)}, u32[]{:S(2)}, u32[]{:S(2)}) async-start(bf16[8,8,4,256]{3,1,2,0:T(8,128)(2,1)} %bitcast.24), calls=%async_computation | async-start | bytes 262144 | tf_op jit(solution)/shard_map/all_to_all | solution.py:137
  58.3 2.6 %fusion.116 = (f32[4,8,64]{2,1,0:T(8,128)S(1)}, f32[4,8,64,64]{2,3,1,0:T(8,128)}) fusion(bf16[4,64,8,32]{1,3,2,0:T(8,128)(2,1)} %bitcast.343, bf16[4,64,8,32]{1,3,2,0:T(8,128)(2,1)} %bitcast.345), kind=kOutput, calls=%fused_computation.230 | convolution fusion | flops 8781887 | bytes 794624 | tf_op jit(solution)/shard_map/jvp()/sub | solution.py:98
  60.9 1.8 fusion.21
  72.4 4.2 %all-to-all-start.3 = ((bf16[8,8,4,256]{3,1,2,0:T(8,128)(2,1)}), bf16[8,8,4,256]{3,1,2,0:T(8,128)(2,1)}, u32[]{:S(2)}, u32[]{:S(2)}) async-start(bf16[8,8,4,256]{3,1,2,0:T(8,128)(2,1)} %bitcast.329), calls=%async_computation.3 | async-start | bytes 262144 | tf_op jit(solution)/shard_map/all_to_all | solution.py:137
  76.6 2.3 %fusion.11 = bf16[4,64,8,32]{1,3,2,0:T(8,128)(2,1)} fusion(bf16[4,64,8,32]{1,3,2,0:T(8,128)(2,1)} %bitcast.315, f32[4,8,64,64]{2,3,1,0:T(8,128)} %get-tuple-element.125, f32[4,8,64]{2,1,0:T(8,128)} %copy-done.67), kind=kOutput, calls=%fused_computation.44 | convolution fusion | flops 8716288 | bytes 794624 | tf_op jit(solution)/shard_map/jvp(whqk,wkhd->wqhd)/dot_general | solution.py:99
  78.8 2.0 %copy.212 = bf16[4,64,8,32]{3,2,1,0:T(8,128)(2,1)} copy(bf16[4,64,8,32]{1,3,2,0:T(8,128)(2,1)} %fusion.11) | data formatting | bytes 262144 | tf_op jit(solution)/shard_map/jvp()/convert_element_type | solution.py:102
  83.9 4.0 %all-to-all-start.1 = ((bf16[8,8,4,256]{3,1,2,0:T(8,128)(2,1)}), bf16[8,8,4,256]{3,1,2,0:T(8,128)(2,1)}, u32[]{:S(2)}, u32[]{:S(2)}) async-start(bf16[8,8,4,256]{3,1,2,0:T(8,128)(2,1)} %bitcast.36), calls=%async_computation.1 | async-start | bytes 262144 | tf_op jit(solution)/shard_map/all_to_all | solution.py:137
  96.5 1.9 fusion.26
  106.6 3.3 %multiply_reduce_fusion.8 = (f32[1024]{0:T(1024)S(1)}, f32[1024]{0:T(1024)S(1)}, f32[1024]{0:T(1024)S(1)}, f32[1024]{0:T(1024)S(1)}, f32[1024]{0:T(1024)S(1)}, /...) fusion(f32[18,18,1024]{2,1,0:T(8,128)S(1)} %convert_element_type.2, ...), kind=kLoop, calls=%fused_computation.115 | loop fusion | flops 14408704 | bytes 11083776 | tf_op jit(solution)/shard_map/transpose(jvp())/reduce_sum | solution.py:114
  111.2 4.5 %collective-permute-start.4 = (f32[1,16,1024]{2,1,0:T(8,128)S(1)}, f32[1,16,1024]{2,1,0:T(8,128)S(1)}, u32[]{:S(2)}, u32[]{:S(2)}) collective-permute-start(f32[1,16,1024]{2,1,0:T(8,128)S(1)} %get-tuple-element.91), channel_id=1, source_target_pairs={{0,4},{1,5},{2,6},{3,7},{8,12},{9,13},{10,14},{11,15},{16,20},{17,... | collective-permute-start | bytes 196616 | tf_op jit(solution)/shard_map/ppermute | solution.py:29
  122.0 3.0 %collective-permute-start.7 = (f32[18,1,1024]{2,1,0:T(1,128)S(1)}, f32[18,1,1024]{2,1,0:T(1,128)S(1)}, u32[]{:S(2)}, u32[]{:S(2)}) collective-permute-start(f32[18,1,1024]{2,1,0:T(1,128)S(1)} %get-tuple-element.84), channel_id=1, source_target_pairs={{0,1},{1,2},{2,3},{4,5},{5,6},{6,7},{8,9},{9,10},{10,11},{12,13},{... | collective-permute-start | bytes 221192 | tf_op jit(solution)/shard_map/ppermute | solution.py:29
  126.8 1.9 fusion.28
  132.6 5.3 %all-to-all-start.4 = ((bf16[4,8,8,4224]{3,2,0,1:T(8,128)(2,1)}), bf16[4,8,8,4224]{3,2,0,1:T(8,128)(2,1)S(1)}, u32[]{:S(2)}, u32[]{:S(2)}) async-start(bf16[4,8,8,4224]{3,2,0,1:T(8,128)(2,1)} %copy.246), calls=%async_computation.4 | async-start | bytes 4325376 | tf_op jit(solution)/shard_map/all_to_all | solution.py:162
  140.6 24.7 %all-to-all-done.4 = bf16[4,8,8,4224]{3,2,0,1:T(8,128)(2,1)S(1)} async-done(((bf16[4,8,8,4224]{3,2,0,1:T(8,128)(2,1)}), bf16[4,8,8,4224]{3,2,0,1:T(8,128)(2,1)S(1)}, u32[]{:S(2)}, u32[]{:S(2)}) %all-to-all-start.4) | async-done | bytes 2162720 | tf_op jit(solution)/shard_map/all_to_all | solution.py:162
  166.3 6.1 %all-to-all-start.5 = ((bf16[4,8,4224]{2,1,0:T(8,128)(2,1)}), bf16[4,8,4224]{2,1,0:T(8,128)(2,1)S(1)}, u32[]{:S(2)}, u32[]{:S(2)}) async-start(bf16[4,8,4224]{2,1,0:T(8,128)(2,1)} %reduce_sum.328), calls=%async_computation.5 | async-start | bytes 540672 | tf_op jit(solution)/shard_map/all_to_all | solution.py:162
  172.6 6.7 %all-to-all-done.5 = bf16[4,8,4224]{2,1,0:T(8,128)(2,1)S(1)} async-done(((bf16[4,8,4224]{2,1,0:T(8,128)(2,1)}), bf16[4,8,4224]{2,1,0:T(8,128)(2,1)S(1)}, u32[]{:S(2)}, u32[]{:S(2)}) %all-to-all-start.5) | async-done | bytes 270368 | tf_op jit(solution)/shard_map/all_to_all | solution.py:162
  180.2 4.3 %all-to-all-start.6 = ((bf16[8,8,4224]{2,1,0:T(8,128)(2,1)}), bf16[8,8,4224]{2,1,0:T(8,128)(2,1)S(1)}, u32[]{:S(2)}, u32[]{:S(2)}) async-start(bf16[8,8,4224]{2,1,0:T(8,128)(2,1)} %broadcast_in_dim.113), calls=%async_computation.6 | async-start | bytes 1081344 | tf_op jit(solution)/shard_map/all_to_all | solution.py:177
  185.7 8.7 %all-to-all-done.6 = bf16[8,8,4224]{2,1,0:T(8,128)(2,1)S(1)} async-done(((bf16[8,8,4224]{2,1,0:T(8,128)(2,1)}), bf16[8,8,4224]{2,1,0:T(8,128)(2,1)S(1)}, u32[]{:S(2)}, u32[]{:S(2)}) %all-to-all-start.6) | async-done | bytes 540704 | tf_op jit(solution)/shard_map/all_to_all | solution.py:177
  (305 shorter events, 83.5 us)
Async XLA Ops:
  1.7 9.9 %copy-start.12 = (bf16[1,16,16,256]{3,2,1,0:T(8,128)(2,1)S(1)}, bf16[1,16,16,256]{3,2,1,0:T(8,128)(2,1)}, u32[]{:S(2)}) copy-start(bf16[1,16,16,256]{3,2,1,0:T(8,128)(2,1)} %param.13) | copy-start | bytes 393220
  1.8 9.9 %copy-start.24 = (bf16[256,256]{1,0:T(8,128)(2,1)S(1)}, bf16[256,256]{1,0:T(8,128)(2,1)}, u32[]{:S(2)}) copy-start(bf16[256,256]{1,0:T(8,128)(2,1)} %param.23) | copy-start | bytes 393220
  2.9 13.8 %copy-start.3 = (bf16[1,16,16,256]{3,2,1,0:T(8,128)(2,1)S(1)}, bf16[1,16,16,256]{3,2,1,0:T(8,128)(2,1)}, u32[]{:S(2)}) copy-start(bf16[1,16,16,256]{3,2,1,0:T(8,128)(2,1)} %param.12) | copy-start | bytes 393220
  2.9 13.8 %copy-start.61 = (f32[256]{0:T(256)S(1)}, f32[256]{0:T(256)}, u32[]{:S(2)}) copy-start(f32[256]{0:T(256)} %param.14) | copy-start | bytes 3076
  5.4 16.0 %copy-start.57 = (f32[1024,9]{0,1:T(8,128)S(1)}, f32[1024,9]{0,1:T(8,128)}, u32[]{:S(2)}) copy-start(f32[1024,9]{0,1:T(8,128)} %param.16) | copy-start | bytes 110596
  5.4 11.5 %collective-permute-start.1 = (bf16[1,16,1024]{2,1,0:T(8,128)(2,1)S(1)}, bf16[1,16,1024]{2,1,0:T(8,128)(2,1)S(1)}, u32[]{:S(2)}, u32[]{:S(2)}) collective-permute-start(bf16[1,16,1024]{2,1,0:T(8,128)(2,1)S(1)} %get-tuple-element.96), channel_id=1, source_target_pairs={{4,0},{5,1},{6,2},{7,3},{12,8},{13,9},{14,10},{15,11},{20,16},{21,... | collective-permute-start | bytes 98312 | tf_op jit(solution)/shard_map/ppermute | solution.py:31
  6.8 10.1 %collective-permute-start = (bf16[1,16,1024]{2,1,0:T(8,128)(2,1)S(1)}, bf16[1,16,1024]{2,1,0:T(8,128)(2,1)S(1)}, u32[]{:S(2)}, u32[]{:S(2)}) collective-permute-start(bf16[1,16,1024]{2,1,0:T(8,128)(2,1)S(1)} %get-tuple-element.95), channel_id=1, source_target_pairs={{0,4},{1,5},{2,6},{3,7},{8,12},{9,13},{10,14},{11,15},{16,20},{17,... | collective-permute-start | bytes 98312 | tf_op jit(solution)/shard_map/ppermute | solution.py:29
  12.7 25.8 %all-to-all-start.2 = ((bf16[8,8,4,256]{3,1,2,0:T(8,128)(2,1)}), bf16[8,8,4,256]{3,1,2,0:T(8,128)(2,1)}, u32[]{:S(2)}, u32[]{:S(2)}) async-start(bf16[8,8,4,256]{3,1,2,0:T(8,128)(2,1)} %bitcast.44), calls=%async_computation.2 | async-start | bytes 262144 | tf_op jit(solution)/shard_map/all_to_all | solution.py:137
  17.0 5.2 %collective-permute-start.3 = (bf16[18,1,1024]{2,1,0:T(2,128)(2,1)S(1)}, bf16[18,1,1024]{2,1,0:T(2,128)(2,1)S(1)}, u32[]{:S(2)}, u32[]{:S(2)}) collective-permute-start(bf16[18,1,1024]{2,1,0:T(2,128)(2,1)S(1)} %get-tuple-element.94), channel_id=1, source_target_pairs={{1,0},{2,1},{3,2},{5,4},{6,5},{7,6},{9,8},{10,9},{11,10},{13,12},{... | collective-permute-start | bytes 110600 | tf_op jit(solution)/shard_map/ppermute | solution.py:31
  18.3 3.9 %collective-permute-start.2 = (bf16[18,1,1024]{2,1,0:T(2,128)(2,1)S(1)}, bf16[18,1,1024]{2,1,0:T(2,128)(2,1)S(1)}, u32[]{:S(2)}, u32[]{:S(2)}) collective-permute-start(bf16[18,1,1024]{2,1,0:T(2,128)(2,1)S(1)} %get-tuple-element.93), channel_id=1, source_target_pairs={{0,1},{1,2},{2,3},{4,5},{5,6},{6,7},{8,9},{9,10},{10,11},{12,13},{... | collective-permute-start | bytes 110600 | tf_op jit(solution)/shard_map/ppermute | solution.py:29
  35.1 56.4 %copy-start.1 = (f32[16,16,256]{2,1,0:T(8,128)}, f32[16,16,256]{2,1,0:T(8,128)S(1)}, u32[]{:S(2)}) copy-start(f32[16,16,256]{2,1,0:T(8,128)S(1)} %get-tuple-element.123) | copy-start | bytes 786436
  38.5 12.4 %all-to-all-start = ((bf16[8,8,4,256]{3,1,2,0:T(8,128)(2,1)}), bf16[8,8,4,256]{3,1,2,0:T(8,128)(2,1)}, u32[]{:S(2)}, u32[]{:S(2)}) async-start(bf16[8,8,4,256]{3,1,2,0:T(8,128)(2,1)} %bitcast.24), calls=%async_computation | async-start | bytes 262144 | tf_op jit(solution)/shard_map/all_to_all | solution.py:137
  67.0 11.9 %copy-start.4 = (bf16[4,64,768]{2,1,0:T(8,128)(2,1)}, bf16[4,64,768]{2,1,0:T(8,128)(2,1)S(1)}, u32[]{:S(2)}) copy-start(bf16[4,64,768]{2,1,0:T(8,128)(2,1)S(1)} %copy.223) | copy-start | bytes 1179652
  72.4 11.5 %all-to-all-start.3 = ((bf16[8,8,4,256]{3,1,2,0:T(8,128)(2,1)}), bf16[8,8,4,256]{3,1,2,0:T(8,128)(2,1)}, u32[]{:S(2)}, u32[]{:S(2)}) async-start(bf16[8,8,4,256]{3,1,2,0:T(8,128)(2,1)} %bitcast.329), calls=%async_computation.3 | async-start | bytes 262144 | tf_op jit(solution)/shard_map/all_to_all | solution.py:137
  83.9 32.5 %all-to-all-start.1 = ((bf16[8,8,4,256]{3,1,2,0:T(8,128)(2,1)}), bf16[8,8,4,256]{3,1,2,0:T(8,128)(2,1)}, u32[]{:S(2)}, u32[]{:S(2)}) async-start(bf16[8,8,4,256]{3,1,2,0:T(8,128)(2,1)} %bitcast.36), calls=%async_computation.1 | async-start | bytes 262144 | tf_op jit(solution)/shard_map/all_to_all | solution.py:137
  109.9 10.6 %collective-permute-start.5 = (f32[1,16,1024]{2,1,0:T(8,128)S(1)}, f32[1,16,1024]{2,1,0:T(8,128)S(1)}, u32[]{:S(2)}, u32[]{:S(2)}) collective-permute-start(f32[1,16,1024]{2,1,0:T(8,128)S(1)} %get-tuple-element.92), channel_id=1, source_target_pairs={{4,0},{5,1},{6,2},{7,3},{12,8},{13,9},{14,10},{15,11},{20,16},{21,... | collective-permute-start | bytes 196616 | tf_op jit(solution)/shard_map/ppermute | solution.py:31
  111.2 9.3 %collective-permute-start.4 = (f32[1,16,1024]{2,1,0:T(8,128)S(1)}, f32[1,16,1024]{2,1,0:T(8,128)S(1)}, u32[]{:S(2)}, u32[]{:S(2)}) collective-permute-start(f32[1,16,1024]{2,1,0:T(8,128)S(1)} %get-tuple-element.91), channel_id=1, source_target_pairs={{0,4},{1,5},{2,6},{3,7},{8,12},{9,13},{10,14},{11,15},{16,20},{17,... | collective-permute-start | bytes 196616 | tf_op jit(solution)/shard_map/ppermute | solution.py:29
  120.7 5.0 %collective-permute-start.6 = (f32[18,1,1024]{2,1,0:T(1,128)S(1)}, f32[18,1,1024]{2,1,0:T(1,128)S(1)}, u32[]{:S(2)}, u32[]{:S(2)}) collective-permute-start(f32[18,1,1024]{2,1,0:T(1,128)S(1)} %get-tuple-element.83), channel_id=1, source_target_pairs={{1,0},{2,1},{3,2},{5,4},{6,5},{7,6},{9,8},{10,9},{11,10},{13,12},{... | collective-permute-start | bytes 221192 | tf_op jit(solution)/shard_map/ppermute | solution.py:31
  122.0 3.9 %collective-permute-start.7 = (f32[18,1,1024]{2,1,0:T(1,128)S(1)}, f32[18,1,1024]{2,1,0:T(1,128)S(1)}, u32[]{:S(2)}, u32[]{:S(2)}) collective-permute-start(f32[18,1,1024]{2,1,0:T(1,128)S(1)} %get-tuple-element.84), channel_id=1, source_target_pairs={{0,1},{1,2},{2,3},{4,5},{5,6},{6,7},{8,9},{9,10},{10,11},{12,13},{... | collective-permute-start | bytes 221192 | tf_op jit(solution)/shard_map/ppermute | solution.py:29
  132.6 32.7 %all-to-all-start.4 = ((bf16[4,8,8,4224]{3,2,0,1:T(8,128)(2,1)}), bf16[4,8,8,4224]{3,2,0,1:T(8,128)(2,1)S(1)}, u32[]{:S(2)}, u32[]{:S(2)}) async-start(bf16[4,8,8,4224]{3,2,0,1:T(8,128)(2,1)} %copy.246), calls=%async_computation.4 | async-start | bytes 4325376 | tf_op jit(solution)/shard_map/all_to_all | solution.py:162
  166.3 18.1 %copy-start.63 = (f32[256]{0:T(256)S(1)}, f32[256]{0:T(256)}, u32[]{:S(2)}) copy-start(f32[256]{0:T(256)} %param.14) | copy-start | bytes 3076
  166.3 18.5 %copy-start.9 = (f32[16,16,256]{2,1,0:T(8,128)S(1)}, f32[16,16,256]{2,1,0:T(8,128)}, u32[]{:S(2)}) copy-start(f32[16,16,256]{2,1,0:T(8,128)} %copy-done.8) | copy-start | bytes 786436
  166.3 13.0 %all-to-all-start.5 = ((bf16[4,8,4224]{2,1,0:T(8,128)(2,1)}), bf16[4,8,4224]{2,1,0:T(8,128)(2,1)S(1)}, u32[]{:S(2)}, u32[]{:S(2)}) async-start(bf16[4,8,4224]{2,1,0:T(8,128)(2,1)} %reduce_sum.328), calls=%async_computation.5 | async-start | bytes 540672 | tf_op jit(solution)/shard_map/all_to_all | solution.py:162
  180.2 14.2 %all-to-all-start.6 = ((bf16[8,8,4224]{2,1,0:T(8,128)(2,1)}), bf16[8,8,4224]{2,1,0:T(8,128)(2,1)S(1)}, u32[]{:S(2)}, u32[]{:S(2)}) async-start(bf16[8,8,4224]{2,1,0:T(8,128)(2,1)} %broadcast_in_dim.113), calls=%async_computation.6 | async-start | bytes 1081344 | tf_op jit(solution)/shard_map/all_to_all | solution.py:177
  (63 other events, 148.7 us)

commit v6 on v5

--- a/solution.py
+++ b/solution.py
@@ -89,18 +89,21 @@
     count, members, channels = windows.shape
     head_width = channels // heads
     qkv_rows = (project_rows(windows, weight) + tap_in).astype(jnp.bfloat16)
-    queries = qkv_rows[..., :channels].reshape(count, members, heads, head_width)
-    key_rows = qkv_rows[..., channels : 2 * channels].reshape(count, members, heads, head_width)
-    value_rows = qkv_rows[..., 2 * channels :].reshape(count, members, heads, head_width)
+    queries = qkv_rows[..., :channels]
+    key_rows = qkv_rows[..., channels : 2 * channels]
+    value_rows = qkv_rows[..., 2 * channels :]
+    owner = lax.broadcasted_iota(jnp.int32, (heads, channels), 1) // head_width
+    mask = (owner == lax.broadcasted_iota(jnp.int32, (heads, channels), 0)).astype(jnp.bfloat16)
+    masked = queries[:, None, :, :] * mask[None, :, None, :]
     scores = jnp.einsum(
-        "wqhd,wkhd->whqk", queries, key_rows, preferred_element_type=jnp.float32
+        "whqc,wkc->whqk", masked, key_rows, preferred_element_type=jnp.float32
     ) * head_width ** (-0.5)
     softmax_out = jax.nn.softmax(scores, axis=-1).astype(jnp.bfloat16)
-    attended = jnp.einsum(
-        "whqk,wkhd->wqhd", softmax_out, value_rows, preferred_element_type=jnp.float32
-    )
-    return attended.astype(jnp.bfloat16).reshape(count, members, channels)
-
+    spread = jnp.einsum(
+        "whqk,wkc->whqc", softmax_out, value_rows, preferred_element_type=jnp.float32
+    )
+    attended = (spread * mask[None, :, None, :].astype(jnp.float32)).sum(axis=1)
+    return attended.astype(jnp.bfloat16)
 
 def depthwise(extended, kernel):
     height = extended.shape[0] - 2

time: 201 us -> 195 us (0.970)
  local copies, waits for them, and re-layouts: 47.7 us -> 40.2 us
  waiting for transfers between devices: 40.8 us -> 47.5 us
  starting transfers between devices: 55.4 us -> 51.1 us
  matrix products: 29.5 us -> 25.8 us
  other arithmetic: 23.3 us -> 26.1 us
    ppermute x4, waiting for transfers between devices: 0.01 us -> 6.43 us  [extended_2(): lax.ppermute(head, axis, [((i + 1) % count, i) for i in range(ends)])]
    slice x8 -> x2, local copies, waits for them, and re-layouts: 6.98 us -> 0.67 us  [window_attention(): queries = qkv_rows[..., :channels]]
    dot_general x12, matrix products: 11.4 us -> 7.27 us  [project_rows(): product = jnp.dot(flattened, weight, preferred_element_type=jnp.float32)]
    convert_element_type x0 -> x4, other arithmetic: none -> 3.05 us  [the longest x2 1.65 us: window_attention(): return attended.astype(jnp.bfloat16)]
    add_any x2 -> x0, local copies, waits for them, and re-layouts: 2.77 us -> none  [window_attention(): qkv_rows[..., :channels].reshape(count, members, heads, head_width)]
    dot_general x10, matrix products: 11.2 us -> 8.48 us  [the longest x6 6.58 us: window_attention(): jnp.einsum('whqk,wkc->whqc', softmax_out, value_rows, preferred_element_t...]
    all_to_all x2, starting transfers between devices: 11.4 us -> 8.73 us  [exchange_sum(): lax.all_to_all(values.astype(jnp.bfloat16), axes, split_axis=axis, concat...]
    reshape x4, local copies, waits for them, and re-layouts: 1.54 us -> 4 us  [to_exchanged(): image.reshape(height // sy_count, sy_count, breadth // sx_count, sx_count...]
  transfers between devices with their start and end apart: 15 -> 15, of which waited for: 5 -> 7; matrix products, arithmetic and copies ran while one was open for 30% -> 26% of each run, Pallas kernels for 0% -> 0%
where the time goes in v6:
time: 195 us; the launch traced here: 193 us
  starting transfers between devices  51.1 us (26%)
  waiting for transfers between devices  47.5 us (24%)
  local copies, waits for them, and re-layouts  40.2 us (21%)
  other arithmetic  26.1 us (13%)
  matrix products  25.8 us (13%)
  between operations  2.42 us (1%)
    all_to_all x2, waiting for transfers between devices, exchange_sum(): lax.all_to_all(values.astype(jnp.bfloat16), axes, split_axis=axis, concat...  31.3 us
    all_to_all x4, starting transfers between devices, swap_blocks(): lax.all_to_all(as_sent(flattened), ('sy', 'sx'), split_axis=0, concat_axi...  18.4 us
    ppermute x4, starting transfers between devices, extended_2(): lax.ppermute(tail, axis, [(i, (i + 1) % count) for i in range(ends)])  14.6 us
    all_to_all x2, starting transfers between devices, exchange_sum(): lax.all_to_all(values.astype(jnp.bfloat16), axes, split_axis=axis, concat...  8.73 us
    all_to_all x1, waiting for transfers between devices, reduce_packed(): lax.all_to_all(spread, ('sy', 'sx'), split_axis=0, concat_axis=0, tiled=T...  8.7 us
    dot_general x12, matrix products, project_rows(): product = jnp.dot(flattened, weight, preferred_element_type=jnp.float32)  7.27 us
    dot_general x6, matrix products, window_attention(): jnp.einsum('whqk,wkc->whqc', softmax_out, value_rows, preferred_element_t...  6.58 us
    sub x2, matrix products, window_attention(): softmax_out = jax.nn.softmax(scores, axis=-1).astype(jnp.bfloat16)  6.51 us
  transfers between devices with their start and end apart: 15, of which 7 were waited for; matrix products, arithmetic and copies ran while one was open for 26% of the time, Pallas kernels for 0%

profile of v6, /device:TPU:0, one launch (start us, length us, event | category | flops | bytes accessed | tf_op | source)
XLA Modules:
  0.0 193.2 jit_solution(14552243439331102729)
XLA Ops:
  2.9 2.4 %multiply_convert_fusion.1 = (bf16[16,16,1024]{2,1,0:T(8,128)(2,1)S(1)}, f32[16,16,1024]{2,1,0:T(8,128)}) fusion(bf16[256,1024]{1,0:T(8,128)(2,1)S(1)} %copy-done, bf16[1,16,16,256]{3,2,1,0:T(8,128)(2,1)} %param.12, f32[256]{0:T(256)} %param.14, f32[16,16]{1,0:T(8,128)S(1)} %fusion.175, f32[16,16]{1,0:T(8,128)S(1)} %broadcast_multiply_fusion.2), kind=kOutput, calls=%fused_computation.150 | convolution fusion | flops 136904704 | bytes 2231296 | tf_op jit(solution)/shard_map/jvp()/dot_general | solution.py:52
  5.4 4.9 %collective-permute-start = (bf16[1,16,1024]{2,1,0:T(8,128)(2,1)S(1)}, bf16[1,16,1024]{2,1,0:T(8,128)(2,1)S(1)}, u32[]{:S(2)}, u32[]{:S(2)}) collective-permute-start(bf16[1,16,1024]{2,1,0:T(8,128)(2,1)S(1)} %get-tuple-element.97), channel_id=1, source_target_pairs={{0,4},{1,5},{2,6},{3,7},{8,12},{9,13},{10,14},{11,15},{16,20},{17,... | collective-permute-start | bytes 98312 | tf_op jit(solution)/shard_map/ppermute | solution.py:29
  12.6 4.8 %all-to-all-start.2 = ((bf16[8,8,4,256]{3,1,2,0:T(8,128)(2,1)}), bf16[8,8,4,256]{3,1,2,0:T(8,128)(2,1)}, u32[]{:S(2)}, u32[]{:S(2)}) async-start(bf16[8,8,4,256]{3,1,2,0:T(8,128)(2,1)} %bitcast.46), calls=%async_computation.2 | async-start | bytes 262144 | tf_op jit(solution)/shard_map/all_to_all | solution.py:140
  17.8 2.4 %collective-permute-start.2 = (bf16[18,1,1024]{2,1,0:T(2,128)(2,1)S(1)}, bf16[18,1,1024]{2,1,0:T(2,128)(2,1)S(1)}, u32[]{:S(2)}, u32[]{:S(2)}) collective-permute-start(bf16[18,1,1024]{2,1,0:T(2,128)(2,1)S(1)} %get-tuple-element.95), channel_id=1, source_target_pairs={{0,1},{1,2},{2,3},{4,5},{5,6},{6,7},{8,9},{9,10},{10,11},{12,13},{... | collective-permute-start | bytes 110600 | tf_op jit(solution)/shard_map/ppermute | solution.py:29
  22.3 2.2 %collective-permute-done.3 = bf16[18,1,1024]{2,1,0:T(2,128)(2,1)S(1)} collective-permute-done((bf16[18,1,1024]{2,1,0:T(2,128)(2,1)S(1)}, bf16[18,1,1024]{2,1,0:T(2,128)(2,1)S(1)}, u32[]{:S(2)}, u32[]{:S(2)}) %collective-permute-start.3) | collective-permute-done | bytes 36896 | tf_op jit(solution)/shard_map/ppermute | solution.py:31
  28.8 3.2 %fusion.190 = (f32[4,8,64]{2,1,0:T(8,128)}, f32[4,8,64,64]{2,3,1,0:T(8,128)}) fusion(bf16[8,256]{1,0:T(8,128)(2,1)S(1)} %get-tuple-element.111, bf16[4,64,256]{2,1,0:T(8,128)(2,1)S(1)} %slice.233, bf16[4,64,768]{2,1,0:T(8,128)(2,1)} %copy-done.24), kind=kOutput, calls=%fused_computation.274 | convolution fusion | flops 68026432 | bytes 798720 | tf_op jit(solution)/shard_map/jvp()/sub | solution.py:101
  43.6 5.4 %all-to-all-start = ((bf16[8,8,4,256]{3,1,2,0:T(8,128)(2,1)}), bf16[8,8,4,256]{3,1,2,0:T(8,128)(2,1)S(1)}, u32[]{:S(2)}, u32[]{:S(2)}) async-start(bf16[8,8,4,256]{3,1,2,0:T(8,128)(2,1)} %bitcast.334), calls=%async_computation | async-start | bytes 262144 | tf_op jit(solution)/shard_map/all_to_all | solution.py:140
  50.6 1.8 reshape.545
  59.5 3.3 %fusion.194 = (f32[4,8,64]{2,1,0:T(8,128)}, f32[4,8,64,64]{2,3,1,0:T(8,128)}) fusion(bf16[4,64,256]{2,1,0:T(8,128)(2,1)} %slice.236, bf16[8,256]{1,0:T(8,128)(2,1)} %copy-done.75, bf16[4,64,768]{2,1,0:T(8,128)(2,1)} %copy-done.26), kind=kOutput, calls=%fused_computation.276 | convolution fusion | flops 68026432 | bytes 798720 | tf_op jit(solution)/shard_map/jvp()/sub | solution.py:101
  63.6 2.1 %fusion.75 = (f32[4,8,64]{2,1,0:T(8,128)S(1)}, bf16[4,8,64,64]{2,3,1,0:T(8,128)(2,1)S(1)}, bf16[4,8,64,64]{2,3,1,0:T(8,128)(2,1)S(1)}) fusion(f32[4,8,64,64]{2,3,1,0:T(8,128)} %get-tuple-element.123, f32[4,8,64]{2,1,0:T(8,128)S(1)} %multiply_divide_fusion.1, f32[4,8,64]{2,1,0:T(8,128)} %get-tuple-element.122, bf16[4,64,768]{2,1,0:T(8,128)(2,1)S(1)} %copy-done.27, ...), kind=kOutput, calls=%fused_computation.86 | convolution fusion | flops 68548608 | bytes 1482752 | tf_op jit(solution)/shard_map/transpose(jvp(whqk,wkc->whqc))/dot_general | solution.py:102
  72.0 4.0 %all-to-all-start.3 = ((bf16[8,8,4,256]{3,1,2,0:T(8,128)(2,1)}), bf16[8,8,4,256]{3,1,2,0:T(8,128)(2,1)}, u32[]{:S(2)}, u32[]{:S(2)}) async-start(bf16[8,8,4,256]{3,1,2,0:T(8,128)(2,1)} %bitcast.335), calls=%async_computation.3 | async-start | bytes 262144 | tf_op jit(solution)/shard_map/all_to_all | solution.py:140
  81.6 4.2 %all-to-all-start.1 = ((bf16[8,8,4,256]{3,1,2,0:T(8,128)(2,1)}), bf16[8,8,4,256]{3,1,2,0:T(8,128)(2,1)}, u32[]{:S(2)}, u32[]{:S(2)}) async-start(bf16[8,8,4,256]{3,1,2,0:T(8,128)(2,1)} %bitcast.38), calls=%async_computation.1 | async-start | bytes 262144 | tf_op jit(solution)/shard_map/all_to_all | solution.py:140
  89.4 1.9 fusion.181
  96.2 2.7 %multiply_reduce_fusion.10 = (f32[1024]{0:T(1024)S(1)}, f32[1024]{0:T(1024)S(1)}, f32[1024]{0:T(1024)S(1)}, f32[1024]{0:T(1024)S(1)}, f32[1024]{0:T(1024)S(1)}, ...) fusion(f32[18,18,1024]{2,1,0:T(8,128)S(1)} %convert_element_typ, ...), kind=kLoop, calls=%fused_computation.137 | loop fusion | flops 14408704 | bytes 11083776 | tf_op jit(solution)/shard_map/transpose(jvp())/reduce_sum | solution.py:117
  98.9 3.6 %collective-permute-start.4 = (f32[1,16,1024]{2,1,0:T(8,128)S(1)}, f32[1,16,1024]{2,1,0:T(8,128)S(1)}, u32[]{:S(2)}, u32[]{:S(2)}) collective-permute-start(f32[1,16,1024]{2,1,0:T(8,128)S(1)} %get-tuple-element.91), channel_id=1, source_target_pairs={{0,4},{1,5},{2,6},{3,7},{8,12},{9,13},{10,14},{11,15},{16,20},{17,... | collective-permute-start | bytes 196616 | tf_op jit(solution)/shard_map/ppermute | solution.py:29
  104.5 4.2 %collective-permute-done.5 = f32[1,16,1024]{2,1,0:T(8,128)S(1)} collective-permute-done((f32[1,16,1024]{2,1,0:T(8,128)S(1)}, f32[1,16,1024]{2,1,0:T(8,128)S(1)}, u32[]{:S(2)}, u32[]{:S(2)}) %collective-permute-start.5) | collective-permute-done | bytes 65568 | tf_op jit(solution)/shard_map/ppermute | solution.py:31
  110.8 3.7 %collective-permute-start.7 = (f32[18,1,1024]{2,1,0:T(1,128)}, f32[18,1,1024]{2,1,0:T(1,128)}, u32[]{:S(2)}, u32[]{:S(2)}) collective-permute-start(f32[18,1,1024]{2,1,0:T(1,128)} %get-tuple-element.84), channel_id=1, source_target_pairs={{0,1},{1,2},{2,3},{4,5},{5,6},{6,7},{8,9},{9,10},{10,11},{12,13},{... | collective-permute-start | bytes 221192 | tf_op jit(solution)/shard_map/ppermute | solution.py:29
  120.7 1.9 fusion.82
  129.7 3.7 %all-to-all-start.4 = ((bf16[4,8,8,4224]{3,2,0,1:T(8,128)(2,1)}), bf16[4,8,8,4224]{3,2,0,1:T(8,128)(2,1)S(1)}, u32[]{:S(2)}, u32[]{:S(2)}) async-start(bf16[4,8,8,4224]{3,2,0,1:T(8,128)(2,1)} %copy.158), calls=%async_computation.4 | async-start | bytes 4325376 | tf_op jit(solution)/shard_map/all_to_all | solution.py:165
  136.1 24.6 %all-to-all-done.4 = bf16[4,8,8,4224]{3,2,0,1:T(8,128)(2,1)S(1)} async-done(((bf16[4,8,8,4224]{3,2,0,1:T(8,128)(2,1)}), bf16[4,8,8,4224]{3,2,0,1:T(8,128)(2,1)S(1)}, u32[]{:S(2)}, u32[]{:S(2)}) %all-to-all-start.4) | async-done | bytes 2162720 | tf_op jit(solution)/shard_map/all_to_all | solution.py:165
  161.7 5.0 %all-to-all-start.5 = ((bf16[4,8,4224]{2,1,0:T(8,128)(2,1)}), bf16[4,8,4224]{2,1,0:T(8,128)(2,1)S(1)}, u32[]{:S(2)}, u32[]{:S(2)}) async-start(bf16[4,8,4224]{2,1,0:T(8,128)(2,1)} %reduce_sum.370), calls=%async_computation.5 | async-start | bytes 540672 | tf_op jit(solution)/shard_map/all_to_all | solution.py:165
  166.8 6.7 %all-to-all-done.5 = bf16[4,8,4224]{2,1,0:T(8,128)(2,1)S(1)} async-done(((bf16[4,8,4224]{2,1,0:T(8,128)(2,1)}), bf16[4,8,4224]{2,1,0:T(8,128)(2,1)S(1)}, u32[]{:S(2)}, u32[]{:S(2)}) %all-to-all-start.5) | async-done | bytes 270368 | tf_op jit(solution)/shard_map/all_to_all | solution.py:165
  174.5 4.3 %all-to-all-start.6 = ((bf16[8,8,4224]{2,1,0:T(8,128)(2,1)}), bf16[8,8,4224]{2,1,0:T(8,128)(2,1)S(1)}, u32[]{:S(2)}, u32[]{:S(2)}) async-start(bf16[8,8,4224]{2,1,0:T(8,128)(2,1)} %broadcast_in_dim.127), calls=%async_computation.6 | async-start | bytes 1081344 | tf_op jit(solution)/shard_map/all_to_all | solution.py:180
  179.9 8.7 %all-to-all-done.6 = bf16[8,8,4224]{2,1,0:T(8,128)(2,1)S(1)} async-done(((bf16[8,8,4224]{2,1,0:T(8,128)(2,1)}), bf16[8,8,4224]{2,1,0:T(8,128)(2,1)S(1)}, u32[]{:S(2)}, u32[]{:S(2)}) %all-to-all-start.6) | async-done | bytes 540704 | tf_op jit(solution)/shard_map/all_to_all | solution.py:180
  (318 shorter events, 79.0 us)
Async XLA Ops:
  2.9 14.5 %copy-start.3 = (bf16[1,16,16,256]{3,2,1,0:T(8,128)(2,1)S(1)}, bf16[1,16,16,256]{3,2,1,0:T(8,128)(2,1)}, u32[]{:S(2)}) copy-start(bf16[1,16,16,256]{3,2,1,0:T(8,128)(2,1)} %param.12) | copy-start | bytes 393220
  2.9 14.5 %copy-start.67 = (f32[256]{0:T(256)S(1)}, f32[256]{0:T(256)}, u32[]{:S(2)}) copy-start(f32[256]{0:T(256)} %param.14) | copy-start | bytes 3076
  2.9 14.6 %copy-start.63 = (f32[1024,9]{0,1:T(8,128)S(1)}, f32[1024,9]{0,1:T(8,128)}, u32[]{:S(2)}) copy-start(f32[1024,9]{0,1:T(8,128)} %param.16) | copy-start | bytes 110596
  5.4 12.3 %collective-permute-start = (bf16[1,16,1024]{2,1,0:T(8,128)(2,1)S(1)}, bf16[1,16,1024]{2,1,0:T(8,128)(2,1)S(1)}, u32[]{:S(2)}, u32[]{:S(2)}) collective-permute-start(bf16[1,16,1024]{2,1,0:T(8,128)(2,1)S(1)} %get-tuple-element.97), channel_id=1, source_target_pairs={{0,4},{1,5},{2,6},{3,7},{8,12},{9,13},{10,14},{11,15},{16,20},{17,... | collective-permute-start | bytes 98312 | tf_op jit(solution)/shard_map/ppermute | solution.py:29
  10.2 7.5 %collective-permute-start.1 = (bf16[1,16,1024]{2,1,0:T(8,128)(2,1)S(1)}, bf16[1,16,1024]{2,1,0:T(8,128)(2,1)S(1)}, u32[]{:S(2)}, u32[]{:S(2)}) collective-permute-start(bf16[1,16,1024]{2,1,0:T(8,128)(2,1)S(1)} %get-tuple-element.98), channel_id=1, source_target_pairs={{4,0},{5,1},{6,2},{7,3},{12,8},{13,9},{14,10},{15,11},{20,16},{21,... | collective-permute-start | bytes 98312 | tf_op jit(solution)/shard_map/ppermute | solution.py:31
  12.6 31.1 %all-to-all-start.2 = ((bf16[8,8,4,256]{3,1,2,0:T(8,128)(2,1)}), bf16[8,8,4,256]{3,1,2,0:T(8,128)(2,1)}, u32[]{:S(2)}, u32[]{:S(2)}) async-start(bf16[8,8,4,256]{3,1,2,0:T(8,128)(2,1)} %bitcast.46), calls=%async_computation.2 | async-start | bytes 262144 | tf_op jit(solution)/shard_map/all_to_all | solution.py:140
  17.8 4.5 %collective-permute-start.2 = (bf16[18,1,1024]{2,1,0:T(2,128)(2,1)S(1)}, bf16[18,1,1024]{2,1,0:T(2,128)(2,1)S(1)}, u32[]{:S(2)}, u32[]{:S(2)}) collective-permute-start(bf16[18,1,1024]{2,1,0:T(2,128)(2,1)S(1)} %get-tuple-element.95), channel_id=1, source_target_pairs={{0,1},{1,2},{2,3},{4,5},{5,6},{6,7},{8,9},{9,10},{10,11},{12,13},{... | collective-permute-start | bytes 110600 | tf_op jit(solution)/shard_map/ppermute | solution.py:29
  20.3 4.3 %collective-permute-start.3 = (bf16[18,1,1024]{2,1,0:T(2,128)(2,1)S(1)}, bf16[18,1,1024]{2,1,0:T(2,128)(2,1)S(1)}, u32[]{:S(2)}, u32[]{:S(2)}) collective-permute-start(bf16[18,1,1024]{2,1,0:T(2,128)(2,1)S(1)} %get-tuple-element.96), channel_id=1, source_target_pairs={{1,0},{2,1},{3,2},{5,4},{6,5},{7,6},{9,8},{10,9},{11,10},{13,12},{... | collective-permute-start | bytes 110600 | tf_op jit(solution)/shard_map/ppermute | solution.py:31
  21.6 11.8 %copy-start.72 = (f32[8,256]{1,0:T(8,128)}, f32[8,256]{1,0:T(8,128)S(1)}, u32[]{:S(2)}) copy-start(f32[8,256]{1,0:T(8,128)S(1)} %get-tuple-element.110) | copy-start | bytes 24580
  35.3 54.1 %copy-start.1 = (f32[16,16,256]{2,1,0:T(8,128)}, f32[16,16,256]{2,1,0:T(8,128)S(1)}, u32[]{:S(2)}) copy-start(f32[16,16,256]{2,1,0:T(8,128)S(1)} %get-tuple-element.121) | copy-start | bytes 786436
  35.6 22.2 %copy-start.11 = (bf16[256,768]{1,0:T(8,128)(2,1)S(1)}, bf16[256,768]{1,0:T(8,128)(2,1)}, u32[]{:S(2)}) copy-start(bf16[256,768]{1,0:T(8,128)(2,1)} %param.22) | copy-start | bytes 1179652
  43.6 10.9 %all-to-all-start = ((bf16[8,8,4,256]{3,1,2,0:T(8,128)(2,1)}), bf16[8,8,4,256]{3,1,2,0:T(8,128)(2,1)S(1)}, u32[]{:S(2)}, u32[]{:S(2)}) async-start(bf16[8,8,4,256]{3,1,2,0:T(8,128)(2,1)} %bitcast.334), calls=%async_computation | async-start | bytes 262144 | tf_op jit(solution)/shard_map/all_to_all | solution.py:140
  67.5 14.1 %copy-start.4 = (bf16[4,64,768]{2,1,0:T(8,128)(2,1)}, bf16[4,64,768]{2,1,0:T(8,128)(2,1)S(1)}, u32[]{:S(2)}) copy-start(bf16[4,64,768]{2,1,0:T(8,128)(2,1)S(1)} %pad_add_fusion.1) | copy-start | bytes 1179652
  72.0 9.6 %all-to-all-start.3 = ((bf16[8,8,4,256]{3,1,2,0:T(8,128)(2,1)}), bf16[8,8,4,256]{3,1,2,0:T(8,128)(2,1)}, u32[]{:S(2)}, u32[]{:S(2)}) async-start(bf16[8,8,4,256]{3,1,2,0:T(8,128)(2,1)} %bitcast.335), calls=%async_computation.3 | async-start | bytes 262144 | tf_op jit(solution)/shard_map/all_to_all | solution.py:140
  81.6 34.5 %all-to-all-start.1 = ((bf16[8,8,4,256]{3,1,2,0:T(8,128)(2,1)}), bf16[8,8,4,256]{3,1,2,0:T(8,128)(2,1)}, u32[]{:S(2)}, u32[]{:S(2)}) async-start(bf16[8,8,4,256]{3,1,2,0:T(8,128)(2,1)} %bitcast.38), calls=%async_computation.1 | async-start | bytes 262144 | tf_op jit(solution)/shard_map/all_to_all | solution.py:140
  98.9 5.6 %collective-permute-start.4 = (f32[1,16,1024]{2,1,0:T(8,128)S(1)}, f32[1,16,1024]{2,1,0:T(8,128)S(1)}, u32[]{:S(2)}, u32[]{:S(2)}) collective-permute-start(f32[1,16,1024]{2,1,0:T(8,128)S(1)} %get-tuple-element.91), channel_id=1, source_target_pairs={{0,4},{1,5},{2,6},{3,7},{8,12},{9,13},{10,14},{11,15},{16,20},{17,... | collective-permute-start | bytes 196616 | tf_op jit(solution)/shard_map/ppermute | solution.py:29
  102.6 6.2 %collective-permute-start.5 = (f32[1,16,1024]{2,1,0:T(8,128)S(1)}, f32[1,16,1024]{2,1,0:T(8,128)S(1)}, u32[]{:S(2)}, u32[]{:S(2)}) collective-permute-start(f32[1,16,1024]{2,1,0:T(8,128)S(1)} %get-tuple-element.92), channel_id=1, source_target_pairs={{4,0},{5,1},{6,2},{7,3},{12,8},{13,9},{14,10},{15,11},{20,16},{21,... | collective-permute-start | bytes 196616 | tf_op jit(solution)/shard_map/ppermute | solution.py:31
  109.5 9.6 %collective-permute-start.6 = (f32[18,1,1024]{2,1,0:T(1,128)}, f32[18,1,1024]{2,1,0:T(1,128)}, u32[]{:S(2)}, u32[]{:S(2)}) collective-permute-start(f32[18,1,1024]{2,1,0:T(1,128)} %get-tuple-element.83), channel_id=1, source_target_pairs={{1,0},{2,1},{3,2},{5,4},{6,5},{7,6},{9,8},{10,9},{11,10},{13,12},{... | collective-permute-start | bytes 221192 | tf_op jit(solution)/shard_map/ppermute | solution.py:31
  110.8 8.4 %collective-permute-start.7 = (f32[18,1,1024]{2,1,0:T(1,128)}, f32[18,1,1024]{2,1,0:T(1,128)}, u32[]{:S(2)}, u32[]{:S(2)}) collective-permute-start(f32[18,1,1024]{2,1,0:T(1,128)} %get-tuple-element.84), channel_id=1, source_target_pairs={{0,1},{1,2},{2,3},{4,5},{5,6},{6,7},{8,9},{9,10},{10,11},{12,13},{... | collective-permute-start | bytes 221192 | tf_op jit(solution)/shard_map/ppermute | solution.py:29
  129.7 31.0 %all-to-all-start.4 = ((bf16[4,8,8,4224]{3,2,0,1:T(8,128)(2,1)}), bf16[4,8,8,4224]{3,2,0,1:T(8,128)(2,1)S(1)}, u32[]{:S(2)}, u32[]{:S(2)}) async-start(bf16[4,8,8,4224]{3,2,0,1:T(8,128)(2,1)} %copy.158), calls=%async_computation.4 | async-start | bytes 4325376 | tf_op jit(solution)/shard_map/all_to_all | solution.py:165
  136.1 42.6 %copy-start.69 = (f32[256]{0:T(256)S(1)}, f32[256]{0:T(256)}, u32[]{:S(2)}) copy-start(f32[256]{0:T(256)} %param.14) | copy-start | bytes 3076
  161.7 17.3 %copy-start.9 = (f32[16,16,256]{2,1,0:T(8,128)S(1)}, f32[16,16,256]{2,1,0:T(8,128)}, u32[]{:S(2)}) copy-start(f32[16,16,256]{2,1,0:T(8,128)} %copy-done.8) | copy-start | bytes 786436
  161.7 11.8 %all-to-all-start.5 = ((bf16[4,8,4224]{2,1,0:T(8,128)(2,1)}), bf16[4,8,4224]{2,1,0:T(8,128)(2,1)S(1)}, u32[]{:S(2)}, u32[]{:S(2)}) async-start(bf16[4,8,4224]{2,1,0:T(8,128)(2,1)} %reduce_sum.370), calls=%async_computation.5 | async-start | bytes 540672 | tf_op jit(solution)/shard_map/all_to_all | solution.py:165
  174.5 14.2 %all-to-all-start.6 = ((bf16[8,8,4224]{2,1,0:T(8,128)(2,1)}), bf16[8,8,4224]{2,1,0:T(8,128)(2,1)S(1)}, u32[]{:S(2)}, u32[]{:S(2)}) async-start(bf16[8,8,4224]{2,1,0:T(8,128)(2,1)} %broadcast_in_dim.127), calls=%async_computation.6 | async-start | bytes 1081344 | tf_op jit(solution)/shard_map/all_to_all | solution.py:180
  (75 other events, 251.2 us)

commit v7 on v6

--- a/solution.py
+++ b/solution.py
@@ -19,21 +19,47 @@
 
 
 def extended_2(cells, sides, width):
-    for axis, dim in sides:
-        count = lax.axis_size(axis)
-        ends = count - 1
-        head = lax.slice_in_dim(cells, 0, width, axis=dim)
-        tail = lax.slice_in_dim(cells, cells.shape[dim] - width, cells.shape[dim], axis=dim)
-        cells = jnp.concatenate(
-            [
-                lax.ppermute(tail, axis, [(i, (i + 1) % count) for i in range(ends)]),
-                cells,
-                lax.ppermute(head, axis, [((i + 1) % count, i) for i in range(ends)]),
-            ],
-            axis=dim,
-        )
-    return cells
-
+    height, breadth, channels = cells.shape
+    row_count = lax.axis_size("sy")
+    col_count = lax.axis_size("sx")
+    tiles = row_count * col_count
+    row_at = lax.axis_index("sy")
+    col_at = lax.axis_index("sx")
+    span = max(height, breadth)
+
+    def lay(line):
+        return jnp.pad(line, ((0, span - line.shape[0]), (0, 0)))
+
+    sends = (
+        ((-1, 0), lay(cells[0])),
+        ((1, 0), lay(cells[height - 1])),
+        ((0, -1), lay(cells[:, 0])),
+        ((0, 1), lay(cells[:, breadth - 1])),
+        ((-1, -1), lay(cells[0, :1])),
+        ((-1, 1), lay(cells[0, breadth - 1 :])),
+        ((1, -1), lay(cells[height - 1, :1])),
+        ((1, 1), lay(cells[height - 1, breadth - 1 :])),
+    )
+    slot = lax.broadcasted_iota(jnp.int32, (tiles, 1, 1), 0)
+    row_step = slot // col_count - row_at
+    col_step = slot % col_count - col_at
+    outgoing = jnp.zeros((tiles, span, channels), cells.dtype)
+    for (up, side), line in sends:
+        outgoing = jnp.where((row_step == up) & (col_step == side), line[None], outgoing)
+    incoming = lax.all_to_all(outgoing, ("sy", "sx"), split_axis=0, concat_axis=0, tiled=True)
+
+    def take(up, side):
+        row = row_at + up
+        col = col_at + side
+        valid = (row >= 0) & (row < row_count) & (col >= 0) & (col < col_count)
+        index = jnp.clip(row, 0, row_count - 1) * col_count + jnp.clip(col, 0, col_count - 1)
+        line = lax.dynamic_index_in_dim(incoming, index, 0, keepdims=False)
+        return jnp.where(valid, line, jnp.zeros_like(line))
+
+    top = jnp.concatenate([take(-1, -1)[:1], take(-1, 0)[:breadth], take(-1, 1)[:1]], axis=0)
+    bottom = jnp.concatenate([take(1, -1)[:1], take(1, 0)[:breadth], take(1, 1)[:1]], axis=0)
+    middle = jnp.concatenate([take(0, -1)[:height, None], cells, take(0, 1)[:height, None]], axis=1)
+    return jnp.concatenate([top[None], middle, bottom[None]], axis=0)
 
 def widen(values):
     return lax.optimization_barrier(values).astype(jnp.float32)

time: 195 us -> 189 us (0.969)
  starting transfers between devices: 51.1 us -> 38.6 us
  waiting for transfers between devices: 47.5 us -> 52.9 us
  matrix products: 25.8 us -> 29.8 us
  local copies, waits for them, and re-layouts: 40.2 us -> 36.8 us
    ppermute x8 -> x0, starting transfers between devices: 19.7 us -> none  [the longest x4 14.6 us: extended_2(): lax.ppermute(tail, axis, [(i, (i + 1) % count) for i in range(ends)])]
    all_to_all x0 -> x2, starting transfers between devices: none -> 8.12 us  [extended_2(): lax.all_to_all(outgoing, ('sy', 'sx'), split_axis=0, concat_axis=0, tiled...]
    all_to_all x0 -> x2, waiting for transfers between devices: none -> 7.21 us  [extended_2(): lax.all_to_all(outgoing, ('sy', 'sx'), split_axis=0, concat_axis=0, tiled...]
    ppermute x8 -> x0, waiting for transfers between devices: 6.44 us -> none  [the longest x4 6.43 us: extended_2(): lax.ppermute(head, axis, [((i + 1) % count, i) for i in range(ends)])]
    dot_general x6, matrix products: 3.59 us -> 7.41 us  [outer_sum(): lax.dot_general(left_flat, right_flat, (((0,), (0,)), ((), ())), preferre...]
    all_to_all x4, waiting for transfers between devices: 1.04 us -> 3.99 us  [swap_blocks(): lax.all_to_all(as_sent(flattened), ('sy', 'sx'), split_axis=0, concat_axi...]
    select_n x0 -> x10, other arithmetic: none -> 2.64 us  [the longest x2 2.06 us: extended_2(): jnp.where((row_step == up) & (col_step == side), line[None], outgoing)]
    convert_element_type x3, local copies, waits for them, and re-layouts: 3.64 us -> 1.03 us  [window_attention(): return attended.astype(jnp.bfloat16)]
  transfers between devices with their start and end apart: 15 -> 9, of which waited for: 7 -> 7; matrix products, arithmetic and copies ran while one was open for 26% -> 21% of each run, Pallas kernels for 0% -> 0%
where the time goes in v7:
time: 189 us; the launch traced here: 187 us
  waiting for transfers between devices  52.9 us (28%)
  starting transfers between devices  38.6 us (20%)
  local copies, waits for them, and re-layouts  36.8 us (19%)
  matrix products  29.8 us (16%)
  other arithmetic  25.7 us (14%)
  between operations  2.93 us (2%)
    all_to_all x2, waiting for transfers between devices, exchange_sum(): lax.all_to_all(values.astype(jnp.bfloat16), axes, split_axis=axis, concat...  33 us
    all_to_all x4, starting transfers between devices, swap_blocks(): lax.all_to_all(as_sent(flattened), ('sy', 'sx'), split_axis=0, concat_axi...  16.7 us
    all_to_all x2, starting transfers between devices, exchange_sum(): lax.all_to_all(values.astype(jnp.bfloat16), axes, split_axis=axis, concat...  9.48 us
    dot_general x12, matrix products, project_rows(): product = jnp.dot(flattened, weight, preferred_element_type=jnp.float32)  9.12 us
    all_to_all x1, waiting for transfers between devices, reduce_packed(): lax.all_to_all(spread, ('sy', 'sx'), split_axis=0, concat_axis=0, tiled=T...  8.7 us
    all_to_all x2, starting transfers between devices, extended_2(): lax.all_to_all(outgoing, ('sy', 'sx'), split_axis=0, concat_axis=0, tiled...  8.12 us
    dot_general x6, matrix products, outer_sum(): lax.dot_general(left_flat, right_flat, (((0,), (0,)), ((), ())), preferre...  7.41 us
    all_to_all x2, waiting for transfers between devices, extended_2(): lax.all_to_all(outgoing, ('sy', 'sx'), split_axis=0, concat_axis=0, tiled...  7.21 us
  transfers between devices with their start and end apart: 9, of which 7 were waited for; matrix products, arithmetic and copies ran while one was open for 21% of the time, Pallas kernels for 0%

profile of v7, /device:TPU:0, one launch (start us, length us, event | category | flops | bytes accessed | tf_op | source)
XLA Modules:
  0.0 186.8 jit_solution(6229854010068843708)
XLA Ops:
  2.7 5.2 %all-to-all-start.3 = ((bf16[8,8,4,256]{3,1,2,0:T(8,128)(2,1)}), bf16[8,8,4,256]{3,1,2,0:T(8,128)(2,1)S(1)}, u32[]{:S(2)}, u32[]{:S(2)}) async-start(bf16[8,8,4,256]{3,1,2,0:T(8,128)(2,1)} %bitcast.60), calls=%async_computation.3 | async-start | bytes 262144 | tf_op jit(solution)/shard_map/all_to_all | solution.py:166
  10.1 2.4 %multiply_convert_fusion.1 = (bf16[16,16,1024]{2,1,0:T(8,128)(2,1)S(1)}, f32[16,16,1024]{2,1,0:T(8,128)}) fusion(bf16[256,1024]{1,0:T(8,128)(2,1)S(1)} %copy-done, bf16[1,16,16,256]{3,2,1,0:T(8,128)(2,1)} %param.12, f32[256]{0:T(256)} %param.14, f32[16,16]{1,0:T(8,128)S(1)} %fusion.193, f32[16,16]{1,0:T(8,128)S(1)} %broadcast_multiply_fusion.2), kind=kOutput, calls=%fused_computation.150 | convolution fusion | flops 136904704 | bytes 2231296 | tf_op jit(solution)/shard_map/jvp()/dot_general | solution.py:78
  15.5 4.2 %all-to-all-start = ((bf16[8,16,1024]{2,1,0:T(8,128)(2,1)}), bf16[8,16,1024]{2,1,0:T(8,128)(2,1)S(1)}, u32[]{:S(2)}, u32[]{:S(2)}) async-start(bf16[8,16,1024]{2,1,0:T(8,128)(2,1)} %select_select_fusion.1), calls=%async_computation | async-start | bytes 524288 | tf_op jit(solution)/shard_map/all_to_all | solution.py:49
  20.8 5.8 %all-to-all-done = bf16[8,16,1024]{2,1,0:T(8,128)(2,1)S(1)} async-done(((bf16[8,16,1024]{2,1,0:T(8,128)(2,1)}), bf16[8,16,1024]{2,1,0:T(8,128)(2,1)S(1)}, u32[]{:S(2)}, u32[]{:S(2)}) %all-to-all-start) | async-done | bytes 262176 | tf_op jit(solution)/shard_map/all_to_all | solution.py:49
  30.7 1.7 fusion.208
  40.4 4.0 %all-to-all-start.1 = ((bf16[8,8,4,256]{3,1,2,0:T(8,128)(2,1)}), bf16[8,8,4,256]{3,1,2,0:T(8,128)(2,1)}, u32[]{:S(2)}, u32[]{:S(2)}) async-start(bf16[8,8,4,256]{3,1,2,0:T(8,128)(2,1)} %bitcast.412), calls=%async_computation.1 | async-start | bytes 262144 | tf_op jit(solution)/shard_map/all_to_all | solution.py:166
  48.1 1.8 all-to-all-done.1
  54.2 3.2 %fusion.212 = (f32[4,8,64]{2,1,0:T(8,128)}, f32[4,8,64,64]{2,3,1,0:T(8,128)}) fusion(bf16[4,64,256]{2,1,0:T(8,128)(2,1)} %slice.342, bf16[8,256]{1,0:T(8,128)(2,1)} %get-tuple-element.135, bf16[4,64,768]{2,1,0:T(8,128)(2,1)} %copy-done.21), kind=kOutput, calls=%fused_computation.359 | convolution fusion | flops 68026432 | bytes 798720 | tf_op jit(solution)/shard_map/jvp()/sub | solution.py:127
  58.2 2.1 %fusion.75 = (f32[4,8,64]{2,1,0:T(8,128)S(1)}, bf16[4,8,64,64]{2,3,1,0:T(8,128)(2,1)S(1)}, bf16[4,8,64,64]{2,3,1,0:T(8,128)(2,1)S(1)}) fusion(f32[4,8,64,64]{2,3,1,0:T(8,128)} %get-tuple-element.147, f32[4,8,64]{2,1,0:T(8,128)S(1)} %multiply_divide_fusion.1, f32[4,8,64]{2,1,0:T(8,128)} %get-tuple-element.146, bf16[4,64,768]{2,1,0:T(8,128)(2,1)} %copy-done.21, ...), kind=kOutput, calls=%fused_computation.86 | convolution fusion | flops 68548608 | bytes 2007040 | tf_op jit(solution)/shard_map/transpose(jvp(whqk,wkc->whqc))/dot_general | solution.py:128
  64.7 3.4 %all-to-all-start.4 = ((bf16[8,8,4,256]{3,1,2,0:T(8,128)(2,1)}), bf16[8,8,4,256]{3,1,2,0:T(8,128)(2,1)S(1)}, u32[]{:S(2)}, u32[]{:S(2)}) async-start(bf16[8,8,4,256]{3,1,2,0:T(8,128)(2,1)} %bitcast.75), calls=%async_computation.4 | async-start | bytes 262144 | tf_op jit(solution)/shard_map/all_to_all | solution.py:166
  71.3 2.2 %all-to-all-done.4 = bf16[8,8,4,256]{3,1,2,0:T(8,128)(2,1)S(1)} async-done(((bf16[8,8,4,256]{3,1,2,0:T(8,128)(2,1)}), bf16[8,8,4,256]{3,1,2,0:T(8,128)(2,1)S(1)}, u32[]{:S(2)}, u32[]{:S(2)}) %all-to-all-start.4) | async-done | bytes 131104 | tf_op jit(solution)/shard_map/all_to_all | solution.py:166
  73.5 4.2 %all-to-all-start.2 = ((bf16[8,8,4,256]{3,1,2,0:T(8,128)(2,1)}), bf16[8,8,4,256]{3,1,2,0:T(8,128)(2,1)}, u32[]{:S(2)}, u32[]{:S(2)}) async-start(bf16[8,8,4,256]{3,1,2,0:T(8,128)(2,1)} %bitcast.52), calls=%async_computation.2 | async-start | bytes 262144 | tf_op jit(solution)/shard_map/all_to_all | solution.py:166
  89.5 2.7 %multiply_reduce_fusion.10 = (f32[1024]{0:T(1024)S(1)}, f32[1024]{0:T(1024)S(1)}, f32[1024]{0:T(1024)S(1)}, f32[1024]{0:T(1024)S(1)}, f32[1024]{0:T(1024)S(1)}, ...) fusion(f32[18,18,1024]{2,1,0:T(8,128)S(1)} %convert_element_typ, ...), kind=kLoop, calls=%fused_computation.137 | loop fusion | flops 14408704 | bytes 11083776 | tf_op jit(solution)/shard_map/transpose(jvp())/reduce_sum | solution.py:143
  94.6 3.9 %all-to-all-start.5 = ((f32[8,16,1024]{2,1,0:T(8,128)}), f32[8,16,1024]{2,1,0:T(8,128)S(1)}, u32[]{:S(2)}, u32[]{:S(2)}) async-start(f32[8,16,1024]{2,1,0:T(8,128)} %select_select_fusion), calls=%async_computation.5 | async-start | bytes 1048576 | tf_op jit(solution)/shard_map/all_to_all | solution.py:49
  102.0 2.6 %fusion.37 = bf16[1024,256]{1,0:T(8,128)(2,1)} fusion(f32[16,16,256]{2,1,0:T(8,128)S(1)} %copy-done.7, f32[16,16,1024]{2,1,0:T(8,128)} %copy-done.16), kind=kOutput, calls=%fused_computation.50 | convolution fusion | flops 136904704 | bytes 1835008 | tf_op jit(solution)/shard_map/dot_general | solution.py:85
  104.6 2.2 %concatenate.62 = bf16[4,8,8,1024]{3,2,1,0:T(8,128)(2,1)} reshape(bf16[1024,256]{1,0:T(8,128)(2,1)} %fusion.37) | data formatting | bytes 1048576 | tf_op jit(solution)/shard_map/concatenate | solution.py:199
  110.1 1.9 %fusion.82 = bf16[16,16,1024]{2,1,0:T(8,128)(2,1)S(1)} fusion(f32[16,16,1024]{2,1,0:T(8,128)S(1)} %copy-done.18, f32[17,18,1024]{2,1,0:T(8,128)S(1)} %get-tuple-element.82, f32[16,16,1024]{2,1,0:T(8,128)S(1)} %copy-done.2, f32[16,1,1024]{2,1,0:T(1,128)S(1)} %fusion.162, f32[16,1,1024]{2,1,0:T(1,128)S(1)} %fusion.164, ...), kind=kLoop, calls=%fused_computation.93 | loop fusion | flops 10747904 | bytes 9080832 | tf_op jit(solution)/shard_map/transpose(jvp())/add_any | solution.py:270
  120.8 4.5 %all-to-all-start.6 = ((bf16[4,8,8,4224]{3,2,0,1:T(8,128)(2,1)}), bf16[4,8,8,4224]{3,2,0,1:T(8,128)(2,1)}, u32[]{:S(2)}, u32[]{:S(2)}) async-start(bf16[4,8,8,4224]{3,2,0,1:T(8,128)(2,1)} %copy.200), calls=%async_computation.6 | async-start | bytes 4325376 | tf_op jit(solution)/shard_map/all_to_all | solution.py:191
  126.4 26.3 %all-to-all-done.6 = bf16[4,8,8,4224]{3,2,0,1:T(8,128)(2,1)} async-done(((bf16[4,8,8,4224]{3,2,0,1:T(8,128)(2,1)}), bf16[4,8,8,4224]{3,2,0,1:T(8,128)(2,1)}, u32[]{:S(2)}, u32[]{:S(2)}) %all-to-all-start.6) | async-done | bytes 2162720 | tf_op jit(solution)/shard_map/all_to_all | solution.py:191
  152.6 2.7 %reduce_sum.370 = bf16[4,8,4224]{2,1,0:T(8,128)(2,1)} reduce(bf16[4,8,8,4224]{3,2,0,1:T(8,128)(2,1)} %all-to-all-done.6, bf16[]{:T(256)} %constant.164.clone.1), dimensions={1}, to_apply=%region_34.35 | reduce | flops 946176 | bytes 2433026 | tf_op jit(solution)/shard_map/reduce_sum | solution.py:192
  155.3 5.0 %all-to-all-start.7 = ((bf16[4,8,4224]{2,1,0:T(8,128)(2,1)}), bf16[4,8,4224]{2,1,0:T(8,128)(2,1)S(1)}, u32[]{:S(2)}, u32[]{:S(2)}) async-start(bf16[4,8,4224]{2,1,0:T(8,128)(2,1)} %reduce_sum.370), calls=%async_computation.7 | async-start | bytes 540672 | tf_op jit(solution)/shard_map/all_to_all | solution.py:191
  160.4 6.7 %all-to-all-done.7 = bf16[4,8,4224]{2,1,0:T(8,128)(2,1)S(1)} async-done(((bf16[4,8,4224]{2,1,0:T(8,128)(2,1)}), bf16[4,8,4224]{2,1,0:T(8,128)(2,1)S(1)}, u32[]{:S(2)}, u32[]{:S(2)}) %all-to-all-start.7) | async-done | bytes 270368 | tf_op jit(solution)/shard_map/all_to_all | solution.py:191
  168.1 4.3 %all-to-all-start.8 = ((bf16[8,8,4224]{2,1,0:T(8,128)(2,1)}), bf16[8,8,4224]{2,1,0:T(8,128)(2,1)S(1)}, u32[]{:S(2)}, u32[]{:S(2)}) async-start(bf16[8,8,4224]{2,1,0:T(8,128)(2,1)} %broadcast_in_dim.375), calls=%async_computation.8 | async-start | bytes 1081344 | tf_op jit(solution)/shard_map/all_to_all | solution.py:206
  173.6 8.7 %all-to-all-done.8 = bf16[8,8,4224]{2,1,0:T(8,128)(2,1)S(1)} async-done(((bf16[8,8,4224]{2,1,0:T(8,128)(2,1)}), bf16[8,8,4224]{2,1,0:T(8,128)(2,1)S(1)}, u32[]{:S(2)}, u32[]{:S(2)}) %all-to-all-start.8) | async-done | bytes 540704 | tf_op jit(solution)/shard_map/all_to_all | solution.py:206
  (377 shorter events, 72.2 us)
Async XLA Ops:
  0.6 9.4 %copy-start = (bf16[256,1024]{1,0:T(8,128)(2,1)S(1)}, bf16[256,1024]{1,0:T(8,128)(2,1)}, u32[]{:S(2)}) copy-start(bf16[256,1024]{1,0:T(8,128)(2,1)} %param.15) | copy-start | bytes 1572868
  2.7 12.8 %all-to-all-start.3 = ((bf16[8,8,4,256]{3,1,2,0:T(8,128)(2,1)}), bf16[8,8,4,256]{3,1,2,0:T(8,128)(2,1)S(1)}, u32[]{:S(2)}, u32[]{:S(2)}) async-start(bf16[8,8,4,256]{3,1,2,0:T(8,128)(2,1)} %bitcast.60), calls=%async_computation.3 | async-start | bytes 262144 | tf_op jit(solution)/shard_map/all_to_all | solution.py:166
  12.7 14.0 %copy-start.68 = (pred[8]{0:T(512)(128)(4,1)}, pred[8]{0:T(512)(128)(4,1)S(1)}, u32[]{:S(2)}) copy-start(pred[8]{0:T(512)(128)(4,1)S(1)} %get-tuple-element.151) | copy-start | bytes 28
  13.2 14.7 %copy-start.34 = (f32[1024,1]{0,1:T(1,128)}, f32[1024,1]{0,1:T(1,128)S(1)}, u32[]{:S(2)}) copy-start(f32[1024,1]{0,1:T(1,128)S(1)} %get-tuple-element.125) | copy-start | bytes 12292
  13.2 14.7 %copy-start.36 = (f32[1024,1]{0,1:T(1,128)}, f32[1024,1]{0,1:T(1,128)S(1)}, u32[]{:S(2)}) copy-start(f32[1024,1]{0,1:T(1,128)S(1)} %get-tuple-element.126) | copy-start | bytes 12292
  13.2 14.7 %copy-start.38 = (f32[1024,1]{0,1:T(1,128)}, f32[1024,1]{0,1:T(1,128)S(1)}, u32[]{:S(2)}) copy-start(f32[1024,1]{0,1:T(1,128)S(1)} %get-tuple-element.127) | copy-start | bytes 12292
  13.2 14.7 %copy-start.41 = (f32[1024,1]{0,1:T(1,128)}, f32[1024,1]{0,1:T(1,128)S(1)}, u32[]{:S(2)}) copy-start(f32[1024,1]{0,1:T(1,128)S(1)} %get-tuple-element.128) | copy-start | bytes 12292
  13.2 14.7 %copy-start.44 = (f32[1024,1]{0,1:T(1,128)}, f32[1024,1]{0,1:T(1,128)S(1)}, u32[]{:S(2)}) copy-start(f32[1024,1]{0,1:T(1,128)S(1)} %get-tuple-element.129) | copy-start | bytes 12292
  13.2 14.7 %copy-start.47 = (f32[1024,1]{0,1:T(1,128)}, f32[1024,1]{0,1:T(1,128)S(1)}, u32[]{:S(2)}) copy-start(f32[1024,1]{0,1:T(1,128)S(1)} %get-tuple-element.130) | copy-start | bytes 12292
  13.2 14.7 %copy-start.50 = (f32[1024,1]{0,1:T(1,128)}, f32[1024,1]{0,1:T(1,128)S(1)}, u32[]{:S(2)}) copy-start(f32[1024,1]{0,1:T(1,128)S(1)} %get-tuple-element.131) | copy-start | bytes 12292
  15.5 11.1 %all-to-all-start = ((bf16[8,16,1024]{2,1,0:T(8,128)(2,1)}), bf16[8,16,1024]{2,1,0:T(8,128)(2,1)S(1)}, u32[]{:S(2)}, u32[]{:S(2)}) async-start(bf16[8,16,1024]{2,1,0:T(8,128)(2,1)} %select_select_fusion.1), calls=%async_computation | async-start | bytes 524288 | tf_op jit(solution)/shard_map/all_to_all | solution.py:49
  34.3 18.3 %copy-start.10 = (bf16[256,768]{1,0:T(8,128)(2,1)S(1)}, bf16[256,768]{1,0:T(8,128)(2,1)}, u32[]{:S(2)}) copy-start(bf16[256,768]{1,0:T(8,128)(2,1)} %param.22) | copy-start | bytes 1179652
  40.4 9.5 %all-to-all-start.1 = ((bf16[8,8,4,256]{3,1,2,0:T(8,128)(2,1)}), bf16[8,8,4,256]{3,1,2,0:T(8,128)(2,1)}, u32[]{:S(2)}, u32[]{:S(2)}) async-start(bf16[8,8,4,256]{3,1,2,0:T(8,128)(2,1)} %bitcast.412), calls=%async_computation.1 | async-start | bytes 262144 | tf_op jit(solution)/shard_map/all_to_all | solution.py:166
  64.7 8.8 %all-to-all-start.4 = ((bf16[8,8,4,256]{3,1,2,0:T(8,128)(2,1)}), bf16[8,8,4,256]{3,1,2,0:T(8,128)(2,1)S(1)}, u32[]{:S(2)}, u32[]{:S(2)}) async-start(bf16[8,8,4,256]{3,1,2,0:T(8,128)(2,1)} %bitcast.75), calls=%async_computation.4 | async-start | bytes 262144 | tf_op jit(solution)/shard_map/all_to_all | solution.py:166
  68.8 13.3 %copy-start.13 = (bf16[1,16,16,256]{3,2,1,0:T(8,128)(2,1)S(1)}, bf16[1,16,16,256]{3,2,1,0:T(8,128)(2,1)}, u32[]{:S(2)}) copy-start(bf16[1,16,16,256]{3,2,1,0:T(8,128)(2,1)} %param.13) | copy-start | bytes 393220
  73.5 21.1 %all-to-all-start.2 = ((bf16[8,8,4,256]{3,1,2,0:T(8,128)(2,1)}), bf16[8,8,4,256]{3,1,2,0:T(8,128)(2,1)}, u32[]{:S(2)}, u32[]{:S(2)}) async-start(bf16[8,8,4,256]{3,1,2,0:T(8,128)(2,1)} %bitcast.52), calls=%async_computation.2 | async-start | bytes 262144 | tf_op jit(solution)/shard_map/all_to_all | solution.py:166
  92.2 7.4 %copy-start.89 = (bf16[256]{0:T(256)(128)(2,1)S(1)}, bf16[256]{0:T(256)(128)(2,1)}, u32[]{:S(2)}) copy-start(bf16[256]{0:T(256)(128)(2,1)} %get-tuple-element.74) | copy-start | bytes 1540
  93.2 8.8 %copy-start.7 = (f32[16,16,256]{2,1,0:T(8,128)S(1)}, f32[16,16,256]{2,1,0:T(8,128)}, u32[]{:S(2)}) copy-start(f32[16,16,256]{2,1,0:T(8,128)} %copy-done.6) | copy-start | bytes 786436
  94.6 13.7 %all-to-all-start.5 = ((f32[8,16,1024]{2,1,0:T(8,128)}), f32[8,16,1024]{2,1,0:T(8,128)S(1)}, u32[]{:S(2)}, u32[]{:S(2)}) async-start(f32[8,16,1024]{2,1,0:T(8,128)} %select_select_fusion), calls=%async_computation.5 | async-start | bytes 1048576 | tf_op jit(solution)/shard_map/all_to_all | solution.py:49
  120.8 31.8 %all-to-all-start.6 = ((bf16[4,8,8,4224]{3,2,0,1:T(8,128)(2,1)}), bf16[4,8,8,4224]{3,2,0,1:T(8,128)(2,1)}, u32[]{:S(2)}, u32[]{:S(2)}) async-start(bf16[4,8,8,4224]{3,2,0,1:T(8,128)(2,1)} %copy.200), calls=%async_computation.6 | async-start | bytes 4325376 | tf_op jit(solution)/shard_map/all_to_all | solution.py:191
  126.3 46.0 %copy-start.62 = (f32[256]{0:T(256)S(1)}, f32[256]{0:T(256)}, u32[]{:S(2)}) copy-start(f32[256]{0:T(256)} %param.14) | copy-start | bytes 3076
  155.3 17.4 %copy-start.8 = (f32[16,16,256]{2,1,0:T(8,128)S(1)}, f32[16,16,256]{2,1,0:T(8,128)}, u32[]{:S(2)}) copy-start(f32[16,16,256]{2,1,0:T(8,128)} %copy-done.6) | copy-start | bytes 786436
  155.3 11.8 %all-to-all-start.7 = ((bf16[4,8,4224]{2,1,0:T(8,128)(2,1)}), bf16[4,8,4224]{2,1,0:T(8,128)(2,1)S(1)}, u32[]{:S(2)}, u32[]{:S(2)}) async-start(bf16[4,8,4224]{2,1,0:T(8,128)(2,1)} %reduce_sum.370), calls=%async_computation.7 | async-start | bytes 540672 | tf_op jit(solution)/shard_map/all_to_all | solution.py:191
  168.1 14.2 %all-to-all-start.8 = ((bf16[8,8,4224]{2,1,0:T(8,128)(2,1)}), bf16[8,8,4224]{2,1,0:T(8,128)(2,1)S(1)}, u32[]{:S(2)}, u32[]{:S(2)}) async-start(bf16[8,8,4224]{2,1,0:T(8,128)(2,1)} %broadcast_in_dim.375), calls=%async_computation.8 | async-start | bytes 1081344 | tf_op jit(solution)/shard_map/all_to_all | solution.py:206
  (78 other events, 238.8 us)

commit v8 on v7

--- a/solution.py
+++ b/solution.py
@@ -192,6 +192,28 @@
     return moved.astype(jnp.float32).sum(axis)
 
 
+def halve_sum(values, axis, dim):
+    count = lax.axis_size(axis)
+    at = lax.axis_index(axis)
+    bit = 1
+    while bit < count:
+        bit *= 2
+    bit //= 2
+    while bit >= 1:
+        shape = values.shape
+        split = shape[:dim] + (shape[dim] // (2 * bit), 2, bit) + shape[dim + 1 :]
+        values = values.reshape(split)
+        mine = (at // bit) % 2
+        keep = lax.dynamic_index_in_dim(values, mine, dim + 1, keepdims=False)
+        send = lax.dynamic_index_in_dim(values, 1 - mine, dim + 1, keepdims=False)
+        pairs = [(i, i ^ bit) for i in range(count)]
+        came = lax.ppermute(send.astype(jnp.bfloat16), axis, pairs)
+        values = keep + came.astype(jnp.float32)
+        values = values.reshape(shape[:dim] + (shape[dim] // 2,) + shape[dim + 1 :])
+        bit //= 2
+    return lax.squeeze(values, (dim,)) if values.shape[dim] == 1 else values
+
+
 def reduce_packed(wide):
     parts = lax.axis_size("rep")
     tiles = lax.axis_size(("sy", "sx"))
@@ -200,7 +222,9 @@
     channels, width = packed.shape
     rows = channels // parts
     piece = rows // tiles
-    local = exchange_sum(packed.reshape(parts, tiles, piece, width), ("sy", "sx"), 1)
+    local = packed.reshape(parts, lax.axis_size("sy"), lax.axis_size("sx"), piece, width)
+    local = halve_sum(local, "sx", 2)
+    local = halve_sum(local, "sy", 1)
     local = exchange_sum(local, "rep", 0)
     spread = jnp.broadcast_to(local[None].astype(jnp.bfloat16), (tiles, piece, width))
     total = lax.all_to_all(spread, ("sy", "sx"), split_axis=0, concat_axis=0, tiled=True)

time: 189 us -> 212 us (1.12)
  waiting for transfers between devices: 52.9 us -> 64.4 us
  other arithmetic: 25.7 us -> 33 us
  local copies, waits for them, and re-layouts: 36.8 us -> 41.6 us
  starting transfers between devices: 38.6 us -> 34.4 us
  matrix products: 29.8 us -> 33.2 us
    ppermute x0 -> x3, waiting for transfers between devices: none -> 32.1 us  [halve_sum(): came = lax.ppermute(send.astype(jnp.bfloat16), axis, pairs)]
    all_to_all x2 -> x1, waiting for transfers between devices: 33 us -> 8.43 us  [exchange_sum(): lax.all_to_all(values.astype(jnp.bfloat16), axes, split_axis=axis, concat...]
    all_to_all x2 -> x1, starting transfers between devices: 9.48 us -> 4.86 us  [exchange_sum(): lax.all_to_all(values.astype(jnp.bfloat16), axes, split_axis=axis, concat...]
    add x0 -> x2, other arithmetic: none -> 4.26 us  [halve_sum(): values = keep + came.astype(jnp.float32)]
    unnamed x196 -> x228, local copies, waits for them, and re-layouts: 6.82 us -> 10.5 us
    all_to_all x4, waiting for transfers between devices: 3.99 us -> 7.06 us  [swap_blocks(): lax.all_to_all(as_sent(flattened), ('sy', 'sx'), split_axis=0, concat_axi...]
    dot_general x6, matrix products: 5.53 us -> 8.55 us  [window_attention(): jnp.einsum('whqk,wkc->whqc', softmax_out, value_rows, preferred_element_t...]
    dot_general x6, matrix products: 7.41 us -> 4.64 us  [outer_sum(): lax.dot_general(left_flat, right_flat, (((0,), (0,)), ((), ())), preferre...]
  transfers between devices with their start and end apart: 9 -> 11, of which waited for: 7 -> 9; matrix products, arithmetic and copies ran while one was open for 21% -> 17% of each run, Pallas kernels for 0% -> 0%
where the time goes in v8:
time: 212 us; the launch traced here: 210 us
  waiting for transfers between devices  64.4 us (30%)
  local copies, waits for them, and re-layouts  41.6 us (20%)
  starting transfers between devices  34.4 us (16%)
  matrix products  33.2 us (16%)
  other arithmetic  33 us (16%)
  between operations  3.02 us (1%)
    ppermute x3, waiting for transfers between devices, halve_sum(): came = lax.ppermute(send.astype(jnp.bfloat16), axis, pairs)  32.1 us
    all_to_all x4, starting transfers between devices, swap_blocks(): lax.all_to_all(as_sent(flattened), ('sy', 'sx'), split_axis=0, concat_axi...  16.1 us
    unnamed x228, local copies, waits for them, and re-layouts  10.5 us
    dot_general x12, matrix products, project_rows(): product = jnp.dot(flattened, weight, preferred_element_type=jnp.float32)  10 us
    all_to_all x1, waiting for transfers between devices, reduce_packed(): lax.all_to_all(spread, ('sy', 'sx'), split_axis=0, concat_axis=0, tiled=T...  8.63 us
    dot_general x6, matrix products, window_attention(): jnp.einsum('whqk,wkc->whqc', softmax_out, value_rows, preferred_element_t...  8.55 us
    all_to_all x1, waiting for transfers between devices, exchange_sum(): lax.all_to_all(values.astype(jnp.bfloat16), axes, split_axis=axis, concat...  8.43 us
    all_to_all x2, starting transfers between devices, extended_2(): lax.all_to_all(outgoing, ('sy', 'sx'), split_axis=0, concat_axis=0, tiled...  8.35 us
  transfers between devices with their start and end apart: 11, of which 9 were waited for; matrix products, arithmetic and copies ran while one was open for 17% of the time, Pallas kernels for 0%

profile of v8, /device:TPU:0, one launch (start us, length us, event | category | flops | bytes accessed | tf_op | source)
XLA Modules:
  0.0 209.7 jit_solution(14876691882415356548)
XLA Ops:
  2.7 5.2 %all-to-all-start.3 = ((bf16[8,8,4,256]{3,1,2,0:T(8,128)(2,1)}), bf16[8,8,4,256]{3,1,2,0:T(8,128)(2,1)S(1)}, u32[]{:S(2)}, u32[]{:S(2)}) async-start(bf16[8,8,4,256]{3,1,2,0:T(8,128)(2,1)} %bitcast.60), calls=%async_computation.3 | async-start | bytes 262144 | tf_op jit(solution)/shard_map/all_to_all | solution.py:166
  11.9 2.4 %multiply_convert_fusion.1 = (bf16[16,16,1024]{2,1,0:T(8,128)(2,1)S(1)}, f32[16,16,1024]{2,1,0:T(8,128)}) fusion(bf16[256,1024]{1,0:T(8,128)(2,1)S(1)} %copy-done, bf16[1,16,16,256]{3,2,1,0:T(8,128)(2,1)} %param.12, f32[256]{0:T(256)} %param.14, f32[16,16]{1,0:T(8,128)S(1)} %fusion.196, f32[16,16]{1,0:T(8,128)S(1)} %broadcast_multiply_fusion.2), kind=kOutput, calls=%fused_computation.154 | convolution fusion | flops 136904704 | bytes 2231296 | tf_op jit(solution)/shard_map/jvp()/dot_general | solution.py:78
  16.4 4.2 %all-to-all-start = ((bf16[8,16,1024]{2,1,0:T(8,128)(2,1)}), bf16[8,16,1024]{2,1,0:T(8,128)(2,1)S(1)}, u32[]{:S(2)}, u32[]{:S(2)}) async-start(bf16[8,16,1024]{2,1,0:T(8,128)(2,1)} %select_select_fusion.1), calls=%async_computation | async-start | bytes 524288 | tf_op jit(solution)/shard_map/all_to_all | solution.py:49
  21.7 5.9 %all-to-all-done = bf16[8,16,1024]{2,1,0:T(8,128)(2,1)S(1)} async-done(((bf16[8,16,1024]{2,1,0:T(8,128)(2,1)}), bf16[8,16,1024]{2,1,0:T(8,128)(2,1)S(1)}, u32[]{:S(2)}, u32[]{:S(2)}) %all-to-all-start) | async-done | bytes 262176 | tf_op jit(solution)/shard_map/all_to_all | solution.py:49
  32.8 2.6 %fusion.211 = (f32[4,8,64]{2,1,0:T(8,128)S(1)}, f32[4,8,64,64]{2,3,1,0:T(8,128)}) fusion(bf16[8,256]{1,0:T(8,128)(2,1)S(1)} %get-tuple-element.123, bf16[4,64,256]{2,1,0:T(8,128)(2,1)S(1)} %slice.339, bf16[4,64,768]{2,1,0:T(8,128)(2,1)} %copy-done.22), kind=kOutput, calls=%fused_computation.366 | convolution fusion | flops 68026432 | bytes 798720 | tf_op jit(solution)/shard_map/jvp()/sub | solution.py:127
  43.7 3.4 %all-to-all-start.1 = ((bf16[8,8,4,256]{3,1,2,0:T(8,128)(2,1)}), bf16[8,8,4,256]{3,1,2,0:T(8,128)(2,1)S(1)}, u32[]{:S(2)}, u32[]{:S(2)}) async-start(bf16[8,8,4,256]{3,1,2,0:T(8,128)(2,1)} %bitcast.448), calls=%async_computation.1 | async-start | bytes 262144 | tf_op jit(solution)/shard_map/all_to_all | solution.py:166
  48.4 4.1 %all-to-all-done.1 = bf16[8,8,4,256]{3,1,2,0:T(8,128)(2,1)S(1)} async-done(((bf16[8,8,4,256]{3,1,2,0:T(8,128)(2,1)}), bf16[8,8,4,256]{3,1,2,0:T(8,128)(2,1)S(1)}, u32[]{:S(2)}, u32[]{:S(2)}) %all-to-all-start.1) | async-done | bytes 131104 | tf_op jit(solution)/shard_map/all_to_all | solution.py:166
  57.6 3.2 %fusion.215 = (f32[4,8,64]{2,1,0:T(8,128)}, f32[4,8,64,64]{2,3,1,0:T(8,128)}) fusion(bf16[4,64,256]{2,1,0:T(8,128)(2,1)} %slice.342, bf16[8,256]{1,0:T(8,128)(2,1)} %copy-done.105, bf16[4,64,768]{2,1,0:T(8,128)(2,1)} %copy-done.24), kind=kOutput, calls=%fused_computation.368 | convolution fusion | flops 68026432 | bytes 798720 | tf_op jit(solution)/shard_map/jvp()/sub | solution.py:127
  61.6 2.9 %fusion.75 = (f32[4,8,64]{2,1,0:T(8,128)S(1)}, bf16[4,8,64,64]{2,3,1,0:T(8,128)(2,1)}, bf16[4,8,64,64]{2,3,1,0:T(8,128)(2,1)S(1)}) fusion(f32[4,8,64,64]{2,3,1,0:T(8,128)} %get-tuple-element.135, f32[4,8,64]{2,1,0:T(8,128)S(1)} %multiply_divide_fusion.1, f32[4,8,64]{2,1,0:T(8,128)} %get-tuple-element.134, bf16[4,64,768]{2,1,0:T(8,128)(2,1)} %copy-done.24, ...), kind=kOutput, calls=%fused_computation.90 | convolution fusion | flops 68548608 | bytes 2007040 | tf_op jit(solution)/shard_map/transpose(jvp(whqk,wkc->whqc))/dot_general | solution.py:128
  72.8 3.4 %all-to-all-start.4 = ((bf16[8,8,4,256]{3,1,2,0:T(8,128)(2,1)}), bf16[8,8,4,256]{3,1,2,0:T(8,128)(2,1)S(1)}, u32[]{:S(2)}, u32[]{:S(2)}) async-start(bf16[8,8,4,256]{3,1,2,0:T(8,128)(2,1)} %bitcast.75), calls=%async_computation.4 | async-start | bytes 262144 | tf_op jit(solution)/shard_map/all_to_all | solution.py:166
  78.7 2.9 %all-to-all-done.4 = bf16[8,8,4,256]{3,1,2,0:T(8,128)(2,1)S(1)} async-done(((bf16[8,8,4,256]{3,1,2,0:T(8,128)(2,1)}), bf16[8,8,4,256]{3,1,2,0:T(8,128)(2,1)S(1)}, u32[]{:S(2)}, u32[]{:S(2)}) %all-to-all-start.4) | async-done | bytes 131104 | tf_op jit(solution)/shard_map/all_to_all | solution.py:166
  81.7 4.2 %all-to-all-start.2 = ((bf16[8,8,4,256]{3,1,2,0:T(8,128)(2,1)}), bf16[8,8,4,256]{3,1,2,0:T(8,128)(2,1)}, u32[]{:S(2)}, u32[]{:S(2)}) async-start(bf16[8,8,4,256]{3,1,2,0:T(8,128)(2,1)} %bitcast.52), calls=%async_computation.2 | async-start | bytes 262144 | tf_op jit(solution)/shard_map/all_to_all | solution.py:166
  97.6 3.3 %multiply_reduce_fusion.10 = (f32[1024]{0:T(1024)}, f32[1024]{0:T(1024)}, f32[1024]{0:T(1024)}, f32[1024]{0:T(1024)}, f32[1024]{0:T(1024)}, /*index=5*/f32[1024]...) fusion(f32[18,18,1024]{2,1,0:T(8,128)S(1)} %convert_element_type.336, ...), kind=kLoop, calls=%fused_computation.141 | loop fusion | flops 14408704 | bytes 11083776 | tf_op jit(solution)/shard_map/transpose(jvp())/reduce_sum | solution.py:143
  105.1 4.1 %all-to-all-start.5 = ((f32[8,16,1024]{2,1,0:T(8,128)}), f32[8,16,1024]{2,1,0:T(8,128)}, u32[]{:S(2)}, u32[]{:S(2)}) async-start(f32[8,16,1024]{2,1,0:T(8,128)} %select_select_fusion), calls=%async_computation.5 | async-start | bytes 1048576 | tf_op jit(solution)/shard_map/all_to_all | solution.py:49
  116.7 2.3 %all-to-all-done.5 = f32[8,16,1024]{2,1,0:T(8,128)} async-done(((f32[8,16,1024]{2,1,0:T(8,128)}), f32[8,16,1024]{2,1,0:T(8,128)}, u32[]{:S(2)}, u32[]{:S(2)}) %all-to-all-start.5) | async-done | bytes 524320 | tf_op jit(solution)/shard_map/all_to_all | solution.py:49
  134.3 24.2 %collective-permute-done = bf16[4,2,1,2,8,4224]{5,4,3,1,0,2:T(8,128)(2,1)} collective-permute-done((bf16[4,2,1,2,8,4224]{5,4,3,1,0,2:T(8,128)(2,1)S(1)}, bf16[4,2,1,2,8,4224]{5,4,3,1,0,2:T(8,128)(2,1)}, u32[]{:S(2)}, u32[]{:S(2)}) %collective-permute-start) | collective-permute-done | bytes 1081376 | tf_op jit(solution)/shard_map/ppermute | solution.py:210
  158.5 2.1 %bitcast_add_fusion = f32[4,2,1,2,8,4224]{5,4,3,1,0,2:T(8,128)S(1)} fusion(bf16[4,2,1,2,8,4224]{5,4,3,1,0,2:T(8,128)(2,1)} %collective-permute-done, f32[4,2,1,2,2,8,4224]{6,5,4,3,1,0,2:T(8,128)} %copy-done.4, s32[]{:T(128)S(6)} %select_n.424), kind=kLoop, calls=%fused_computation.10 | loop fusion | flops 1081344 | bytes 5406724 | tf_op jit(solution)/shard_map/add | solution.py:211
  161.5 2.3 %collective-permute-done.1 = bf16[4,2,1,1,8,4224]{5,4,3,1,0,2:T(8,128)(2,1)} collective-permute-done((bf16[4,2,1,1,8,4224]{5,4,3,1,0,2:T(8,128)(2,1)}, bf16[4,2,1,1,8,4224]{5,4,3,1,0,2:T(8,128)(2,1)}, u32[]{:S(2)}, u32[]{:S(2)}) %collective-permute-start.1) | collective-permute-done | bytes 540704 | tf_op jit(solution)/shard_map/ppermute | solution.py:210
  163.8 2.1 %convert_add_fusion = f32[4,2,1,1,8,4224]{5,4,3,1,0,2:T(8,128)} fusion(bf16[4,2,1,1,8,4224]{5,4,3,1,0,2:T(8,128)(2,1)} %collective-permute-done.1, f32[4,2,1,2,8,4224]{5,4,3,1,0,2:T(8,128)S(1)} %bitcast_add_fusion, s32[]{:T(128)S(6)} %select_n.427), kind=kLoop, calls=%fused_computation.84 | loop fusion | flops 540672 | bytes 2703364 | tf_op jit(solution)/shard_map/add | solution.py:211
  170.0 5.6 %collective-permute-done.2 = bf16[4,1,1,8,4224]{4,3,0,2,1:T(8,128)(2,1)S(1)} collective-permute-done((bf16[4,1,1,8,4224]{4,3,0,2,1:T(8,128)(2,1)S(1)}, bf16[4,1,1,8,4224]{4,3,0,2,1:T(8,128)(2,1)S(1)}, u32[]{:S(2)}, u32[]{:S(2)}) %collective-permute-start.2) | collective-permute-done | bytes 270368 | tf_op jit(solution)/shard_map/ppermute | solution.py:210
  177.4 4.9 %all-to-all-start.6 = ((bf16[4,8,4224]{2,1,0:T(8,128)(2,1)}), bf16[4,8,4224]{2,1,0:T(8,128)(2,1)S(1)}, u32[]{:S(2)}, u32[]{:S(2)}) async-start(bf16[4,8,4224]{2,1,0:T(8,128)(2,1)} %fusion.133), calls=%async_computation.6 | async-start | bytes 540672 | tf_op jit(solution)/shard_map/all_to_all | solution.py:191
  182.4 8.4 %all-to-all-done.6 = bf16[4,8,4224]{2,1,0:T(8,128)(2,1)S(1)} async-done(((bf16[4,8,4224]{2,1,0:T(8,128)(2,1)}), bf16[4,8,4224]{2,1,0:T(8,128)(2,1)S(1)}, u32[]{:S(2)}, u32[]{:S(2)}) %all-to-all-start.6) | async-done | bytes 270368 | tf_op jit(solution)/shard_map/all_to_all | solution.py:191
  191.7 3.5 %all-to-all-start.7 = ((bf16[8,8,4224]{2,1,0:T(8,128)(2,1)}), bf16[8,8,4224]{2,1,0:T(8,128)(2,1)S(1)}, u32[]{:S(2)}, u32[]{:S(2)}) async-start(bf16[8,8,4224]{2,1,0:T(8,128)(2,1)} %broadcast_in_dim.372), calls=%async_computation.7 | async-start | bytes 1081344 | tf_op jit(solution)/shard_map/all_to_all | solution.py:230
  196.5 8.6 %all-to-all-done.7 = bf16[8,8,4224]{2,1,0:T(8,128)(2,1)S(1)} async-done(((bf16[8,8,4224]{2,1,0:T(8,128)(2,1)}), bf16[8,8,4224]{2,1,0:T(8,128)(2,1)S(1)}, u32[]{:S(2)}, u32[]{:S(2)}) %all-to-all-start.7) | async-done | bytes 540704 | tf_op jit(solution)/shard_map/all_to_all | solution.py:230
  (414 shorter events, 90.7 us)
Async XLA Ops:
  2.7 13.7 %all-to-all-start.3 = ((bf16[8,8,4,256]{3,1,2,0:T(8,128)(2,1)}), bf16[8,8,4,256]{3,1,2,0:T(8,128)(2,1)S(1)}, u32[]{:S(2)}, u32[]{:S(2)}) async-start(bf16[8,8,4,256]{3,1,2,0:T(8,128)(2,1)} %bitcast.60), calls=%async_computation.3 | async-start | bytes 262144 | tf_op jit(solution)/shard_map/all_to_all | solution.py:166
  14.5 14.3 %copy-start.44 = (f32[1024,1]{0,1:T(1,128)}, f32[1024,1]{0,1:T(1,128)S(1)}, u32[]{:S(2)}) copy-start(f32[1024,1]{0,1:T(1,128)S(1)} %get-tuple-element.113) | copy-start | bytes 12292
  14.5 14.3 %copy-start.47 = (f32[1024,1]{0,1:T(1,128)}, f32[1024,1]{0,1:T(1,128)S(1)}, u32[]{:S(2)}) copy-start(f32[1024,1]{0,1:T(1,128)S(1)} %get-tuple-element.114) | copy-start | bytes 12292
  14.5 14.3 %copy-start.50 = (f32[1024,1]{0,1:T(1,128)}, f32[1024,1]{0,1:T(1,128)S(1)}, u32[]{:S(2)}) copy-start(f32[1024,1]{0,1:T(1,128)S(1)} %get-tuple-element.115) | copy-start | bytes 12292
  14.5 14.3 %copy-start.53 = (f32[1024,1]{0,1:T(1,128)}, f32[1024,1]{0,1:T(1,128)S(1)}, u32[]{:S(2)}) copy-start(f32[1024,1]{0,1:T(1,128)S(1)} %get-tuple-element.116) | copy-start | bytes 12292
  14.5 82.9 %copy-start.40 = (f32[1024,1]{0,1:T(1,128)}, f32[1024,1]{0,1:T(1,128)S(1)}, u32[]{:S(2)}) copy-start(f32[1024,1]{0,1:T(1,128)S(1)} %get-tuple-element.111) | copy-start | bytes 12292
  14.5 82.9 %copy-start.42 = (f32[1024,1]{0,1:T(1,128)}, f32[1024,1]{0,1:T(1,128)S(1)}, u32[]{:S(2)}) copy-start(f32[1024,1]{0,1:T(1,128)S(1)} %get-tuple-element.112) | copy-start | bytes 12292
  16.4 16.4 %copy-start.105 = (bf16[8,256]{1,0:T(8,128)(2,1)}, bf16[8,256]{1,0:T(8,128)(2,1)S(1)}, u32[]{:S(2)}) copy-start(bf16[8,256]{1,0:T(8,128)(2,1)S(1)} %get-tuple-element.123) | copy-start | bytes 12292
  16.4 20.4 %copy-start.84 = (f32[8,256]{1,0:T(8,128)}, f32[8,256]{1,0:T(8,128)S(1)}, u32[]{:S(2)}) copy-start(f32[8,256]{1,0:T(8,128)S(1)} %get-tuple-element.122) | copy-start | bytes 24580
  16.4 11.1 %all-to-all-start = ((bf16[8,16,1024]{2,1,0:T(8,128)(2,1)}), bf16[8,16,1024]{2,1,0:T(8,128)(2,1)S(1)}, u32[]{:S(2)}, u32[]{:S(2)}) async-start(bf16[8,16,1024]{2,1,0:T(8,128)(2,1)} %select_select_fusion.1), calls=%async_computation | async-start | bytes 524288 | tf_op jit(solution)/shard_map/all_to_all | solution.py:49
  36.8 19.1 %copy-start.11 = (bf16[256,768]{1,0:T(8,128)(2,1)S(1)}, bf16[256,768]{1,0:T(8,128)(2,1)}, u32[]{:S(2)}) copy-start(bf16[256,768]{1,0:T(8,128)(2,1)} %param.22) | copy-start | bytes 1179652
  43.7 8.8 %all-to-all-start.1 = ((bf16[8,8,4,256]{3,1,2,0:T(8,128)(2,1)}), bf16[8,8,4,256]{3,1,2,0:T(8,128)(2,1)S(1)}, u32[]{:S(2)}, u32[]{:S(2)}) async-start(bf16[8,8,4,256]{3,1,2,0:T(8,128)(2,1)} %bitcast.448), calls=%async_computation.1 | async-start | bytes 262144 | tf_op jit(solution)/shard_map/all_to_all | solution.py:166
  72.1 15.7 %copy-start.68 = (f32[256]{0:T(256)S(1)}, f32[256]{0:T(256)}, u32[]{:S(2)}) copy-start(f32[256]{0:T(256)} %param.21) | copy-start | bytes 3076
  72.8 8.8 %all-to-all-start.4 = ((bf16[8,8,4,256]{3,1,2,0:T(8,128)(2,1)}), bf16[8,8,4,256]{3,1,2,0:T(8,128)(2,1)S(1)}, u32[]{:S(2)}, u32[]{:S(2)}) async-start(bf16[8,8,4,256]{3,1,2,0:T(8,128)(2,1)} %bitcast.75), calls=%async_computation.4 | async-start | bytes 262144 | tf_op jit(solution)/shard_map/all_to_all | solution.py:166
  81.7 20.3 %all-to-all-start.2 = ((bf16[8,8,4,256]{3,1,2,0:T(8,128)(2,1)}), bf16[8,8,4,256]{3,1,2,0:T(8,128)(2,1)}, u32[]{:S(2)}, u32[]{:S(2)}) async-start(bf16[8,8,4,256]{3,1,2,0:T(8,128)(2,1)} %bitcast.52), calls=%async_computation.2 | async-start | bytes 262144 | tf_op jit(solution)/shard_map/all_to_all | solution.py:166
  105.1 13.9 %all-to-all-start.5 = ((f32[8,16,1024]{2,1,0:T(8,128)}), f32[8,16,1024]{2,1,0:T(8,128)}, u32[]{:S(2)}, u32[]{:S(2)}) async-start(f32[8,16,1024]{2,1,0:T(8,128)} %select_select_fusion), calls=%async_computation.5 | async-start | bytes 1048576 | tf_op jit(solution)/shard_map/all_to_all | solution.py:49
  133.7 24.8 %collective-permute-start = (bf16[4,2,1,2,8,4224]{5,4,3,1,0,2:T(8,128)(2,1)S(1)}, bf16[4,2,1,2,8,4224]{5,4,3,1,0,2:T(8,128)(2,1)}, u32[]{:S(2)}, u32[]{:S(2)}) collective-permute-start(bf16[4,2,1,2,8,4224]{5,4,3,1,0,2:T(8,128)(2,1)S(1)} %fusion.70), channel_id=1, source_target_pairs={{0,2},{1,3},{2,0},{3,1},{4,6},{5,7},{6,4},{7,5},{8,10},{9,11},{10,... | collective-permute-start | bytes 3244040 | tf_op jit(solution)/shard_map/ppermute | solution.py:210
  161.5 2.3 %collective-permute-start.1 = (bf16[4,2,1,1,8,4224]{5,4,3,1,0,2:T(8,128)(2,1)}, bf16[4,2,1,1,8,4224]{5,4,3,1,0,2:T(8,128)(2,1)}, u32[]{:S(2)}, u32[]{:S(2)}) collective-permute-start(bf16[4,2,1,1,8,4224]{5,4,3,1,0,2:T(8,128)(2,1)} %dynamic-slice_convert_fusion.1), channel_id=1, source_target_pairs={{0,1},{1,0},{2,3},{3,2},{4,5},{5,4},{6,7},{7,6},{8,9},{9,8},{10,11... | collective-permute-start | bytes 1622024 | tf_op jit(solution)/shard_map/ppermute | solution.py:210
  165.9 16.4 %copy-start.39 = (f32[16,16]{1,0:T(8,128)S(1)}, f32[16,16]{1,0:T(8,128)}, u32[]{:S(2)}) copy-start(f32[16,16]{1,0:T(8,128)} %copy-done.38) | copy-start | bytes 3076
  167.0 8.6 %collective-permute-start.2 = (bf16[4,1,1,8,4224]{4,3,0,2,1:T(8,128)(2,1)S(1)}, bf16[4,1,1,8,4224]{4,3,0,2,1:T(8,128)(2,1)S(1)}, u32[]{:S(2)}, u32[]{:S(2)}) collective-permute-start(bf16[4,1,1,8,4224]{4,3,0,2,1:T(8,128)(2,1)S(1)} %fusion.132), channel_id=1, source_target_pairs={{0,4},{4,0},{1,5},{5,1},{2,6},{6,2},{3,7},{7,3},{8,12},{12,8},{9,1... | collective-permute-start | bytes 811016 | tf_op jit(solution)/shard_map/ppermute | solution.py:210
  168.1 27.1 %copy-start.72 = (f32[256]{0:T(256)S(1)}, f32[256]{0:T(256)}, u32[]{:S(2)}) copy-start(f32[256]{0:T(256)} %param.14) | copy-start | bytes 3076
  169.9 25.7 %copy-start.10 = (f32[16,16,256]{2,1,0:T(8,128)S(1)}, f32[16,16,256]{2,1,0:T(8,128)}, u32[]{:S(2)}) copy-start(f32[16,16,256]{2,1,0:T(8,128)} %copy-done.9) | copy-start | bytes 786436
  177.4 13.4 %all-to-all-start.6 = ((bf16[4,8,4224]{2,1,0:T(8,128)(2,1)}), bf16[4,8,4224]{2,1,0:T(8,128)(2,1)S(1)}, u32[]{:S(2)}, u32[]{:S(2)}) async-start(bf16[4,8,4224]{2,1,0:T(8,128)(2,1)} %fusion.133), calls=%async_computation.6 | async-start | bytes 540672 | tf_op jit(solution)/shard_map/all_to_all | solution.py:191
  191.7 13.4 %all-to-all-start.7 = ((bf16[8,8,4224]{2,1,0:T(8,128)(2,1)}), bf16[8,8,4224]{2,1,0:T(8,128)(2,1)S(1)}, u32[]{:S(2)}, u32[]{:S(2)}) async-start(bf16[8,8,4224]{2,1,0:T(8,128)(2,1)} %broadcast_in_dim.372), calls=%async_computation.7 | async-start | bytes 1081344 | tf_op jit(solution)/shard_map/all_to_all | solution.py:230
  (96 other events, 382.9 us)

commit v9 on v7

--- a/solution.py
+++ b/solution.py
@@ -163,9 +163,7 @@
 def swap_blocks(blocks):
     sy_count, sx_count, row_part, col_part, channels = blocks.shape
     flattened = blocks.reshape(sy_count * sx_count, row_part, col_part, channels)
-    moved = lax.all_to_all(
-        as_sent(flattened), ("sy", "sx"), split_axis=0, concat_axis=0, tiled=True
-    ).astype(flattened.dtype)
+    moved = lax.all_to_all(flattened, ("sy", "sx"), split_axis=0, concat_axis=0, tiled=True)
     return moved.reshape(blocks.shape)
 
 
@@ -302,25 +300,25 @@
     def grid_front(stream_in, gain_in):
         return layer_norm(stream_in, gain_in).astype(jnp.bfloat16)
 
-    normed_three, grid_front_back = jax.vjp(grid_front, stream_two, gain_grid)
-    grid_windows = to_grid(to_exchanged(normed_three), WIN)
+    stream_two_grid = to_grid(to_exchanged(stream_two), WIN)
+    grid_windows, grid_front_back = jax.vjp(grid_front, stream_two_grid, gain_grid)
 
     def grid_core(windows_in, tap_in):
         return window_attention(windows_in, grid_inward, tap_in, HEADS)
 
     grid_attended, grid_core_back = jax.vjp(grid_core, grid_windows, zero_qkv)
-    grid_home = to_home(from_grid(grid_attended, height, breadth, WIN))
 
     def grid_tail(stream_in, attended_in, tap_in):
         return (stream_in + project_rows(attended_in, grid_outward) + tap_in).astype(jnp.bfloat16)
 
-    output_tile, grid_tail_back = jax.vjp(grid_tail, stream_two, grid_home, zero_width)
-    d_stream_two, d_grid_home, tap_grid_out = grid_tail_back(cotangent[0])
-    d_grid_attended = to_grid(to_exchanged(d_grid_home), WIN)
+    zero_grid = jnp.zeros(stream_two_grid.shape, jnp.float32)
+    output_grid, grid_tail_back = jax.vjp(grid_tail, stream_two_grid, grid_attended, zero_grid)
+    output_tile = to_home(from_grid(output_grid, height, breadth, WIN))
+    cotangent_grid = to_grid(to_exchanged(cotangent[0]), WIN)
+    d_stream_grid, d_grid_attended, tap_grid_out = grid_tail_back(cotangent_grid)
     d_grid_windows, tap_grid_in = grid_core_back(d_grid_attended)
-    d_normed_three = to_home(from_grid(d_grid_windows, height, breadth, WIN))
-    d_stream_extra, d_gain_grid = grid_front_back(d_normed_three)
-    d_stream_two = d_stream_two + d_stream_extra
+    d_stream_extra, d_gain_grid = grid_front_back(d_grid_windows)
+    d_stream_two = to_home(from_grid(d_stream_grid + d_stream_extra, height, breadth, WIN))
     d_stream_one, d_gain_block, tap_block_in, tap_block_out = block_back(d_stream_two)
     d_conv, d_wide_tail, tap_project = tail_back(d_stream_one)
     d_conv_ext = extended_2(d_conv, (("sy", 0), ("sx", 1)), 1)
@@ -339,7 +337,7 @@
         outer_sum(block_saved[1], tap_block_out),
         d_gain_grid,
         outer_sum(grid_windows, tap_grid_in),
-        outer_sum(grid_home, tap_grid_out),
+        outer_sum(grid_attended, tap_grid_out),
     )
     summed = reduce_grads(local_grads)
     return (

time: 189 us -> 193 us (1.021)
  matrix products: 29.8 us -> 37.3 us
  other arithmetic: 25.7 us -> 23.5 us
    dot_general x6, matrix products: 5.53 us -> 8.97 us  [window_attention(): jnp.einsum('whqk,wkc->whqc', softmax_out, value_rows, preferred_element_t...]
    dot_general x12, matrix products: 9.12 us -> 11.3 us  [project_rows(): product = jnp.dot(flattened, weight, preferred_element_type=jnp.float32)]
    all_to_all x2, waiting for transfers between devices: 7.21 us -> 9.34 us  [extended_2(): lax.all_to_all(outgoing, ('sy', 'sx'), split_axis=0, concat_axis=0, tiled...]
    reshape x4 -> x2, local copies, waits for them, and re-layouts: 4 us -> 2.6 us  [to_exchanged(): image.reshape(height // sy_count, sy_count, breadth // sx_count, sx_count...]
    dot_general x5 -> x4, local copies, waits for them, and re-layouts: 4.7 us -> 3.94 us  [outer_sum(): lax.dot_general(left_flat, right_flat, (((0,), (0,)), ((), ())), preferre...]
    unnamed x196 -> x212, local copies, waits for them, and re-layouts: 6.82 us -> 6.65 us
  transfers between devices with their start and end apart: 9 -> 9, of which waited for: 7 -> 7; matrix products, arithmetic and copies ran while one was open for 21% -> 20% of each run, Pallas kernels for 0% -> 0%
where the time goes in v9:
time: 193 us; the launch traced here: 191 us
  waiting for transfers between devices  53.9 us (28%)
  starting transfers between devices  37.6 us (19%)
  matrix products  37.3 us (19%)
  local copies, waits for them, and re-layouts  36 us (19%)
  other arithmetic  23.5 us (12%)
  between operations  2.89 us (1%)
    all_to_all x2, waiting for transfers between devices, exchange_sum(): lax.all_to_all(values.astype(jnp.bfloat16), axes, split_axis=axis, concat...  32.2 us
    all_to_all x4, starting transfers between devices, swap_blocks(): lax.all_to_all(flattened, ('sy', 'sx'), split_axis=0, concat_axis=0, tile...  16.3 us
    dot_general x12, matrix products, project_rows(): product = jnp.dot(flattened, weight, preferred_element_type=jnp.float32)  11.3 us
    all_to_all x2, waiting for transfers between devices, extended_2(): lax.all_to_all(outgoing, ('sy', 'sx'), split_axis=0, concat_axis=0, tiled...  9.34 us
    all_to_all x2, starting transfers between devices, exchange_sum(): lax.all_to_all(values.astype(jnp.bfloat16), axes, split_axis=axis, concat...  9.09 us
    dot_general x6, matrix products, window_attention(): jnp.einsum('whqk,wkc->whqc', softmax_out, value_rows, preferred_element_t...  8.97 us
    all_to_all x1, waiting for transfers between devices, reduce_packed(): lax.all_to_all(spread, ('sy', 'sx'), split_axis=0, concat_axis=0, tiled=T...  8.7 us
    all_to_all x2, starting transfers between devices, extended_2(): lax.all_to_all(outgoing, ('sy', 'sx'), split_axis=0, concat_axis=0, tiled...  7.92 us
  transfers between devices with their start and end apart: 9, of which 7 were waited for; matrix products, arithmetic and copies ran while one was open for 20% of the time, Pallas kernels for 0%

profile of v9, /device:TPU:0, one launch (start us, length us, event | category | flops | bytes accessed | tf_op | source)
XLA Modules:
  0.0 191.1 jit_solution(8898954747811513775)
XLA Ops:
  2.4 5.3 %all-to-all-start.3 = ((bf16[8,8,4,256]{3,1,2,0:T(8,128)(2,1)}), bf16[8,8,4,256]{3,1,2,0:T(8,128)(2,1)S(1)}, u32[]{:S(2)}, u32[]{:S(2)}) async-start(bf16[8,8,4,256]{3,1,2,0:T(8,128)(2,1)} %bitcast.58), calls=%async_computation.3 | async-start | bytes 262144 | tf_op jit(solution)/shard_map/all_to_all | solution.py:166
  9.9 2.3 %multiply_convert_fusion.1 = (bf16[16,16,1024]{2,1,0:T(8,128)(2,1)S(1)}, f32[16,16,1024]{2,1,0:T(8,128)}) fusion(bf16[256,1024]{1,0:T(8,128)(2,1)S(1)} %copy-done, bf16[1,16,16,256]{3,2,1,0:T(8,128)(2,1)} %param.12, f32[256]{0:T(256)} %param.14, f32[16,16]{1,0:T(8,128)S(1)} %fusion.200, f32[16,16]{1,0:T(8,128)S(1)} %broadcast_multiply_fusion.2), kind=kOutput, calls=%fused_computation.150 | convolution fusion | flops 136904704 | bytes 2231296 | tf_op jit(solution)/shard_map/jvp()/dot_general | solution.py:78
  13.8 4.2 %all-to-all-start = ((bf16[8,16,1024]{2,1,0:T(8,128)(2,1)}), bf16[8,16,1024]{2,1,0:T(8,128)(2,1)S(1)}, u32[]{:S(2)}, u32[]{:S(2)}) async-start(bf16[8,16,1024]{2,1,0:T(8,128)(2,1)} %select_select_fusion.1), calls=%async_computation | async-start | bytes 524288 | tf_op jit(solution)/shard_map/all_to_all | solution.py:49
  19.0 5.9 %all-to-all-done = bf16[8,16,1024]{2,1,0:T(8,128)(2,1)S(1)} async-done(((bf16[8,16,1024]{2,1,0:T(8,128)(2,1)}), bf16[8,16,1024]{2,1,0:T(8,128)(2,1)S(1)}, u32[]{:S(2)}, u32[]{:S(2)}) %all-to-all-start) | async-done | bytes 262176 | tf_op jit(solution)/shard_map/all_to_all | solution.py:49
  29.7 2.6 %fusion.216 = (f32[4,8,64]{2,1,0:T(8,128)S(1)}, f32[4,8,64,64]{2,3,1,0:T(8,128)}) fusion(bf16[8,256]{1,0:T(8,128)(2,1)S(1)} %get-tuple-element.172, bf16[4,64,256]{2,1,0:T(8,128)(2,1)S(1)} %slice.339, bf16[4,64,768]{2,1,0:T(8,128)(2,1)} %copy-done.19), kind=kOutput, calls=%fused_computation.369 | convolution fusion | flops 68026432 | bytes 798720 | tf_op jit(solution)/shard_map/jvp()/sub | solution.py:127
  38.2 3.6 %all-to-all-start.1 = ((f32[8,8,4,256]{3,1,2,0:T(8,128)}), f32[8,8,4,256]{3,1,2,0:T(8,128)S(1)}, u32[]{:S(2)}, u32[]{:S(2)}) async-start(f32[8,8,4,256]{3,1,2,0:T(8,128)} %bitcast.433), calls=%async_computation.1 | async-start | bytes 524288 | tf_op jit(solution)/shard_map/all_to_all | solution.py:166
  45.8 2.7 %all-to-all-done.1 = f32[8,8,4,256]{3,1,2,0:T(8,128)S(1)} async-done(((f32[8,8,4,256]{3,1,2,0:T(8,128)}), f32[8,8,4,256]{3,1,2,0:T(8,128)S(1)}, u32[]{:S(2)}, u32[]{:S(2)}) %all-to-all-start.1) | async-done | bytes 262176 | tf_op jit(solution)/shard_map/all_to_all | solution.py:166
  52.3 2.6 %fusion.219 = (f32[4,8,64]{2,1,0:T(8,128)S(1)}, f32[4,8,64,64]{2,3,1,0:T(8,128)}) fusion(bf16[4,64,256]{2,1,0:T(8,128)(2,1)} %slice.342, bf16[8,256]{1,0:T(8,128)(2,1)} %copy-done.94, bf16[4,64,768]{2,1,0:T(8,128)(2,1)} %copy-done.21), kind=kOutput, calls=%fused_computation.370 | convolution fusion | flops 68026432 | bytes 798720 | tf_op jit(solution)/shard_map/jvp()/sub | solution.py:127
  55.0 2.1 %fusion.75 = (f32[4,8,64]{2,1,0:T(8,128)S(1)}, bf16[4,8,64,64]{2,3,1,0:T(8,128)(2,1)S(1)}, bf16[4,8,64,64]{2,3,1,0:T(8,128)(2,1)S(1)}) fusion(f32[4,8,64,64]{2,3,1,0:T(8,128)} %get-tuple-element.184, f32[4,8,64]{2,1,0:T(8,128)S(1)} %multiply_divide_fusion.1, f32[4,8,64]{2,1,0:T(8,128)S(1)} %get-tuple-element.183, bf16[4,64,768]{2,1,0:T(8,128)(2,1)} %copy-done.21, ...), kind=kOutput, calls=%fused_computation.86 | convolution fusion | flops 68548608 | bytes 1998848 | tf_op jit(solution)/shard_map/transpose(jvp(whqk,wkc->whqc))/dot_general | solution.py:128
  62.7 2.3 %multiply_reduce_fusion = bf16[4,64,256]{2,1,0:T(8,128)(2,1)} fusion(bf16[4,8,64,64]{2,3,1,0:T(8,128)(2,1)} %copy-done.99, f32[8,256]{1,0:T(8,128)} %copy-done.75, bf16[4,64,768]{2,1,0:T(8,128)(2,1)} %copy-done.21), kind=kOutput, calls=%fused_computation.10 | convolution fusion | flops 68091904 | bytes 794624 | tf_op jit(solution)/shard_map/jvp(whqk,wkc->whqc)/dot_general | solution.py:128
  69.2 3.4 %all-to-all-start.4 = ((f32[8,8,4,256]{3,1,2,0:T(8,128)}), f32[8,8,4,256]{3,1,2,0:T(8,128)S(1)}, u32[]{:S(2)}, u32[]{:S(2)}) async-start(f32[8,8,4,256]{3,1,2,0:T(8,128)} %bitcast.75), calls=%async_computation.4 | async-start | bytes 524288 | tf_op jit(solution)/shard_map/all_to_all | solution.py:166
  81.1 2.0 %fusion.61 = bf16[4,64,256]{2,1,0:T(8,128)(2,1)} fusion(bf16[4,8,64,64]{2,3,1,0:T(8,128)(2,1)} %copy-done.22, f32[4,64,256]{2,1,0:T(8,128)S(1)} %bitcast.455, f32[8,256]{1,0:T(8,128)S(1)} %copy-done.77), kind=kOutput, calls=%fused_computation.69 | convolution fusion | flops 67698688 | bytes 663552 | tf_op jit(solution)/shard_map/transpose(jvp(whqk,wkc->whqc))/dot_general | solution.py:128
  91.4 2.7 %multiply_reduce_fusion.10 = (f32[1024]{0:T(1024)S(1)}, f32[1024]{0:T(1024)S(1)}, f32[1024]{0:T(1024)S(1)}, f32[1024]{0:T(1024)S(1)}, f32[1024]{0:T(1024)S(1)}, ...) fusion(f32[18,18,1024]{2,1,0:T(8,128)S(1)} %convert_element_typ, ...), kind=kLoop, calls=%fused_computation.137 | loop fusion | flops 14408704 | bytes 11083776 | tf_op jit(solution)/shard_map/transpose(jvp())/reduce_sum | solution.py:143
  95.6 3.7 %all-to-all-start.5 = ((f32[8,16,1024]{2,1,0:T(8,128)}), f32[8,16,1024]{2,1,0:T(8,128)S(1)}, u32[]{:S(2)}, u32[]{:S(2)}) async-start(f32[8,16,1024]{2,1,0:T(8,128)} %select_select_fusion), calls=%async_computation.5 | async-start | bytes 1048576 | tf_op jit(solution)/shard_map/all_to_all | solution.py:49
  101.4 2.6 %fusion.37 = bf16[1024,256]{1,0:T(8,128)(2,1)} fusion(f32[16,16,256]{2,1,0:T(8,128)S(1)} %copy-done.7, f32[16,16,1024]{2,1,0:T(8,128)} %copy-done.16), kind=kOutput, calls=%fused_computation.50 | convolution fusion | flops 136904704 | bytes 1835008 | tf_op jit(solution)/shard_map/dot_general | solution.py:85
  105.3 3.5 %all-to-all-done.5 = f32[8,16,1024]{2,1,0:T(8,128)S(1)} async-done(((f32[8,16,1024]{2,1,0:T(8,128)}), f32[8,16,1024]{2,1,0:T(8,128)S(1)}, u32[]{:S(2)}, u32[]{:S(2)}) %all-to-all-start.5) | async-done | bytes 524320 | tf_op jit(solution)/shard_map/all_to_all | solution.py:49
  108.8 4.0 %all-to-all-start.2 = ((bf16[8,8,4,256]{3,1,2,0:T(8,128)(2,1)}), bf16[8,8,4,256]{3,1,2,0:T(8,128)(2,1)}, u32[]{:S(2)}, u32[]{:S(2)}) async-start(bf16[8,8,4,256]{3,1,2,0:T(8,128)(2,1)} %bitcast.54), calls=%async_computation.2 | async-start | bytes 262144 | tf_op jit(solution)/shard_map/all_to_all | solution.py:166
  124.1 3.1 %copy.389 = bf16[4,8,8,4224]{3,2,0,1:T(8,128)(2,1)} copy(bf16[4,8,8,4224]{3,2,1,0:T(8,128)(2,1)} %constant_dynamic-update-slice_fusion) | data formatting | bytes 4325376 | tf_op jit(solution)/shard_map/concatenate | solution.py:197
  127.2 4.1 %all-to-all-start.6 = ((bf16[4,8,8,4224]{3,2,0,1:T(8,128)(2,1)}), bf16[4,8,8,4224]{3,2,0,1:T(8,128)(2,1)S(1)}, u32[]{:S(2)}, u32[]{:S(2)}) async-start(bf16[4,8,8,4224]{3,2,0,1:T(8,128)(2,1)} %copy.389), calls=%async_computation.6 | async-start | bytes 4325376 | tf_op jit(solution)/shard_map/all_to_all | solution.py:189
  133.1 25.5 %all-to-all-done.6 = bf16[4,8,8,4224]{3,2,0,1:T(8,128)(2,1)S(1)} async-done(((bf16[4,8,8,4224]{3,2,0,1:T(8,128)(2,1)}), bf16[4,8,8,4224]{3,2,0,1:T(8,128)(2,1)S(1)}, u32[]{:S(2)}, u32[]{:S(2)}) %all-to-all-start.6) | async-done | bytes 2162720 | tf_op jit(solution)/shard_map/all_to_all | solution.py:189
  159.7 5.0 %all-to-all-start.7 = ((bf16[4,8,4224]{2,1,0:T(8,128)(2,1)}), bf16[4,8,4224]{2,1,0:T(8,128)(2,1)S(1)}, u32[]{:S(2)}, u32[]{:S(2)}) async-start(bf16[4,8,4224]{2,1,0:T(8,128)(2,1)} %reduce_sum.373), calls=%async_computation.7 | async-start | bytes 540672 | tf_op jit(solution)/shard_map/all_to_all | solution.py:189
  164.8 6.7 %all-to-all-done.7 = bf16[4,8,4224]{2,1,0:T(8,128)(2,1)S(1)} async-done(((bf16[4,8,4224]{2,1,0:T(8,128)(2,1)}), bf16[4,8,4224]{2,1,0:T(8,128)(2,1)S(1)}, u32[]{:S(2)}, u32[]{:S(2)}) %all-to-all-start.7) | async-done | bytes 270368 | tf_op jit(solution)/shard_map/all_to_all | solution.py:189
  172.4 4.3 %all-to-all-start.8 = ((bf16[8,8,4224]{2,1,0:T(8,128)(2,1)}), bf16[8,8,4224]{2,1,0:T(8,128)(2,1)S(1)}, u32[]{:S(2)}, u32[]{:S(2)}) async-start(bf16[8,8,4224]{2,1,0:T(8,128)(2,1)} %broadcast_in_dim.374), calls=%async_computation.8 | async-start | bytes 1081344 | tf_op jit(solution)/shard_map/all_to_all | solution.py:204
  177.9 8.7 %all-to-all-done.8 = bf16[8,8,4224]{2,1,0:T(8,128)(2,1)S(1)} async-done(((bf16[8,8,4224]{2,1,0:T(8,128)(2,1)}), bf16[8,8,4224]{2,1,0:T(8,128)(2,1)S(1)}, u32[]{:S(2)}, u32[]{:S(2)}) %all-to-all-start.8) | async-done | bytes 540704 | tf_op jit(solution)/shard_map/all_to_all | solution.py:204
  (402 shorter events, 75.2 us)
Async XLA Ops:
  2.4 11.4 %all-to-all-start.3 = ((bf16[8,8,4,256]{3,1,2,0:T(8,128)(2,1)}), bf16[8,8,4,256]{3,1,2,0:T(8,128)(2,1)S(1)}, u32[]{:S(2)}, u32[]{:S(2)}) async-start(bf16[8,8,4,256]{3,1,2,0:T(8,128)(2,1)} %bitcast.58), calls=%async_computation.3 | async-start | bytes 262144 | tf_op jit(solution)/shard_map/all_to_all | solution.py:166
  12.4 13.0 %copy-start.78 = (pred[8]{0:T(512)(128)(4,1)}, pred[8]{0:T(512)(128)(4,1)S(1)}, u32[]{:S(2)}) copy-start(pred[8]{0:T(512)(128)(4,1)S(1)} %get-tuple-element.188) | copy-start | bytes 28
  12.4 13.0 %copy-start.80 = (pred[8]{0:T(512)(128)(4,1)}, pred[8]{0:T(512)(128)(4,1)S(1)}, u32[]{:S(2)}) copy-start(pred[8]{0:T(512)(128)(4,1)S(1)} %get-tuple-element.189) | copy-start | bytes 28
  12.4 13.0 %copy-start.82 = (pred[8]{0:T(512)(128)(4,1)}, pred[8]{0:T(512)(128)(4,1)S(1)}, u32[]{:S(2)}) copy-start(pred[8]{0:T(512)(128)(4,1)S(1)} %get-tuple-element.190) | copy-start | bytes 28
  12.4 13.0 %copy-start.84 = (pred[8]{0:T(512)(128)(4,1)}, pred[8]{0:T(512)(128)(4,1)S(1)}, u32[]{:S(2)}) copy-start(pred[8]{0:T(512)(128)(4,1)S(1)} %get-tuple-element.191) | copy-start | bytes 28
  12.4 13.0 %copy-start.86 = (pred[8]{0:T(512)(128)(4,1)}, pred[8]{0:T(512)(128)(4,1)S(1)}, u32[]{:S(2)}) copy-start(pred[8]{0:T(512)(128)(4,1)S(1)} %get-tuple-element.192) | copy-start | bytes 28
  12.5 13.0 %copy-start.88 = (pred[8]{0:T(512)(128)(4,1)}, pred[8]{0:T(512)(128)(4,1)S(1)}, u32[]{:S(2)}) copy-start(pred[8]{0:T(512)(128)(4,1)S(1)} %get-tuple-element.193) | copy-start | bytes 28
  12.5 12.9 %copy-start.90 = (pred[8]{0:T(512)(128)(4,1)}, pred[8]{0:T(512)(128)(4,1)S(1)}, u32[]{:S(2)}) copy-start(pred[8]{0:T(512)(128)(4,1)S(1)} %get-tuple-element.194) | copy-start | bytes 28
  12.5 12.9 %copy-start.92 = (pred[8]{0:T(512)(128)(4,1)}, pred[8]{0:T(512)(128)(4,1)S(1)}, u32[]{:S(2)}) copy-start(pred[8]{0:T(512)(128)(4,1)S(1)} %get-tuple-element.195) | copy-start | bytes 28
  13.7 16.0 %copy-start.94 = (bf16[8,256]{1,0:T(8,128)(2,1)}, bf16[8,256]{1,0:T(8,128)(2,1)S(1)}, u32[]{:S(2)}) copy-start(bf16[8,256]{1,0:T(8,128)(2,1)S(1)} %get-tuple-element.172) | copy-start | bytes 12292
  13.7 20.0 %copy-start.75 = (f32[8,256]{1,0:T(8,128)}, f32[8,256]{1,0:T(8,128)S(1)}, u32[]{:S(2)}) copy-start(f32[8,256]{1,0:T(8,128)S(1)} %get-tuple-element.171) | copy-start | bytes 24580
  13.8 11.1 %all-to-all-start = ((bf16[8,16,1024]{2,1,0:T(8,128)(2,1)}), bf16[8,16,1024]{2,1,0:T(8,128)(2,1)S(1)}, u32[]{:S(2)}, u32[]{:S(2)}) async-start(bf16[8,16,1024]{2,1,0:T(8,128)(2,1)} %select_select_fusion.1), calls=%async_computation | async-start | bytes 524288 | tf_op jit(solution)/shard_map/all_to_all | solution.py:49
  19.0 22.8 %copy-start.14 = (bf16[8,2,8,2,256]{4,2,0,3,1:T(8,128)(2,1)}, bf16[8,2,8,2,256]{4,2,0,3,1:T(8,128)(2,1)S(1)}, u32[]{:S(2)}) copy-start(bf16[8,2,8,2,256]{4,2,0,3,1:T(8,128)(2,1)S(1)} %copy.359) | copy-start | bytes 393220
  36.4 13.1 %copy-start.73 = (f32[256]{0:T(256)S(1)}, f32[256]{0:T(256)}, u32[]{:S(2)}) copy-start(f32[256]{0:T(256)} %param.21) | copy-start | bytes 3076
  38.2 10.3 %all-to-all-start.1 = ((f32[8,8,4,256]{3,1,2,0:T(8,128)}), f32[8,8,4,256]{3,1,2,0:T(8,128)S(1)}, u32[]{:S(2)}, u32[]{:S(2)}) async-start(f32[8,8,4,256]{3,1,2,0:T(8,128)} %bitcast.433), calls=%async_computation.1 | async-start | bytes 524288 | tf_op jit(solution)/shard_map/all_to_all | solution.py:166
  69.2 10.3 %all-to-all-start.4 = ((f32[8,8,4,256]{3,1,2,0:T(8,128)}), f32[8,8,4,256]{3,1,2,0:T(8,128)S(1)}, u32[]{:S(2)}, u32[]{:S(2)}) async-start(f32[8,8,4,256]{3,1,2,0:T(8,128)} %bitcast.75), calls=%async_computation.4 | async-start | bytes 524288 | tf_op jit(solution)/shard_map/all_to_all | solution.py:166
  95.6 13.2 %all-to-all-start.5 = ((f32[8,16,1024]{2,1,0:T(8,128)}), f32[8,16,1024]{2,1,0:T(8,128)S(1)}, u32[]{:S(2)}, u32[]{:S(2)}) async-start(f32[8,16,1024]{2,1,0:T(8,128)} %select_select_fusion), calls=%async_computation.5 | async-start | bytes 1048576 | tf_op jit(solution)/shard_map/all_to_all | solution.py:49
  108.8 18.4 %all-to-all-start.2 = ((bf16[8,8,4,256]{3,1,2,0:T(8,128)(2,1)}), bf16[8,8,4,256]{3,1,2,0:T(8,128)(2,1)}, u32[]{:S(2)}, u32[]{:S(2)}) async-start(bf16[8,8,4,256]{3,1,2,0:T(8,128)(2,1)} %bitcast.54), calls=%async_computation.2 | async-start | bytes 262144 | tf_op jit(solution)/shard_map/all_to_all | solution.py:166
  127.2 31.4 %all-to-all-start.6 = ((bf16[4,8,8,4224]{3,2,0,1:T(8,128)(2,1)}), bf16[4,8,8,4224]{3,2,0,1:T(8,128)(2,1)S(1)}, u32[]{:S(2)}, u32[]{:S(2)}) async-start(bf16[4,8,8,4224]{3,2,0,1:T(8,128)(2,1)} %copy.389), calls=%async_computation.6 | async-start | bytes 4325376 | tf_op jit(solution)/shard_map/all_to_all | solution.py:189
  131.3 33.4 %copy-start.43 = (f32[16,16]{1,0:T(8,128)S(1)}, f32[16,16]{1,0:T(8,128)}, u32[]{:S(2)}) copy-start(f32[16,16]{1,0:T(8,128)} %copy-done.42) | copy-start | bytes 3076
  133.1 43.5 %copy-start.71 = (f32[256]{0:T(256)S(1)}, f32[256]{0:T(256)}, u32[]{:S(2)}) copy-start(f32[256]{0:T(256)} %param.14) | copy-start | bytes 3076
  159.7 17.4 %copy-start.8 = (f32[16,16,256]{2,1,0:T(8,128)S(1)}, f32[16,16,256]{2,1,0:T(8,128)}, u32[]{:S(2)}) copy-start(f32[16,16,256]{2,1,0:T(8,128)} %copy-done.6) | copy-start | bytes 786436
  159.7 11.8 %all-to-all-start.7 = ((bf16[4,8,4224]{2,1,0:T(8,128)(2,1)}), bf16[4,8,4224]{2,1,0:T(8,128)(2,1)S(1)}, u32[]{:S(2)}, u32[]{:S(2)}) async-start(bf16[4,8,4224]{2,1,0:T(8,128)(2,1)} %reduce_sum.373), calls=%async_computation.7 | async-start | bytes 540672 | tf_op jit(solution)/shard_map/all_to_all | solution.py:189
  172.4 14.2 %all-to-all-start.8 = ((bf16[8,8,4224]{2,1,0:T(8,128)(2,1)}), bf16[8,8,4224]{2,1,0:T(8,128)(2,1)S(1)}, u32[]{:S(2)}, u32[]{:S(2)}) async-start(bf16[8,8,4224]{2,1,0:T(8,128)(2,1)} %broadcast_in_dim.374), calls=%async_computation.8 | async-start | bytes 1081344 | tf_op jit(solution)/shard_map/all_to_all | solution.py:204
  (86 other events, 326.2 us)

commit v10 on v7

--- a/solution.py
+++ b/solution.py
@@ -270,7 +270,21 @@
         return jax.nn.gelu(project_rows(normed_in, expand_weight) + tap_in).astype(jnp.bfloat16)
 
     inner, expand_back = jax.vjp(expand_fn, normed, zero_expand)
-    inner_ext = extended_2(inner, (("sy", 0), ("sx", 1)), 1)
+    features_ext = extended_2(image, (("sy", 0), ("sx", 1)), 1)
+    border = jnp.concatenate(
+        [features_ext[0], features_ext[height + 1], features_ext[1 : height + 1, 0], features_ext[1 : height + 1, breadth + 1]],
+        axis=0,
+    )
+    border_normed = conv_front(border.astype(jnp.float32), gain_conv)
+    border_inner = expand_fn(border_normed, jnp.zeros((border.shape[0], expand_units), jnp.float32))
+    top_inner = border_inner[: breadth + 2]
+    bottom_inner = border_inner[breadth + 2 : 2 * breadth + 4]
+    left_inner = border_inner[2 * breadth + 4 : 2 * breadth + 4 + height]
+    right_inner = border_inner[2 * breadth + 4 + height :]
+    inner_ext = jnp.concatenate(
+        [top_inner[None], jnp.concatenate([left_inner[:, None], inner, right_inner[:, None]], axis=1), bottom_inner[None]],
+        axis=0,
+    )
 
     def conv_only(kernel_in):
         return depthwise(inner_ext, kernel_in)

time: 189 us -> 195 us (1.032)
  local copies, waits for them, and re-layouts: 36.8 us -> 46.8 us
  waiting for transfers between devices: 52.9 us -> 44.9 us
  other arithmetic: 25.7 us -> 28 us
    all_to_all x2, waiting for transfers between devices: 7.21 us -> 1.39 us  [extended_2(): lax.all_to_all(outgoing, ('sy', 'sx'), split_axis=0, concat_axis=0, tiled...]
    convert_element_type x3, local copies, waits for them, and re-layouts: 1.03 us -> 3.62 us  [window_attention(): return attended.astype(jnp.bfloat16)]
    all_to_all x4, waiting for transfers between devices: 3.99 us -> 1.78 us  [swap_blocks(): lax.all_to_all(as_sent(flattened), ('sy', 'sx'), split_axis=0, concat_axi...]
    unnamed x196 -> x200, local copies, waits for them, and re-layouts: 6.82 us -> 7.91 us
    dot_general x12 -> x13, matrix products: 9.12 us -> 8.38 us  [project_rows(): product = jnp.dot(flattened, weight, preferred_element_type=jnp.float32)]
  transfers between devices with their start and end apart: 9 -> 9, of which waited for: 7 -> 6; matrix products, arithmetic and copies ran while one was open for 21% -> 31% of each run, Pallas kernels for 0% -> 0%
where the time goes in v10:
time: 195 us; the launch traced here: 193 us
  local copies, waits for them, and re-layouts  46.8 us (24%)
  waiting for transfers between devices  44.9 us (23%)
  starting transfers between devices  39.2 us (20%)
  matrix products  31.1 us (16%)
  other arithmetic  28 us (14%)
  between operations  2.78 us (1%)
    all_to_all x2, waiting for transfers between devices, exchange_sum(): lax.all_to_all(values.astype(jnp.bfloat16), axes, split_axis=axis, concat...  33 us
    all_to_all x4, starting transfers between devices, swap_blocks(): lax.all_to_all(as_sent(flattened), ('sy', 'sx'), split_axis=0, concat_axi...  16.4 us
    all_to_all x2, starting transfers between devices, exchange_sum(): lax.all_to_all(values.astype(jnp.bfloat16), axes, split_axis=axis, concat...  9.48 us
    all_to_all x2, starting transfers between devices, extended_2(): lax.all_to_all(outgoing, ('sy', 'sx'), split_axis=0, concat_axis=0, tiled...  9.09 us
    all_to_all x1, waiting for transfers between devices, reduce_packed(): lax.all_to_all(spread, ('sy', 'sx'), split_axis=0, concat_axis=0, tiled=T...  8.7 us
    dot_general x13, matrix products, project_rows(): product = jnp.dot(flattened, weight, preferred_element_type=jnp.float32)  8.38 us
    unnamed x200, local copies, waits for them, and re-layouts  7.91 us
    dot_general x6, matrix products, outer_sum(): lax.dot_general(left_flat, right_flat, (((0,), (0,)), ((), ())), preferre...  7.41 us
  transfers between devices with their start and end apart: 9, of which 6 were waited for; matrix products, arithmetic and copies ran while one was open for 31% of the time, Pallas kernels for 0%

profile of v10, /device:TPU:0, one launch (start us, length us, event | category | flops | bytes accessed | tf_op | source)
XLA Modules:
  0.0 192.7 jit_solution(5170278325654907592)
XLA Ops:
  4.1 5.2 %all-to-all-start = ((bf16[8,16,256]{2,1,0:T(8,128)(2,1)}), bf16[8,16,256]{2,1,0:T(8,128)(2,1)S(1)}, u32[]{:S(2)}, u32[]{:S(2)}) async-start(bf16[8,16,256]{2,1,0:T(8,128)(2,1)} %select_select_fusion.1), calls=%async_computation | async-start | bytes 131072 | tf_op jit(solution)/shard_map/all_to_all | solution.py:49
  12.6 2.4 %multiply_convert_fusion.1 = (bf16[16,16,1024]{2,1,0:T(8,128)(2,1)S(1)}, f32[16,16,1024]{2,1,0:T(8,128)}) fusion(bf16[256,1024]{1,0:T(8,128)(2,1)S(1)} %copy-done, f32[256]{0:T(256)} %param.14, f32[16,16]{1,0:T(8,128)S(1)} %fusion.209, f32[16,16]{1,0:T(8,128)S(1)} %broadcast_multiply_fusion.2, bf16[1,16,16,256]{3,2,1,0:T(8,128)(2,1)} %param.12), kind=kOutput, calls=%fused_computation.150 | convolution fusion | flops 136904704 | bytes 2231296 | tf_op jit(solution)/shard_map/jvp()/dot_general | solution.py:78
  17.5 4.2 %all-to-all-start.3 = ((bf16[8,8,4,256]{3,1,2,0:T(8,128)(2,1)}), bf16[8,8,4,256]{3,1,2,0:T(8,128)(2,1)}, u32[]{:S(2)}, u32[]{:S(2)}) async-start(bf16[8,8,4,256]{3,1,2,0:T(8,128)(2,1)} %bitcast.64), calls=%async_computation.3 | async-start | bytes 262144 | tf_op jit(solution)/shard_map/all_to_all | solution.py:166
  27.2 2.6 %fusion.224 = (f32[4,8,64]{2,1,0:T(8,128)S(1)}, f32[4,8,64,64]{2,3,1,0:T(8,128)}) fusion(bf16[8,256]{1,0:T(8,128)(2,1)S(1)} %get-tuple-element.139, bf16[4,64,256]{2,1,0:T(8,128)(2,1)S(1)} %slice.355, bf16[4,64,768]{2,1,0:T(8,128)(2,1)} %copy-done.21), kind=kOutput, calls=%fused_computation.371 | convolution fusion | flops 68026432 | bytes 798720 | tf_op jit(solution)/shard_map/jvp()/sub | solution.py:127
  42.4 4.2 %all-to-all-start.1 = ((bf16[8,8,4,256]{3,1,2,0:T(8,128)(2,1)}), bf16[8,8,4,256]{3,1,2,0:T(8,128)(2,1)}, u32[]{:S(2)}, u32[]{:S(2)}) async-start(bf16[8,8,4,256]{3,1,2,0:T(8,128)(2,1)} %bitcast.399), calls=%async_computation.1 | async-start | bytes 262144 | tf_op jit(solution)/shard_map/all_to_all | solution.py:166
  48.3 1.8 reshape.743
  50.1 1.8 copy.157
  59.7 3.2 %fusion.228 = (f32[4,8,64]{2,1,0:T(8,128)}, f32[4,8,64,64]{2,3,1,0:T(8,128)}) fusion(bf16[4,64,256]{2,1,0:T(8,128)(2,1)} %slice.358, bf16[8,256]{1,0:T(8,128)(2,1)} %copy-done.87, bf16[4,64,768]{2,1,0:T(8,128)(2,1)} %copy-done.23), kind=kOutput, calls=%fused_computation.373 | convolution fusion | flops 68026432 | bytes 798720 | tf_op jit(solution)/shard_map/jvp()/sub | solution.py:127
  63.7 2.1 %fusion.75 = (f32[4,8,64]{2,1,0:T(8,128)S(1)}, bf16[4,8,64,64]{2,3,1,0:T(8,128)(2,1)S(1)}, bf16[4,8,64,64]{2,3,1,0:T(8,128)(2,1)S(1)}) fusion(f32[4,8,64,64]{2,3,1,0:T(8,128)} %get-tuple-element.151, f32[4,8,64]{2,1,0:T(8,128)S(1)} %multiply_divide_fusion.1, f32[4,8,64]{2,1,0:T(8,128)} %get-tuple-element.150, bf16[4,64,768]{2,1,0:T(8,128)(2,1)} %copy-done.23, ...), kind=kOutput, calls=%fused_computation.86 | convolution fusion | flops 68548608 | bytes 2007040 | tf_op jit(solution)/shard_map/transpose(jvp(whqk,wkc->whqc))/dot_general | solution.py:128
  70.1 3.8 %all-to-all-start.4 = ((bf16[8,8,4,256]{3,1,2,0:T(8,128)(2,1)}), bf16[8,8,4,256]{3,1,2,0:T(8,128)(2,1)S(1)}, u32[]{:S(2)}, u32[]{:S(2)}) async-start(bf16[8,8,4,256]{3,1,2,0:T(8,128)(2,1)} %bitcast.79), calls=%async_computation.4 | async-start | bytes 262144 | tf_op jit(solution)/shard_map/all_to_all | solution.py:166
  73.9 1.7 copy.178
  79.4 4.2 %all-to-all-start.2 = ((bf16[8,8,4,256]{3,1,2,0:T(8,128)(2,1)}), bf16[8,8,4,256]{3,1,2,0:T(8,128)(2,1)}, u32[]{:S(2)}, u32[]{:S(2)}) async-start(bf16[8,8,4,256]{3,1,2,0:T(8,128)(2,1)} %bitcast.56), calls=%async_computation.2 | async-start | bytes 262144 | tf_op jit(solution)/shard_map/all_to_all | solution.py:166
  95.4 2.7 %multiply_reduce_fusion.10 = (f32[1024]{0:T(1024)S(1)}, f32[1024]{0:T(1024)S(1)}, f32[1024]{0:T(1024)S(1)}, f32[1024]{0:T(1024)S(1)}, f32[1024]{0:T(1024)S(1)}, ...) fusion(f32[18,18,1024]{2,1,0:T(8,128)S(1)} %convert_element_typ, ...), kind=kLoop, calls=%fused_computation.137 | loop fusion | flops 14408704 | bytes 11083776 | tf_op jit(solution)/shard_map/transpose(jvp())/reduce_sum | solution.py:143
  100.5 3.9 %all-to-all-start.5 = ((f32[8,16,1024]{2,1,0:T(8,128)}), f32[8,16,1024]{2,1,0:T(8,128)S(1)}, u32[]{:S(2)}, u32[]{:S(2)}) async-start(f32[8,16,1024]{2,1,0:T(8,128)} %select_select_fusion), calls=%async_computation.5 | async-start | bytes 1048576 | tf_op jit(solution)/shard_map/all_to_all | solution.py:49
  107.9 2.6 %fusion.37 = bf16[1024,256]{1,0:T(8,128)(2,1)} fusion(f32[16,16,256]{2,1,0:T(8,128)S(1)} %copy-done.7, f32[16,16,1024]{2,1,0:T(8,128)} %copy-done.18), kind=kOutput, calls=%fused_computation.50 | convolution fusion | flops 136904704 | bytes 1835008 | tf_op jit(solution)/shard_map/dot_general | solution.py:85
  110.5 2.2 %concatenate.58 = bf16[4,8,8,1024]{3,2,1,0:T(8,128)(2,1)} reshape(bf16[1024,256]{1,0:T(8,128)(2,1)} %fusion.37) | data formatting | bytes 1048576 | tf_op jit(solution)/shard_map/concatenate | solution.py:199
  116.0 1.9 %fusion.82 = bf16[16,16,1024]{2,1,0:T(8,128)(2,1)S(1)} fusion(f32[16,16,1024]{2,1,0:T(8,128)S(1)} %copy-done.20, f32[17,18,1024]{2,1,0:T(8,128)S(1)} %get-tuple-element.82, f32[16,16,1024]{2,1,0:T(8,128)S(1)} %copy-done.2, f32[16,1,1024]{2,1,0:T(1,128)S(1)} %fusion.171, f32[16,1,1024]{2,1,0:T(1,128)S(1)} %fusion.172, ...), kind=kLoop, calls=%fused_computation.93 | loop fusion | flops 10747904 | bytes 9080832 | tf_op jit(solution)/shard_map/transpose(jvp())/add_any | solution.py:270
  126.7 4.5 %all-to-all-start.6 = ((bf16[4,8,8,4224]{3,2,0,1:T(8,128)(2,1)}), bf16[4,8,8,4224]{3,2,0,1:T(8,128)(2,1)}, u32[]{:S(2)}, u32[]{:S(2)}) async-start(bf16[4,8,8,4224]{3,2,0,1:T(8,128)(2,1)} %copy.184), calls=%async_computation.6 | async-start | bytes 4325376 | tf_op jit(solution)/shard_map/all_to_all | solution.py:191
  132.3 26.3 %all-to-all-done.6 = bf16[4,8,8,4224]{3,2,0,1:T(8,128)(2,1)} async-done(((bf16[4,8,8,4224]{3,2,0,1:T(8,128)(2,1)}), bf16[4,8,8,4224]{3,2,0,1:T(8,128)(2,1)}, u32[]{:S(2)}, u32[]{:S(2)}) %all-to-all-start.6) | async-done | bytes 2162720 | tf_op jit(solution)/shard_map/all_to_all | solution.py:191
  158.6 2.7 %reduce_sum.391 = bf16[4,8,4224]{2,1,0:T(8,128)(2,1)} reduce(bf16[4,8,8,4224]{3,2,0,1:T(8,128)(2,1)} %all-to-all-done.6, bf16[]{:T(256)} %constant.165.clone.1), dimensions={1}, to_apply=%region_36.37 | reduce | flops 946176 | bytes 2433026 | tf_op jit(solution)/shard_map/reduce_sum | solution.py:192
  161.3 5.0 %all-to-all-start.7 = ((bf16[4,8,4224]{2,1,0:T(8,128)(2,1)}), bf16[4,8,4224]{2,1,0:T(8,128)(2,1)S(1)}, u32[]{:S(2)}, u32[]{:S(2)}) async-start(bf16[4,8,4224]{2,1,0:T(8,128)(2,1)} %reduce_sum.391), calls=%async_computation.7 | async-start | bytes 540672 | tf_op jit(solution)/shard_map/all_to_all | solution.py:191
  166.4 6.7 %all-to-all-done.7 = bf16[4,8,4224]{2,1,0:T(8,128)(2,1)S(1)} async-done(((bf16[4,8,4224]{2,1,0:T(8,128)(2,1)}), bf16[4,8,4224]{2,1,0:T(8,128)(2,1)S(1)}, u32[]{:S(2)}, u32[]{:S(2)}) %all-to-all-start.7) | async-done | bytes 270368 | tf_op jit(solution)/shard_map/all_to_all | solution.py:191
  174.0 4.3 %all-to-all-start.8 = ((bf16[8,8,4224]{2,1,0:T(8,128)(2,1)}), bf16[8,8,4224]{2,1,0:T(8,128)(2,1)S(1)}, u32[]{:S(2)}, u32[]{:S(2)}) async-start(bf16[8,8,4224]{2,1,0:T(8,128)(2,1)} %broadcast_in_dim.408), calls=%async_computation.8 | async-start | bytes 1081344 | tf_op jit(solution)/shard_map/all_to_all | solution.py:206
  179.5 8.7 %all-to-all-done.8 = bf16[8,8,4224]{2,1,0:T(8,128)(2,1)S(1)} async-done(((bf16[8,8,4224]{2,1,0:T(8,128)(2,1)}), bf16[8,8,4224]{2,1,0:T(8,128)(2,1)S(1)}, u32[]{:S(2)}, u32[]{:S(2)}) %all-to-all-start.8) | async-done | bytes 540704 | tf_op jit(solution)/shard_map/all_to_all | solution.py:206
  (378 shorter events, 81.3 us)
Async XLA Ops:
  0.6 11.9 %copy-start = (bf16[256,1024]{1,0:T(8,128)(2,1)S(1)}, bf16[256,1024]{1,0:T(8,128)(2,1)}, u32[]{:S(2)}) copy-start(bf16[256,1024]{1,0:T(8,128)(2,1)} %param.15) | copy-start | bytes 1572868
  0.7 10.7 %copy-start.71 = (pred[8]{0:T(512)(128)(4,1)}, pred[8]{0:T(512)(128)(4,1)S(1)}, u32[]{:S(2)}) copy-start(pred[8]{0:T(512)(128)(4,1)S(1)} %get-tuple-element.155) | copy-start | bytes 28
  0.7 10.7 %copy-start.73 = (pred[8]{0:T(512)(128)(4,1)}, pred[8]{0:T(512)(128)(4,1)S(1)}, u32[]{:S(2)}) copy-start(pred[8]{0:T(512)(128)(4,1)S(1)} %get-tuple-element.156) | copy-start | bytes 28
  0.7 10.7 %copy-start.75 = (pred[8]{0:T(512)(128)(4,1)}, pred[8]{0:T(512)(128)(4,1)S(1)}, u32[]{:S(2)}) copy-start(pred[8]{0:T(512)(128)(4,1)S(1)} %get-tuple-element.157) | copy-start | bytes 28
  0.7 10.7 %copy-start.77 = (pred[8]{0:T(512)(128)(4,1)}, pred[8]{0:T(512)(128)(4,1)S(1)}, u32[]{:S(2)}) copy-start(pred[8]{0:T(512)(128)(4,1)S(1)} %get-tuple-element.158) | copy-start | bytes 28
  0.7 10.7 %copy-start.79 = (pred[8]{0:T(512)(128)(4,1)}, pred[8]{0:T(512)(128)(4,1)S(1)}, u32[]{:S(2)}) copy-start(pred[8]{0:T(512)(128)(4,1)S(1)} %get-tuple-element.159) | copy-start | bytes 28
  0.8 10.7 %copy-start.81 = (pred[8]{0:T(512)(128)(4,1)}, pred[8]{0:T(512)(128)(4,1)S(1)}, u32[]{:S(2)}) copy-start(pred[8]{0:T(512)(128)(4,1)S(1)} %get-tuple-element.160) | copy-start | bytes 28
  0.8 10.7 %copy-start.83 = (pred[8]{0:T(512)(128)(4,1)}, pred[8]{0:T(512)(128)(4,1)S(1)}, u32[]{:S(2)}) copy-start(pred[8]{0:T(512)(128)(4,1)S(1)} %get-tuple-element.161) | copy-start | bytes 28
  3.2 11.7 %copy-start.58 = (f32[1024,9]{0,1:T(8,128)S(1)}, f32[1024,9]{0,1:T(8,128)}, u32[]{:S(2)}) copy-start(f32[1024,9]{0,1:T(8,128)} %param.16) | copy-start | bytes 110596
  3.3 11.8 %copy-start.13 = (bf16[1,16,16,256]{3,2,1,0:T(8,128)(2,1)S(1)}, bf16[1,16,16,256]{3,2,1,0:T(8,128)(2,1)}, u32[]{:S(2)}) copy-start(bf16[1,16,16,256]{3,2,1,0:T(8,128)(2,1)} %param.13) | copy-start | bytes 393220
  3.3 11.8 %copy-start.26 = (bf16[256,256]{1,0:T(8,128)(2,1)S(1)}, bf16[256,256]{1,0:T(8,128)(2,1)}, u32[]{:S(2)}) copy-start(bf16[256,256]{1,0:T(8,128)(2,1)} %param.23) | copy-start | bytes 393220
  4.1 13.4 %all-to-all-start = ((bf16[8,16,256]{2,1,0:T(8,128)(2,1)}), bf16[8,16,256]{2,1,0:T(8,128)(2,1)S(1)}, u32[]{:S(2)}, u32[]{:S(2)}) async-start(bf16[8,16,256]{2,1,0:T(8,128)(2,1)} %select_select_fusion.1), calls=%async_computation | async-start | bytes 131072 | tf_op jit(solution)/shard_map/all_to_all | solution.py:49
  15.9 11.3 %copy-start.87 = (bf16[8,256]{1,0:T(8,128)(2,1)}, bf16[8,256]{1,0:T(8,128)(2,1)S(1)}, u32[]{:S(2)}) copy-start(bf16[8,256]{1,0:T(8,128)(2,1)S(1)} %get-tuple-element.139) | copy-start | bytes 12292
  17.5 25.0 %all-to-all-start.3 = ((bf16[8,8,4,256]{3,1,2,0:T(8,128)(2,1)}), bf16[8,8,4,256]{3,1,2,0:T(8,128)(2,1)}, u32[]{:S(2)}, u32[]{:S(2)}) async-start(bf16[8,8,4,256]{3,1,2,0:T(8,128)(2,1)} %bitcast.64), calls=%async_computation.3 | async-start | bytes 262144 | tf_op jit(solution)/shard_map/all_to_all | solution.py:166
  33.5 23.5 %copy-start.10 = (bf16[256,768]{1,0:T(8,128)(2,1)S(1)}, bf16[256,768]{1,0:T(8,128)(2,1)}, u32[]{:S(2)}) copy-start(bf16[256,768]{1,0:T(8,128)(2,1)} %param.22) | copy-start | bytes 1179652
  42.4 9.8 %all-to-all-start.1 = ((bf16[8,8,4,256]{3,1,2,0:T(8,128)(2,1)}), bf16[8,8,4,256]{3,1,2,0:T(8,128)(2,1)}, u32[]{:S(2)}, u32[]{:S(2)}) async-start(bf16[8,8,4,256]{3,1,2,0:T(8,128)(2,1)} %bitcast.399), calls=%async_computation.1 | async-start | bytes 262144 | tf_op jit(solution)/shard_map/all_to_all | solution.py:166
  70.1 9.3 %all-to-all-start.4 = ((bf16[8,8,4,256]{3,1,2,0:T(8,128)(2,1)}), bf16[8,8,4,256]{3,1,2,0:T(8,128)(2,1)S(1)}, u32[]{:S(2)}, u32[]{:S(2)}) async-start(bf16[8,8,4,256]{3,1,2,0:T(8,128)(2,1)} %bitcast.79), calls=%async_computation.4 | async-start | bytes 262144 | tf_op jit(solution)/shard_map/all_to_all | solution.py:166
  79.4 21.1 %all-to-all-start.2 = ((bf16[8,8,4,256]{3,1,2,0:T(8,128)(2,1)}), bf16[8,8,4,256]{3,1,2,0:T(8,128)(2,1)}, u32[]{:S(2)}, u32[]{:S(2)}) async-start(bf16[8,8,4,256]{3,1,2,0:T(8,128)(2,1)} %bitcast.56), calls=%async_computation.2 | async-start | bytes 262144 | tf_op jit(solution)/shard_map/all_to_all | solution.py:166
  100.5 13.7 %all-to-all-start.5 = ((f32[8,16,1024]{2,1,0:T(8,128)}), f32[8,16,1024]{2,1,0:T(8,128)S(1)}, u32[]{:S(2)}, u32[]{:S(2)}) async-start(f32[8,16,1024]{2,1,0:T(8,128)} %select_select_fusion), calls=%async_computation.5 | async-start | bytes 1048576 | tf_op jit(solution)/shard_map/all_to_all | solution.py:49
  126.7 31.8 %all-to-all-start.6 = ((bf16[4,8,8,4224]{3,2,0,1:T(8,128)(2,1)}), bf16[4,8,8,4224]{3,2,0,1:T(8,128)(2,1)}, u32[]{:S(2)}, u32[]{:S(2)}) async-start(bf16[4,8,8,4224]{3,2,0,1:T(8,128)(2,1)} %copy.184), calls=%async_computation.6 | async-start | bytes 4325376 | tf_op jit(solution)/shard_map/all_to_all | solution.py:191
  132.3 46.0 %copy-start.65 = (f32[256]{0:T(256)S(1)}, f32[256]{0:T(256)}, u32[]{:S(2)}) copy-start(f32[256]{0:T(256)} %param.14) | copy-start | bytes 3076
  161.3 17.4 %copy-start.8 = (f32[16,16,256]{2,1,0:T(8,128)S(1)}, f32[16,16,256]{2,1,0:T(8,128)}, u32[]{:S(2)}) copy-start(f32[16,16,256]{2,1,0:T(8,128)} %copy-done.6) | copy-start | bytes 786436
  161.3 11.8 %all-to-all-start.7 = ((bf16[4,8,4224]{2,1,0:T(8,128)(2,1)}), bf16[4,8,4224]{2,1,0:T(8,128)(2,1)S(1)}, u32[]{:S(2)}, u32[]{:S(2)}) async-start(bf16[4,8,4224]{2,1,0:T(8,128)(2,1)} %reduce_sum.391), calls=%async_computation.7 | async-start | bytes 540672 | tf_op jit(solution)/shard_map/all_to_all | solution.py:191
  174.0 14.2 %all-to-all-start.8 = ((bf16[8,8,4224]{2,1,0:T(8,128)(2,1)}), bf16[8,8,4224]{2,1,0:T(8,128)(2,1)S(1)}, u32[]{:S(2)}, u32[]{:S(2)}) async-start(bf16[8,8,4224]{2,1,0:T(8,128)(2,1)} %broadcast_in_dim.408), calls=%async_computation.8 | async-start | bytes 1081344 | tf_op jit(solution)/shard_map/all_to_all | solution.py:206
  (81 other events, 281.9 us)

commit v11 on v7

--- a/solution.py
+++ b/solution.py
@@ -192,19 +192,24 @@
     return moved.astype(jnp.float32).sum(axis)
 
 
-def reduce_packed(wide):
+def tile_sum(wide):
     parts = lax.axis_size("rep")
     tiles = lax.axis_size(("sy", "sx"))
-    widths = [piece.shape[1] for piece in wide]
     packed = jnp.concatenate(wide, axis=1)
     channels, width = packed.shape
-    rows = channels // parts
-    piece = rows // tiles
-    local = exchange_sum(packed.reshape(parts, tiles, piece, width), ("sy", "sx"), 1)
+    piece = channels // parts // tiles
+    return exchange_sum(packed.reshape(parts, tiles, piece, width), ("sy", "sx"), 1)
+
+
+def reduce_packed(groups):
+    tiles = lax.axis_size(("sy", "sx"))
+    widths = [piece.shape[1] for wide in groups for piece in wide]
+    local = jnp.concatenate([tile_sum(wide) for wide in groups], axis=-1)
+    parts, piece, width = local.shape
     local = exchange_sum(local, "rep", 0)
     spread = jnp.broadcast_to(local[None].astype(jnp.bfloat16), (tiles, piece, width))
     total = lax.all_to_all(spread, ("sy", "sx"), split_axis=0, concat_axis=0, tiled=True)
-    total = total.astype(jnp.float32).reshape(rows, width)
+    total = total.astype(jnp.float32).reshape(piece * tiles, width)
     cuts = []
     offset = 0
     for size in widths:
@@ -222,20 +227,23 @@
     channels = grads[0].shape[0]
     taps = grads[2].shape[1]
     kernel_cols = taps * grads[2].shape[0] // channels
-    small = pad_lanes([grads[2].reshape(channels, -1), grads[0][:, None], grads[4][:, None], grads[7][:, None]])
-    cuts = reduce_packed([grads[1], grads[5], grads[6], grads[8], grads[9], grads[3].reshape(channels, -1), small])
-    small = cuts[6]
+    cuts = reduce_packed(
+        (
+            [grads[5], grads[6], grads[8], grads[9], pad_lanes([grads[4][:, None], grads[7][:, None]])],
+            [grads[1], grads[3].reshape(channels, -1), pad_lanes([grads[2].reshape(channels, -1), grads[0][:, None]])],
+        )
+    )
     return (
-        small[:, kernel_cols],
+        cuts[7][:, kernel_cols],
+        cuts[5],
+        cuts[7][:, :kernel_cols].reshape(-1, taps),
+        cuts[6].reshape(-1, grads[3].shape[1]),
+        cuts[4][:, 0],
         cuts[0],
-        small[:, :kernel_cols].reshape(-1, taps),
-        cuts[5].reshape(-1, grads[3].shape[1]),
-        small[:, kernel_cols + 1],
         cuts[1],
+        cuts[4][:, 1],
         cuts[2],
-        small[:, kernel_cols + 2],
         cuts[3],
-        cuts[4],
     )
 
 def body(

time: 189 us -> 183 us (0.968)
  local copies, waits for them, and re-layouts: 36.8 us -> 29.1 us
  matrix products: 29.8 us -> 23.8 us
  waiting for transfers between devices: 52.9 us -> 58.9 us
  starting transfers between devices: 38.6 us -> 41.3 us
    all_to_all x2, waiting for transfers between devices: 7.21 us -> 14.1 us  [extended_2(): lax.all_to_all(outgoing, ('sy', 'sx'), split_axis=0, concat_axis=0, tiled...]
    dot_general x6, matrix products: 7.41 us -> 1.93 us  [outer_sum(): lax.dot_general(left_flat, right_flat, (((0,), (0,)), ((), ())), preferre...]
    dot_general x5 -> x1, local copies, waits for them, and re-layouts: 4.7 us -> 0.76 us  [outer_sum(): lax.dot_general(left_flat, right_flat, (((0,), (0,)), ((), ())), preferre...]
    all_to_all x2 -> x3, waiting for transfers between devices: 33 us -> 29.7 us  [exchange_sum(): lax.all_to_all(values.astype(jnp.bfloat16), axes, split_axis=axis, concat...]
    all_to_all x2 -> x3, starting transfers between devices: 9.48 us -> 12.7 us  [exchange_sum(): lax.all_to_all(values.astype(jnp.bfloat16), axes, split_axis=axis, concat...]
    reshape x4, local copies, waits for them, and re-layouts: 4 us -> 1.54 us  [to_exchanged(): image.reshape(height // sy_count, sy_count, breadth // sx_count, sx_count...]
    all_to_all x4, waiting for transfers between devices: 3.99 us -> 6.24 us  [swap_blocks(): lax.all_to_all(as_sent(flattened), ('sy', 'sx'), split_axis=0, concat_axi...]
    unnamed x196 -> x203, local copies, waits for them, and re-layouts: 6.82 us -> 6.27 us
  transfers between devices with their start and end apart: 9 -> 10, of which waited for: 7 -> 8; matrix products, arithmetic and copies ran while one was open for 21% -> 21% of each run, Pallas kernels for 0% -> 0%
where the time goes in v11:
time: 183 us; the launch traced here: 182 us
  waiting for transfers between devices  58.9 us (32%)
  starting transfers between devices  41.3 us (23%)
  local copies, waits for them, and re-layouts  29.1 us (16%)
  other arithmetic  25.6 us (14%)
  matrix products  23.8 us (13%)
  between operations  2.93 us (2%)
    all_to_all x3, waiting for transfers between devices, exchange_sum(): lax.all_to_all(values.astype(jnp.bfloat16), axes, split_axis=axis, concat...  29.7 us
    all_to_all x4, starting transfers between devices, swap_blocks(): lax.all_to_all(as_sent(flattened), ('sy', 'sx'), split_axis=0, concat_axi...  16.1 us
    all_to_all x2, waiting for transfers between devices, extended_2(): lax.all_to_all(outgoing, ('sy', 'sx'), split_axis=0, concat_axis=0, tiled...  14.1 us
    all_to_all x3, starting transfers between devices, exchange_sum(): lax.all_to_all(values.astype(jnp.bfloat16), axes, split_axis=axis, concat...  12.7 us
    all_to_all x1, waiting for transfers between devices, reduce_packed(): lax.all_to_all(spread, ('sy', 'sx'), split_axis=0, concat_axis=0, tiled=T...  8.89 us
    dot_general x12, matrix products, project_rows(): product = jnp.dot(flattened, weight, preferred_element_type=jnp.float32)  8.38 us
    all_to_all x2, starting transfers between devices, extended_2(): lax.all_to_all(outgoing, ('sy', 'sx'), split_axis=0, concat_axis=0, tiled...  8.12 us
    unnamed x203, local copies, waits for them, and re-layouts  6.27 us
  transfers between devices with their start and end apart: 10, of which 8 were waited for; matrix products, arithmetic and copies ran while one was open for 21% of the time, Pallas kernels for 0%

profile of v11, /device:TPU:0, one launch (start us, length us, event | category | flops | bytes accessed | tf_op | source)
XLA Modules:
  0.0 181.5 jit_solution(327288009469138819)
XLA Ops:
  2.7 5.2 %all-to-all-start.3 = ((bf16[8,8,4,256]{3,1,2,0:T(8,128)(2,1)}), bf16[8,8,4,256]{3,1,2,0:T(8,128)(2,1)S(1)}, u32[]{:S(2)}, u32[]{:S(2)}) async-start(bf16[8,8,4,256]{3,1,2,0:T(8,128)(2,1)} %bitcast.60), calls=%async_computation.3 | async-start | bytes 262144 | tf_op jit(solution)/shard_map/all_to_all | solution.py:166
  10.0 2.4 %multiply_convert_fusion.1 = (bf16[16,16,1024]{2,1,0:T(8,128)(2,1)S(1)}, f32[16,16,1024]{2,1,0:T(8,128)}) fusion(bf16[256,1024]{1,0:T(8,128)(2,1)S(1)} %copy-done, bf16[1,16,16,256]{3,2,1,0:T(8,128)(2,1)} %param.12, f32[256]{0:T(256)} %param.14, f32[16,16]{1,0:T(8,128)S(1)} %fusion.192, f32[16,16]{1,0:T(8,128)S(1)} %broadcast_multiply_fusion.2), kind=kOutput, calls=%fused_computation.150 | convolution fusion | flops 136904704 | bytes 2231296 | tf_op jit(solution)/shard_map/jvp()/dot_general | solution.py:78
  14.9 4.2 %all-to-all-start = ((bf16[8,16,1024]{2,1,0:T(8,128)(2,1)}), bf16[8,16,1024]{2,1,0:T(8,128)(2,1)S(1)}, u32[]{:S(2)}, u32[]{:S(2)}) async-start(bf16[8,16,1024]{2,1,0:T(8,128)(2,1)} %select_select_fusion.1), calls=%async_computation | async-start | bytes 524288 | tf_op jit(solution)/shard_map/all_to_all | solution.py:49
  20.2 5.8 %all-to-all-done = bf16[8,16,1024]{2,1,0:T(8,128)(2,1)S(1)} async-done(((bf16[8,16,1024]{2,1,0:T(8,128)(2,1)}), bf16[8,16,1024]{2,1,0:T(8,128)(2,1)S(1)}, u32[]{:S(2)}, u32[]{:S(2)}) %all-to-all-start) | async-done | bytes 262176 | tf_op jit(solution)/shard_map/all_to_all | solution.py:49
  30.0 1.7 fusion.207
  35.3 3.4 %all-to-all-start.1 = ((bf16[8,8,4,256]{3,1,2,0:T(8,128)(2,1)}), bf16[8,8,4,256]{3,1,2,0:T(8,128)(2,1)S(1)}, u32[]{:S(2)}, u32[]{:S(2)}) async-start(bf16[8,8,4,256]{3,1,2,0:T(8,128)(2,1)} %bitcast.39), calls=%async_computation.1 | async-start | bytes 262144 | tf_op jit(solution)/shard_map/all_to_all | solution.py:166
  39.3 4.8 %all-to-all-done.1 = bf16[8,8,4,256]{3,1,2,0:T(8,128)(2,1)S(1)} async-done(((bf16[8,8,4,256]{3,1,2,0:T(8,128)(2,1)}), bf16[8,8,4,256]{3,1,2,0:T(8,128)(2,1)S(1)}, u32[]{:S(2)}, u32[]{:S(2)}) %all-to-all-start.1) | async-done | bytes 131104 | tf_op jit(solution)/shard_map/all_to_all | solution.py:166
  46.4 2.6 %fusion.211 = (f32[4,8,64]{2,1,0:T(8,128)S(1)}, f32[4,8,64,64]{2,3,1,0:T(8,128)}) fusion(bf16[4,64,256]{2,1,0:T(8,128)(2,1)S(1)} %slice.343, bf16[8,256]{1,0:T(8,128)(2,1)} %copy-done.92, bf16[4,64,768]{2,1,0:T(8,128)(2,1)} %copy-done.18), kind=kOutput, calls=%fused_computation.360 | convolution fusion | flops 68026432 | bytes 798720 | tf_op jit(solution)/shard_map/jvp()/sub | solution.py:127
  49.1 2.1 %fusion.74 = (f32[4,8,64]{2,1,0:T(8,128)S(1)}, bf16[4,8,64,64]{2,3,1,0:T(8,128)(2,1)S(1)}, bf16[4,8,64,64]{2,3,1,0:T(8,128)(2,1)S(1)}) fusion(f32[4,8,64,64]{2,3,1,0:T(8,128)} %get-tuple-element.147, f32[4,8,64]{2,1,0:T(8,128)S(1)} %multiply_divide_fusion.1, f32[4,8,64]{2,1,0:T(8,128)S(1)} %get-tuple-element.146, bf16[4,64,768]{2,1,0:T(8,128)(2,1)} %copy-done.18, ...), kind=kOutput, calls=%fused_computation.86 | convolution fusion | flops 68548608 | bytes 1998848 | tf_op jit(solution)/shard_map/transpose(jvp(whqk,wkc->whqc))/dot_general | solution.py:128
  56.4 3.4 %all-to-all-start.4 = ((bf16[8,8,4,256]{3,1,2,0:T(8,128)(2,1)}), bf16[8,8,4,256]{3,1,2,0:T(8,128)(2,1)S(1)}, u32[]{:S(2)}, u32[]{:S(2)}) async-start(bf16[8,8,4,256]{3,1,2,0:T(8,128)(2,1)} %bitcast.75), calls=%async_computation.4 | async-start | bytes 262144 | tf_op jit(solution)/shard_map/all_to_all | solution.py:166
  59.8 1.6 multiply_reduce_fusion
  65.3 4.2 %all-to-all-start.2 = ((bf16[8,8,4,256]{3,1,2,0:T(8,128)(2,1)}), bf16[8,8,4,256]{3,1,2,0:T(8,128)(2,1)}, u32[]{:S(2)}, u32[]{:S(2)}) async-start(bf16[8,8,4,256]{3,1,2,0:T(8,128)(2,1)} %bitcast.52), calls=%async_computation.2 | async-start | bytes 262144 | tf_op jit(solution)/shard_map/all_to_all | solution.py:166
  81.7 3.3 %multiply_reduce_fusion.10 = (f32[1024]{0:T(1024)S(1)}, f32[1024]{0:T(1024)S(1)}, f32[1024]{0:T(1024)S(1)}, f32[1024]{0:T(1024)S(1)}, f32[1024]{0:T(1024)S(1)}, ...) fusion(f32[18,18,1024]{2,1,0:T(8,128)S(1)} %convert_element_type., ...), kind=kLoop, calls=%fused_computation.137 | loop fusion | flops 14408704 | bytes 11083776 | tf_op jit(solution)/shard_map/transpose(jvp())/reduce_sum | solution.py:143
  95.3 3.9 %all-to-all-start.5 = ((f32[8,16,1024]{2,1,0:T(8,128)}), f32[8,16,1024]{2,1,0:T(8,128)S(1)}, u32[]{:S(2)}, u32[]{:S(2)}) async-start(f32[8,16,1024]{2,1,0:T(8,128)} %select_select_fusion), calls=%async_computation.5 | async-start | bytes 1048576 | tf_op jit(solution)/shard_map/all_to_all | solution.py:49
  100.7 8.3 %all-to-all-done.5 = f32[8,16,1024]{2,1,0:T(8,128)S(1)} async-done(((f32[8,16,1024]{2,1,0:T(8,128)}), f32[8,16,1024]{2,1,0:T(8,128)S(1)}, u32[]{:S(2)}, u32[]{:S(2)}) %all-to-all-start.5) | async-done | bytes 524320 | tf_op jit(solution)/shard_map/all_to_all | solution.py:49
  109.0 4.2 %all-to-all-start.6 = ((bf16[4,8,8,2176]{3,2,0,1:T(8,128)(2,1)}), bf16[4,8,8,2176]{3,2,0,1:T(8,128)(2,1)}, u32[]{:S(2)}, u32[]{:S(2)}) async-start(bf16[4,8,8,2176]{3,2,0,1:T(8,128)(2,1)} %copy.191), calls=%async_computation.6 | async-start | bytes 2228224 | tf_op jit(solution)/shard_map/all_to_all | solution.py:191
  115.7 1.9 %fusion.81 = bf16[16,16,1024]{2,1,0:T(8,128)(2,1)S(1)} fusion(f32[16,16,1024]{2,1,0:T(8,128)S(1)} %copy-done.15, f32[17,18,1024]{2,1,0:T(8,128)S(1)} %get-tuple-element.82, f32[16,16,1024]{2,1,0:T(8,128)S(1)} %copy-done.2, f32[16,1,1024]{2,1,0:T(1,128)S(1)} %fusion.161, f32[16,1,1024]{2,1,0:T(1,128)S(1)} %fusion.163, ...), kind=kLoop, calls=%fused_computation.93 | loop fusion | flops 10747904 | bytes 9080832 | tf_op jit(solution)/shard_map/transpose(jvp())/add_any | solution.py:278
  120.1 9.3 %all-to-all-done.6 = bf16[4,8,8,2176]{3,2,0,1:T(8,128)(2,1)} async-done(((bf16[4,8,8,2176]{3,2,0,1:T(8,128)(2,1)}), bf16[4,8,8,2176]{3,2,0,1:T(8,128)(2,1)}, u32[]{:S(2)}, u32[]{:S(2)}) %all-to-all-start.6) | async-done | bytes 1114144 | tf_op jit(solution)/shard_map/all_to_all | solution.py:191
  129.4 3.6 %all-to-all-start.7 = ((bf16[4,8,8,2176]{3,2,0,1:T(8,128)(2,1)}), bf16[4,8,8,2176]{3,2,0,1:T(8,128)(2,1)S(1)}, u32[]{:S(2)}, u32[]{:S(2)}) async-start(bf16[4,8,8,2176]{3,2,0,1:T(8,128)(2,1)} %copy.196), calls=%async_computation.7 | async-start | bytes 2228224 | tf_op jit(solution)/shard_map/all_to_all | solution.py:191
  135.4 13.6 %all-to-all-done.7 = bf16[4,8,8,2176]{3,2,0,1:T(8,128)(2,1)S(1)} async-done(((bf16[4,8,8,2176]{3,2,0,1:T(8,128)(2,1)}), bf16[4,8,8,2176]{3,2,0,1:T(8,128)(2,1)S(1)}, u32[]{:S(2)}, u32[]{:S(2)}) %all-to-all-start.7) | async-done | bytes 1114144 | tf_op jit(solution)/shard_map/all_to_all | solution.py:191
  149.9 4.9 %all-to-all-start.8 = ((bf16[4,8,4352]{2,1,0:T(8,128)(2,1)}), bf16[4,8,4352]{2,1,0:T(8,128)(2,1)S(1)}, u32[]{:S(2)}, u32[]{:S(2)}) async-start(bf16[4,8,4352]{2,1,0:T(8,128)(2,1)} %pad_maximum_fusion.5), calls=%async_computation.8 | async-start | bytes 557056 | tf_op jit(solution)/shard_map/all_to_all | solution.py:191
  154.8 6.8 %all-to-all-done.8 = bf16[4,8,4352]{2,1,0:T(8,128)(2,1)S(1)} async-done(((bf16[4,8,4352]{2,1,0:T(8,128)(2,1)}), bf16[4,8,4352]{2,1,0:T(8,128)(2,1)S(1)}, u32[]{:S(2)}, u32[]{:S(2)}) %all-to-all-start.8) | async-done | bytes 278560 | tf_op jit(solution)/shard_map/all_to_all | solution.py:191
  162.5 4.4 %all-to-all-start.9 = ((bf16[8,8,4352]{2,1,0:T(8,128)(2,1)}), bf16[8,8,4352]{2,1,0:T(8,128)(2,1)S(1)}, u32[]{:S(2)}, u32[]{:S(2)}) async-start(bf16[8,8,4352]{2,1,0:T(8,128)(2,1)} %broadcast_in_dim.375), calls=%async_computation.9 | async-start | bytes 1114112 | tf_op jit(solution)/shard_map/all_to_all | solution.py:211
  168.1 8.9 %all-to-all-done.9 = bf16[8,8,4352]{2,1,0:T(8,128)(2,1)S(1)} async-done(((bf16[8,8,4352]{2,1,0:T(8,128)(2,1)}), bf16[8,8,4352]{2,1,0:T(8,128)(2,1)S(1)}, u32[]{:S(2)}, u32[]{:S(2)}) %all-to-all-start.9) | async-done | bytes 557088 | tf_op jit(solution)/shard_map/all_to_all | solution.py:211
  (388 shorter events, 64.2 us)
Async XLA Ops:
  0.6 9.4 %copy-start = (bf16[256,1024]{1,0:T(8,128)(2,1)S(1)}, bf16[256,1024]{1,0:T(8,128)(2,1)}, u32[]{:S(2)}) copy-start(bf16[256,1024]{1,0:T(8,128)(2,1)} %param.15) | copy-start | bytes 1572868
  2.7 12.2 %all-to-all-start.3 = ((bf16[8,8,4,256]{3,1,2,0:T(8,128)(2,1)}), bf16[8,8,4,256]{3,1,2,0:T(8,128)(2,1)S(1)}, u32[]{:S(2)}, u32[]{:S(2)}) async-start(bf16[8,8,4,256]{3,1,2,0:T(8,128)(2,1)} %bitcast.60), calls=%async_computation.3 | async-start | bytes 262144 | tf_op jit(solution)/shard_map/all_to_all | solution.py:166
  12.6 7.6 %copy-start.76 = (pred[8]{0:T(512)(128)(4,1)}, pred[8]{0:T(512)(128)(4,1)S(1)}, u32[]{:S(2)}) copy-start(pred[8]{0:T(512)(128)(4,1)S(1)} %get-tuple-element.151) | copy-start | bytes 28
  13.1 14.1 %copy-start.39 = (f32[1024,1]{0,1:T(1,128)}, f32[1024,1]{0,1:T(1,128)S(1)}, u32[]{:S(2)}) copy-start(f32[1024,1]{0,1:T(1,128)S(1)} %get-tuple-element.125) | copy-start | bytes 12292
  13.1 14.1 %copy-start.41 = (f32[1024,1]{0,1:T(1,128)}, f32[1024,1]{0,1:T(1,128)S(1)}, u32[]{:S(2)}) copy-start(f32[1024,1]{0,1:T(1,128)S(1)} %get-tuple-element.126) | copy-start | bytes 12292
  13.1 14.1 %copy-start.43 = (f32[1024,1]{0,1:T(1,128)}, f32[1024,1]{0,1:T(1,128)S(1)}, u32[]{:S(2)}) copy-start(f32[1024,1]{0,1:T(1,128)S(1)} %get-tuple-element.127) | copy-start | bytes 12292
  13.2 14.1 %copy-start.45 = (f32[1024,1]{0,1:T(1,128)}, f32[1024,1]{0,1:T(1,128)S(1)}, u32[]{:S(2)}) copy-start(f32[1024,1]{0,1:T(1,128)S(1)} %get-tuple-element.128) | copy-start | bytes 12292
  13.2 14.1 %copy-start.47 = (f32[1024,1]{0,1:T(1,128)}, f32[1024,1]{0,1:T(1,128)S(1)}, u32[]{:S(2)}) copy-start(f32[1024,1]{0,1:T(1,128)S(1)} %get-tuple-element.129) | copy-start | bytes 12292
  13.2 14.1 %copy-start.50 = (f32[1024,1]{0,1:T(1,128)}, f32[1024,1]{0,1:T(1,128)S(1)}, u32[]{:S(2)}) copy-start(f32[1024,1]{0,1:T(1,128)S(1)} %get-tuple-element.130) | copy-start | bytes 12292
  13.2 14.1 %copy-start.53 = (f32[1024,1]{0,1:T(1,128)}, f32[1024,1]{0,1:T(1,128)S(1)}, u32[]{:S(2)}) copy-start(f32[1024,1]{0,1:T(1,128)S(1)} %get-tuple-element.131) | copy-start | bytes 12292
  14.9 15.1 %copy-start.92 = (bf16[8,256]{1,0:T(8,128)(2,1)}, bf16[8,256]{1,0:T(8,128)(2,1)S(1)}, u32[]{:S(2)}) copy-start(bf16[8,256]{1,0:T(8,128)(2,1)S(1)} %get-tuple-element.135) | copy-start | bytes 12292
  14.9 18.2 %copy-start.72 = (f32[8,256]{1,0:T(8,128)}, f32[8,256]{1,0:T(8,128)S(1)}, u32[]{:S(2)}) copy-start(f32[8,256]{1,0:T(8,128)S(1)} %get-tuple-element.134) | copy-start | bytes 24580
  14.9 11.1 %all-to-all-start = ((bf16[8,16,1024]{2,1,0:T(8,128)(2,1)}), bf16[8,16,1024]{2,1,0:T(8,128)(2,1)S(1)}, u32[]{:S(2)}, u32[]{:S(2)}) async-start(bf16[8,16,1024]{2,1,0:T(8,128)(2,1)} %select_select_fusion.1), calls=%async_computation | async-start | bytes 524288 | tf_op jit(solution)/shard_map/all_to_all | solution.py:49
  31.7 7.0 %copy-start.56 = (f32[4,8,64]{2,1,0:T(8,128)}, f32[4,8,64]{2,1,0:T(8,128)S(1)}, u32[]{:S(2)}) copy-start(f32[4,8,64]{2,1,0:T(8,128)S(1)} %get-tuple-element.142) | copy-start | bytes 24580
  35.3 8.8 %all-to-all-start.1 = ((bf16[8,8,4,256]{3,1,2,0:T(8,128)(2,1)}), bf16[8,8,4,256]{3,1,2,0:T(8,128)(2,1)S(1)}, u32[]{:S(2)}, u32[]{:S(2)}) async-start(bf16[8,8,4,256]{3,1,2,0:T(8,128)(2,1)} %bitcast.39), calls=%async_computation.1 | async-start | bytes 262144 | tf_op jit(solution)/shard_map/all_to_all | solution.py:166
  56.4 8.8 %all-to-all-start.4 = ((bf16[8,8,4,256]{3,1,2,0:T(8,128)(2,1)}), bf16[8,8,4,256]{3,1,2,0:T(8,128)(2,1)S(1)}, u32[]{:S(2)}, u32[]{:S(2)}) async-start(bf16[8,8,4,256]{3,1,2,0:T(8,128)(2,1)} %bitcast.75), calls=%async_computation.4 | async-start | bytes 262144 | tf_op jit(solution)/shard_map/all_to_all | solution.py:166
  61.6 13.2 %copy-start.9 = (bf16[1,16,16,256]{3,2,1,0:T(8,128)(2,1)S(1)}, bf16[1,16,16,256]{3,2,1,0:T(8,128)(2,1)}, u32[]{:S(2)}) copy-start(bf16[1,16,16,256]{3,2,1,0:T(8,128)(2,1)} %param.13) | copy-start | bytes 393220
  65.3 22.2 %all-to-all-start.2 = ((bf16[8,8,4,256]{3,1,2,0:T(8,128)(2,1)}), bf16[8,8,4,256]{3,1,2,0:T(8,128)(2,1)}, u32[]{:S(2)}, u32[]{:S(2)}) async-start(bf16[8,8,4,256]{3,1,2,0:T(8,128)(2,1)} %bitcast.52), calls=%async_computation.2 | async-start | bytes 262144 | tf_op jit(solution)/shard_map/all_to_all | solution.py:166
  95.3 13.7 %all-to-all-start.5 = ((f32[8,16,1024]{2,1,0:T(8,128)}), f32[8,16,1024]{2,1,0:T(8,128)S(1)}, u32[]{:S(2)}, u32[]{:S(2)}) async-start(f32[8,16,1024]{2,1,0:T(8,128)} %select_select_fusion), calls=%async_computation.5 | async-start | bytes 1048576 | tf_op jit(solution)/shard_map/all_to_all | solution.py:49
  109.0 20.4 %all-to-all-start.6 = ((bf16[4,8,8,2176]{3,2,0,1:T(8,128)(2,1)}), bf16[4,8,8,2176]{3,2,0,1:T(8,128)(2,1)}, u32[]{:S(2)}, u32[]{:S(2)}) async-start(bf16[4,8,8,2176]{3,2,0,1:T(8,128)(2,1)} %copy.191), calls=%async_computation.6 | async-start | bytes 2228224 | tf_op jit(solution)/shard_map/all_to_all | solution.py:191
  120.1 13.0 %copy-start.21 = (bf16[256,256]{1,0:T(8,128)(2,1)S(1)}, bf16[256,256]{1,0:T(8,128)(2,1)}, u32[]{:S(2)}) copy-start(bf16[256,256]{1,0:T(8,128)(2,1)} %param.23) | copy-start | bytes 393220
  129.4 19.6 %all-to-all-start.7 = ((bf16[4,8,8,2176]{3,2,0,1:T(8,128)(2,1)}), bf16[4,8,8,2176]{3,2,0,1:T(8,128)(2,1)S(1)}, u32[]{:S(2)}, u32[]{:S(2)}) async-start(bf16[4,8,8,2176]{3,2,0,1:T(8,128)(2,1)} %copy.196), calls=%async_computation.7 | async-start | bytes 2228224 | tf_op jit(solution)/shard_map/all_to_all | solution.py:191
  149.9 11.8 %all-to-all-start.8 = ((bf16[4,8,4352]{2,1,0:T(8,128)(2,1)}), bf16[4,8,4352]{2,1,0:T(8,128)(2,1)S(1)}, u32[]{:S(2)}, u32[]{:S(2)}) async-start(bf16[4,8,4352]{2,1,0:T(8,128)(2,1)} %pad_maximum_fusion.5), calls=%async_computation.8 | async-start | bytes 557056 | tf_op jit(solution)/shard_map/all_to_all | solution.py:191
  162.5 14.5 %all-to-all-start.9 = ((bf16[8,8,4352]{2,1,0:T(8,128)(2,1)}), bf16[8,8,4352]{2,1,0:T(8,128)(2,1)S(1)}, u32[]{:S(2)}, u32[]{:S(2)}) async-start(bf16[8,8,4352]{2,1,0:T(8,128)(2,1)} %broadcast_in_dim.375), calls=%async_computation.9 | async-start | bytes 1114112 | tf_op jit(solution)/shard_map/all_to_all | solution.py:211
  (83 other events, 209.1 us)

commit v12 on v11

--- a/solution.py
+++ b/solution.py
@@ -229,19 +229,19 @@
     kernel_cols = taps * grads[2].shape[0] // channels
     cuts = reduce_packed(
         (
-            [grads[5], grads[6], grads[8], grads[9], pad_lanes([grads[4][:, None], grads[7][:, None]])],
-            [grads[1], grads[3].reshape(channels, -1), pad_lanes([grads[2].reshape(channels, -1), grads[0][:, None]])],
+            [grads[5], grads[6], grads[8], grads[9], grads[3].reshape(channels, -1), pad_lanes([grads[4][:, None], grads[7][:, None]])],
+            [grads[1], pad_lanes([grads[2].reshape(channels, -1), grads[0][:, None]])],
         )
     )
     return (
         cuts[7][:, kernel_cols],
-        cuts[5],
+        cuts[6],
         cuts[7][:, :kernel_cols].reshape(-1, taps),
-        cuts[6].reshape(-1, grads[3].shape[1]),
-        cuts[4][:, 0],
+        cuts[4].reshape(-1, grads[3].shape[1]),
+        cuts[5][:, 0],
         cuts[0],
         cuts[1],
-        cuts[4][:, 1],
+        cuts[5][:, 1],
         cuts[2],
         cuts[3],
     )
@@ -331,7 +331,8 @@
     d_stream_two = d_stream_two + d_stream_extra
     d_stream_one, d_gain_block, tap_block_in, tap_block_out = block_back(d_stream_two)
     d_conv, d_wide_tail, tap_project = tail_back(d_stream_one)
-    d_conv_ext = extended_2(d_conv, (("sy", 0), ("sx", 1)), 1)
+    d_conv_ext = extended_2(d_conv.astype(jnp.bfloat16), (("sy", 0), ("sx", 1)), 1)
+    d_conv_ext = d_conv_ext.astype(jnp.float32).at[1:-1, 1:-1].set(d_conv)
     d_kernel = kernel_back(d_conv)[0]
     d_inner = depthwise_back(d_conv_ext, dw_kernel).astype(jnp.bfloat16)
     d_normed, tap_expand = expand_back(d_inner)

time: 183 us -> 202 us (1.10)
  local copies, waits for them, and re-layouts: 29.1 us -> 50 us
  waiting for transfers between devices: 58.9 us -> 45 us
  matrix products: 23.8 us -> 31.9 us
  other arithmetic: 25.6 us -> 28 us
    all_to_all x2, waiting for transfers between devices: 14.1 us -> 7.09 us  [extended_2(): lax.all_to_all(outgoing, ('sy', 'sx'), split_axis=0, concat_axis=0, tiled...]
    dot_general x6, matrix products: 1.93 us -> 8.27 us  [outer_sum(): lax.dot_general(left_flat, right_flat, (((0,), (0,)), ((), ())), preferre...]
    all_to_all x4, waiting for transfers between devices: 6.24 us -> 1.8 us  [swap_blocks(): lax.all_to_all(as_sent(flattened), ('sy', 'sx'), split_axis=0, concat_axi...]
    pad x8, local copies, waits for them, and re-layouts: 0.06 us -> 2.8 us  [lay(): return jnp.pad(line, ((0, span - line.shape[0]), (0, 0)))]
    dot_general x1 -> x4, local copies, waits for them, and re-layouts: 0.76 us -> 3.27 us  [outer_sum(): lax.dot_general(left_flat, right_flat, (((0,), (0,)), ((), ())), preferre...]
    reshape x4, local copies, waits for them, and re-layouts: 1.54 us -> 4 us  [to_exchanged(): image.reshape(height // sy_count, sy_count, breadth // sx_count, sx_count...]
    another operation x2, local copies, waits for them, and re-layouts: 0.77 us -> 3.23 us  [to_home(): image.reshape(sy_count, height // sy_count, sx_count, breadth // sx_count...]
    all_to_all x3, waiting for transfers between devices: 29.7 us -> 27.2 us  [exchange_sum(): lax.all_to_all(values.astype(jnp.bfloat16), axes, split_axis=axis, concat...]
  transfers between devices with their start and end apart: 10 -> 10, of which waited for: 8 -> 7; matrix products, arithmetic and copies ran while one was open for 21% -> 22% of each run, Pallas kernels for 0% -> 0%
where the time goes in v12:
time: 202 us; the launch traced here: 200 us
  local copies, waits for them, and re-layouts  50 us (25%)
  waiting for transfers between devices  45 us (22%)
  starting transfers between devices  42.5 us (21%)
  matrix products  31.9 us (16%)
  other arithmetic  28 us (14%)
  between operations  2.48 us (1%)
    all_to_all x3, waiting for transfers between devices, exchange_sum(): lax.all_to_all(values.astype(jnp.bfloat16), axes, split_axis=axis, concat...  27.2 us
    all_to_all x4, starting transfers between devices, swap_blocks(): lax.all_to_all(as_sent(flattened), ('sy', 'sx'), split_axis=0, concat_axi...  17.4 us
    all_to_all x3, starting transfers between devices, exchange_sum(): lax.all_to_all(values.astype(jnp.bfloat16), axes, split_axis=axis, concat...  12.7 us
    dot_general x12, matrix products, project_rows(): product = jnp.dot(flattened, weight, preferred_element_type=jnp.float32)  9.25 us
    all_to_all x1, waiting for transfers between devices, reduce_packed(): lax.all_to_all(spread, ('sy', 'sx'), split_axis=0, concat_axis=0, tiled=T...  8.89 us
    dot_general x6, matrix products, outer_sum(): lax.dot_general(left_flat, right_flat, (((0,), (0,)), ((), ())), preferre...  8.27 us
    all_to_all x2, starting transfers between devices, extended_2(): lax.all_to_all(outgoing, ('sy', 'sx'), split_axis=0, concat_axis=0, tiled...  8.13 us
    all_to_all x2, waiting for transfers between devices, extended_2(): lax.all_to_all(outgoing, ('sy', 'sx'), split_axis=0, concat_axis=0, tiled...  7.09 us
  transfers between devices with their start and end apart: 10, of which 7 were waited for; matrix products, arithmetic and copies ran while one was open for 22% of the time, Pallas kernels for 0%

profile of v12, /device:TPU:0, one launch (start us, length us, event | category | flops | bytes accessed | tf_op | source)
XLA Modules:
  0.0 200.0 jit_solution(8229149555611343783)
XLA Ops:
  2.7 5.2 %all-to-all-start.3 = ((bf16[8,8,4,256]{3,1,2,0:T(8,128)(2,1)}), bf16[8,8,4,256]{3,1,2,0:T(8,128)(2,1)S(1)}, u32[]{:S(2)}, u32[]{:S(2)}) async-start(bf16[8,8,4,256]{3,1,2,0:T(8,128)(2,1)} %bitcast.62), calls=%async_computation.3 | async-start | bytes 262144 | tf_op jit(solution)/shard_map/all_to_all | solution.py:166
  10.0 2.4 %multiply_convert_fusion.1 = (bf16[16,16,1024]{2,1,0:T(8,128)(2,1)S(1)}, f32[16,16,1024]{2,1,0:T(8,128)}) fusion(bf16[256,1024]{1,0:T(8,128)(2,1)S(1)} %copy-done, bf16[1,16,16,256]{3,2,1,0:T(8,128)(2,1)} %param.14, f32[256]{0:T(256)} %param.16, f32[16,16]{1,0:T(8,128)S(1)} %fusion.189, f32[16,16]{1,0:T(8,128)S(1)} %broadcast_multiply_fusion.2), kind=kOutput, calls=%fused_computation.145 | convolution fusion | flops 136904704 | bytes 2231296 | tf_op jit(solution)/shard_map/jvp()/dot_general | solution.py:78
  15.4 4.2 %all-to-all-start = ((bf16[8,16,1024]{2,1,0:T(8,128)(2,1)}), bf16[8,16,1024]{2,1,0:T(8,128)(2,1)S(1)}, u32[]{:S(2)}, u32[]{:S(2)}) async-start(bf16[8,16,1024]{2,1,0:T(8,128)(2,1)} %select_select_fusion.1), calls=%async_computation | async-start | bytes 524288 | tf_op jit(solution)/shard_map/all_to_all | solution.py:49
  20.7 5.9 %all-to-all-done = bf16[8,16,1024]{2,1,0:T(8,128)(2,1)S(1)} async-done(((bf16[8,16,1024]{2,1,0:T(8,128)(2,1)}), bf16[8,16,1024]{2,1,0:T(8,128)(2,1)S(1)}, u32[]{:S(2)}, u32[]{:S(2)}) %all-to-all-start) | async-done | bytes 262176 | tf_op jit(solution)/shard_map/all_to_all | solution.py:49
  30.9 2.6 %fusion.204 = (f32[4,8,64]{2,1,0:T(8,128)S(1)}, f32[4,8,64,64]{2,3,1,0:T(8,128)}) fusion(bf16[8,256]{1,0:T(8,128)(2,1)S(1)} %copy-done.78, bf16[4,64,256]{2,1,0:T(8,128)(2,1)S(1)} %slice.355, bf16[4,64,768]{2,1,0:T(8,128)(2,1)} %copy-done.21), kind=kOutput, calls=%fused_computation.335 | convolution fusion | flops 68026432 | bytes 798720 | tf_op jit(solution)/shard_map/jvp()/sub | solution.py:127
  42.7 4.0 %all-to-all-start.1 = ((bf16[8,8,4,256]{3,1,2,0:T(8,128)(2,1)}), bf16[8,8,4,256]{3,1,2,0:T(8,128)(2,1)}, u32[]{:S(2)}, u32[]{:S(2)}) async-start(bf16[8,8,4,256]{3,1,2,0:T(8,128)(2,1)} %bitcast.403), calls=%async_computation.1 | async-start | bytes 262144 | tf_op jit(solution)/shard_map/all_to_all | solution.py:166
  56.6 3.3 %fusion.208 = (f32[4,8,64]{2,1,0:T(8,128)}, f32[4,8,64,64]{2,3,1,0:T(8,128)}) fusion(bf16[4,64,256]{2,1,0:T(8,128)(2,1)} %slice.358, bf16[8,256]{1,0:T(8,128)(2,1)} %get-tuple-element.145, bf16[4,64,768]{2,1,0:T(8,128)(2,1)} %copy-done.23), kind=kOutput, calls=%fused_computation.337 | convolution fusion | flops 68026432 | bytes 798720 | tf_op jit(solution)/shard_map/jvp()/sub | solution.py:127
  60.6 2.1 %fusion.74 = (f32[4,8,64]{2,1,0:T(8,128)S(1)}, bf16[4,8,64,64]{2,3,1,0:T(8,128)(2,1)S(1)}, bf16[4,8,64,64]{2,3,1,0:T(8,128)(2,1)S(1)}) fusion(f32[4,8,64,64]{2,3,1,0:T(8,128)} %get-tuple-element.157, f32[4,8,64]{2,1,0:T(8,128)S(1)} %multiply_divide_fusion.1, f32[4,8,64]{2,1,0:T(8,128)} %get-tuple-element.156, bf16[4,64,768]{2,1,0:T(8,128)(2,1)S(1)} %copy-done.24, ...), kind=kOutput, calls=%fused_computation.83 | convolution fusion | flops 68548608 | bytes 1482752 | tf_op jit(solution)/shard_map/transpose(jvp(whqk,wkc->whqc))/dot_general | solution.py:128
  69.0 4.2 %all-to-all-start.4 = ((bf16[8,8,4,256]{3,1,2,0:T(8,128)(2,1)}), bf16[8,8,4,256]{3,1,2,0:T(8,128)(2,1)}, u32[]{:S(2)}, u32[]{:S(2)}) async-start(bf16[8,8,4,256]{3,1,2,0:T(8,128)(2,1)} %bitcast.402), calls=%async_computation.4 | async-start | bytes 262144 | tf_op jit(solution)/shard_map/all_to_all | solution.py:166
  92.0 2.7 %multiply_reduce_fusion.10 = (f32[1024]{0:T(1024)S(1)}, f32[1024]{0:T(1024)S(1)}, f32[1024]{0:T(1024)S(1)}, f32[1024]{0:T(1024)S(1)}, f32[1024]{0:T(1024)S(1)}, ...) fusion(f32[18,18,1024]{2,1,0:T(8,128)S(1)} %convert_element_typ, ...), kind=kLoop, calls=%fused_computation.132 | loop fusion | flops 14408704 | bytes 11083776 | tf_op jit(solution)/shard_map/transpose(jvp())/reduce_sum | solution.py:143
  104.4 3.9 %all-to-all-start.5 = ((bf16[8,16,1024]{2,1,0:T(8,128)(2,1)}), bf16[8,16,1024]{2,1,0:T(8,128)(2,1)S(1)}, u32[]{:S(2)}, u32[]{:S(2)}) async-start(bf16[8,16,1024]{2,1,0:T(8,128)(2,1)} %select_select_fusion), calls=%async_computation.5 | async-start | bytes 524288 | tf_op jit(solution)/shard_map/all_to_all | solution.py:49
  108.4 2.0 fusion.40
  112.1 2.0 fusion.39
  115.3 4.0 %all-to-all-start.2 = ((bf16[8,8,4,256]{3,1,2,0:T(8,128)(2,1)}), bf16[8,8,4,256]{3,1,2,0:T(8,128)(2,1)}, u32[]{:S(2)}, u32[]{:S(2)}) async-start(bf16[8,8,4,256]{3,1,2,0:T(8,128)(2,1)} %bitcast.401), calls=%async_computation.2 | async-start | bytes 262144 | tf_op jit(solution)/shard_map/all_to_all | solution.py:166
  122.4 2.7 %fusion.81 = bf16[16,16,1024]{2,1,0:T(8,128)(2,1)S(1)} fusion(f32[16,16,1024]{2,1,0:T(8,128)} %get-tuple-element.149, f32[18,18,1024]{2,1,0:T(8,128)S(1)} %scatter.4, f32[16,16,1024]{2,1,0:T(8,128)S(1)} %get-tuple-element.92, f32[1024]{0:T(1024)S(1)} %bitcast.443, f32[1024]{0:T(1024)S(1)} %bitcast.446, f32[1024]{0:T(1024)S(1)} %bitcast.425, ...), kind=kLoop, calls=%fused_computation.90 | loop fusion | flops 10223616 | bytes 11046912 | tf_op jit(solution)/shard_map/transpose(jvp())/add_any | solution.py:278
  127.3 4.2 %all-to-all-start.7 = ((bf16[4,8,8,1152]{3,2,0,1:T(8,128)(2,1)}), bf16[4,8,8,1152]{3,2,0,1:T(8,128)(2,1)S(1)}, u32[]{:S(2)}, u32[]{:S(2)}) async-start(bf16[4,8,8,1152]{3,2,0,1:T(8,128)(2,1)} %copy.184), calls=%async_computation.7 | async-start | bytes 1179648 | tf_op jit(solution)/shard_map/all_to_all | solution.py:191
  136.2 2.7 %copy.202 = bf16[4,8,8,3200]{3,2,0,1:T(8,128)(2,1)} copy(bf16[4,8,8,3200]{3,2,1,0:T(8,128)(2,1)} %constant_dynamic-update-slice_fusion) | data formatting | bytes 3276800 | tf_op jit(solution)/shard_map/concatenate | solution.py:198
  139.0 3.1 %all-to-all-done.7 = bf16[4,8,8,1152]{3,2,0,1:T(8,128)(2,1)S(1)} async-done(((bf16[4,8,8,1152]{3,2,0,1:T(8,128)(2,1)}), bf16[4,8,8,1152]{3,2,0,1:T(8,128)(2,1)S(1)}, u32[]{:S(2)}, u32[]{:S(2)}) %all-to-all-start.7) | async-done | bytes 589856 | tf_op jit(solution)/shard_map/all_to_all | solution.py:191
  142.0 3.6 %all-to-all-start.6 = ((bf16[4,8,8,3200]{3,2,0,1:T(8,128)(2,1)}), bf16[4,8,8,3200]{3,2,0,1:T(8,128)(2,1)S(1)}, u32[]{:S(2)}, u32[]{:S(2)}) async-start(bf16[4,8,8,3200]{3,2,0,1:T(8,128)(2,1)} %copy.202), calls=%async_computation.6 | async-start | bytes 3276800 | tf_op jit(solution)/shard_map/all_to_all | solution.py:191
  149.9 17.4 %all-to-all-done.6 = bf16[4,8,8,3200]{3,2,0,1:T(8,128)(2,1)S(1)} async-done(((bf16[4,8,8,3200]{3,2,0,1:T(8,128)(2,1)}), bf16[4,8,8,3200]{3,2,0,1:T(8,128)(2,1)S(1)}, u32[]{:S(2)}, u32[]{:S(2)}) %all-to-all-start.6) | async-done | bytes 1638432 | tf_op jit(solution)/shard_map/all_to_all | solution.py:191
  168.3 4.9 %all-to-all-start.8 = ((bf16[4,8,4352]{2,1,0:T(8,128)(2,1)}), bf16[4,8,4352]{2,1,0:T(8,128)(2,1)S(1)}, u32[]{:S(2)}, u32[]{:S(2)}) async-start(bf16[4,8,4352]{2,1,0:T(8,128)(2,1)} %pad_maximum_fusion.2), calls=%async_computation.8 | async-start | bytes 557056 | tf_op jit(solution)/shard_map/all_to_all | solution.py:191
  173.2 6.8 %all-to-all-done.8 = bf16[4,8,4352]{2,1,0:T(8,128)(2,1)S(1)} async-done(((bf16[4,8,4352]{2,1,0:T(8,128)(2,1)}), bf16[4,8,4352]{2,1,0:T(8,128)(2,1)S(1)}, u32[]{:S(2)}, u32[]{:S(2)}) %all-to-all-start.8) | async-done | bytes 278560 | tf_op jit(solution)/shard_map/all_to_all | solution.py:191
  180.9 4.4 %all-to-all-start.9 = ((bf16[8,8,4352]{2,1,0:T(8,128)(2,1)}), bf16[8,8,4352]{2,1,0:T(8,128)(2,1)S(1)}, u32[]{:S(2)}, u32[]{:S(2)}) async-start(bf16[8,8,4352]{2,1,0:T(8,128)(2,1)} %broadcast_in_dim.361), calls=%async_computation.9 | async-start | bytes 1114112 | tf_op jit(solution)/shard_map/all_to_all | solution.py:211
  186.5 8.9 %all-to-all-done.9 = bf16[8,8,4352]{2,1,0:T(8,128)(2,1)S(1)} async-done(((bf16[8,8,4352]{2,1,0:T(8,128)(2,1)}), bf16[8,8,4352]{2,1,0:T(8,128)(2,1)S(1)}, u32[]{:S(2)}, u32[]{:S(2)}) %all-to-all-start.9) | async-done | bytes 557088 | tf_op jit(solution)/shard_map/all_to_all | solution.py:211
  (346 shorter events, 90.5 us)
Async XLA Ops:
  2.7 12.7 %all-to-all-start.3 = ((bf16[8,8,4,256]{3,1,2,0:T(8,128)(2,1)}), bf16[8,8,4,256]{3,1,2,0:T(8,128)(2,1)S(1)}, u32[]{:S(2)}, u32[]{:S(2)}) async-start(bf16[8,8,4,256]{3,1,2,0:T(8,128)(2,1)} %bitcast.62), calls=%async_computation.3 | async-start | bytes 262144 | tf_op jit(solution)/shard_map/all_to_all | solution.py:166
  13.8 13.6 %copy-start.40 = (f32[1024,1]{0,1:T(1,128)}, f32[1024,1]{0,1:T(1,128)S(1)}, u32[]{:S(2)}) copy-start(f32[1024,1]{0,1:T(1,128)S(1)} %get-tuple-element.135) | copy-start | bytes 12292
  13.8 13.6 %copy-start.42 = (f32[1024,1]{0,1:T(1,128)}, f32[1024,1]{0,1:T(1,128)S(1)}, u32[]{:S(2)}) copy-start(f32[1024,1]{0,1:T(1,128)S(1)} %get-tuple-element.136) | copy-start | bytes 12292
  13.8 13.6 %copy-start.44 = (f32[1024,1]{0,1:T(1,128)}, f32[1024,1]{0,1:T(1,128)S(1)}, u32[]{:S(2)}) copy-start(f32[1024,1]{0,1:T(1,128)S(1)} %get-tuple-element.137) | copy-start | bytes 12292
  13.8 13.6 %copy-start.46 = (f32[1024,1]{0,1:T(1,128)}, f32[1024,1]{0,1:T(1,128)S(1)}, u32[]{:S(2)}) copy-start(f32[1024,1]{0,1:T(1,128)S(1)} %get-tuple-element.138) | copy-start | bytes 12292
  13.8 13.6 %copy-start.48 = (f32[1024,1]{0,1:T(1,128)}, f32[1024,1]{0,1:T(1,128)S(1)}, u32[]{:S(2)}) copy-start(f32[1024,1]{0,1:T(1,128)S(1)} %get-tuple-element.139) | copy-start | bytes 12292
  13.8 13.6 %copy-start.51 = (f32[1024,1]{0,1:T(1,128)}, f32[1024,1]{0,1:T(1,128)S(1)}, u32[]{:S(2)}) copy-start(f32[1024,1]{0,1:T(1,128)S(1)} %get-tuple-element.140) | copy-start | bytes 12292
  13.8 13.6 %copy-start.54 = (f32[1024,1]{0,1:T(1,128)}, f32[1024,1]{0,1:T(1,128)S(1)}, u32[]{:S(2)}) copy-start(f32[1024,1]{0,1:T(1,128)S(1)} %get-tuple-element.141) | copy-start | bytes 12292
  15.4 11.1 %all-to-all-start = ((bf16[8,16,1024]{2,1,0:T(8,128)(2,1)}), bf16[8,16,1024]{2,1,0:T(8,128)(2,1)S(1)}, u32[]{:S(2)}, u32[]{:S(2)}) async-start(bf16[8,16,1024]{2,1,0:T(8,128)(2,1)} %select_select_fusion.1), calls=%async_computation | async-start | bytes 524288 | tf_op jit(solution)/shard_map/all_to_all | solution.py:49
  37.2 17.7 %copy-start.11 = (bf16[256,768]{1,0:T(8,128)(2,1)S(1)}, bf16[256,768]{1,0:T(8,128)(2,1)}, u32[]{:S(2)}) copy-start(bf16[256,768]{1,0:T(8,128)(2,1)} %param.24) | copy-start | bytes 1179652
  38.4 46.0 %copy-start.1 = (f32[16,16,256]{2,1,0:T(8,128)}, f32[16,16,256]{2,1,0:T(8,128)S(1)}, u32[]{:S(2)}) copy-start(f32[16,16,256]{2,1,0:T(8,128)S(1)} %get-tuple-element.155) | copy-start | bytes 786436
  42.7 9.5 %all-to-all-start.1 = ((bf16[8,8,4,256]{3,1,2,0:T(8,128)(2,1)}), bf16[8,8,4,256]{3,1,2,0:T(8,128)(2,1)}, u32[]{:S(2)}, u32[]{:S(2)}) async-start(bf16[8,8,4,256]{3,1,2,0:T(8,128)(2,1)} %bitcast.403), calls=%async_computation.1 | async-start | bytes 262144 | tf_op jit(solution)/shard_map/all_to_all | solution.py:166
  69.0 10.6 %all-to-all-start.4 = ((bf16[8,8,4,256]{3,1,2,0:T(8,128)(2,1)}), bf16[8,8,4,256]{3,1,2,0:T(8,128)(2,1)}, u32[]{:S(2)}, u32[]{:S(2)}) async-start(bf16[8,8,4,256]{3,1,2,0:T(8,128)(2,1)} %bitcast.402), calls=%async_computation.4 | async-start | bytes 262144 | tf_op jit(solution)/shard_map/all_to_all | solution.py:166
  94.9 24.7 %copy-start.8 = (bf16[16,16,1024]{2,1,0:T(8,128)(2,1)}, bf16[16,16,1024]{2,1,0:T(8,128)(2,1)S(1)}, u32[]{:S(2)}) copy-start(bf16[16,16,1024]{2,1,0:T(8,128)(2,1)S(1)} %convert_element_type.358) | copy-start | bytes 1572868
  94.9 15.5 %copy-start.27 = (bf16[16,16,256]{2,1,0:T(8,128)(2,1)S(1)}, bf16[16,16,256]{2,1,0:T(8,128)(2,1)}, u32[]{:S(2)}) copy-start(bf16[16,16,256]{2,1,0:T(8,128)(2,1)} %get-tuple-element.90) | copy-start | bytes 393220
  96.2 15.9 %copy-start.5 = (bf16[4,64,768]{2,1,0:T(8,128)(2,1)S(1)}, bf16[4,64,768]{2,1,0:T(8,128)(2,1)}, u32[]{:S(2)}) copy-start(bf16[4,64,768]{2,1,0:T(8,128)(2,1)} %copy-done.4) | copy-start | bytes 1179652
  104.4 10.9 %all-to-all-start.5 = ((bf16[8,16,1024]{2,1,0:T(8,128)(2,1)}), bf16[8,16,1024]{2,1,0:T(8,128)(2,1)S(1)}, u32[]{:S(2)}, u32[]{:S(2)}) async-start(bf16[8,16,1024]{2,1,0:T(8,128)(2,1)} %select_select_fusion), calls=%async_computation.5 | async-start | bytes 524288 | tf_op jit(solution)/shard_map/all_to_all | solution.py:49
  115.3 12.0 %all-to-all-start.2 = ((bf16[8,8,4,256]{3,1,2,0:T(8,128)(2,1)}), bf16[8,8,4,256]{3,1,2,0:T(8,128)(2,1)}, u32[]{:S(2)}, u32[]{:S(2)}) async-start(bf16[8,8,4,256]{3,1,2,0:T(8,128)(2,1)} %bitcast.401), calls=%async_computation.2 | async-start | bytes 262144 | tf_op jit(solution)/shard_map/all_to_all | solution.py:166
  127.3 14.7 %all-to-all-start.7 = ((bf16[4,8,8,1152]{3,2,0,1:T(8,128)(2,1)}), bf16[4,8,8,1152]{3,2,0,1:T(8,128)(2,1)S(1)}, u32[]{:S(2)}, u32[]{:S(2)}) async-start(bf16[4,8,8,1152]{3,2,0,1:T(8,128)(2,1)} %copy.184), calls=%async_computation.7 | async-start | bytes 1179648 | tf_op jit(solution)/shard_map/all_to_all | solution.py:191
  142.0 25.3 %all-to-all-start.6 = ((bf16[4,8,8,3200]{3,2,0,1:T(8,128)(2,1)}), bf16[4,8,8,3200]{3,2,0,1:T(8,128)(2,1)S(1)}, u32[]{:S(2)}, u32[]{:S(2)}) async-start(bf16[4,8,8,3200]{3,2,0,1:T(8,128)(2,1)} %copy.202), calls=%async_computation.6 | async-start | bytes 3276800 | tf_op jit(solution)/shard_map/all_to_all | solution.py:191
  149.9 17.6 %copy-start.34 = (bf16[4,8,1152]{2,1,0:T(8,128)(2,1)S(1)}, bf16[4,8,1152]{2,1,0:T(8,128)(2,1)}, u32[]{:S(2)}) copy-start(bf16[4,8,1152]{2,1,0:T(8,128)(2,1)} %reduce.6) | copy-start | bytes 221188
  167.5 18.1 %copy-start.10 = (f32[16,16,256]{2,1,0:T(8,128)S(1)}, f32[16,16,256]{2,1,0:T(8,128)}, u32[]{:S(2)}) copy-start(f32[16,16,256]{2,1,0:T(8,128)} %copy-done.9) | copy-start | bytes 786436
  168.3 11.8 %all-to-all-start.8 = ((bf16[4,8,4352]{2,1,0:T(8,128)(2,1)}), bf16[4,8,4352]{2,1,0:T(8,128)(2,1)S(1)}, u32[]{:S(2)}, u32[]{:S(2)}) async-start(bf16[4,8,4352]{2,1,0:T(8,128)(2,1)} %pad_maximum_fusion.2), calls=%async_computation.8 | async-start | bytes 557056 | tf_op jit(solution)/shard_map/all_to_all | solution.py:191
  180.9 14.5 %all-to-all-start.9 = ((bf16[8,8,4352]{2,1,0:T(8,128)(2,1)}), bf16[8,8,4352]{2,1,0:T(8,128)(2,1)S(1)}, u32[]{:S(2)}, u32[]{:S(2)}) async-start(bf16[8,8,4352]{2,1,0:T(8,128)(2,1)} %broadcast_in_dim.361), calls=%async_computation.9 | async-start | bytes 1114112 | tf_op jit(solution)/shard_map/all_to_all | solution.py:211
  (71 other events, 238.6 us)

commit v13 on v11

--- a/solution.py
+++ b/solution.py
@@ -331,7 +331,8 @@
     d_stream_two = d_stream_two + d_stream_extra
     d_stream_one, d_gain_block, tap_block_in, tap_block_out = block_back(d_stream_two)
     d_conv, d_wide_tail, tap_project = tail_back(d_stream_one)
-    d_conv_ext = extended_2(d_conv, (("sy", 0), ("sx", 1)), 1)
+    d_conv_ext = extended_2(d_conv.astype(jnp.bfloat16), (("sy", 0), ("sx", 1)), 1)
+    d_conv_ext = d_conv_ext.astype(jnp.float32).at[1:-1, 1:-1].set(d_conv)
     d_kernel = kernel_back(d_conv)[0]
     d_inner = depthwise_back(d_conv_ext, dw_kernel).astype(jnp.bfloat16)
     d_normed, tap_expand = expand_back(d_inner)

time: 183 us -> 195 us (1.066)
  local copies, waits for them, and re-layouts: 29.1 us -> 42.9 us
  waiting for transfers between devices: 58.9 us -> 48.8 us
  matrix products: 23.8 us -> 28.2 us
  other arithmetic: 25.6 us -> 27.8 us
    dot_general x6, matrix products: 1.93 us -> 8.53 us  [outer_sum(): lax.dot_general(left_flat, right_flat, (((0,), (0,)), ((), ())), preferre...]
    all_to_all x2, waiting for transfers between devices: 14.1 us -> 9.27 us  [extended_2(): lax.all_to_all(outgoing, ('sy', 'sx'), split_axis=0, concat_axis=0, tiled...]
    all_to_all x3, waiting for transfers between devices: 29.7 us -> 26.5 us  [exchange_sum(): lax.all_to_all(values.astype(jnp.bfloat16), axes, split_axis=axis, concat...]
    pad x8, local copies, waits for them, and re-layouts: 0.06 us -> 2.77 us  [lay(): return jnp.pad(line, ((0, span - line.shape[0]), (0, 0)))]
    concatenate x3, local copies, waits for them, and re-layouts: 1.44 us -> 3.88 us  [tile_sum(): packed = jnp.concatenate(wide, axis=1)]
    all_to_all x4, waiting for transfers between devices: 6.24 us -> 4.14 us  [swap_blocks(): lax.all_to_all(as_sent(flattened), ('sy', 'sx'), split_axis=0, concat_axi...]
  transfers between devices with their start and end apart: 10 -> 10, of which waited for: 8 -> 7; matrix products, arithmetic and copies ran while one was open for 21% -> 26% of each run, Pallas kernels for 0% -> 0%
where the time goes in v13:
time: 195 us; the launch traced here: 192 us
  waiting for transfers between devices  48.8 us (25%)
  local copies, waits for them, and re-layouts  42.9 us (22%)
  starting transfers between devices  42.1 us (22%)
  matrix products  28.2 us (14%)
  other arithmetic  27.8 us (14%)
  between operations  2.73 us (1%)
    all_to_all x3, waiting for transfers between devices, exchange_sum(): lax.all_to_all(values.astype(jnp.bfloat16), axes, split_axis=axis, concat...  26.5 us
    all_to_all x4, starting transfers between devices, swap_blocks(): lax.all_to_all(as_sent(flattened), ('sy', 'sx'), split_axis=0, concat_axi...  16.7 us
    all_to_all x3, starting transfers between devices, exchange_sum(): lax.all_to_all(values.astype(jnp.bfloat16), axes, split_axis=axis, concat...  12.7 us
    all_to_all x2, waiting for transfers between devices, extended_2(): lax.all_to_all(outgoing, ('sy', 'sx'), split_axis=0, concat_axis=0, tiled...  9.27 us
    all_to_all x1, waiting for transfers between devices, reduce_packed(): lax.all_to_all(spread, ('sy', 'sx'), split_axis=0, concat_axis=0, tiled=T...  8.89 us
    dot_general x6, matrix products, outer_sum(): lax.dot_general(left_flat, right_flat, (((0,), (0,)), ((), ())), preferre...  8.53 us
    all_to_all x2, starting transfers between devices, extended_2(): lax.all_to_all(outgoing, ('sy', 'sx'), split_axis=0, concat_axis=0, tiled...  8.31 us
    dot_general x12, matrix products, project_rows(): product = jnp.dot(flattened, weight, preferred_element_type=jnp.float32)  7.35 us
  transfers between devices with their start and end apart: 10, of which 7 were waited for; matrix products, arithmetic and copies ran while one was open for 26% of the time, Pallas kernels for 0%

profile of v13, /device:TPU:0, one launch (start us, length us, event | category | flops | bytes accessed | tf_op | source)
XLA Modules:
  0.0 192.4 jit_solution(6171052225630153368)
XLA Ops:
  2.7 5.2 %all-to-all-start.3 = ((bf16[8,8,4,256]{3,1,2,0:T(8,128)(2,1)}), bf16[8,8,4,256]{3,1,2,0:T(8,128)(2,1)S(1)}, u32[]{:S(2)}, u32[]{:S(2)}) async-start(bf16[8,8,4,256]{3,1,2,0:T(8,128)(2,1)} %bitcast.62), calls=%async_computation.3 | async-start | bytes 262144 | tf_op jit(solution)/shard_map/all_to_all | solution.py:166
  10.0 2.4 %multiply_convert_fusion.1 = (bf16[16,16,1024]{2,1,0:T(8,128)(2,1)S(1)}, f32[16,16,1024]{2,1,0:T(8,128)}) fusion(bf16[256,1024]{1,0:T(8,128)(2,1)S(1)} %copy-done, bf16[1,16,16,256]{3,2,1,0:T(8,128)(2,1)} %param.14, f32[256]{0:T(256)} %param.16, f32[16,16]{1,0:T(8,128)S(1)} %fusion.186, f32[16,16]{1,0:T(8,128)S(1)} %broadcast_multiply_fusion.2), kind=kOutput, calls=%fused_computation.146 | convolution fusion | flops 136904704 | bytes 2231296 | tf_op jit(solution)/shard_map/jvp()/dot_general | solution.py:78
  15.0 4.2 %all-to-all-start = ((bf16[8,16,1024]{2,1,0:T(8,128)(2,1)}), bf16[8,16,1024]{2,1,0:T(8,128)(2,1)S(1)}, u32[]{:S(2)}, u32[]{:S(2)}) async-start(bf16[8,16,1024]{2,1,0:T(8,128)(2,1)} %select_select_fusion.1), calls=%async_computation | async-start | bytes 524288 | tf_op jit(solution)/shard_map/all_to_all | solution.py:49
  20.3 5.9 %all-to-all-done = bf16[8,16,1024]{2,1,0:T(8,128)(2,1)S(1)} async-done(((bf16[8,16,1024]{2,1,0:T(8,128)(2,1)}), bf16[8,16,1024]{2,1,0:T(8,128)(2,1)S(1)}, u32[]{:S(2)}, u32[]{:S(2)}) %all-to-all-start) | async-done | bytes 262176 | tf_op jit(solution)/shard_map/all_to_all | solution.py:49
  37.2 3.4 %all-to-all-start.1 = ((bf16[8,8,4,256]{3,1,2,0:T(8,128)(2,1)}), bf16[8,8,4,256]{3,1,2,0:T(8,128)(2,1)S(1)}, u32[]{:S(2)}, u32[]{:S(2)}) async-start(bf16[8,8,4,256]{3,1,2,0:T(8,128)(2,1)} %bitcast.381), calls=%async_computation.1 | async-start | bytes 262144 | tf_op jit(solution)/shard_map/all_to_all | solution.py:166
  42.0 4.1 %all-to-all-done.1 = bf16[8,8,4,256]{3,1,2,0:T(8,128)(2,1)S(1)} async-done(((bf16[8,8,4,256]{3,1,2,0:T(8,128)(2,1)}), bf16[8,8,4,256]{3,1,2,0:T(8,128)(2,1)S(1)}, u32[]{:S(2)}, u32[]{:S(2)}) %all-to-all-start.1) | async-done | bytes 131104 | tf_op jit(solution)/shard_map/all_to_all | solution.py:166
  49.2 3.2 %fusion.205 = (f32[4,8,64]{2,1,0:T(8,128)}, f32[4,8,64,64]{2,3,1,0:T(8,128)}) fusion(bf16[4,64,256]{2,1,0:T(8,128)(2,1)S(1)} %slice.358, bf16[8,256]{1,0:T(8,128)(2,1)} %copy-done.94, bf16[4,64,768]{2,1,0:T(8,128)(2,1)} %copy-done.31), kind=kOutput, calls=%fused_computation.333 | convolution fusion | flops 68026432 | bytes 798720 | tf_op jit(solution)/shard_map/jvp()/sub | solution.py:127
  53.2 2.1 %fusion.74 = (f32[4,8,64]{2,1,0:T(8,128)S(1)}, bf16[4,8,64,64]{2,3,1,0:T(8,128)(2,1)S(1)}, bf16[4,8,64,64]{2,3,1,0:T(8,128)(2,1)S(1)}) fusion(f32[4,8,64,64]{2,3,1,0:T(8,128)} %get-tuple-element.157, f32[4,8,64]{2,1,0:T(8,128)S(1)} %multiply_divide_fusion.1, f32[4,8,64]{2,1,0:T(8,128)} %get-tuple-element.156, bf16[4,64,768]{2,1,0:T(8,128)(2,1)S(1)} %copy-done.32, ...), kind=kOutput, calls=%fused_computation.84 | convolution fusion | flops 68548608 | bytes 1482752 | tf_op jit(solution)/shard_map/transpose(jvp(whqk,wkc->whqc))/dot_general | solution.py:128
  60.1 4.0 %all-to-all-start.4 = ((bf16[8,8,4,256]{3,1,2,0:T(8,128)(2,1)}), bf16[8,8,4,256]{3,1,2,0:T(8,128)(2,1)}, u32[]{:S(2)}, u32[]{:S(2)}) async-start(bf16[8,8,4,256]{3,1,2,0:T(8,128)(2,1)} %bitcast.77), calls=%async_computation.4 | async-start | bytes 262144 | tf_op jit(solution)/shard_map/all_to_all | solution.py:166
  69.7 4.2 %all-to-all-start.2 = ((bf16[8,8,4,256]{3,1,2,0:T(8,128)(2,1)}), bf16[8,8,4,256]{3,1,2,0:T(8,128)(2,1)}, u32[]{:S(2)}, u32[]{:S(2)}) async-start(bf16[8,8,4,256]{3,1,2,0:T(8,128)(2,1)} %bitcast.54), calls=%async_computation.2 | async-start | bytes 262144 | tf_op jit(solution)/shard_map/all_to_all | solution.py:166
  85.5 3.3 %multiply_reduce_fusion.10 = (f32[1024]{0:T(1024)S(1)}, f32[1024]{0:T(1024)S(1)}, f32[1024]{0:T(1024)S(1)}, f32[1024]{0:T(1024)S(1)}, f32[1024]{0:T(1024)}, /*in...) fusion(f32[18,18,1024]{2,1,0:T(8,128)S(1)} %convert_element_type.307, ...), kind=kLoop, calls=%fused_computation.133 | loop fusion | flops 14408704 | bytes 11083776 | tf_op jit(solution)/shard_map/transpose(jvp())/reduce_sum | solution.py:143
  99.9 2.4 %copy.169 = bf16[4,8,8,2176]{3,2,0,1:T(8,128)(2,1)} copy(bf16[4,8,8,2176]{3,2,1,0:T(8,128)(2,1)} %bitcast.369) | data formatting | bytes 2228224 | tf_op jit(solution)/shard_map/convert_element_type | solution.py:191
  108.8 4.1 %all-to-all-start.5 = ((bf16[8,16,1024]{2,1,0:T(8,128)(2,1)}), bf16[8,16,1024]{2,1,0:T(8,128)(2,1)S(1)}, u32[]{:S(2)}, u32[]{:S(2)}) async-start(bf16[8,16,1024]{2,1,0:T(8,128)(2,1)} %select_select_fusion), calls=%async_computation.5 | async-start | bytes 524288 | tf_op jit(solution)/shard_map/all_to_all | solution.py:49
  114.3 2.2 %concatenate.61 = bf16[4,8,8,1024]{3,2,1,0:T(8,128)(2,1)} reshape(bf16[1024,256]{1,0:T(8,128)(2,1)} %fusion.36) | data formatting | bytes 1048576 | tf_op jit(solution)/shard_map/concatenate | solution.py:198
  116.5 3.4 %all-to-all-done.5 = bf16[8,16,1024]{2,1,0:T(8,128)(2,1)S(1)} async-done(((bf16[8,16,1024]{2,1,0:T(8,128)(2,1)}), bf16[8,16,1024]{2,1,0:T(8,128)(2,1)S(1)}, u32[]{:S(2)}, u32[]{:S(2)}) %all-to-all-start.5) | async-done | bytes 262176 | tf_op jit(solution)/shard_map/all_to_all | solution.py:49
  119.8 4.3 %all-to-all-start.6 = ((bf16[4,8,8,2176]{3,2,0,1:T(8,128)(2,1)}), bf16[4,8,8,2176]{3,2,0,1:T(8,128)(2,1)}, u32[]{:S(2)}, u32[]{:S(2)}) async-start(bf16[4,8,8,2176]{3,2,0,1:T(8,128)(2,1)} %copy.169), calls=%async_computation.6 | async-start | bytes 2228224 | tf_op jit(solution)/shard_map/all_to_all | solution.py:191
  127.2 2.7 %fusion.81 = bf16[16,16,1024]{2,1,0:T(8,128)(2,1)S(1)} fusion(f32[16,16,1024]{2,1,0:T(8,128)} %get-tuple-element.149, f32[18,18,1024]{2,1,0:T(8,128)S(1)} %scatter.4, f32[16,16,1024]{2,1,0:T(8,128)S(1)} %get-tuple-element.92, f32[1024]{0:T(1024)S(1)} %bitcast.420, f32[1024]{0:T(1024)S(1)} %bitcast.423, f32[1024]{0:T(1024)S(1)} %bitcast.402, ...), kind=kLoop, calls=%fused_computation.91 | loop fusion | flops 10223616 | bytes 11046912 | tf_op jit(solution)/shard_map/transpose(jvp())/add_any | solution.py:278
  134.1 6.1 %all-to-all-done.6 = bf16[4,8,8,2176]{3,2,0,1:T(8,128)(2,1)} async-done(((bf16[4,8,8,2176]{3,2,0,1:T(8,128)(2,1)}), bf16[4,8,8,2176]{3,2,0,1:T(8,128)(2,1)}, u32[]{:S(2)}, u32[]{:S(2)}) %all-to-all-start.6) | async-done | bytes 1114144 | tf_op jit(solution)/shard_map/all_to_all | solution.py:191
  140.2 3.6 %all-to-all-start.7 = ((bf16[4,8,8,2176]{3,2,0,1:T(8,128)(2,1)}), bf16[4,8,8,2176]{3,2,0,1:T(8,128)(2,1)S(1)}, u32[]{:S(2)}, u32[]{:S(2)}) async-start(bf16[4,8,8,2176]{3,2,0,1:T(8,128)(2,1)} %copy.174), calls=%async_computation.7 | async-start | bytes 2228224 | tf_op jit(solution)/shard_map/all_to_all | solution.py:191
  146.3 13.6 %all-to-all-done.7 = bf16[4,8,8,2176]{3,2,0,1:T(8,128)(2,1)S(1)} async-done(((bf16[4,8,8,2176]{3,2,0,1:T(8,128)(2,1)}), bf16[4,8,8,2176]{3,2,0,1:T(8,128)(2,1)S(1)}, u32[]{:S(2)}, u32[]{:S(2)}) %all-to-all-start.7) | async-done | bytes 1114144 | tf_op jit(solution)/shard_map/all_to_all | solution.py:191
  160.7 4.9 %all-to-all-start.8 = ((bf16[4,8,4352]{2,1,0:T(8,128)(2,1)}), bf16[4,8,4352]{2,1,0:T(8,128)(2,1)S(1)}, u32[]{:S(2)}, u32[]{:S(2)}) async-start(bf16[4,8,4352]{2,1,0:T(8,128)(2,1)} %pad_maximum_fusion.2), calls=%async_computation.8 | async-start | bytes 557056 | tf_op jit(solution)/shard_map/all_to_all | solution.py:191
  165.7 6.8 %all-to-all-done.8 = bf16[4,8,4352]{2,1,0:T(8,128)(2,1)S(1)} async-done(((bf16[4,8,4352]{2,1,0:T(8,128)(2,1)}), bf16[4,8,4352]{2,1,0:T(8,128)(2,1)S(1)}, u32[]{:S(2)}, u32[]{:S(2)}) %all-to-all-start.8) | async-done | bytes 278560 | tf_op jit(solution)/shard_map/all_to_all | solution.py:191
  173.4 4.4 %all-to-all-start.9 = ((bf16[8,8,4352]{2,1,0:T(8,128)(2,1)}), bf16[8,8,4352]{2,1,0:T(8,128)(2,1)S(1)}, u32[]{:S(2)}, u32[]{:S(2)}) async-start(bf16[8,8,4352]{2,1,0:T(8,128)(2,1)} %broadcast_in_dim.361), calls=%async_computation.9 | async-start | bytes 1114112 | tf_op jit(solution)/shard_map/all_to_all | solution.py:211
  179.0 8.9 %all-to-all-done.9 = bf16[8,8,4352]{2,1,0:T(8,128)(2,1)S(1)} async-done(((bf16[8,8,4352]{2,1,0:T(8,128)(2,1)}), bf16[8,8,4352]{2,1,0:T(8,128)(2,1)S(1)}, u32[]{:S(2)}, u32[]{:S(2)}) %all-to-all-start.9) | async-done | bytes 557088 | tf_op jit(solution)/shard_map/all_to_all | solution.py:211
  (372 shorter events, 80.4 us)
Async XLA Ops:
  2.7 12.2 %all-to-all-start.3 = ((bf16[8,8,4,256]{3,1,2,0:T(8,128)(2,1)}), bf16[8,8,4,256]{3,1,2,0:T(8,128)(2,1)S(1)}, u32[]{:S(2)}, u32[]{:S(2)}) async-start(bf16[8,8,4,256]{3,1,2,0:T(8,128)(2,1)} %bitcast.62), calls=%async_computation.3 | async-start | bytes 262144 | tf_op jit(solution)/shard_map/all_to_all | solution.py:166
  13.2 13.8 %copy-start.47 = (f32[1024,1]{0,1:T(1,128)}, f32[1024,1]{0,1:T(1,128)S(1)}, u32[]{:S(2)}) copy-start(f32[1024,1]{0,1:T(1,128)S(1)} %get-tuple-element.135) | copy-start | bytes 12292
  13.2 13.8 %copy-start.50 = (f32[1024,1]{0,1:T(1,128)}, f32[1024,1]{0,1:T(1,128)S(1)}, u32[]{:S(2)}) copy-start(f32[1024,1]{0,1:T(1,128)S(1)} %get-tuple-element.136) | copy-start | bytes 12292
  13.2 13.8 %copy-start.53 = (f32[1024,1]{0,1:T(1,128)}, f32[1024,1]{0,1:T(1,128)S(1)}, u32[]{:S(2)}) copy-start(f32[1024,1]{0,1:T(1,128)S(1)} %get-tuple-element.137) | copy-start | bytes 12292
  13.2 13.8 %copy-start.56 = (f32[1024,1]{0,1:T(1,128)}, f32[1024,1]{0,1:T(1,128)S(1)}, u32[]{:S(2)}) copy-start(f32[1024,1]{0,1:T(1,128)S(1)} %get-tuple-element.138) | copy-start | bytes 12292
  13.2 13.8 %copy-start.59 = (f32[1024,1]{0,1:T(1,128)}, f32[1024,1]{0,1:T(1,128)S(1)}, u32[]{:S(2)}) copy-start(f32[1024,1]{0,1:T(1,128)S(1)} %get-tuple-element.139) | copy-start | bytes 12292
  13.2 13.8 %copy-start.62 = (f32[1024,1]{0,1:T(1,128)}, f32[1024,1]{0,1:T(1,128)S(1)}, u32[]{:S(2)}) copy-start(f32[1024,1]{0,1:T(1,128)S(1)} %get-tuple-element.140) | copy-start | bytes 12292
  13.2 13.8 %copy-start.65 = (f32[1024,1]{0,1:T(1,128)}, f32[1024,1]{0,1:T(1,128)S(1)}, u32[]{:S(2)}) copy-start(f32[1024,1]{0,1:T(1,128)S(1)} %get-tuple-element.141) | copy-start | bytes 12292
  14.9 15.0 %copy-start.94 = (bf16[8,256]{1,0:T(8,128)(2,1)}, bf16[8,256]{1,0:T(8,128)(2,1)S(1)}, u32[]{:S(2)}) copy-start(bf16[8,256]{1,0:T(8,128)(2,1)S(1)} %get-tuple-element.145) | copy-start | bytes 12292
  14.9 18.1 %copy-start.83 = (f32[8,256]{1,0:T(8,128)}, f32[8,256]{1,0:T(8,128)S(1)}, u32[]{:S(2)}) copy-start(f32[8,256]{1,0:T(8,128)S(1)} %get-tuple-element.144) | copy-start | bytes 24580
  15.0 11.1 %all-to-all-start = ((bf16[8,16,1024]{2,1,0:T(8,128)(2,1)}), bf16[8,16,1024]{2,1,0:T(8,128)(2,1)S(1)}, u32[]{:S(2)}, u32[]{:S(2)}) async-start(bf16[8,16,1024]{2,1,0:T(8,128)(2,1)} %select_select_fusion.1), calls=%async_computation | async-start | bytes 524288 | tf_op jit(solution)/shard_map/all_to_all | solution.py:49
  33.6 14.2 %copy-start.12 = (bf16[256,768]{1,0:T(8,128)(2,1)S(1)}, bf16[256,768]{1,0:T(8,128)(2,1)}, u32[]{:S(2)}) copy-start(bf16[256,768]{1,0:T(8,128)(2,1)} %param.24) | copy-start | bytes 1179652
  34.5 44.2 %copy-start.1 = (f32[16,16,256]{2,1,0:T(8,128)}, f32[16,16,256]{2,1,0:T(8,128)S(1)}, u32[]{:S(2)}) copy-start(f32[16,16,256]{2,1,0:T(8,128)S(1)} %get-tuple-element.155) | copy-start | bytes 786436
  37.2 8.8 %all-to-all-start.1 = ((bf16[8,8,4,256]{3,1,2,0:T(8,128)(2,1)}), bf16[8,8,4,256]{3,1,2,0:T(8,128)(2,1)S(1)}, u32[]{:S(2)}, u32[]{:S(2)}) async-start(bf16[8,8,4,256]{3,1,2,0:T(8,128)(2,1)} %bitcast.381), calls=%async_computation.1 | async-start | bytes 262144 | tf_op jit(solution)/shard_map/all_to_all | solution.py:166
  60.1 9.6 %all-to-all-start.4 = ((bf16[8,8,4,256]{3,1,2,0:T(8,128)(2,1)}), bf16[8,8,4,256]{3,1,2,0:T(8,128)(2,1)}, u32[]{:S(2)}, u32[]{:S(2)}) async-start(bf16[8,8,4,256]{3,1,2,0:T(8,128)(2,1)} %bitcast.77), calls=%async_computation.4 | async-start | bytes 262144 | tf_op jit(solution)/shard_map/all_to_all | solution.py:166
  69.7 24.6 %all-to-all-start.2 = ((bf16[8,8,4,256]{3,1,2,0:T(8,128)(2,1)}), bf16[8,8,4,256]{3,1,2,0:T(8,128)(2,1)}, u32[]{:S(2)}, u32[]{:S(2)}) async-start(bf16[8,8,4,256]{3,1,2,0:T(8,128)(2,1)} %bitcast.54), calls=%async_computation.2 | async-start | bytes 262144 | tf_op jit(solution)/shard_map/all_to_all | solution.py:166
  99.8 13.1 %copy-start.9 = (f32[16,16,256]{2,1,0:T(8,128)S(1)}, f32[16,16,256]{2,1,0:T(8,128)}, u32[]{:S(2)}) copy-start(f32[16,16,256]{2,1,0:T(8,128)} %copy-done.8) | copy-start | bytes 786436
  99.9 13.1 %copy-start.27 = (f32[16,16,1024]{2,1,0:T(8,128)S(1)}, f32[16,16,1024]{2,1,0:T(8,128)}, u32[]{:S(2)}) copy-start(f32[16,16,1024]{2,1,0:T(8,128)} %copy-done.26) | copy-start | bytes 3145732
  108.8 11.0 %all-to-all-start.5 = ((bf16[8,16,1024]{2,1,0:T(8,128)(2,1)}), bf16[8,16,1024]{2,1,0:T(8,128)(2,1)S(1)}, u32[]{:S(2)}, u32[]{:S(2)}) async-start(bf16[8,16,1024]{2,1,0:T(8,128)(2,1)} %select_select_fusion), calls=%async_computation.5 | async-start | bytes 524288 | tf_op jit(solution)/shard_map/all_to_all | solution.py:49
  119.8 20.4 %all-to-all-start.6 = ((bf16[4,8,8,2176]{3,2,0,1:T(8,128)(2,1)}), bf16[4,8,8,2176]{3,2,0,1:T(8,128)(2,1)}, u32[]{:S(2)}, u32[]{:S(2)}) async-start(bf16[4,8,8,2176]{3,2,0,1:T(8,128)(2,1)} %copy.169), calls=%async_computation.6 | async-start | bytes 2228224 | tf_op jit(solution)/shard_map/all_to_all | solution.py:191
  140.2 19.6 %all-to-all-start.7 = ((bf16[4,8,8,2176]{3,2,0,1:T(8,128)(2,1)}), bf16[4,8,8,2176]{3,2,0,1:T(8,128)(2,1)S(1)}, u32[]{:S(2)}, u32[]{:S(2)}) async-start(bf16[4,8,8,2176]{3,2,0,1:T(8,128)(2,1)} %copy.174), calls=%async_computation.7 | async-start | bytes 2228224 | tf_op jit(solution)/shard_map/all_to_all | solution.py:191
  160.0 18.1 %copy-start.10 = (f32[16,16,256]{2,1,0:T(8,128)S(1)}, f32[16,16,256]{2,1,0:T(8,128)}, u32[]{:S(2)}) copy-start(f32[16,16,256]{2,1,0:T(8,128)} %copy-done.8) | copy-start | bytes 786436
  160.7 11.8 %all-to-all-start.8 = ((bf16[4,8,4352]{2,1,0:T(8,128)(2,1)}), bf16[4,8,4352]{2,1,0:T(8,128)(2,1)S(1)}, u32[]{:S(2)}, u32[]{:S(2)}) async-start(bf16[4,8,4352]{2,1,0:T(8,128)(2,1)} %pad_maximum_fusion.2), calls=%async_computation.8 | async-start | bytes 557056 | tf_op jit(solution)/shard_map/all_to_all | solution.py:191
  173.4 14.5 %all-to-all-start.9 = ((bf16[8,8,4352]{2,1,0:T(8,128)(2,1)}), bf16[8,8,4352]{2,1,0:T(8,128)(2,1)S(1)}, u32[]{:S(2)}, u32[]{:S(2)}) async-start(bf16[8,8,4352]{2,1,0:T(8,128)(2,1)} %broadcast_in_dim.361), calls=%async_computation.9 | async-start | bytes 1114112 | tf_op jit(solution)/shard_map/all_to_all | solution.py:211
  (85 other events, 289.1 us)

commit v14 on v12

--- a/solution.py
+++ b/solution.py
@@ -204,7 +204,12 @@
 def reduce_packed(groups):
     tiles = lax.axis_size(("sy", "sx"))
     widths = [piece.shape[1] for wide in groups for piece in wide]
-    local = jnp.concatenate([tile_sum(wide) for wide in groups], axis=-1)
+    sums = []
+    for wide in groups:
+        if sums:
+            sums[-1], wide = lax.optimization_barrier((sums[-1], wide))
+        sums.append(tile_sum(wide))
+    local = jnp.concatenate(sums, axis=-1)
     parts, piece, width = local.shape
     local = exchange_sum(local, "rep", 0)
     spread = jnp.broadcast_to(local[None].astype(jnp.bfloat16), (tiles, piece, width))
@@ -331,8 +336,7 @@
     d_stream_two = d_stream_two + d_stream_extra
     d_stream_one, d_gain_block, tap_block_in, tap_block_out = block_back(d_stream_two)
     d_conv, d_wide_tail, tap_project = tail_back(d_stream_one)
-    d_conv_ext = extended_2(d_conv.astype(jnp.bfloat16), (("sy", 0), ("sx", 1)), 1)
-    d_conv_ext = d_conv_ext.astype(jnp.float32).at[1:-1, 1:-1].set(d_conv)
+    d_conv_ext = extended_2(d_conv, (("sy", 0), ("sx", 1)), 1)
     d_kernel = kernel_back(d_conv)[0]
     d_inner = depthwise_back(d_conv_ext, dw_kernel).astype(jnp.bfloat16)
     d_normed, tap_expand = expand_back(d_inner)

time: 202 us -> 188 us (0.931)
  local copies, waits for them, and re-layouts: 50 us -> 35.4 us
  waiting for transfers between devices: 45 us -> 52.4 us
  matrix products: 31.9 us -> 26.1 us
    all_to_all x3, waiting for transfers between devices: 27.2 us -> 32.2 us  [exchange_sum(): lax.all_to_all(values.astype(jnp.bfloat16), axes, split_axis=axis, concat...]
    dot_general x6, matrix products: 8.27 us -> 3.51 us  [outer_sum(): lax.dot_general(left_flat, right_flat, (((0,), (0,)), ((), ())), preferre...]
    another operation x2, local copies, waits for them, and re-layouts: 3.23 us -> 0.11 us  [to_home(): image.reshape(sy_count, height // sy_count, sx_count, breadth // sx_count...]
    pad x8, local copies, waits for them, and re-layouts: 2.8 us -> 0.06 us  [lay(): return jnp.pad(line, ((0, span - line.shape[0]), (0, 0)))]
    all_to_all x4, waiting for transfers between devices: 1.8 us -> 3.99 us  [swap_blocks(): lax.all_to_all(as_sent(flattened), ('sy', 'sx'), split_axis=0, concat_axi...]
    unnamed x176 -> x188, local copies, waits for them, and re-layouts: 7.06 us -> 7.95 us
  transfers between devices with their start and end apart: 10 -> 10, of which waited for: 7 -> 8; matrix products, arithmetic and copies ran while one was open for 22% -> 24% of each run, Pallas kernels for 0% -> 0%
where the time goes in v14:
time: 188 us; the launch traced here: 186 us
  waiting for transfers between devices  52.4 us (28%)
  starting transfers between devices  42.1 us (22%)
  local copies, waits for them, and re-layouts  35.4 us (19%)
  other arithmetic  27 us (14%)
  matrix products  26.1 us (14%)
  between operations  2.87 us (2%)
    all_to_all x3, waiting for transfers between devices, exchange_sum(): lax.all_to_all(values.astype(jnp.bfloat16), axes, split_axis=axis, concat...  32.2 us
    all_to_all x4, starting transfers between devices, swap_blocks(): lax.all_to_all(as_sent(flattened), ('sy', 'sx'), split_axis=0, concat_axi...  16.7 us
    all_to_all x3, starting transfers between devices, exchange_sum(): lax.all_to_all(values.astype(jnp.bfloat16), axes, split_axis=axis, concat...  12.9 us
    all_to_all x1, waiting for transfers between devices, reduce_packed(): lax.all_to_all(spread, ('sy', 'sx'), split_axis=0, concat_axis=0, tiled=T...  8.89 us
    all_to_all x2, starting transfers between devices, extended_2(): lax.all_to_all(outgoing, ('sy', 'sx'), split_axis=0, concat_axis=0, tiled...  8.13 us
    unnamed x188, local copies, waits for them, and re-layouts  7.95 us
    dot_general x12, matrix products, project_rows(): product = jnp.dot(flattened, weight, preferred_element_type=jnp.float32)  7.34 us
    all_to_all x2, waiting for transfers between devices, extended_2(): lax.all_to_all(outgoing, ('sy', 'sx'), split_axis=0, concat_axis=0, tiled...  7.34 us
  transfers between devices with their start and end apart: 10, of which 8 were waited for; matrix products, arithmetic and copies ran while one was open for 24% of the time, Pallas kernels for 0%

profile of v14, /device:TPU:0, one launch (start us, length us, event | category | flops | bytes accessed | tf_op | source)
XLA Modules:
  0.0 185.9 jit_solution(4804816720004958743)
XLA Ops:
  2.7 5.2 %all-to-all-start.3 = ((bf16[8,8,4,256]{3,1,2,0:T(8,128)(2,1)}), bf16[8,8,4,256]{3,1,2,0:T(8,128)(2,1)S(1)}, u32[]{:S(2)}, u32[]{:S(2)}) async-start(bf16[8,8,4,256]{3,1,2,0:T(8,128)(2,1)} %bitcast.60), calls=%async_computation.3 | async-start | bytes 262144 | tf_op jit(solution)/shard_map/all_to_all | solution.py:166
  10.0 2.4 %multiply_convert_fusion.1 = (bf16[16,16,1024]{2,1,0:T(8,128)(2,1)S(1)}, f32[16,16,1024]{2,1,0:T(8,128)}) fusion(bf16[256,1024]{1,0:T(8,128)(2,1)S(1)} %copy-done, bf16[1,16,16,256]{3,2,1,0:T(8,128)(2,1)} %param.12, f32[256]{0:T(256)} %param.14, f32[16,16]{1,0:T(8,128)S(1)} %fusion.192, f32[16,16]{1,0:T(8,128)S(1)} %broadcast_multiply_fusion.2), kind=kOutput, calls=%fused_computation.149 | convolution fusion | flops 136904704 | bytes 2231296 | tf_op jit(solution)/shard_map/jvp()/dot_general | solution.py:78
  15.4 4.2 %all-to-all-start = ((bf16[8,16,1024]{2,1,0:T(8,128)(2,1)}), bf16[8,16,1024]{2,1,0:T(8,128)(2,1)S(1)}, u32[]{:S(2)}, u32[]{:S(2)}) async-start(bf16[8,16,1024]{2,1,0:T(8,128)(2,1)} %select_select_fusion.1), calls=%async_computation | async-start | bytes 524288 | tf_op jit(solution)/shard_map/all_to_all | solution.py:49
  20.7 5.8 %all-to-all-done = bf16[8,16,1024]{2,1,0:T(8,128)(2,1)S(1)} async-done(((bf16[8,16,1024]{2,1,0:T(8,128)(2,1)}), bf16[8,16,1024]{2,1,0:T(8,128)(2,1)S(1)}, u32[]{:S(2)}, u32[]{:S(2)}) %all-to-all-start) | async-done | bytes 262176 | tf_op jit(solution)/shard_map/all_to_all | solution.py:49
  31.2 2.6 %fusion.207 = (f32[4,8,64]{2,1,0:T(8,128)S(1)}, f32[4,8,64,64]{2,3,1,0:T(8,128)}) fusion(bf16[8,256]{1,0:T(8,128)(2,1)S(1)} %copy-done.82, bf16[4,64,256]{2,1,0:T(8,128)(2,1)S(1)} %slice.340, bf16[4,64,768]{2,1,0:T(8,128)(2,1)} %copy-done.17), kind=kOutput, calls=%fused_computation.360 | convolution fusion | flops 68026432 | bytes 798720 | tf_op jit(solution)/shard_map/jvp()/sub | solution.py:127
  42.0 4.0 %all-to-all-start.1 = ((bf16[8,8,4,256]{3,1,2,0:T(8,128)(2,1)}), bf16[8,8,4,256]{3,1,2,0:T(8,128)(2,1)}, u32[]{:S(2)}, u32[]{:S(2)}) async-start(bf16[8,8,4,256]{3,1,2,0:T(8,128)(2,1)} %bitcast.409), calls=%async_computation.1 | async-start | bytes 262144 | tf_op jit(solution)/shard_map/all_to_all | solution.py:166
  46.8 1.7 copy.192
  49.8 1.8 all-to-all-done.1
  55.9 3.2 %fusion.211 = (f32[4,8,64]{2,1,0:T(8,128)}, f32[4,8,64,64]{2,3,1,0:T(8,128)}) fusion(bf16[4,64,256]{2,1,0:T(8,128)(2,1)} %slice.343, bf16[8,256]{1,0:T(8,128)(2,1)} %get-tuple-element.141, bf16[4,64,768]{2,1,0:T(8,128)(2,1)} %copy-done.19), kind=kOutput, calls=%fused_computation.362 | convolution fusion | flops 68026432 | bytes 798720 | tf_op jit(solution)/shard_map/jvp()/sub | solution.py:127
  59.9 2.1 %fusion.74 = (f32[4,8,64]{2,1,0:T(8,128)S(1)}, bf16[4,8,64,64]{2,3,1,0:T(8,128)(2,1)S(1)}, bf16[4,8,64,64]{2,3,1,0:T(8,128)(2,1)S(1)}) fusion(f32[4,8,64,64]{2,3,1,0:T(8,128)} %get-tuple-element.153, f32[4,8,64]{2,1,0:T(8,128)S(1)} %multiply_divide_fusion.1, f32[4,8,64]{2,1,0:T(8,128)} %get-tuple-element.152, bf16[4,64,768]{2,1,0:T(8,128)(2,1)} %copy-done.19, ...), kind=kOutput, calls=%fused_computation.85 | convolution fusion | flops 68548608 | bytes 2007040 | tf_op jit(solution)/shard_map/transpose(jvp(whqk,wkc->whqc))/dot_general | solution.py:128
  66.3 3.4 %all-to-all-start.4 = ((bf16[8,8,4,256]{3,1,2,0:T(8,128)(2,1)}), bf16[8,8,4,256]{3,1,2,0:T(8,128)(2,1)S(1)}, u32[]{:S(2)}, u32[]{:S(2)}) async-start(bf16[8,8,4,256]{3,1,2,0:T(8,128)(2,1)} %bitcast.75), calls=%async_computation.4 | async-start | bytes 262144 | tf_op jit(solution)/shard_map/all_to_all | solution.py:166
  73.0 2.2 %all-to-all-done.4 = bf16[8,8,4,256]{3,1,2,0:T(8,128)(2,1)S(1)} async-done(((bf16[8,8,4,256]{3,1,2,0:T(8,128)(2,1)}), bf16[8,8,4,256]{3,1,2,0:T(8,128)(2,1)S(1)}, u32[]{:S(2)}, u32[]{:S(2)}) %all-to-all-start.4) | async-done | bytes 131104 | tf_op jit(solution)/shard_map/all_to_all | solution.py:166
  75.2 4.2 %all-to-all-start.2 = ((bf16[8,8,4,256]{3,1,2,0:T(8,128)(2,1)}), bf16[8,8,4,256]{3,1,2,0:T(8,128)(2,1)}, u32[]{:S(2)}, u32[]{:S(2)}) async-start(bf16[8,8,4,256]{3,1,2,0:T(8,128)(2,1)} %bitcast.52), calls=%async_computation.2 | async-start | bytes 262144 | tf_op jit(solution)/shard_map/all_to_all | solution.py:166
  90.7 2.7 %multiply_reduce_fusion.10 = (f32[1024]{0:T(1024)S(1)}, f32[1024]{0:T(1024)S(1)}, f32[1024]{0:T(1024)S(1)}, f32[1024]{0:T(1024)S(1)}, f32[1024]{0:T(1024)S(1)}, ...) fusion(f32[18,18,1024]{2,1,0:T(8,128)S(1)} %convert_element_typ, ...), kind=kLoop, calls=%fused_computation.136 | loop fusion | flops 14408704 | bytes 11083776 | tf_op jit(solution)/shard_map/transpose(jvp())/reduce_sum | solution.py:143
  96.9 3.9 %all-to-all-start.5 = ((f32[8,16,1024]{2,1,0:T(8,128)}), f32[8,16,1024]{2,1,0:T(8,128)S(1)}, u32[]{:S(2)}, u32[]{:S(2)}) async-start(f32[8,16,1024]{2,1,0:T(8,128)} %select_select_fusion), calls=%async_computation.5 | async-start | bytes 1048576 | tf_op jit(solution)/shard_map/all_to_all | solution.py:49
  110.6 4.3 %all-to-all-start.6 = ((bf16[4,8,8,3200]{3,2,0,1:T(8,128)(2,1)}), bf16[4,8,8,3200]{3,2,0,1:T(8,128)(2,1)}, u32[]{:S(2)}, u32[]{:S(2)}) async-start(bf16[4,8,8,3200]{3,2,0,1:T(8,128)(2,1)} %copy.224), calls=%async_computation.6 | async-start | bytes 3276800 | tf_op jit(solution)/shard_map/all_to_all | solution.py:191
  117.4 1.9 %fusion.81 = bf16[16,16,1024]{2,1,0:T(8,128)(2,1)S(1)} fusion(f32[16,16,1024]{2,1,0:T(8,128)S(1)} %copy-done.16, f32[17,18,1024]{2,1,0:T(8,128)S(1)} %get-tuple-element.88, f32[16,16,1024]{2,1,0:T(8,128)S(1)} %copy-done.2, f32[16,1,1024]{2,1,0:T(1,128)S(1)} %fusion.161, f32[16,1,1024]{2,1,0:T(1,128)S(1)} %fusion.163, ...), kind=kLoop, calls=%fused_computation.92 | loop fusion | flops 10747904 | bytes 9080832 | tf_op jit(solution)/shard_map/transpose(jvp())/add_any | solution.py:283
  120.6 16.1 %all-to-all-done.6 = bf16[4,8,8,3200]{3,2,0,1:T(8,128)(2,1)} async-done(((bf16[4,8,8,3200]{3,2,0,1:T(8,128)(2,1)}), bf16[4,8,8,3200]{3,2,0,1:T(8,128)(2,1)}, u32[]{:S(2)}, u32[]{:S(2)}) %all-to-all-start.6) | async-done | bytes 1638432 | tf_op jit(solution)/shard_map/all_to_all | solution.py:191
  139.3 3.5 %all-to-all-start.7 = ((bf16[4,8,8,1152]{3,2,0,1:T(8,128)(2,1)}), bf16[4,8,8,1152]{3,2,0,1:T(8,128)(2,1)S(1)}, u32[]{:S(2)}, u32[]{:S(2)}) async-start(bf16[4,8,8,1152]{3,2,0,1:T(8,128)(2,1)} %copy.206), calls=%async_computation.7 | async-start | bytes 1179648 | tf_op jit(solution)/shard_map/all_to_all | solution.py:191
  143.9 9.3 %all-to-all-done.7 = bf16[4,8,8,1152]{3,2,0,1:T(8,128)(2,1)S(1)} async-done(((bf16[4,8,8,1152]{3,2,0,1:T(8,128)(2,1)}), bf16[4,8,8,1152]{3,2,0,1:T(8,128)(2,1)S(1)}, u32[]{:S(2)}, u32[]{:S(2)}) %all-to-all-start.7) | async-done | bytes 589856 | tf_op jit(solution)/shard_map/all_to_all | solution.py:191
  154.0 5.0 %all-to-all-start.8 = ((bf16[4,8,4352]{2,1,0:T(8,128)(2,1)}), bf16[4,8,4352]{2,1,0:T(8,128)(2,1)S(1)}, u32[]{:S(2)}, u32[]{:S(2)}) async-start(bf16[4,8,4352]{2,1,0:T(8,128)(2,1)} %pad_maximum_fusion.5), calls=%async_computation.8 | async-start | bytes 557056 | tf_op jit(solution)/shard_map/all_to_all | solution.py:191
  159.1 6.8 %all-to-all-done.8 = bf16[4,8,4352]{2,1,0:T(8,128)(2,1)S(1)} async-done(((bf16[4,8,4352]{2,1,0:T(8,128)(2,1)}), bf16[4,8,4352]{2,1,0:T(8,128)(2,1)S(1)}, u32[]{:S(2)}, u32[]{:S(2)}) %all-to-all-start.8) | async-done | bytes 278560 | tf_op jit(solution)/shard_map/all_to_all | solution.py:191
  166.8 4.4 %all-to-all-start.9 = ((bf16[8,8,4352]{2,1,0:T(8,128)(2,1)}), bf16[8,8,4352]{2,1,0:T(8,128)(2,1)S(1)}, u32[]{:S(2)}, u32[]{:S(2)}) async-start(bf16[8,8,4352]{2,1,0:T(8,128)(2,1)} %broadcast_in_dim.374), calls=%async_computation.9 | async-start | bytes 1114112 | tf_op jit(solution)/shard_map/all_to_all | solution.py:216
  172.5 8.9 %all-to-all-done.9 = bf16[8,8,4352]{2,1,0:T(8,128)(2,1)S(1)} async-done(((bf16[8,8,4352]{2,1,0:T(8,128)(2,1)}), bf16[8,8,4352]{2,1,0:T(8,128)(2,1)S(1)}, u32[]{:S(2)}, u32[]{:S(2)}) %all-to-all-start.9) | async-done | bytes 557088 | tf_op jit(solution)/shard_map/all_to_all | solution.py:216
  (374 shorter events, 73.3 us)
Async XLA Ops:
  0.6 9.4 %copy-start = (bf16[256,1024]{1,0:T(8,128)(2,1)S(1)}, bf16[256,1024]{1,0:T(8,128)(2,1)}, u32[]{:S(2)}) copy-start(bf16[256,1024]{1,0:T(8,128)(2,1)} %param.15) | copy-start | bytes 1572868
  2.7 12.7 %all-to-all-start.3 = ((bf16[8,8,4,256]{3,1,2,0:T(8,128)(2,1)}), bf16[8,8,4,256]{3,1,2,0:T(8,128)(2,1)S(1)}, u32[]{:S(2)}, u32[]{:S(2)}) async-start(bf16[8,8,4,256]{3,1,2,0:T(8,128)(2,1)} %bitcast.60), calls=%async_computation.3 | async-start | bytes 262144 | tf_op jit(solution)/shard_map/all_to_all | solution.py:166
  12.6 8.0 %copy-start.66 = (pred[8]{0:T(512)(128)(4,1)}, pred[8]{0:T(512)(128)(4,1)S(1)}, u32[]{:S(2)}) copy-start(pred[8]{0:T(512)(128)(4,1)S(1)} %get-tuple-element.157) | copy-start | bytes 28
  13.8 13.9 %copy-start.36 = (f32[1024,1]{0,1:T(1,128)}, f32[1024,1]{0,1:T(1,128)S(1)}, u32[]{:S(2)}) copy-start(f32[1024,1]{0,1:T(1,128)S(1)} %get-tuple-element.131) | copy-start | bytes 12292
  13.8 13.9 %copy-start.38 = (f32[1024,1]{0,1:T(1,128)}, f32[1024,1]{0,1:T(1,128)S(1)}, u32[]{:S(2)}) copy-start(f32[1024,1]{0,1:T(1,128)S(1)} %get-tuple-element.132) | copy-start | bytes 12292
  13.8 13.9 %copy-start.40 = (f32[1024,1]{0,1:T(1,128)}, f32[1024,1]{0,1:T(1,128)S(1)}, u32[]{:S(2)}) copy-start(f32[1024,1]{0,1:T(1,128)S(1)} %get-tuple-element.133) | copy-start | bytes 12292
  13.8 13.9 %copy-start.42 = (f32[1024,1]{0,1:T(1,128)}, f32[1024,1]{0,1:T(1,128)S(1)}, u32[]{:S(2)}) copy-start(f32[1024,1]{0,1:T(1,128)S(1)} %get-tuple-element.134) | copy-start | bytes 12292
  13.8 13.9 %copy-start.44 = (f32[1024,1]{0,1:T(1,128)}, f32[1024,1]{0,1:T(1,128)S(1)}, u32[]{:S(2)}) copy-start(f32[1024,1]{0,1:T(1,128)S(1)} %get-tuple-element.135) | copy-start | bytes 12292
  13.8 13.9 %copy-start.47 = (f32[1024,1]{0,1:T(1,128)}, f32[1024,1]{0,1:T(1,128)S(1)}, u32[]{:S(2)}) copy-start(f32[1024,1]{0,1:T(1,128)S(1)} %get-tuple-element.136) | copy-start | bytes 12292
  13.8 13.9 %copy-start.50 = (f32[1024,1]{0,1:T(1,128)}, f32[1024,1]{0,1:T(1,128)S(1)}, u32[]{:S(2)}) copy-start(f32[1024,1]{0,1:T(1,128)S(1)} %get-tuple-element.137) | copy-start | bytes 12292
  15.4 11.1 %all-to-all-start = ((bf16[8,16,1024]{2,1,0:T(8,128)(2,1)}), bf16[8,16,1024]{2,1,0:T(8,128)(2,1)S(1)}, u32[]{:S(2)}, u32[]{:S(2)}) async-start(bf16[8,16,1024]{2,1,0:T(8,128)(2,1)} %select_select_fusion.1), calls=%async_computation | async-start | bytes 524288 | tf_op jit(solution)/shard_map/all_to_all | solution.py:49
  37.5 16.7 %copy-start.8 = (bf16[256,768]{1,0:T(8,128)(2,1)S(1)}, bf16[256,768]{1,0:T(8,128)(2,1)}, u32[]{:S(2)}) copy-start(bf16[256,768]{1,0:T(8,128)(2,1)} %param.22) | copy-start | bytes 1179652
  42.0 9.5 %all-to-all-start.1 = ((bf16[8,8,4,256]{3,1,2,0:T(8,128)(2,1)}), bf16[8,8,4,256]{3,1,2,0:T(8,128)(2,1)}, u32[]{:S(2)}, u32[]{:S(2)}) async-start(bf16[8,8,4,256]{3,1,2,0:T(8,128)(2,1)} %bitcast.409), calls=%async_computation.1 | async-start | bytes 262144 | tf_op jit(solution)/shard_map/all_to_all | solution.py:166
  66.3 8.8 %all-to-all-start.4 = ((bf16[8,8,4,256]{3,1,2,0:T(8,128)(2,1)}), bf16[8,8,4,256]{3,1,2,0:T(8,128)(2,1)S(1)}, u32[]{:S(2)}, u32[]{:S(2)}) async-start(bf16[8,8,4,256]{3,1,2,0:T(8,128)(2,1)} %bitcast.75), calls=%async_computation.4 | async-start | bytes 262144 | tf_op jit(solution)/shard_map/all_to_all | solution.py:166
  72.2 11.5 %copy-start.11 = (bf16[1,16,16,256]{3,2,1,0:T(8,128)(2,1)S(1)}, bf16[1,16,16,256]{3,2,1,0:T(8,128)(2,1)}, u32[]{:S(2)}) copy-start(bf16[1,16,16,256]{3,2,1,0:T(8,128)(2,1)} %param.13) | copy-start | bytes 393220
  75.2 21.8 %all-to-all-start.2 = ((bf16[8,8,4,256]{3,1,2,0:T(8,128)(2,1)}), bf16[8,8,4,256]{3,1,2,0:T(8,128)(2,1)}, u32[]{:S(2)}, u32[]{:S(2)}) async-start(bf16[8,8,4,256]{3,1,2,0:T(8,128)(2,1)} %bitcast.52), calls=%async_computation.2 | async-start | bytes 262144 | tf_op jit(solution)/shard_map/all_to_all | solution.py:166
  96.7 7.4 %copy-start.85 = (bf16[256]{0:T(256)(128)(2,1)S(1)}, bf16[256]{0:T(256)(128)(2,1)}, u32[]{:S(2)}) copy-start(bf16[256]{0:T(256)(128)(2,1)} %get-tuple-element.80) | copy-start | bytes 1540
  96.8 9.1 %copy-start.26 = (bf16[256,256]{1,0:T(8,128)(2,1)S(1)}, bf16[256,256]{1,0:T(8,128)(2,1)}, u32[]{:S(2)}) copy-start(bf16[256,256]{1,0:T(8,128)(2,1)} %copy.190) | copy-start | bytes 393220
  96.9 13.7 %all-to-all-start.5 = ((f32[8,16,1024]{2,1,0:T(8,128)}), f32[8,16,1024]{2,1,0:T(8,128)S(1)}, u32[]{:S(2)}, u32[]{:S(2)}) async-start(f32[8,16,1024]{2,1,0:T(8,128)} %select_select_fusion), calls=%async_computation.5 | async-start | bytes 1048576 | tf_op jit(solution)/shard_map/all_to_all | solution.py:49
  110.6 26.1 %all-to-all-start.6 = ((bf16[4,8,8,3200]{3,2,0,1:T(8,128)(2,1)}), bf16[4,8,8,3200]{3,2,0,1:T(8,128)(2,1)}, u32[]{:S(2)}, u32[]{:S(2)}) async-start(bf16[4,8,8,3200]{3,2,0,1:T(8,128)(2,1)} %copy.224), calls=%async_computation.6 | async-start | bytes 3276800 | tf_op jit(solution)/shard_map/all_to_all | solution.py:191
  139.3 13.9 %all-to-all-start.7 = ((bf16[4,8,8,1152]{3,2,0,1:T(8,128)(2,1)}), bf16[4,8,8,1152]{3,2,0,1:T(8,128)(2,1)S(1)}, u32[]{:S(2)}, u32[]{:S(2)}) async-start(bf16[4,8,8,1152]{3,2,0,1:T(8,128)(2,1)} %copy.206), calls=%async_computation.7 | async-start | bytes 1179648 | tf_op jit(solution)/shard_map/all_to_all | solution.py:191
  154.0 17.6 %copy-start.7 = (f32[16,16,256]{2,1,0:T(8,128)S(1)}, f32[16,16,256]{2,1,0:T(8,128)}, u32[]{:S(2)}) copy-start(f32[16,16,256]{2,1,0:T(8,128)} %copy-done.6) | copy-start | bytes 786436
  154.0 11.9 %all-to-all-start.8 = ((bf16[4,8,4352]{2,1,0:T(8,128)(2,1)}), bf16[4,8,4352]{2,1,0:T(8,128)(2,1)S(1)}, u32[]{:S(2)}, u32[]{:S(2)}) async-start(bf16[4,8,4352]{2,1,0:T(8,128)(2,1)} %pad_maximum_fusion.5), calls=%async_computation.8 | async-start | bytes 557056 | tf_op jit(solution)/shard_map/all_to_all | solution.py:191
  166.8 14.5 %all-to-all-start.9 = ((bf16[8,8,4352]{2,1,0:T(8,128)(2,1)}), bf16[8,8,4352]{2,1,0:T(8,128)(2,1)S(1)}, u32[]{:S(2)}, u32[]{:S(2)}) async-start(bf16[8,8,4352]{2,1,0:T(8,128)(2,1)} %broadcast_in_dim.374), calls=%async_computation.9 | async-start | bytes 1114112 | tf_op jit(solution)/shard_map/all_to_all | solution.py:216
  (75 other events, 198.3 us)

commit v15 on v11

--- a/solution.py
+++ b/solution.py
@@ -187,6 +187,28 @@
     return moved.transpose(2, 0, 3, 1, 4).reshape(height, breadth, channels)
 
 
+def home_with_sums(image, grads):
+    height, breadth, channels = image.shape
+    sy_count = lax.axis_size("sy")
+    sx_count = lax.axis_size("sx")
+    tiles = sy_count * sx_count
+    parts = lax.axis_size("rep")
+    blocks = image.reshape(sy_count, height // sy_count, sx_count, breadth // sx_count, channels)
+    blocks = blocks.transpose(0, 2, 1, 3, 4)
+    block_shape = blocks.shape
+    rows, width = grads.shape
+    piece = rows // parts // tiles
+    pieces = grads.reshape(parts, tiles, piece, width).transpose(1, 0, 2, 3)
+    joined = jnp.concatenate(
+        [blocks.reshape(tiles, -1), pieces.astype(jnp.bfloat16).reshape(tiles, -1)], axis=1
+    )
+    moved = lax.all_to_all(joined, ("sy", "sx"), split_axis=0, concat_axis=0, tiled=True)
+    image_part = moved[:, : blocks.size // tiles].reshape(block_shape)
+    home = image_part.transpose(2, 0, 3, 1, 4).reshape(height, breadth, channels)
+    sums = moved[:, blocks.size // tiles :].reshape(tiles, parts, piece, width)
+    return home, sums.astype(jnp.float32).sum(0)
+
+
 def exchange_sum(values, axes, axis):
     moved = lax.all_to_all(values.astype(jnp.bfloat16), axes, split_axis=axis, concat_axis=axis, tiled=True)
     return moved.astype(jnp.float32).sum(axis)
@@ -203,8 +225,10 @@
 
 def reduce_packed(groups):
     tiles = lax.axis_size(("sy", "sx"))
-    widths = [piece.shape[1] for wide in groups for piece in wide]
-    local = jnp.concatenate([tile_sum(wide) for wide in groups], axis=-1)
+    widths = [piece.shape[-1] for wide in groups for piece in wide]
+    local = jnp.concatenate(
+        [wide[0] if wide[0].ndim == 3 else tile_sum(wide) for wide in groups], axis=-1
+    )
     parts, piece, width = local.shape
     local = exchange_sum(local, "rep", 0)
     spread = jnp.broadcast_to(local[None].astype(jnp.bfloat16), (tiles, piece, width))
@@ -229,21 +253,22 @@
     kernel_cols = taps * grads[2].shape[0] // channels
     cuts = reduce_packed(
         (
-            [grads[5], grads[6], grads[8], grads[9], pad_lanes([grads[4][:, None], grads[7][:, None]])],
+            [grads[9]],
+            [grads[5], grads[6], pad_lanes([grads[4][:, None], grads[7][:, None]])],
             [grads[1], grads[3].reshape(channels, -1), pad_lanes([grads[2].reshape(channels, -1), grads[0][:, None]])],
         )
     )
     return (
-        cuts[7][:, kernel_cols],
-        cuts[5],
-        cuts[7][:, :kernel_cols].reshape(-1, taps),
-        cuts[6].reshape(-1, grads[3].shape[1]),
-        cuts[4][:, 0],
-        cuts[0],
+        cuts[6][:, kernel_cols],
+        cuts[4],
+        cuts[6][:, :kernel_cols].reshape(-1, taps),
+        cuts[5].reshape(-1, grads[3].shape[1]),
+        cuts[3][:, 0],
         cuts[1],
-        cuts[4][:, 1],
         cuts[2],
-        cuts[3],
+        cuts[3][:, 1],
+        cuts[0][:, : grads[5].shape[1]],
+        cuts[0][:, grads[5].shape[1] :],
     )
 
 def body(
@@ -326,7 +351,12 @@
     d_stream_two, d_grid_home, tap_grid_out = grid_tail_back(cotangent[0])
     d_grid_attended = to_grid(to_exchanged(d_grid_home), WIN)
     d_grid_windows, tap_grid_in = grid_core_back(d_grid_attended)
-    d_normed_three = to_home(from_grid(d_grid_windows, height, breadth, WIN))
+    grid_weight_grads = jnp.concatenate(
+        [outer_sum(grid_windows, tap_grid_in), outer_sum(grid_home, tap_grid_out)], axis=1
+    )
+    d_normed_three, grid_tile_sum = home_with_sums(
+        from_grid(d_grid_windows, height, breadth, WIN), grid_weight_grads
+    )
     d_stream_extra, d_gain_grid = grid_front_back(d_normed_three)
     d_stream_two = d_stream_two + d_stream_extra
     d_stream_one, d_gain_block, tap_block_in, tap_block_out = block_back(d_stream_two)
@@ -346,8 +376,8 @@
         outer_sum(block_saved[0], tap_block_in),
         outer_sum(block_saved[1], tap_block_out),
         d_gain_grid,
-        outer_sum(grid_windows, tap_grid_in),
-        outer_sum(grid_home, tap_grid_out),
+        grid_weight_grads,
+        grid_tile_sum,
     )
     summed = reduce_grads(local_grads)
     return (

time: 183 us -> 214 us (1.17)
  local copies, waits for them, and re-layouts: 29.1 us -> 57.5 us
  other arithmetic: 25.6 us -> 32.4 us
  waiting for transfers between devices: 58.9 us -> 52.3 us
    unnamed x203 -> x201, local copies, waits for them, and re-layouts: 6.27 us -> 16.8 us
    all_to_all x0 -> x1, waiting for transfers between devices: none -> 9.63 us  [home_with_sums(): lax.all_to_all(joined, ('sy', 'sx'), split_axis=0, concat_axis=0, tiled=T...]
    all_to_all x3, waiting for transfers between devices: 29.7 us -> 22.7 us  [exchange_sum(): lax.all_to_all(values.astype(jnp.bfloat16), axes, split_axis=axis, concat...]
    all_to_all x4 -> x3, waiting for transfers between devices: 6.24 us -> 0.4 us  [swap_blocks(): lax.all_to_all(as_sent(flattened), ('sy', 'sx'), split_axis=0, concat_axi...]
    all_to_all x0 -> x1, starting transfers between devices: none -> 4.19 us  [home_with_sums(): lax.all_to_all(joined, ('sy', 'sx'), split_axis=0, concat_axis=0, tiled=T...]
    all_to_all x4 -> x3, starting transfers between devices: 16.1 us -> 12.3 us  [swap_blocks(): lax.all_to_all(as_sent(flattened), ('sy', 'sx'), split_axis=0, concat_axi...]
    all_to_all x0 -> x2, other arithmetic: none -> 3.8 us  [home_with_sums(): lax.all_to_all(joined, ('sy', 'sx'), split_axis=0, concat_axis=0, tiled=T...]
    all_to_all x2, waiting for transfers between devices: 14.1 us -> 10.7 us  [extended_2(): lax.all_to_all(outgoing, ('sy', 'sx'), split_axis=0, concat_axis=0, tiled...]
  transfers between devices with their start and end apart: 10 -> 10, of which waited for: 8 -> 8; matrix products, arithmetic and copies ran while one was open for 21% -> 20% of each run, Pallas kernels for 0% -> 0%
where the time goes in v15:
time: 214 us; the launch traced here: 212 us
  local copies, waits for them, and re-layouts  57.5 us (27%)
  waiting for transfers between devices  52.3 us (24%)
  starting transfers between devices  42.3 us (20%)
  other arithmetic  32.4 us (15%)
  matrix products  24.6 us (11%)
  between operations  2.74 us (1%)
    all_to_all x3, waiting for transfers between devices, exchange_sum(): lax.all_to_all(values.astype(jnp.bfloat16), axes, split_axis=axis, concat...  22.7 us
    unnamed x201, local copies, waits for them, and re-layouts  16.8 us
    all_to_all x3, starting transfers between devices, exchange_sum(): lax.all_to_all(values.astype(jnp.bfloat16), axes, split_axis=axis, concat...  12.8 us
    all_to_all x3, starting transfers between devices, swap_blocks(): lax.all_to_all(as_sent(flattened), ('sy', 'sx'), split_axis=0, concat_axi...  12.3 us
    all_to_all x2, waiting for transfers between devices, extended_2(): lax.all_to_all(outgoing, ('sy', 'sx'), split_axis=0, concat_axis=0, tiled...  10.7 us
    all_to_all x1, waiting for transfers between devices, home_with_sums(): lax.all_to_all(joined, ('sy', 'sx'), split_axis=0, concat_axis=0, tiled=T...  9.63 us
    all_to_all x1, waiting for transfers between devices, reduce_packed(): lax.all_to_all(spread, ('sy', 'sx'), split_axis=0, concat_axis=0, tiled=T...  8.89 us
    all_to_all x2, starting transfers between devices, extended_2(): lax.all_to_all(outgoing, ('sy', 'sx'), split_axis=0, concat_axis=0, tiled...  8.66 us
  transfers between devices with their start and end apart: 10, of which 8 were waited for; matrix products, arithmetic and copies ran while one was open for 20% of the time, Pallas kernels for 0%

profile of v15, /device:TPU:0, one launch (start us, length us, event | category | flops | bytes accessed | tf_op | source)
XLA Modules:
  0.0 211.8 jit_solution(10983342530224943988)
XLA Ops:
  2.9 2.3 %multiply_convert_fusion.1 = (bf16[16,16,1024]{2,1,0:T(8,128)(2,1)S(1)}, f32[16,16,1024]{2,1,0:T(8,128)}) fusion(bf16[256,1024]{1,0:T(8,128)(2,1)S(1)} %copy-done, bf16[1,16,16,256]{3,2,1,0:T(8,128)(2,1)} %param.12, f32[256]{0:T(256)} %param.14, f32[16,16]{1,0:T(8,128)S(1)} %fusion.190, f32[16,16]{1,0:T(8,128)S(1)} %broadcast_multiply_fusion.2), kind=kOutput, calls=%fused_computation.148 | convolution fusion | flops 136904704 | bytes 2231296 | tf_op jit(solution)/shard_map/jvp()/dot_general | solution.py:78
  6.5 5.2 %all-to-all-start = ((bf16[8,16,1024]{2,1,0:T(8,128)(2,1)}), bf16[8,16,1024]{2,1,0:T(8,128)(2,1)S(1)}, u32[]{:S(2)}, u32[]{:S(2)}) async-start(bf16[8,16,1024]{2,1,0:T(8,128)(2,1)} %select_select_fusion.1), calls=%async_computation | async-start | bytes 524288 | tf_op jit(solution)/shard_map/all_to_all | solution.py:49
  13.5 5.1 %all-to-all-done = bf16[8,16,1024]{2,1,0:T(8,128)(2,1)S(1)} async-done(((bf16[8,16,1024]{2,1,0:T(8,128)(2,1)}), bf16[8,16,1024]{2,1,0:T(8,128)(2,1)S(1)}, u32[]{:S(2)}, u32[]{:S(2)}) %all-to-all-start) | async-done | bytes 262176 | tf_op jit(solution)/shard_map/all_to_all | solution.py:49
  18.6 4.0 %all-to-all-start.3 = ((bf16[8,8,4,256]{3,1,2,0:T(8,128)(2,1)}), bf16[8,8,4,256]{3,1,2,0:T(8,128)(2,1)}, u32[]{:S(2)}, u32[]{:S(2)}) async-start(bf16[8,8,4,256]{3,1,2,0:T(8,128)(2,1)} %bitcast.60), calls=%async_computation.3 | async-start | bytes 262144 | tf_op jit(solution)/shard_map/all_to_all | solution.py:166
  26.7 2.3 %fusion.205 = (f32[4,8,64]{2,1,0:T(8,128)}, f32[4,8,64,64]{2,3,1,0:T(8,128)}) fusion(bf16[8,256]{1,0:T(8,128)(2,1)S(1)} %copy-done.90, bf16[4,64,256]{2,1,0:T(8,128)(2,1)S(1)} %slice.351, bf16[4,64,768]{2,1,0:T(8,128)(2,1)S(1)} %convolution_convert_fusion.7), kind=kOutput, calls=%fused_computation.361 | convolution fusion | flops 68026432 | bytes 798720 | tf_op jit(solution)/shard_map/jvp()/sub | solution.py:127
  35.7 4.1 %all-to-all-start.1 = ((bf16[8,8,4,256]{3,1,2,0:T(8,128)(2,1)}), bf16[8,8,4,256]{3,1,2,0:T(8,128)(2,1)}, u32[]{:S(2)}, u32[]{:S(2)}) async-start(bf16[8,8,4,256]{3,1,2,0:T(8,128)(2,1)} %bitcast.397), calls=%async_computation.1 | async-start | bytes 262144 | tf_op jit(solution)/shard_map/all_to_all | solution.py:166
  51.9 3.2 %fusion.209 = (f32[4,8,64]{2,1,0:T(8,128)}, f32[4,8,64,64]{2,3,1,0:T(8,128)}) fusion(bf16[4,64,256]{2,1,0:T(8,128)(2,1)} %slice.354, bf16[8,256]{1,0:T(8,128)(2,1)} %get-tuple-element.147, bf16[4,64,768]{2,1,0:T(8,128)(2,1)} %copy-done.26), kind=kOutput, calls=%fused_computation.363 | convolution fusion | flops 68026432 | bytes 798720 | tf_op jit(solution)/shard_map/jvp()/sub | solution.py:127
  65.8 4.2 %all-to-all-start.2 = ((bf16[8,8,4,256]{3,1,2,0:T(8,128)(2,1)}), bf16[8,8,4,256]{3,1,2,0:T(8,128)(2,1)}, u32[]{:S(2)}, u32[]{:S(2)}) async-start(bf16[8,8,4,256]{3,1,2,0:T(8,128)(2,1)} %bitcast.396), calls=%async_computation.2 | async-start | bytes 262144 | tf_op jit(solution)/shard_map/all_to_all | solution.py:166
  84.1 2.9 %reduce.14 = bf16[8,40960]{1,0:T(8,128)(2,1)} reduce(bf16[8,1,40960]{2,0,1:T(8,128)(2,1)} %maximum_bitcast_fusion, bf16[]{:T(256)} %broadcast.1038), dimensions={1}, to_apply=%copy.234.reduce_sub_computation | reduce | bytes 1310722 | tf_op jit(solution)/shard_map/all_to_all | solution.py:205
  87.0 2.5 %reshape.776 = bf16[8,2,20480]{2,1,0:T(2,128)(2,1)} reshape(bf16[8,40960]{1,0:T(8,128)(2,1)} %reduce.14) | data formatting | bytes 1310720
  89.5 4.2 %all-to-all-start.4 = ((bf16[8,2,20480]{2,1,0:T(2,128)(2,1)}), bf16[8,2,20480]{2,1,0:T(2,128)(2,1)}, u32[]{:S(2)}, u32[]{:S(2)}) async-start(bf16[8,2,20480]{2,1,0:T(2,128)(2,1)} %reshape.776), calls=%async_computation.4 | async-start | bytes 1310720 | tf_op jit(solution)/shard_map/all_to_all | solution.py:205
  95.2 9.6 %all-to-all-done.4 = bf16[8,2,20480]{2,1,0:T(2,128)(2,1)} async-done(((bf16[8,2,20480]{2,1,0:T(2,128)(2,1)}), bf16[8,2,20480]{2,1,0:T(2,128)(2,1)}, u32[]{:S(2)}, u32[]{:S(2)}) %all-to-all-start.4) | async-done | bytes 655392 | tf_op jit(solution)/shard_map/all_to_all | solution.py:205
  104.9 3.6 %reshape.777 = bf16[8,1,40960]{2,1,0:T(2,128)(2,1)} reshape(bf16[8,2,20480]{2,1,0:T(2,128)(2,1)} %all-to-all-done.4) | data formatting | bytes 1310720
  124.3 3.3 %multiply_reduce_fusion.10 = (f32[1024]{0:T(1024)S(1)}, f32[1024]{0:T(1024)S(1)}, f32[1024]{0:T(1024)S(1)}, f32[1024]{0:T(1024)S(1)}, f32[1024]{0:T(1024)S(1)}, ...) fusion(f32[18,18,1024]{2,1,0:T(8,128)S(1)} %convert_element_type., ...), kind=kLoop, calls=%fused_computation.135 | loop fusion | flops 14408704 | bytes 11083776 | tf_op jit(solution)/shard_map/transpose(jvp())/reduce_sum | solution.py:143
  131.8 3.5 %all-to-all-start.5 = ((f32[8,16,1024]{2,1,0:T(8,128)}), f32[8,16,1024]{2,1,0:T(8,128)S(1)}, u32[]{:S(2)}, u32[]{:S(2)}) async-start(f32[8,16,1024]{2,1,0:T(8,128)} %select_select_fusion), calls=%async_computation.5 | async-start | bytes 1048576 | tf_op jit(solution)/shard_map/all_to_all | solution.py:49
  139.4 5.5 %all-to-all-done.5 = f32[8,16,1024]{2,1,0:T(8,128)S(1)} async-done(((f32[8,16,1024]{2,1,0:T(8,128)}), f32[8,16,1024]{2,1,0:T(8,128)S(1)}, u32[]{:S(2)}, u32[]{:S(2)}) %all-to-all-start.5) | async-done | bytes 524320 | tf_op jit(solution)/shard_map/all_to_all | solution.py:49
  145.0 4.4 %all-to-all-start.6 = ((bf16[4,8,8,1152]{3,2,0,1:T(8,128)(2,1)}), bf16[4,8,8,1152]{3,2,0,1:T(8,128)(2,1)}, u32[]{:S(2)}, u32[]{:S(2)}) async-start(bf16[4,8,8,1152]{3,2,0,1:T(8,128)(2,1)} %copy.250), calls=%async_computation.6 | async-start | bytes 1179648 | tf_op jit(solution)/shard_map/all_to_all | solution.py:213
  155.6 4.0 %all-to-all-done.6 = bf16[4,8,8,1152]{3,2,0,1:T(8,128)(2,1)} async-done(((bf16[4,8,8,1152]{3,2,0,1:T(8,128)(2,1)}), bf16[4,8,8,1152]{3,2,0,1:T(8,128)(2,1)}, u32[]{:S(2)}, u32[]{:S(2)}) %all-to-all-start.6) | async-done | bytes 589856 | tf_op jit(solution)/shard_map/all_to_all | solution.py:213
  159.6 3.6 %all-to-all-start.7 = ((bf16[4,8,8,2176]{3,2,0,1:T(8,128)(2,1)}), bf16[4,8,8,2176]{3,2,0,1:T(8,128)(2,1)S(1)}, u32[]{:S(2)}, u32[]{:S(2)}) async-start(bf16[4,8,8,2176]{3,2,0,1:T(8,128)(2,1)} %copy.255), calls=%async_computation.7 | async-start | bytes 2228224 | tf_op jit(solution)/shard_map/all_to_all | solution.py:213
  167.4 11.9 %all-to-all-done.7 = bf16[4,8,8,2176]{3,2,0,1:T(8,128)(2,1)S(1)} async-done(((bf16[4,8,8,2176]{3,2,0,1:T(8,128)(2,1)}), bf16[4,8,8,2176]{3,2,0,1:T(8,128)(2,1)S(1)}, u32[]{:S(2)}, u32[]{:S(2)}) %all-to-all-start.7) | async-done | bytes 1114144 | tf_op jit(solution)/shard_map/all_to_all | solution.py:213
  180.1 4.9 %all-to-all-start.8 = ((bf16[4,8,4352]{2,1,0:T(8,128)(2,1)}), bf16[4,8,4352]{2,1,0:T(8,128)(2,1)S(1)}, u32[]{:S(2)}, u32[]{:S(2)}) async-start(bf16[4,8,4352]{2,1,0:T(8,128)(2,1)} %pad_maximum_fusion.6), calls=%async_computation.8 | async-start | bytes 557056 | tf_op jit(solution)/shard_map/all_to_all | solution.py:213
  185.1 6.8 %all-to-all-done.8 = bf16[4,8,4352]{2,1,0:T(8,128)(2,1)S(1)} async-done(((bf16[4,8,4352]{2,1,0:T(8,128)(2,1)}), bf16[4,8,4352]{2,1,0:T(8,128)(2,1)S(1)}, u32[]{:S(2)}, u32[]{:S(2)}) %all-to-all-start.8) | async-done | bytes 278560 | tf_op jit(solution)/shard_map/all_to_all | solution.py:213
  192.8 4.4 %all-to-all-start.9 = ((bf16[8,8,4352]{2,1,0:T(8,128)(2,1)}), bf16[8,8,4352]{2,1,0:T(8,128)(2,1)S(1)}, u32[]{:S(2)}, u32[]{:S(2)}) async-start(bf16[8,8,4352]{2,1,0:T(8,128)(2,1)} %broadcast_in_dim.375), calls=%async_computation.9 | async-start | bytes 1114112 | tf_op jit(solution)/shard_map/all_to_all | solution.py:235
  198.4 8.9 %all-to-all-done.9 = bf16[8,8,4352]{2,1,0:T(8,128)(2,1)S(1)} async-done(((bf16[8,8,4352]{2,1,0:T(8,128)(2,1)}), bf16[8,8,4352]{2,1,0:T(8,128)(2,1)S(1)}, u32[]{:S(2)}, u32[]{:S(2)}) %all-to-all-start.9) | async-done | bytes 557088 | tf_op jit(solution)/shard_map/all_to_all | solution.py:235
  (395 shorter events, 94.7 us)
Async XLA Ops:
  5.4 17.2 %copy-start.80 = (pred[8]{0:T(512)(128)(4,1)}, pred[8]{0:T(512)(128)(4,1)S(1)}, u32[]{:S(2)}) copy-start(pred[8]{0:T(512)(128)(4,1)S(1)} %get-tuple-element.166) | copy-start | bytes 28
  5.5 17.2 %copy-start.82 = (pred[8]{0:T(512)(128)(4,1)}, pred[8]{0:T(512)(128)(4,1)S(1)}, u32[]{:S(2)}) copy-start(pred[8]{0:T(512)(128)(4,1)S(1)} %get-tuple-element.167) | copy-start | bytes 28
  5.5 17.2 %copy-start.84 = (pred[8]{0:T(512)(128)(4,1)}, pred[8]{0:T(512)(128)(4,1)S(1)}, u32[]{:S(2)}) copy-start(pred[8]{0:T(512)(128)(4,1)S(1)} %get-tuple-element.168) | copy-start | bytes 28
  6.5 12.1 %all-to-all-start = ((bf16[8,16,1024]{2,1,0:T(8,128)(2,1)}), bf16[8,16,1024]{2,1,0:T(8,128)(2,1)S(1)}, u32[]{:S(2)}, u32[]{:S(2)}) async-start(bf16[8,16,1024]{2,1,0:T(8,128)(2,1)} %select_select_fusion.1), calls=%async_computation | async-start | bytes 524288 | tf_op jit(solution)/shard_map/all_to_all | solution.py:49
  12.6 17.8 %copy-start.71 = (f32[8,256]{1,0:T(8,128)}, f32[8,256]{1,0:T(8,128)S(1)}, u32[]{:S(2)}) copy-start(f32[8,256]{1,0:T(8,128)S(1)} %get-tuple-element.146) | copy-start | bytes 24580
  13.4 10.5 %copy-start.43 = (f32[1024,1]{0,1:T(1,128)}, f32[1024,1]{0,1:T(1,128)S(1)}, u32[]{:S(2)}) copy-start(f32[1024,1]{0,1:T(1,128)S(1)} %get-tuple-element.137) | copy-start | bytes 12292
  13.4 10.5 %copy-start.45 = (f32[1024,1]{0,1:T(1,128)}, f32[1024,1]{0,1:T(1,128)S(1)}, u32[]{:S(2)}) copy-start(f32[1024,1]{0,1:T(1,128)S(1)} %get-tuple-element.138) | copy-start | bytes 12292
  13.4 10.5 %copy-start.47 = (f32[1024,1]{0,1:T(1,128)}, f32[1024,1]{0,1:T(1,128)S(1)}, u32[]{:S(2)}) copy-start(f32[1024,1]{0,1:T(1,128)S(1)} %get-tuple-element.139) | copy-start | bytes 12292
  13.4 10.5 %copy-start.49 = (f32[1024,1]{0,1:T(1,128)}, f32[1024,1]{0,1:T(1,128)S(1)}, u32[]{:S(2)}) copy-start(f32[1024,1]{0,1:T(1,128)S(1)} %get-tuple-element.140) | copy-start | bytes 12292
  13.4 10.5 %copy-start.51 = (f32[1024,1]{0,1:T(1,128)}, f32[1024,1]{0,1:T(1,128)S(1)}, u32[]{:S(2)}) copy-start(f32[1024,1]{0,1:T(1,128)S(1)} %get-tuple-element.141) | copy-start | bytes 12292
  13.5 10.5 %copy-start.54 = (f32[1024,1]{0,1:T(1,128)}, f32[1024,1]{0,1:T(1,128)S(1)}, u32[]{:S(2)}) copy-start(f32[1024,1]{0,1:T(1,128)S(1)} %get-tuple-element.142) | copy-start | bytes 12292
  13.5 10.5 %copy-start.57 = (f32[1024,1]{0,1:T(1,128)}, f32[1024,1]{0,1:T(1,128)S(1)}, u32[]{:S(2)}) copy-start(f32[1024,1]{0,1:T(1,128)S(1)} %get-tuple-element.143) | copy-start | bytes 12292
  18.6 17.0 %all-to-all-start.3 = ((bf16[8,8,4,256]{3,1,2,0:T(8,128)(2,1)}), bf16[8,8,4,256]{3,1,2,0:T(8,128)(2,1)}, u32[]{:S(2)}, u32[]{:S(2)}) async-start(bf16[8,8,4,256]{3,1,2,0:T(8,128)(2,1)} %bitcast.60), calls=%async_computation.3 | async-start | bytes 262144 | tf_op jit(solution)/shard_map/all_to_all | solution.py:166
  31.6 18.6 %copy-start.9 = (bf16[256,768]{1,0:T(8,128)(2,1)S(1)}, bf16[256,768]{1,0:T(8,128)(2,1)}, u32[]{:S(2)}) copy-start(bf16[256,768]{1,0:T(8,128)(2,1)} %param.22) | copy-start | bytes 1179652
  35.7 9.7 %all-to-all-start.1 = ((bf16[8,8,4,256]{3,1,2,0:T(8,128)(2,1)}), bf16[8,8,4,256]{3,1,2,0:T(8,128)(2,1)}, u32[]{:S(2)}, u32[]{:S(2)}) async-start(bf16[8,8,4,256]{3,1,2,0:T(8,128)(2,1)} %bitcast.397), calls=%async_computation.1 | async-start | bytes 262144 | tf_op jit(solution)/shard_map/all_to_all | solution.py:166
  65.8 11.6 %all-to-all-start.2 = ((bf16[8,8,4,256]{3,1,2,0:T(8,128)(2,1)}), bf16[8,8,4,256]{3,1,2,0:T(8,128)(2,1)}, u32[]{:S(2)}, u32[]{:S(2)}) async-start(bf16[8,8,4,256]{3,1,2,0:T(8,128)(2,1)} %bitcast.396), calls=%async_computation.2 | async-start | bytes 262144 | tf_op jit(solution)/shard_map/all_to_all | solution.py:166
  89.5 15.4 %all-to-all-start.4 = ((bf16[8,2,20480]{2,1,0:T(2,128)(2,1)}), bf16[8,2,20480]{2,1,0:T(2,128)(2,1)}, u32[]{:S(2)}, u32[]{:S(2)}) async-start(bf16[8,2,20480]{2,1,0:T(2,128)(2,1)} %reshape.776), calls=%async_computation.4 | async-start | bytes 1310720 | tf_op jit(solution)/shard_map/all_to_all | solution.py:205
  131.8 13.2 %all-to-all-start.5 = ((f32[8,16,1024]{2,1,0:T(8,128)}), f32[8,16,1024]{2,1,0:T(8,128)S(1)}, u32[]{:S(2)}, u32[]{:S(2)}) async-start(f32[8,16,1024]{2,1,0:T(8,128)} %select_select_fusion), calls=%async_computation.5 | async-start | bytes 1048576 | tf_op jit(solution)/shard_map/all_to_all | solution.py:49
  139.4 10.6 %copy-start.2 = (f32[16,16,1024]{2,1,0:T(8,128)S(1)}, f32[16,16,1024]{2,1,0:T(8,128)}, u32[]{:S(2)}) copy-start(f32[16,16,1024]{2,1,0:T(8,128)} %copy-done.1) | copy-start | bytes 3145732
  145.0 14.7 %all-to-all-start.6 = ((bf16[4,8,8,1152]{3,2,0,1:T(8,128)(2,1)}), bf16[4,8,8,1152]{3,2,0,1:T(8,128)(2,1)}, u32[]{:S(2)}, u32[]{:S(2)}) async-start(bf16[4,8,8,1152]{3,2,0,1:T(8,128)(2,1)} %copy.250), calls=%async_computation.6 | async-start | bytes 1179648 | tf_op jit(solution)/shard_map/all_to_all | solution.py:213
  155.6 10.1 %copy-start.5 = (bf16[8,1,40960]{2,0,1:T(8,128)(2,1)S(1)}, bf16[8,1,40960]{2,0,1:T(8,128)(2,1)}, u32[]{:S(2)}) copy-start(bf16[8,1,40960]{2,0,1:T(8,128)(2,1)} %copy-done.4) | copy-start | bytes 1966084
  159.6 19.6 %all-to-all-start.7 = ((bf16[4,8,8,2176]{3,2,0,1:T(8,128)(2,1)}), bf16[4,8,8,2176]{3,2,0,1:T(8,128)(2,1)S(1)}, u32[]{:S(2)}, u32[]{:S(2)}) async-start(bf16[4,8,8,2176]{3,2,0,1:T(8,128)(2,1)} %copy.255), calls=%async_computation.7 | async-start | bytes 2228224 | tf_op jit(solution)/shard_map/all_to_all | solution.py:213
  180.1 11.8 %all-to-all-start.8 = ((bf16[4,8,4352]{2,1,0:T(8,128)(2,1)}), bf16[4,8,4352]{2,1,0:T(8,128)(2,1)S(1)}, u32[]{:S(2)}, u32[]{:S(2)}) async-start(bf16[4,8,4352]{2,1,0:T(8,128)(2,1)} %pad_maximum_fusion.6), calls=%async_computation.8 | async-start | bytes 557056 | tf_op jit(solution)/shard_map/all_to_all | solution.py:213
  192.8 14.5 %all-to-all-start.9 = ((bf16[8,8,4352]{2,1,0:T(8,128)(2,1)}), bf16[8,8,4352]{2,1,0:T(8,128)(2,1)S(1)}, u32[]{:S(2)}, u32[]{:S(2)}) async-start(bf16[8,8,4352]{2,1,0:T(8,128)(2,1)} %broadcast_in_dim.375), calls=%async_computation.9 | async-start | bytes 1114112 | tf_op jit(solution)/shard_map/all_to_all | solution.py:235
  (80 other events, 222.6 us)

commit v16 on v11

--- a/solution.py
+++ b/solution.py
@@ -187,6 +187,37 @@
     return moved.transpose(2, 0, 3, 1, 4).reshape(height, breadth, channels)
 
 
+def grid_split(image):
+    height, breadth, channels = image.shape
+    rows = lax.axis_size("sy")
+    cols = lax.axis_size("sx")
+    row_part, col_part = height // rows, breadth // cols
+    row_class, col_class = height // WIN, breadth // WIN
+    return rows, cols, row_part, col_part, row_class, col_class
+
+
+def grid_from_home(image):
+    height, breadth, channels = image.shape
+    rows, cols, row_part, col_part, row_class, col_class = grid_split(image)
+    if row_part % row_class or col_part % col_class:
+        return to_grid(to_exchanged(image), WIN)
+    blocks = image.reshape(row_part, rows, col_part, cols, channels)
+    moved = swap_blocks(blocks.transpose(1, 3, 0, 2, 4))
+    moved = moved.reshape(rows, cols, row_part // row_class, row_class, col_part // col_class, col_class, channels)
+    return moved.transpose(3, 5, 0, 2, 1, 4, 6).reshape(row_class * col_class, -1, channels)
+
+
+def grid_to_home(windows, height, breadth):
+    channels = windows.shape[-1]
+    rows, cols, row_part, col_part, row_class, col_class = grid_split(jax.ShapeDtypeStruct((height, breadth, channels), windows.dtype))
+    if row_part % row_class or col_part % col_class:
+        return to_home(from_grid(windows, height, breadth, WIN))
+    parts = windows.reshape(row_class, col_class, rows, row_part // row_class, cols, col_part // col_class, channels)
+    blocks = parts.transpose(2, 4, 3, 0, 5, 1, 6).reshape(rows, cols, row_part, col_part, channels)
+    moved = swap_blocks(blocks)
+    return moved.transpose(2, 0, 3, 1, 4).reshape(height, breadth, channels)
+
+
 def exchange_sum(values, axes, axis):
     moved = lax.all_to_all(values.astype(jnp.bfloat16), axes, split_axis=axis, concat_axis=axis, tiled=True)
     return moved.astype(jnp.float32).sum(axis)
@@ -311,22 +342,22 @@
         return layer_norm(stream_in, gain_in).astype(jnp.bfloat16)
 
     normed_three, grid_front_back = jax.vjp(grid_front, stream_two, gain_grid)
-    grid_windows = to_grid(to_exchanged(normed_three), WIN)
+    grid_windows = grid_from_home(normed_three)
 
     def grid_core(windows_in, tap_in):
         return window_attention(windows_in, grid_inward, tap_in, HEADS)
 
     grid_attended, grid_core_back = jax.vjp(grid_core, grid_windows, zero_qkv)
-    grid_home = to_home(from_grid(grid_attended, height, breadth, WIN))
+    grid_home = grid_to_home(grid_attended, height, breadth)
 
     def grid_tail(stream_in, attended_in, tap_in):
         return (stream_in + project_rows(attended_in, grid_outward) + tap_in).astype(jnp.bfloat16)
 
     output_tile, grid_tail_back = jax.vjp(grid_tail, stream_two, grid_home, zero_width)
     d_stream_two, d_grid_home, tap_grid_out = grid_tail_back(cotangent[0])
-    d_grid_attended = to_grid(to_exchanged(d_grid_home), WIN)
+    d_grid_attended = grid_from_home(d_grid_home)
     d_grid_windows, tap_grid_in = grid_core_back(d_grid_attended)
-    d_normed_three = to_home(from_grid(d_grid_windows, height, breadth, WIN))
+    d_normed_three = grid_to_home(d_grid_windows, height, breadth)
     d_stream_extra, d_gain_grid = grid_front_back(d_normed_three)
     d_stream_two = d_stream_two + d_stream_extra
     d_stream_one, d_gain_block, tap_block_in, tap_block_out = block_back(d_stream_two)

time: 183 us -> 185 us (1.011)
    dot_general x6, matrix products: 5.55 us -> 7.47 us  [window_attention(): jnp.einsum('whqk,wkc->whqc', softmax_out, value_rows, preferred_element_t...]
    unnamed x203 -> x193, local copies, waits for them, and re-layouts: 6.27 us -> 6.26 us
where the time goes in v16:
time: 185 us; the launch traced here: 183 us
  waiting for transfers between devices  57.8 us (31%)
  starting transfers between devices  41.3 us (22%)
  local copies, waits for them, and re-layouts  30.2 us (16%)
  matrix products  25.6 us (14%)
  other arithmetic  25.6 us (14%)
  between operations  2.75 us (1%)
    all_to_all x3, waiting for transfers between devices, exchange_sum(): lax.all_to_all(values.astype(jnp.bfloat16), axes, split_axis=axis, concat...  29.7 us
    all_to_all x4, starting transfers between devices, swap_blocks(): lax.all_to_all(as_sent(flattened), ('sy', 'sx'), split_axis=0, concat_axi...  16.1 us
    all_to_all x2, waiting for transfers between devices, extended_2(): lax.all_to_all(outgoing, ('sy', 'sx'), split_axis=0, concat_axis=0, tiled...  13.1 us
    all_to_all x3, starting transfers between devices, exchange_sum(): lax.all_to_all(values.astype(jnp.bfloat16), axes, split_axis=axis, concat...  12.7 us
    all_to_all x1, waiting for transfers between devices, reduce_packed(): lax.all_to_all(spread, ('sy', 'sx'), split_axis=0, concat_axis=0, tiled=T...  8.89 us
    dot_general x12, matrix products, project_rows(): product = jnp.dot(flattened, weight, preferred_element_type=jnp.float32)  8.33 us
    all_to_all x2, starting transfers between devices, extended_2(): lax.all_to_all(outgoing, ('sy', 'sx'), split_axis=0, concat_axis=0, tiled...  8.13 us
    dot_general x6, matrix products, window_attention(): jnp.einsum('whqk,wkc->whqc', softmax_out, value_rows, preferred_element_t...  7.47 us
  transfers between devices with their start and end apart: 10, of which 8 were waited for; matrix products, arithmetic and copies ran while one was open for 21% of the time, Pallas kernels for 0%

profile of v16, /device:TPU:0, one launch (start us, length us, event | category | flops | bytes accessed | tf_op | source)
XLA Modules:
  0.0 183.2 jit_solution(7510556048628030116)
XLA Ops:
  2.7 5.2 %all-to-all-start.3 = ((bf16[8,8,4,256]{3,1,2,0:T(8,128)(2,1)}), bf16[8,8,4,256]{3,1,2,0:T(8,128)(2,1)S(1)}, u32[]{:S(2)}, u32[]{:S(2)}) async-start(bf16[8,8,4,256]{3,1,2,0:T(8,128)(2,1)} %bitcast.54), calls=%async_computation.3 | async-start | bytes 262144 | tf_op jit(solution)/shard_map/all_to_all | solution.py:166
  10.0 2.4 %multiply_convert_fusion.1 = (bf16[16,16,1024]{2,1,0:T(8,128)(2,1)S(1)}, f32[16,16,1024]{2,1,0:T(8,128)}) fusion(bf16[256,1024]{1,0:T(8,128)(2,1)S(1)} %copy-done, bf16[1,16,16,256]{3,2,1,0:T(8,128)(2,1)} %param.12, f32[256]{0:T(256)} %param.14, f32[16,16]{1,0:T(8,128)S(1)} %fusion.192, f32[16,16]{1,0:T(8,128)S(1)} %broadcast_multiply_fusion.2), kind=kOutput, calls=%fused_computation.150 | convolution fusion | flops 136904704 | bytes 2231296 | tf_op jit(solution)/shard_map/jvp()/dot_general | solution.py:78
  14.0 4.2 %all-to-all-start = ((bf16[8,16,1024]{2,1,0:T(8,128)(2,1)}), bf16[8,16,1024]{2,1,0:T(8,128)(2,1)S(1)}, u32[]{:S(2)}, u32[]{:S(2)}) async-start(bf16[8,16,1024]{2,1,0:T(8,128)(2,1)} %select_select_fusion.1), calls=%async_computation | async-start | bytes 524288 | tf_op jit(solution)/shard_map/all_to_all | solution.py:49
  20.3 4.8 %all-to-all-done = bf16[8,16,1024]{2,1,0:T(8,128)(2,1)S(1)} async-done(((bf16[8,16,1024]{2,1,0:T(8,128)(2,1)}), bf16[8,16,1024]{2,1,0:T(8,128)(2,1)S(1)}, u32[]{:S(2)}, u32[]{:S(2)}) %all-to-all-start) | async-done | bytes 262176 | tf_op jit(solution)/shard_map/all_to_all | solution.py:49
  29.1 1.7 fusion.207
  34.4 3.4 %all-to-all-start.1 = ((bf16[8,8,4,256]{3,1,2,0:T(8,128)(2,1)}), bf16[8,8,4,256]{3,1,2,0:T(8,128)(2,1)S(1)}, u32[]{:S(2)}, u32[]{:S(2)}) async-start(bf16[8,8,4,256]{3,1,2,0:T(8,128)(2,1)} %bitcast.39), calls=%async_computation.1 | async-start | bytes 262144 | tf_op jit(solution)/shard_map/all_to_all | solution.py:166
  38.4 4.8 %all-to-all-done.1 = bf16[8,8,4,256]{3,1,2,0:T(8,128)(2,1)S(1)} async-done(((bf16[8,8,4,256]{3,1,2,0:T(8,128)(2,1)}), bf16[8,8,4,256]{3,1,2,0:T(8,128)(2,1)S(1)}, u32[]{:S(2)}, u32[]{:S(2)}) %all-to-all-start.1) | async-done | bytes 131104 | tf_op jit(solution)/shard_map/all_to_all | solution.py:166
  45.6 2.6 %fusion.211 = (f32[4,8,64]{2,1,0:T(8,128)S(1)}, f32[4,8,64,64]{2,3,1,0:T(8,128)}) fusion(bf16[4,64,256]{2,1,0:T(8,128)(2,1)S(1)} %slice.343, bf16[8,256]{1,0:T(8,128)(2,1)S(1)} %get-tuple-element.135, bf16[4,64,768]{2,1,0:T(8,128)(2,1)} %copy-done.16), kind=kOutput, calls=%fused_computation.358 | convolution fusion | flops 68026432 | bytes 798720 | tf_op jit(solution)/shard_map/jvp()/sub | solution.py:127
  48.2 2.9 %fusion.74 = (f32[4,8,64]{2,1,0:T(8,128)S(1)}, bf16[4,8,64,64]{2,3,1,0:T(8,128)(2,1)}, bf16[4,8,64,64]{2,3,1,0:T(8,128)(2,1)S(1)}) fusion(f32[4,8,64,64]{2,3,1,0:T(8,128)} %get-tuple-element.147, f32[4,8,64]{2,1,0:T(8,128)S(1)} %multiply_divide_fusion.1, f32[4,8,64]{2,1,0:T(8,128)S(1)} %get-tuple-element.146, bf16[4,64,768]{2,1,0:T(8,128)(2,1)} %copy-done.16, ...), kind=kOutput, calls=%fused_computation.86 | convolution fusion | flops 68548608 | bytes 1998848 | tf_op jit(solution)/shard_map/transpose(jvp(whqk,wkc->whqc))/dot_general | solution.py:128
  58.0 3.4 %all-to-all-start.4 = ((bf16[8,8,4,256]{3,1,2,0:T(8,128)(2,1)}), bf16[8,8,4,256]{3,1,2,0:T(8,128)(2,1)S(1)}, u32[]{:S(2)}, u32[]{:S(2)}) async-start(bf16[8,8,4,256]{3,1,2,0:T(8,128)(2,1)} %reshape_reshape.20), calls=%async_computation.4 | async-start | bytes 262144 | tf_op jit(solution)/shard_map/all_to_all | solution.py:166
  61.4 1.6 multiply_reduce_fusion
  66.8 4.2 %all-to-all-start.2 = ((bf16[8,8,4,256]{3,1,2,0:T(8,128)(2,1)}), bf16[8,8,4,256]{3,1,2,0:T(8,128)(2,1)}, u32[]{:S(2)}, u32[]{:S(2)}) async-start(bf16[8,8,4,256]{3,1,2,0:T(8,128)(2,1)} %reshape_reshape.19), calls=%async_computation.2 | async-start | bytes 262144 | tf_op jit(solution)/shard_map/all_to_all | solution.py:166
  83.3 3.3 %multiply_reduce_fusion.10 = (f32[1024]{0:T(1024)S(1)}, f32[1024]{0:T(1024)S(1)}, f32[1024]{0:T(1024)S(1)}, f32[1024]{0:T(1024)S(1)}, f32[1024]{0:T(1024)S(1)}, ...) fusion(f32[18,18,1024]{2,1,0:T(8,128)S(1)} %convert_element_type., ...), kind=kLoop, calls=%fused_computation.137 | loop fusion | flops 14408704 | bytes 11083776 | tf_op jit(solution)/shard_map/transpose(jvp())/reduce_sum | solution.py:143
  96.9 3.9 %all-to-all-start.5 = ((f32[8,16,1024]{2,1,0:T(8,128)}), f32[8,16,1024]{2,1,0:T(8,128)S(1)}, u32[]{:S(2)}, u32[]{:S(2)}) async-start(f32[8,16,1024]{2,1,0:T(8,128)} %select_select_fusion), calls=%async_computation.5 | async-start | bytes 1048576 | tf_op jit(solution)/shard_map/all_to_all | solution.py:49
  102.3 8.3 %all-to-all-done.5 = f32[8,16,1024]{2,1,0:T(8,128)S(1)} async-done(((f32[8,16,1024]{2,1,0:T(8,128)}), f32[8,16,1024]{2,1,0:T(8,128)S(1)}, u32[]{:S(2)}, u32[]{:S(2)}) %all-to-all-start.5) | async-done | bytes 524320 | tf_op jit(solution)/shard_map/all_to_all | solution.py:49
  110.6 4.2 %all-to-all-start.6 = ((bf16[4,8,8,2176]{3,2,0,1:T(8,128)(2,1)}), bf16[4,8,8,2176]{3,2,0,1:T(8,128)(2,1)}, u32[]{:S(2)}, u32[]{:S(2)}) async-start(bf16[4,8,8,2176]{3,2,0,1:T(8,128)(2,1)} %copy.175), calls=%async_computation.6 | async-start | bytes 2228224 | tf_op jit(solution)/shard_map/all_to_all | solution.py:222
  117.3 1.9 %fusion.81 = bf16[16,16,1024]{2,1,0:T(8,128)(2,1)S(1)} fusion(f32[16,16,1024]{2,1,0:T(8,128)S(1)} %copy-done.13, f32[17,18,1024]{2,1,0:T(8,128)S(1)} %get-tuple-element.82, f32[16,16,1024]{2,1,0:T(8,128)S(1)} %copy-done.2, f32[16,1,1024]{2,1,0:T(1,128)S(1)} %fusion.161, f32[16,1,1024]{2,1,0:T(1,128)S(1)} %fusion.163, ...), kind=kLoop, calls=%fused_computation.93 | loop fusion | flops 10747904 | bytes 9080832 | tf_op jit(solution)/shard_map/transpose(jvp())/add_any | solution.py:309
  121.7 9.3 %all-to-all-done.6 = bf16[4,8,8,2176]{3,2,0,1:T(8,128)(2,1)} async-done(((bf16[4,8,8,2176]{3,2,0,1:T(8,128)(2,1)}), bf16[4,8,8,2176]{3,2,0,1:T(8,128)(2,1)}, u32[]{:S(2)}, u32[]{:S(2)}) %all-to-all-start.6) | async-done | bytes 1114144 | tf_op jit(solution)/shard_map/all_to_all | solution.py:222
  131.0 3.6 %all-to-all-start.7 = ((bf16[4,8,8,2176]{3,2,0,1:T(8,128)(2,1)}), bf16[4,8,8,2176]{3,2,0,1:T(8,128)(2,1)S(1)}, u32[]{:S(2)}, u32[]{:S(2)}) async-start(bf16[4,8,8,2176]{3,2,0,1:T(8,128)(2,1)} %copy.180), calls=%async_computation.7 | async-start | bytes 2228224 | tf_op jit(solution)/shard_map/all_to_all | solution.py:222
  137.0 13.6 %all-to-all-done.7 = bf16[4,8,8,2176]{3,2,0,1:T(8,128)(2,1)S(1)} async-done(((bf16[4,8,8,2176]{3,2,0,1:T(8,128)(2,1)}), bf16[4,8,8,2176]{3,2,0,1:T(8,128)(2,1)S(1)}, u32[]{:S(2)}, u32[]{:S(2)}) %all-to-all-start.7) | async-done | bytes 1114144 | tf_op jit(solution)/shard_map/all_to_all | solution.py:222
  151.5 4.9 %all-to-all-start.8 = ((bf16[4,8,4352]{2,1,0:T(8,128)(2,1)}), bf16[4,8,4352]{2,1,0:T(8,128)(2,1)S(1)}, u32[]{:S(2)}, u32[]{:S(2)}) async-start(bf16[4,8,4352]{2,1,0:T(8,128)(2,1)} %pad_maximum_fusion.5), calls=%async_computation.8 | async-start | bytes 557056 | tf_op jit(solution)/shard_map/all_to_all | solution.py:222
  156.4 6.8 %all-to-all-done.8 = bf16[4,8,4352]{2,1,0:T(8,128)(2,1)S(1)} async-done(((bf16[4,8,4352]{2,1,0:T(8,128)(2,1)}), bf16[4,8,4352]{2,1,0:T(8,128)(2,1)S(1)}, u32[]{:S(2)}, u32[]{:S(2)}) %all-to-all-start.8) | async-done | bytes 278560 | tf_op jit(solution)/shard_map/all_to_all | solution.py:222
  164.1 4.4 %all-to-all-start.9 = ((bf16[8,8,4352]{2,1,0:T(8,128)(2,1)}), bf16[8,8,4352]{2,1,0:T(8,128)(2,1)S(1)}, u32[]{:S(2)}, u32[]{:S(2)}) async-start(bf16[8,8,4352]{2,1,0:T(8,128)(2,1)} %broadcast_in_dim.375), calls=%async_computation.9 | async-start | bytes 1114112 | tf_op jit(solution)/shard_map/all_to_all | solution.py:242
  169.7 8.9 %all-to-all-done.9 = bf16[8,8,4352]{2,1,0:T(8,128)(2,1)S(1)} async-done(((bf16[8,8,4352]{2,1,0:T(8,128)(2,1)}), bf16[8,8,4352]{2,1,0:T(8,128)(2,1)S(1)}, u32[]{:S(2)}, u32[]{:S(2)}) %all-to-all-start.9) | async-done | bytes 557088 | tf_op jit(solution)/shard_map/all_to_all | solution.py:242
  (379 shorter events, 66.3 us)
Async XLA Ops:
  0.6 9.4 %copy-start = (bf16[256,1024]{1,0:T(8,128)(2,1)S(1)}, bf16[256,1024]{1,0:T(8,128)(2,1)}, u32[]{:S(2)}) copy-start(bf16[256,1024]{1,0:T(8,128)(2,1)} %param.15) | copy-start | bytes 1572868
  2.7 11.3 %all-to-all-start.3 = ((bf16[8,8,4,256]{3,1,2,0:T(8,128)(2,1)}), bf16[8,8,4,256]{3,1,2,0:T(8,128)(2,1)S(1)}, u32[]{:S(2)}, u32[]{:S(2)}) async-start(bf16[8,8,4,256]{3,1,2,0:T(8,128)(2,1)} %bitcast.54), calls=%async_computation.3 | async-start | bytes 262144 | tf_op jit(solution)/shard_map/all_to_all | solution.py:166
  12.6 7.7 %copy-start.76 = (pred[8]{0:T(512)(128)(4,1)}, pred[8]{0:T(512)(128)(4,1)S(1)}, u32[]{:S(2)}) copy-start(pred[8]{0:T(512)(128)(4,1)S(1)} %get-tuple-element.153) | copy-start | bytes 28
  13.9 31.6 %copy-start.88 = (bf16[8,256]{1,0:T(8,128)(2,1)}, bf16[8,256]{1,0:T(8,128)(2,1)S(1)}, u32[]{:S(2)}) copy-start(bf16[8,256]{1,0:T(8,128)(2,1)S(1)} %get-tuple-element.135) | copy-start | bytes 12292
  13.9 34.2 %copy-start.70 = (f32[8,256]{1,0:T(8,128)}, f32[8,256]{1,0:T(8,128)S(1)}, u32[]{:S(2)}) copy-start(f32[8,256]{1,0:T(8,128)S(1)} %get-tuple-element.134) | copy-start | bytes 24580
  14.0 11.1 %all-to-all-start = ((bf16[8,16,1024]{2,1,0:T(8,128)(2,1)}), bf16[8,16,1024]{2,1,0:T(8,128)(2,1)S(1)}, u32[]{:S(2)}, u32[]{:S(2)}) async-start(bf16[8,16,1024]{2,1,0:T(8,128)(2,1)} %select_select_fusion.1), calls=%async_computation | async-start | bytes 524288 | tf_op jit(solution)/shard_map/all_to_all | solution.py:49
  19.0 7.3 %copy-start.37 = (f32[1024,1]{0,1:T(1,128)}, f32[1024,1]{0,1:T(1,128)S(1)}, u32[]{:S(2)}) copy-start(f32[1024,1]{0,1:T(1,128)S(1)} %get-tuple-element.125) | copy-start | bytes 12292
  19.0 7.3 %copy-start.39 = (f32[1024,1]{0,1:T(1,128)}, f32[1024,1]{0,1:T(1,128)S(1)}, u32[]{:S(2)}) copy-start(f32[1024,1]{0,1:T(1,128)S(1)} %get-tuple-element.126) | copy-start | bytes 12292
  19.0 7.3 %copy-start.41 = (f32[1024,1]{0,1:T(1,128)}, f32[1024,1]{0,1:T(1,128)S(1)}, u32[]{:S(2)}) copy-start(f32[1024,1]{0,1:T(1,128)S(1)} %get-tuple-element.127) | copy-start | bytes 12292
  19.0 7.3 %copy-start.43 = (f32[1024,1]{0,1:T(1,128)}, f32[1024,1]{0,1:T(1,128)S(1)}, u32[]{:S(2)}) copy-start(f32[1024,1]{0,1:T(1,128)S(1)} %get-tuple-element.128) | copy-start | bytes 12292
  19.0 7.3 %copy-start.45 = (f32[1024,1]{0,1:T(1,128)}, f32[1024,1]{0,1:T(1,128)S(1)}, u32[]{:S(2)}) copy-start(f32[1024,1]{0,1:T(1,128)S(1)} %get-tuple-element.129) | copy-start | bytes 12292
  19.1 7.3 %copy-start.48 = (f32[1024,1]{0,1:T(1,128)}, f32[1024,1]{0,1:T(1,128)S(1)}, u32[]{:S(2)}) copy-start(f32[1024,1]{0,1:T(1,128)S(1)} %get-tuple-element.130) | copy-start | bytes 12292
  19.1 7.3 %copy-start.51 = (f32[1024,1]{0,1:T(1,128)}, f32[1024,1]{0,1:T(1,128)S(1)}, u32[]{:S(2)}) copy-start(f32[1024,1]{0,1:T(1,128)S(1)} %get-tuple-element.131) | copy-start | bytes 12292
  30.8 7.0 %copy-start.54 = (f32[4,8,64]{2,1,0:T(8,128)}, f32[4,8,64]{2,1,0:T(8,128)S(1)}, u32[]{:S(2)}) copy-start(f32[4,8,64]{2,1,0:T(8,128)S(1)} %get-tuple-element.142) | copy-start | bytes 24580
  34.4 8.8 %all-to-all-start.1 = ((bf16[8,8,4,256]{3,1,2,0:T(8,128)(2,1)}), bf16[8,8,4,256]{3,1,2,0:T(8,128)(2,1)S(1)}, u32[]{:S(2)}, u32[]{:S(2)}) async-start(bf16[8,8,4,256]{3,1,2,0:T(8,128)(2,1)} %bitcast.39), calls=%async_computation.1 | async-start | bytes 262144 | tf_op jit(solution)/shard_map/all_to_all | solution.py:166
  58.0 8.8 %all-to-all-start.4 = ((bf16[8,8,4,256]{3,1,2,0:T(8,128)(2,1)}), bf16[8,8,4,256]{3,1,2,0:T(8,128)(2,1)S(1)}, u32[]{:S(2)}, u32[]{:S(2)}) async-start(bf16[8,8,4,256]{3,1,2,0:T(8,128)(2,1)} %reshape_reshape.20), calls=%async_computation.4 | async-start | bytes 262144 | tf_op jit(solution)/shard_map/all_to_all | solution.py:166
  63.0 13.3 %copy-start.9 = (bf16[1,16,16,256]{3,2,1,0:T(8,128)(2,1)S(1)}, bf16[1,16,16,256]{3,2,1,0:T(8,128)(2,1)}, u32[]{:S(2)}) copy-start(bf16[1,16,16,256]{3,2,1,0:T(8,128)(2,1)} %param.13) | copy-start | bytes 393220
  66.8 22.2 %all-to-all-start.2 = ((bf16[8,8,4,256]{3,1,2,0:T(8,128)(2,1)}), bf16[8,8,4,256]{3,1,2,0:T(8,128)(2,1)}, u32[]{:S(2)}, u32[]{:S(2)}) async-start(bf16[8,8,4,256]{3,1,2,0:T(8,128)(2,1)} %reshape_reshape.19), calls=%async_computation.2 | async-start | bytes 262144 | tf_op jit(solution)/shard_map/all_to_all | solution.py:166
  96.9 13.7 %all-to-all-start.5 = ((f32[8,16,1024]{2,1,0:T(8,128)}), f32[8,16,1024]{2,1,0:T(8,128)S(1)}, u32[]{:S(2)}, u32[]{:S(2)}) async-start(f32[8,16,1024]{2,1,0:T(8,128)} %select_select_fusion), calls=%async_computation.5 | async-start | bytes 1048576 | tf_op jit(solution)/shard_map/all_to_all | solution.py:49
  110.6 20.4 %all-to-all-start.6 = ((bf16[4,8,8,2176]{3,2,0,1:T(8,128)(2,1)}), bf16[4,8,8,2176]{3,2,0,1:T(8,128)(2,1)}, u32[]{:S(2)}, u32[]{:S(2)}) async-start(bf16[4,8,8,2176]{3,2,0,1:T(8,128)(2,1)} %copy.175), calls=%async_computation.6 | async-start | bytes 2228224 | tf_op jit(solution)/shard_map/all_to_all | solution.py:222
  121.7 13.0 %copy-start.19 = (bf16[256,256]{1,0:T(8,128)(2,1)S(1)}, bf16[256,256]{1,0:T(8,128)(2,1)}, u32[]{:S(2)}) copy-start(bf16[256,256]{1,0:T(8,128)(2,1)} %param.23) | copy-start | bytes 393220
  131.0 19.6 %all-to-all-start.7 = ((bf16[4,8,8,2176]{3,2,0,1:T(8,128)(2,1)}), bf16[4,8,8,2176]{3,2,0,1:T(8,128)(2,1)S(1)}, u32[]{:S(2)}, u32[]{:S(2)}) async-start(bf16[4,8,8,2176]{3,2,0,1:T(8,128)(2,1)} %copy.180), calls=%async_computation.7 | async-start | bytes 2228224 | tf_op jit(solution)/shard_map/all_to_all | solution.py:222
  151.5 11.8 %all-to-all-start.8 = ((bf16[4,8,4352]{2,1,0:T(8,128)(2,1)}), bf16[4,8,4352]{2,1,0:T(8,128)(2,1)S(1)}, u32[]{:S(2)}, u32[]{:S(2)}) async-start(bf16[4,8,4352]{2,1,0:T(8,128)(2,1)} %pad_maximum_fusion.5), calls=%async_computation.8 | async-start | bytes 557056 | tf_op jit(solution)/shard_map/all_to_all | solution.py:222
  164.1 14.5 %all-to-all-start.9 = ((bf16[8,8,4352]{2,1,0:T(8,128)(2,1)}), bf16[8,8,4352]{2,1,0:T(8,128)(2,1)S(1)}, u32[]{:S(2)}, u32[]{:S(2)}) async-start(bf16[8,8,4352]{2,1,0:T(8,128)(2,1)} %broadcast_in_dim.375), calls=%async_computation.9 | async-start | bytes 1114112 | tf_op jit(solution)/shard_map/all_to_all | solution.py:242
  (78 other events, 201.3 us)
